TPU v7x, 32 devices: a whole 2x2x4 slice. The times are simulated.
32 devices in a mesh: parts: 2 (over y), cols: 4 (over z), rows: 2 (over x), rep: 2 (over core).
Axes of the slice: x: 2, y: 2, z: 4, core: 2. Of those that a mesh axis runs over, the one named last changes fastest.
Arguments:
- sources: float32 [4096, 64], P(('parts', 'rows')), parts along dimension 0, may hold values from -11 to 11
- source_mass: float32 [4096], P(('parts', 'rows')), parts along dimension 0, may hold values from 0.2 to 5
- targets: float32 [4096, 64], P(('parts', 'cols', 'rep')), parts along dimension 0, may hold values from -6 to 6
- target_mass: float32 [4096], P(('parts', 'cols', 'rep')), parts along dimension 0, may hold values from 0.2 to 5
- fate_panel: float32 [4096, 64], P(('parts', 'cols', 'rep')), parts along dimension 0, may hold values from 0 to 1
Outputs:
- f_pot: float32 [4096], P(('parts', 'rows')), parts along dimension 0
- g_pot: float32 [4096], P(('parts', 'cols', 'rep')), parts along dimension 0
- fate_rows: float32 [4096, 64], P(('parts', 'rows', 'cols', 'rep')), parts along dimension 0
There are 2 independent parts, one for each index of `parts`. A program takes and returns all parts, laid end to end along the dimension named above; each array names one. Nothing has to cross between parts.
All inputs are finite; a program needn't handle non-finite values.
Results may differ from a plain program's by a relative error of at most 0.0003.
Values sent between devices are 32-bit elements; how exact they have to be, the bound alone decides.
No kernel may reach another device: no remote copies, remote signals or barrier semaphores. Data moves between devices by JAX's collectives and lax.ppermute only.
A program may use at most 64 MiB of HBM per device.

v0:
```python
import math

import jax
import jax.numpy as jnp
from jax import lax
from jax.sharding import PartitionSpec as P

ITERS = 8


entropic = 0.1
relaxed = 1.0 / 1.1


def pair_cost(lhs_rows, lhs_sq, rhs_rows, rhs_sq):
    products = lax.dot_general(
        lhs_rows,
        rhs_rows,
        (((1,), (1,)), ((), ())),
        precision=lax.Precision.HIGHEST,
        preferred_element_type=jnp.float32,
    )
    return (lhs_sq[:, None] + rhs_sq[None, :] - 2.0 * products) / lhs_rows.shape[1]


def row_potential(maxima, totals):
    whole_peak = lax.pmax(maxima, ("cols", "rep"))
    whole_total = lax.psum(totals * jnp.exp(maxima - whole_peak), ("cols", "rep"))
    return -relaxed * entropic * (whole_peak + jnp.log(whole_total))


def col_potential(maxima, totals):
    whole_peak = lax.pmax(maxima, "rows")
    whole_total = lax.psum(totals * jnp.exp(maxima - whole_peak), "rows")
    return -relaxed * entropic * (whole_peak + jnp.log(whole_total))


def body(sources, source_mass, targets, target_mass, fate_panel):
    src_count = sources.shape[0]
    tgt_count = targets.shape[0]
    feature_dim = sources.shape[1]
    all_sources = src_count * lax.axis_size("rows")
    all_targets = tgt_count * lax.axis_size(("cols", "rep"))
    log_a = jnp.log(source_mass / all_sources)
    log_b = jnp.log(target_mass / all_targets)
    src_sq = jnp.sum(sources * sources, axis=1)
    tgt_sq = jnp.sum(targets * targets, axis=1)
    row_size = math.gcd(src_count, 512)
    block_count = src_count // row_size
    src_blocks = sources.reshape(block_count, row_size, feature_dim)
    sq_blocks = src_sq.reshape(block_count, row_size)
    loga_blocks = log_a.reshape(block_count, row_size)

    def row_scores(packed, g_pot):
        return (
            log_b[None, :]
            + (g_pot[None, :] - pair_cost(packed[0], packed[1], targets, tgt_sq)) / entropic
        )

    g_pot = jnp.zeros((tgt_count,), jnp.float32)
    f_pot = jnp.zeros((src_count,), jnp.float32)
    for iteration in range(ITERS):

        def row_per_block(packed):
            scores = row_scores(packed, g_pot)
            maxima = jnp.max(scores, axis=1)
            return (maxima, jnp.sum(jnp.exp(scores - maxima[:, None]), axis=1))

        maxima, row_totals = lax.map(row_per_block, (src_blocks, sq_blocks))
        maxima, totals = (maxima.reshape(src_count), row_totals.reshape(src_count))
        f_pot = row_potential(maxima, totals)
        f_blocks = f_pot.reshape(block_count, row_size)

        def col_per_block(running, packed):
            scores = (
                packed[2][:, None]
                + (packed[3][:, None] - pair_cost(packed[0], packed[1], targets, tgt_sq)) / entropic
            )
            highest = jnp.maximum(running[0], jnp.max(scores, axis=0))
            totals = running[1] * jnp.exp(running[0] - highest) + jnp.sum(
                jnp.exp(scores - highest[None, :]), axis=0
            )
            return ((highest, totals), None)

        initial = (
            jnp.full((tgt_count,), -jnp.inf, jnp.float32),
            jnp.zeros((tgt_count,), jnp.float32),
        )
        running, unused = lax.scan(
            col_per_block, initial, (src_blocks, sq_blocks, loga_blocks, f_blocks)
        )
        maxima, totals = running
        g_pot = col_potential(maxima, totals)

    def fate_block(packed):
        scores = row_scores(packed, g_pot)
        maxima = jnp.max(scores, axis=1)
        weights = jnp.exp(scores - maxima[:, None])
        totals = jnp.sum(weights, axis=1)
        weighted = jnp.dot(
            weights, fate_panel, precision=lax.Precision.HIGHEST, preferred_element_type=jnp.float32
        )
        return (maxima, totals, weighted)

    maxima, totals, weighted = lax.map(fate_block, (src_blocks, sq_blocks))
    maxima = maxima.reshape(src_count)
    totals = totals.reshape(src_count)
    weighted = weighted.reshape(src_count, fate_panel.shape[1])
    whole_peak = lax.pmax(maxima, ("cols", "rep"))
    factor = jnp.exp(maxima - whole_peak)
    part_weighted, part_total = (
        lax.psum_scatter(
            weighted * factor[:, None], ("cols", "rep"), scatter_dimension=0, tiled=True
        ),
        lax.psum_scatter(totals * factor, ("cols", "rep"), scatter_dimension=0, tiled=True),
    )
    fate_rows = part_weighted / part_total[:, None]
    return (f_pot, g_pot, fate_rows)


def solution(mesh):
    in_specs = (
        P(("parts", "rows"), None),
        P(("parts", "rows")),
        P(("parts", "cols", "rep"), None),
        P(("parts", "cols", "rep")),
        P(("parts", "cols", "rep"), None),
    )
    out_specs = (
        P(("parts", "rows")),
        P(("parts", "cols", "rep")),
        P(("parts", "rows", "cols", "rep"), None),
    )
    return jax.shard_map(body, mesh=mesh, in_specs=in_specs, out_specs=out_specs, check_vma=False)
```

profile of v0, /device:TPU:0, one launch (start us, length us, event | category | flops | bytes accessed | tf_op | source)
XLA Modules:
  0.0 399.3 jit_solution(12835680924114328844)
XLA Ops:
  9.4 1.9 while.214
  11.3 18.1 %pmax.119 = f32[1024]{0:T(1024)S(1)} all-reduce(f32[1024]{0:T(1024)S(1)} %bitcast.428), channel_id=1, replica_groups=mesh['parts'=2,'cols'=4,'rows'=2,'rep'=2] {'cols','rep'}, use_global_device_ids=true, to_apply=%region_6.7 | all-reduce | flops 1024 | bytes 8192 | tf_op jit(solution)/shard_map/pmax | solution.py:27
  29.5 13.6 %psum.112 = f32[1024]{0:T(1024)S(1)} all-reduce(f32[1024]{0:T(1024)S(1)} %exponential_multiply_fusion.7), channel_id=1, replica_groups=mesh['parts'=2,'cols'=4,'rows'=2,'rep'=2] {'cols','rep'}, use_global_device_ids=true, to_apply=%region_7.8 | all-reduce | flops 1024 | bytes 8192 | tf_op jit(solution)/shard_map/psum | solution.py:28
  43.1 1.7 while.223
  44.8 4.9 %pmax.120 = f32[256]{0:T(256)S(1)} all-reduce(f32[256]{0:T(256)S(1)} %get-tuple-element.827), channel_id=1, replica_groups=mesh['parts'=2,'cols'=4,'rows'=2,'rep'=2] {'rows'}, use_global_device_ids=true, to_apply=%region_12.13 | all-reduce | flops 256 | bytes 2048 | tf_op jit(solution)/shard_map/pmax | solution.py:33
  49.7 4.9 %psum.113 = f32[256]{0:T(256)S(1)} all-reduce(f32[256]{0:T(256)S(1)} %exponential_multiply_fusion.15), channel_id=1, replica_groups=mesh['parts'=2,'cols'=4,'rows'=2,'rep'=2] {'rows'}, use_global_device_ids=true, to_apply=%region_13.14 | all-reduce | flops 256 | bytes 2048 | tf_op jit(solution)/shard_map/psum | solution.py:34
  54.7 1.9 while.215
  56.6 13.6 %pmax.121 = f32[1024]{0:T(1024)S(1)} all-reduce(f32[1024]{0:T(1024)S(1)} %bitcast.430), channel_id=1, replica_groups=mesh['parts'=2,'cols'=4,'rows'=2,'rep'=2] {'cols','rep'}, use_global_device_ids=true, to_apply=%region_18.19 | all-reduce | flops 1024 | bytes 8192 | tf_op jit(solution)/shard_map/pmax | solution.py:27
  70.2 13.6 %psum.114 = f32[1024]{0:T(1024)S(1)} all-reduce(f32[1024]{0:T(1024)S(1)} %exponential_multiply_fusion.6), channel_id=1, replica_groups=mesh['parts'=2,'cols'=4,'rows'=2,'rep'=2] {'cols','rep'}, use_global_device_ids=true, to_apply=%region_19.20 | all-reduce | flops 1024 | bytes 8192 | tf_op jit(solution)/shard_map/psum | solution.py:28
  83.9 1.7 while.224
  85.6 4.9 %pmax.122 = f32[256]{0:T(256)S(1)} all-reduce(f32[256]{0:T(256)S(1)} %get-tuple-element.831), channel_id=1, replica_groups=mesh['parts'=2,'cols'=4,'rows'=2,'rep'=2] {'rows'}, use_global_device_ids=true, to_apply=%region_24.25 | all-reduce | flops 256 | bytes 2048 | tf_op jit(solution)/shard_map/pmax | solution.py:33
  90.5 4.9 %psum.115 = f32[256]{0:T(256)S(1)} all-reduce(f32[256]{0:T(256)S(1)} %exponential_multiply_fusion.14), channel_id=1, replica_groups=mesh['parts'=2,'cols'=4,'rows'=2,'rep'=2] {'rows'}, use_global_device_ids=true, to_apply=%region_25.26 | all-reduce | flops 256 | bytes 2048 | tf_op jit(solution)/shard_map/psum | solution.py:34
  95.5 1.9 while.216
  97.4 13.6 %pmax.123 = f32[1024]{0:T(1024)S(1)} all-reduce(f32[1024]{0:T(1024)S(1)} %bitcast.432), channel_id=1, replica_groups=mesh['parts'=2,'cols'=4,'rows'=2,'rep'=2] {'cols','rep'}, use_global_device_ids=true, to_apply=%region_30.31 | all-reduce | flops 1024 | bytes 8192 | tf_op jit(solution)/shard_map/pmax | solution.py:27
  111.0 13.6 %psum.116 = f32[1024]{0:T(1024)S(1)} all-reduce(f32[1024]{0:T(1024)S(1)} %exponential_multiply_fusion.5), channel_id=1, replica_groups=mesh['parts'=2,'cols'=4,'rows'=2,'rep'=2] {'cols','rep'}, use_global_device_ids=true, to_apply=%region_31.32 | all-reduce | flops 1024 | bytes 8192 | tf_op jit(solution)/shard_map/psum | solution.py:28
  126.4 4.9 %pmax.124 = f32[256]{0:T(256)S(1)} all-reduce(f32[256]{0:T(256)S(1)} %get-tuple-element.835), channel_id=1, replica_groups=mesh['parts'=2,'cols'=4,'rows'=2,'rep'=2] {'rows'}, use_global_device_ids=true, to_apply=%region_36.37 | all-reduce | flops 256 | bytes 2048 | tf_op jit(solution)/shard_map/pmax | solution.py:33
  131.3 4.9 %psum.117 = f32[256]{0:T(256)S(1)} all-reduce(f32[256]{0:T(256)S(1)} %exponential_multiply_fusion.13), channel_id=1, replica_groups=mesh['parts'=2,'cols'=4,'rows'=2,'rep'=2] {'rows'}, use_global_device_ids=true, to_apply=%region_37.38 | all-reduce | flops 256 | bytes 2048 | tf_op jit(solution)/shard_map/psum | solution.py:34
  136.3 1.9 while.217
  138.2 13.6 %pmax.125 = f32[1024]{0:T(1024)S(1)} all-reduce(f32[1024]{0:T(1024)S(1)} %bitcast.434), channel_id=1, replica_groups=mesh['parts'=2,'cols'=4,'rows'=2,'rep'=2] {'cols','rep'}, use_global_device_ids=true, to_apply=%region_42.43 | all-reduce | flops 1024 | bytes 8192 | tf_op jit(solution)/shard_map/pmax | solution.py:27
  151.8 13.6 %psum.118 = f32[1024]{0:T(1024)S(1)} all-reduce(f32[1024]{0:T(1024)S(1)} %exponential_multiply_fusion.4), channel_id=1, replica_groups=mesh['parts'=2,'cols'=4,'rows'=2,'rep'=2] {'cols','rep'}, use_global_device_ids=true, to_apply=%region_43.44 | all-reduce | flops 1024 | bytes 8192 | tf_op jit(solution)/shard_map/psum | solution.py:28
  165.5 1.7 while.226
  167.2 4.9 %pmax.126 = f32[256]{0:T(256)S(1)} all-reduce(f32[256]{0:T(256)S(1)} %get-tuple-element.839), channel_id=1, replica_groups=mesh['parts'=2,'cols'=4,'rows'=2,'rep'=2] {'rows'}, use_global_device_ids=true, to_apply=%region_48.49 | all-reduce | flops 256 | bytes 2048 | tf_op jit(solution)/shard_map/pmax | solution.py:33
  172.1 4.9 %psum.119 = f32[256]{0:T(256)S(1)} all-reduce(f32[256]{0:T(256)S(1)} %exponential_multiply_fusion.12), channel_id=1, replica_groups=mesh['parts'=2,'cols'=4,'rows'=2,'rep'=2] {'rows'}, use_global_device_ids=true, to_apply=%region_49.50 | all-reduce | flops 256 | bytes 2048 | tf_op jit(solution)/shard_map/psum | solution.py:34
  177.1 1.9 while.218
  179.0 13.6 %pmax.127 = f32[1024]{0:T(1024)S(1)} all-reduce(f32[1024]{0:T(1024)S(1)} %bitcast.436), channel_id=1, replica_groups=mesh['parts'=2,'cols'=4,'rows'=2,'rep'=2] {'cols','rep'}, use_global_device_ids=true, to_apply=%region_54.55 | all-reduce | flops 1024 | bytes 8192 | tf_op jit(solution)/shard_map/pmax | solution.py:27
  192.6 13.6 %psum.120 = f32[1024]{0:T(1024)S(1)} all-reduce(f32[1024]{0:T(1024)S(1)} %exponential_multiply_fusion.3), channel_id=1, replica_groups=mesh['parts'=2,'cols'=4,'rows'=2,'rep'=2] {'cols','rep'}, use_global_device_ids=true, to_apply=%region_55.56 | all-reduce | flops 1024 | bytes 8192 | tf_op jit(solution)/shard_map/psum | solution.py:28
  208.0 4.9 %pmax.128 = f32[256]{0:T(256)S(1)} all-reduce(f32[256]{0:T(256)S(1)} %get-tuple-element.843), channel_id=1, replica_groups=mesh['parts'=2,'cols'=4,'rows'=2,'rep'=2] {'rows'}, use_global_device_ids=true, to_apply=%region_60.61 | all-reduce | flops 256 | bytes 2048 | tf_op jit(solution)/shard_map/pmax | solution.py:33
  212.9 5.1 %psum.121 = f32[256]{0:T(256)S(1)} all-reduce(f32[256]{0:T(256)S(1)} %exponential_multiply_fusion.11), channel_id=1, replica_groups=mesh['parts'=2,'cols'=4,'rows'=2,'rep'=2] {'rows'}, use_global_device_ids=true, to_apply=%region_61.62 | all-reduce | flops 256 | bytes 2048 | tf_op jit(solution)/shard_map/psum | solution.py:34
  218.0 1.9 while.219
  220.0 13.6 %pmax.129 = f32[1024]{0:T(1024)S(1)} all-reduce(f32[1024]{0:T(1024)S(1)} %bitcast.438), channel_id=1, replica_groups=mesh['parts'=2,'cols'=4,'rows'=2,'rep'=2] {'cols','rep'}, use_global_device_ids=true, to_apply=%region_66.67 | all-reduce | flops 1024 | bytes 8192 | tf_op jit(solution)/shard_map/pmax | solution.py:27
  233.6 13.6 %psum.122 = f32[1024]{0:T(1024)S(1)} all-reduce(f32[1024]{0:T(1024)S(1)} %exponential_multiply_fusion.2), channel_id=1, replica_groups=mesh['parts'=2,'cols'=4,'rows'=2,'rep'=2] {'cols','rep'}, use_global_device_ids=true, to_apply=%region_67.68 | all-reduce | flops 1024 | bytes 8192 | tf_op jit(solution)/shard_map/psum | solution.py:28
  248.9 4.9 %pmax.130 = f32[256]{0:T(256)S(1)} all-reduce(f32[256]{0:T(256)S(1)} %get-tuple-element.847), channel_id=1, replica_groups=mesh['parts'=2,'cols'=4,'rows'=2,'rep'=2] {'rows'}, use_global_device_ids=true, to_apply=%region_72.73 | all-reduce | flops 256 | bytes 2048 | tf_op jit(solution)/shard_map/pmax | solution.py:33
  253.9 4.9 %psum.123 = f32[256]{0:T(256)S(1)} all-reduce(f32[256]{0:T(256)S(1)} %exponential_multiply_fusion.10), channel_id=1, replica_groups=mesh['parts'=2,'cols'=4,'rows'=2,'rep'=2] {'rows'}, use_global_device_ids=true, to_apply=%region_73.74 | all-reduce | flops 256 | bytes 2048 | tf_op jit(solution)/shard_map/psum | solution.py:34
  258.8 1.9 while.220
  260.8 13.6 %pmax.131 = f32[1024]{0:T(1024)S(1)} all-reduce(f32[1024]{0:T(1024)S(1)} %bitcast.440), channel_id=1, replica_groups=mesh['parts'=2,'cols'=4,'rows'=2,'rep'=2] {'cols','rep'}, use_global_device_ids=true, to_apply=%region_78.79 | all-reduce | flops 1024 | bytes 8192 | tf_op jit(solution)/shard_map/pmax | solution.py:27
  274.4 13.6 %psum.124 = f32[1024]{0:T(1024)S(1)} all-reduce(f32[1024]{0:T(1024)S(1)} %exponential_multiply_fusion.1), channel_id=1, replica_groups=mesh['parts'=2,'cols'=4,'rows'=2,'rep'=2] {'cols','rep'}, use_global_device_ids=true, to_apply=%region_79.80 | all-reduce | flops 1024 | bytes 8192 | tf_op jit(solution)/shard_map/psum | solution.py:28
  288.0 1.7 while.229
  289.7 4.9 %pmax.132 = f32[256]{0:T(256)S(1)} all-reduce(f32[256]{0:T(256)S(1)} %get-tuple-element.851), channel_id=1, replica_groups=mesh['parts'=2,'cols'=4,'rows'=2,'rep'=2] {'rows'}, use_global_device_ids=true, to_apply=%region_84.85 | all-reduce | flops 256 | bytes 2048 | tf_op jit(solution)/shard_map/pmax | solution.py:33
  294.7 4.9 %psum.125 = f32[256]{0:T(256)S(1)} all-reduce(f32[256]{0:T(256)S(1)} %exponential_multiply_fusion.9), channel_id=1, replica_groups=mesh['parts'=2,'cols'=4,'rows'=2,'rep'=2] {'rows'}, use_global_device_ids=true, to_apply=%region_85.86 | all-reduce | flops 256 | bytes 2048 | tf_op jit(solution)/shard_map/psum | solution.py:34
  299.6 1.9 while.221
  301.6 13.6 %pmax.133 = f32[1024]{0:T(1024)S(1)} all-reduce(f32[1024]{0:T(1024)S(1)} %bitcast.442), channel_id=1, replica_groups=mesh['parts'=2,'cols'=4,'rows'=2,'rep'=2] {'cols','rep'}, use_global_device_ids=true, to_apply=%region_90.91 | all-reduce | flops 1024 | bytes 8192 | tf_op jit(solution)/shard_map/pmax | solution.py:27
  315.2 13.6 %psum.126 = f32[1024]{0:T(1024)S(1)} all-reduce(f32[1024]{0:T(1024)S(1)} %exponential_multiply_fusion), channel_id=1, replica_groups=mesh['parts'=2,'cols'=4,'rows'=2,'rep'=2] {'cols','rep'}, use_global_device_ids=true, to_apply=%region_91.92 | all-reduce | flops 1024 | bytes 8192 | tf_op jit(solution)/shard_map/psum | solution.py:28
  331.1 4.9 %pmax.134 = f32[256]{0:T(256)S(1)} all-reduce(f32[256]{0:T(256)S(1)} %get-tuple-element.855), channel_id=1, replica_groups=mesh['parts'=2,'cols'=4,'rows'=2,'rep'=2] {'rows'}, use_global_device_ids=true, to_apply=%region_96.97 | all-reduce | flops 256 | bytes 2048 | tf_op jit(solution)/shard_map/pmax | solution.py:33
  336.0 4.9 %psum.127 = f32[256]{0:T(256)S(1)} all-reduce(f32[256]{0:T(256)S(1)} %exponential_multiply_fusion.8), channel_id=1, replica_groups=mesh['parts'=2,'cols'=4,'rows'=2,'rep'=2] {'rows'}, use_global_device_ids=true, to_apply=%region_97.98 | all-reduce | flops 256 | bytes 2048 | tf_op jit(solution)/shard_map/psum | solution.py:34
  341.0 5.7 %while.222 = (s32[]{:T(128)}, f32[2,512]{1,0:T(2,128)S(1)}, f32[2,512]{1,0:T(2,128)S(1)}, f32[2,512,64]{1,0,2:T(2,128)S(1)}, f32[256]{0:T(256)S(1)}, /*index=5*/...) while((s32[]{:T(128)}, f32[2,512]{1,0:T(2,128)S(1)}, ...), condition=%wide.region_101.102_spmd, body=%wide.region_98.101_spmd.sunk | while | flops 202767360 | bytes 2647193 | solution.py:105
  347.3 13.6 %pmax.135 = f32[1024]{0:T(1024)S(1)} all-reduce(f32[1024]{0:T(1024)S(1)} %bitcast.426), channel_id=1, replica_groups=mesh['parts'=2,'cols'=4,'rows'=2,'rep'=2] {'cols','rep'}, use_global_device_ids=true, to_apply=%region_102.103 | all-reduce | flops 1024 | bytes 8192 | tf_op jit(solution)/shard_map/pmax | solution.py:109
  363.6 13.7 %all-reduce = f32[1024]{0:T(1024)S(1)} all-reduce(f32[1024]{0:T(1024)S(1)} %get-tuple-element.1408), channel_id=3, replica_groups=mesh['parts'=2,'cols'=4,'rows'=2,'rep'=2] {'cols','rep'}, use_global_device_ids=true, to_apply=%region_104.105.clone | all-reduce | flops 1024 | bytes 8192
  377.3 13.7 %reduce-scatter.2.cloned.1.call-done = f32[128,64]{0,1:T(8,128)} async-done(((f32[1024,64]{0,1:T(8,128)}), f32[128,64]{0,1:T(8,128)}) %reduce-scatter.2.cloned.1.call-update) | async-done | bytes 32784 | tf_op jit(solution)/shard_map/reduce_scatter | solution.py:112
  (336 shorter events, 47.6 us)
Async XLA Ops:
  7.2 1.2 copy-start.1
  7.2 383.9 %reduce-scatter.2.cloned.1.call-start = ((), (), s32[]{:S(2)}) async-start(), calls=%async_computation.1 | async-start | bytes 294912 | tf_op jit(solution)/shard_map/reduce_scatter | solution.py:112
  8.4 1.0 copy-start.2
  8.6 0.7 copy-start.4
  8.6 0.7 copy-start.6
  328.8 0.6 copy-start.3
  329.4 11.6 %copy-start = (f32[256,64]{0,1:T(8,128)S(1)}, f32[256,64]{0,1:T(8,128)}, u32[]{:S(2)}) copy-start(f32[256,64]{0,1:T(8,128)} %param.43) | copy-start | bytes 196612
  346.7 0.6 copy-start.5
  361.7 0.7 copy-start.7
Sparse Core Ops, SparseCore 0:
  361.8 29.2 reduce-scatter.1
where the time goes:
time: 400 us; the launch traced here: 399 us
  blocking collectives  328 us (82%)
  matrix products  24.7 us (6%)
  between operations  15.2 us (4%)
  waiting for transfers between devices  13.8 us (3%)
  local copies, waits for them, and re-layouts  8.2 us (2%)
  other arithmetic  7.79 us (2%)
    pmax x8, blocking collectives, row_potential(): whole_peak = lax.pmax(maxima, ('cols', 'rep'))  113 us
    psum x8, blocking collectives, row_potential(): lax.psum(totals * jnp.exp(maxima - whole_peak), ('cols', 'rep'))  109 us
    psum x8, blocking collectives, col_potential(): whole_total = lax.psum(totals * jnp.exp(maxima - whole_peak), 'rows')  39.5 us
    pmax x8, blocking collectives, col_potential(): whole_peak = lax.pmax(maxima, 'rows')  39.5 us
    dot_general x34, matrix products, pair_cost(): lax.dot_general(lhs_rows, rhs_rows, (((1,), (1,)), ((), ())), precision=l...  23.7 us
    reduce_scatter x1, waiting for transfers between devices, body(): lax.psum_scatter(weighted * factor[:, None], ('cols', 'rep'), scatter_dim...  13.7 us
    unnamed x1, blocking collectives  13.7 us
    pmax x1, blocking collectives, body(): whole_peak = lax.pmax(maxima, ('cols', 'rep'))  13.6 us
  transfers between devices with their start and end apart: 1, of which 1 were waited for; matrix products, arithmetic and copies ran while one was open for 0% of the time, Pallas kernels for 0%

commit v1 on v0

v1 whole, which is shorter than its diff:
```python
import jax
import jax.numpy as jnp
from jax import lax
from jax.sharding import PartitionSpec as P

ITERS = 8


entropic = 0.1
relaxed = 1.0 / 1.1


def pair_cost(lhs_rows, lhs_sq, rhs_rows, rhs_sq):
    products = lax.dot_general(
        lhs_rows,
        rhs_rows,
        (((1,), (1,)), ((), ())),
        precision=lax.Precision.HIGHEST,
        preferred_element_type=jnp.float32,
    )
    return (lhs_sq[:, None] + rhs_sq[None, :] - 2.0 * products) / lhs_rows.shape[1]


def is_pow2(n):
    return n > 0 and (n & (n - 1)) == 0


def merge(m_one, s_one, m_two, s_two):
    top = jnp.maximum(m_one, m_two)
    return top, s_one * jnp.exp(m_one - top) + s_two * jnp.exp(m_two - top)


def lse_allreduce(maxima, totals, axes):
    if not all(is_pow2(lax.axis_size(name)) for name in axes):
        peak = lax.pmax(maxima, axes)
        return peak, lax.psum(totals * jnp.exp(maxima - peak), axes)
    for name in axes:
        size = lax.axis_size(name)
        index = lax.axis_index(name)
        step = 1
        while step < size:
            perm = [(i, i ^ step) for i in range(size)]
            other = lax.ppermute(jnp.stack([maxima, totals]), name, perm)
            other_m, other_s = other[0], other[1]
            low = (index & step) == 0
            lo_m = jnp.where(low, maxima, other_m)
            hi_m = jnp.where(low, other_m, maxima)
            lo_s = jnp.where(low, totals, other_s)
            hi_s = jnp.where(low, other_s, totals)
            maxima, totals = merge(lo_m, lo_s, hi_m, hi_s)
            step *= 2
    return maxima, totals


def lse_halving(maxima, totals, weighted, dims):
    for name, step in dims:
        size = lax.axis_size(name)
        perm = [(i, i ^ step) for i in range(size)]
        high = (lax.axis_index(name) & step) != 0

        def split(x):
            lower = lax.index_in_dim(x, 0, axis=0, keepdims=False)
            upper = lax.index_in_dim(x, 1, axis=0, keepdims=False)
            return jnp.where(high, upper, lower), jnp.where(high, lower, upper)

        keep_m, send_m = split(maxima)
        keep_s, send_s = split(totals)
        keep_w, send_w = split(weighted)
        packed = jnp.concatenate([send_w, send_m[..., None], send_s[..., None]], axis=-1)
        packed = lax.ppermute(packed, name, perm)
        fates = weighted.shape[-1]
        recv_w, recv_m, recv_s = packed[..., :fates], packed[..., fates], packed[..., fates + 1]
        top = jnp.maximum(keep_m, recv_m)
        keep_f = jnp.exp(keep_m - top)
        recv_f = jnp.exp(recv_m - top)
        maxima = top
        totals = keep_s * keep_f + recv_s * recv_f
        weighted = keep_w * keep_f[..., None] + recv_w * recv_f[..., None]
    return maxima, totals, weighted


def body(sources, source_mass, targets, target_mass, fate_panel):
    src_count = sources.shape[0]
    tgt_count = targets.shape[0]
    all_sources = src_count * lax.axis_size("rows")
    all_targets = tgt_count * lax.axis_size(("cols", "rep"))
    log_a = jnp.log(source_mass / all_sources)
    log_b = jnp.log(target_mass / all_targets)
    src_sq = jnp.sum(sources * sources, axis=1)
    tgt_sq = jnp.sum(targets * targets, axis=1)
    cost = pair_cost(sources, src_sq, targets, tgt_sq)

    g_pot = jnp.zeros((tgt_count,), jnp.float32)
    f_pot = jnp.zeros((src_count,), jnp.float32)
    for iteration in range(ITERS):
        scores = log_b[None, :] + (g_pot[None, :] - cost) / entropic
        maxima = jnp.max(scores, axis=1)
        totals = jnp.sum(jnp.exp(scores - maxima[:, None]), axis=1)
        peak, whole = lse_allreduce(maxima, totals, ("rep", "cols"))
        f_pot = -relaxed * entropic * (peak + jnp.log(whole))

        scores = log_a[:, None] + (f_pot[:, None] - cost) / entropic
        maxima = jnp.max(scores, axis=0)
        totals = jnp.sum(jnp.exp(scores - maxima[None, :]), axis=0)
        peak, whole = lse_allreduce(maxima, totals, ("rows",))
        g_pot = -relaxed * entropic * (peak + jnp.log(whole))

    scores = log_b[None, :] + (g_pot[None, :] - cost) / entropic
    maxima = jnp.max(scores, axis=1)
    weights = jnp.exp(scores - maxima[:, None])
    totals = jnp.sum(weights, axis=1)
    weighted = jnp.dot(
        weights, fate_panel, precision=lax.Precision.HIGHEST, preferred_element_type=jnp.float32
    )

    col_size = lax.axis_size("cols")
    rep_size = lax.axis_size("rep")
    fates = fate_panel.shape[1]
    if is_pow2(col_size) and is_pow2(rep_size):
        col_bits = col_size.bit_length() - 1
        rep_bits = rep_size.bit_length() - 1
        lead = (2,) * (col_bits + rep_bits)
        block = src_count // (col_size * rep_size)
        maxima = maxima.reshape(lead + (block,))
        totals = totals.reshape(lead + (block,))
        weighted = weighted.reshape(lead + (block, fates))
        order = [("cols", 1 << b) for b in range(col_bits - 1, -1, -1)]
        order += [("rep", 1 << b) for b in range(rep_bits - 1, -1, -1)]
        plan = list(range(len(order) - 1, col_bits - 1, -1)) + list(range(col_bits - 1, -1, -1))
        perm_dims = plan + list(range(len(order), len(order) + 1))
        maxima = jnp.transpose(maxima, perm_dims)
        totals = jnp.transpose(totals, perm_dims)
        weighted = jnp.transpose(weighted, perm_dims + [len(order) + 1])
        maxima, totals, weighted = lse_halving(
            maxima, totals, weighted, [order[d] for d in plan]
        )
        fate_rows = weighted / totals[:, None]
    else:
        whole_peak = lax.pmax(maxima, ("cols", "rep"))
        factor = jnp.exp(maxima - whole_peak)
        part_weighted, part_total = (
            lax.psum_scatter(
                weighted * factor[:, None], ("cols", "rep"), scatter_dimension=0, tiled=True
            ),
            lax.psum_scatter(totals * factor, ("cols", "rep"), scatter_dimension=0, tiled=True),
        )
        fate_rows = part_weighted / part_total[:, None]
    return (f_pot, g_pot, fate_rows)


def solution(mesh):
    in_specs = (
        P(("parts", "rows"), None),
        P(("parts", "rows")),
        P(("parts", "cols", "rep"), None),
        P(("parts", "cols", "rep")),
        P(("parts", "cols", "rep"), None),
    )
    out_specs = (
        P(("parts", "rows")),
        P(("parts", "cols", "rep")),
        P(("parts", "rows", "cols", "rep"), None),
    )
    return jax.shard_map(body, mesh=mesh, in_specs=in_specs, out_specs=out_specs, check_vma=False)
```

time: 400 us -> 137 us (0.34)
  blocking collectives: 328 us -> 0 us
  starting transfers between devices: 0.04 us -> 61.9 us
  waiting for transfers between devices: 13.8 us -> 55.2 us
  matrix products: 24.7 us -> 2.32 us
  between operations: 15.2 us -> 1.44 us
  other arithmetic: 7.79 us -> 14.8 us
  local copies, waits for them, and re-layouts: 8.2 us -> 1.49 us
    pmax x17 -> x0, blocking collectives: 166 us -> none  [the longest x8 113 us: row_potential(): whole_peak = lax.pmax(maxima, ('cols', 'rep'))]
    psum x16 -> x0, blocking collectives: 148 us -> none  [the longest x8 109 us: row_potential(): lax.psum(totals * jnp.exp(maxima - whole_peak), ('cols', 'rep'))]
    ppermute x0 -> x35, starting transfers between devices: none -> 61.9 us  [the longest x32 56.9 us: lse_allreduce(): other = lax.ppermute(jnp.stack([maxima, totals]), name, perm)]
    ppermute x0 -> x35, waiting for transfers between devices: none -> 55.2 us  [the longest x32 49.9 us: lse_allreduce(): other = lax.ppermute(jnp.stack([maxima, totals]), name, perm)]
    dot_general x34 -> x1, matrix products: 23.7 us -> 1.26 us  [pair_cost(): lax.dot_general(lhs_rows, rhs_rows, (((1,), (1,)), ((), ())), precision=l...]
    reduce_scatter x1 -> x0, waiting for transfers between devices: 13.7 us -> none  [body(): lax.psum_scatter(weighted * factor[:, None], ('cols', 'rep'), scatter_dim...]
    unnamed x1 -> x0, blocking collectives: 13.7 us -> none
    dynamic_update_slice x40 -> x0, local copies, waits for them, and re-layouts: 4.15 us -> none  [the longest x4 2.69 us: body(): maxima, totals, weighted = lax.map(fate_block, (src_blocks, sq_blocks))]
  transfers between devices with their start and end apart: 1 -> 35, of which waited for: 1 -> 35; matrix products, arithmetic and copies ran while one was open for 0% -> 0% of each run, Pallas kernels for 0% -> 0%
where the time goes in v1:
time: 137 us
  starting transfers between devices  61.9 us (45%)
  waiting for transfers between devices  55.2 us (40%)
  other arithmetic  14.8 us (11%)
  matrix products  2.32 us (2%)
  local copies, waits for them, and re-layouts  1.49 us (1%)
  between operations  1.44 us (1%)
    ppermute x32, starting transfers between devices, lse_allreduce(): other = lax.ppermute(jnp.stack([maxima, totals]), name, perm)  56.9 us
    ppermute x32, waiting for transfers between devices, lse_allreduce(): other = lax.ppermute(jnp.stack([maxima, totals]), name, perm)  49.9 us
    ppermute x3, waiting for transfers between devices, lse_halving(): packed = lax.ppermute(packed, name, perm)  5.21 us
    ppermute x3, starting transfers between devices, lse_halving(): packed = lax.ppermute(packed, name, perm)  4.96 us
    reduce_sum x8, other arithmetic, body(): totals = jnp.sum(jnp.exp(scores - maxima[None, :]), axis=0)  2.93 us
  transfers between devices with their start and end apart: 35, of which 35 were waited for; matrix products, arithmetic and copies ran while one was open for 0% of the time, Pallas kernels for 0%

profile of v1, /device:TPU:0, one launch (start us, length us, event | category | flops | bytes accessed | tf_op | source)
XLA Modules:
  0.0 137.1 jit_solution(15174074448553244158)
XLA Ops:
  6.3 3.0 %collective-permute-start.1 = (f32[2,1024]{1,0:T(2,128)S(1)}, f32[2,1024]{1,0:T(2,128)S(1)}, u32[]{:S(2)}, u32[]{:S(2)}) collective-permute-start(f32[2,1024]{1,0:T(2,128)S(1)} %pad_maximum_fusion.4), channel_id=1, source_target_pairs={{0,4},{4,0},{8,12},{12,8},{1,5},{5,1},{9,13},{13,9},{2,6},{6,2},{1... | collective-permute-start | bytes 24584 | tf_op jit(solution)/shard_map/ppermute | solution.py:43
  9.3 1.6 %collective-permute-done.1 = f32[2,1024]{1,0:T(2,128)S(1)} collective-permute-done((f32[2,1024]{1,0:T(2,128)S(1)}, f32[2,1024]{1,0:T(2,128)S(1)}, u32[]{:S(2)}, u32[]{:S(2)}) %collective-permute-start.1) | collective-permute-done | bytes 8224 | tf_op jit(solution)/shard_map/ppermute | solution.py:43
  11.0 3.1 %collective-permute-start.2 = (f32[2,1024]{1,0:T(2,128)S(1)}, f32[2,1024]{1,0:T(2,128)S(1)}, u32[]{:S(2)}, u32[]{:S(2)}) collective-permute-start(f32[2,1024]{1,0:T(2,128)S(1)} %pad_maximum_fusion.5), channel_id=1, source_target_pairs={{0,8},{4,12},{8,0},{12,4},{1,9},{5,13},{9,1},{13,5},{2,10},{6,14},... | collective-permute-start | bytes 24584 | tf_op jit(solution)/shard_map/ppermute | solution.py:43
  14.1 1.6 %collective-permute-done.2 = f32[2,1024]{1,0:T(2,128)S(1)} collective-permute-done((f32[2,1024]{1,0:T(2,128)S(1)}, f32[2,1024]{1,0:T(2,128)S(1)}, u32[]{:S(2)}, u32[]{:S(2)}) %collective-permute-start.2) | collective-permute-done | bytes 8224 | tf_op jit(solution)/shard_map/ppermute | solution.py:43
  17.0 1.9 %collective-permute-start.3 = (f32[2,256]{1,0:T(2,128)S(1)}, f32[2,256]{1,0:T(2,128)S(1)}, u32[]{:S(2)}, u32[]{:S(2)}) collective-permute-start(f32[2,256]{1,0:T(2,128)S(1)} %pad_maximum_fusion.27), channel_id=1, source_target_pairs={{0,2},{2,0},{1,3},{3,1},{4,6},{6,4},{5,7},{7,5},{8,10},{10,8},{9,1... | collective-permute-start | bytes 6152 | tf_op jit(solution)/shard_map/ppermute | solution.py:43
  18.9 1.8 %collective-permute-done.3 = f32[2,256]{1,0:T(2,128)S(1)} collective-permute-done((f32[2,256]{1,0:T(2,128)S(1)}, f32[2,256]{1,0:T(2,128)S(1)}, u32[]{:S(2)}, u32[]{:S(2)}) %collective-permute-start.3) | collective-permute-done | bytes 2080 | tf_op jit(solution)/shard_map/ppermute | solution.py:43
  22.6 2.0 %collective-permute-start.5 = (f32[2,1024]{1,0:T(2,128)S(1)}, f32[2,1024]{1,0:T(2,128)S(1)}, u32[]{:S(2)}, u32[]{:S(2)}) collective-permute-start(f32[2,1024]{1,0:T(2,128)S(1)} %pad_maximum_fusion.7), channel_id=1, source_target_pairs={{0,4},{4,0},{8,12},{12,8},{1,5},{5,1},{9,13},{13,9},{2,6},{6,2},{1... | collective-permute-start | bytes 24584 | tf_op jit(solution)/shard_map/ppermute | solution.py:43
  24.5 1.7 %collective-permute-done.5 = f32[2,1024]{1,0:T(2,128)S(1)} collective-permute-done((f32[2,1024]{1,0:T(2,128)S(1)}, f32[2,1024]{1,0:T(2,128)S(1)}, u32[]{:S(2)}, u32[]{:S(2)}) %collective-permute-start.5) | collective-permute-done | bytes 8224 | tf_op jit(solution)/shard_map/ppermute | solution.py:43
  26.3 3.0 %collective-permute-start.6 = (f32[2,1024]{1,0:T(2,128)S(1)}, f32[2,1024]{1,0:T(2,128)S(1)}, u32[]{:S(2)}, u32[]{:S(2)}) collective-permute-start(f32[2,1024]{1,0:T(2,128)S(1)} %pad_maximum_fusion.8), channel_id=1, source_target_pairs={{0,8},{4,12},{8,0},{12,4},{1,9},{5,13},{9,1},{13,5},{2,10},{6,14},... | collective-permute-start | bytes 24584 | tf_op jit(solution)/shard_map/ppermute | solution.py:43
  29.3 1.6 %collective-permute-done.6 = f32[2,1024]{1,0:T(2,128)S(1)} collective-permute-done((f32[2,1024]{1,0:T(2,128)S(1)}, f32[2,1024]{1,0:T(2,128)S(1)}, u32[]{:S(2)}, u32[]{:S(2)}) %collective-permute-start.6) | collective-permute-done | bytes 8224 | tf_op jit(solution)/shard_map/ppermute | solution.py:43
  31.6 1.9 %collective-permute-start.7 = (f32[2,256]{1,0:T(2,128)S(1)}, f32[2,256]{1,0:T(2,128)S(1)}, u32[]{:S(2)}, u32[]{:S(2)}) collective-permute-start(f32[2,256]{1,0:T(2,128)S(1)} %pad_maximum_fusion.28), channel_id=1, source_target_pairs={{0,2},{2,0},{1,3},{3,1},{4,6},{6,4},{5,7},{7,5},{8,10},{10,8},{9,1... | collective-permute-start | bytes 6152 | tf_op jit(solution)/shard_map/ppermute | solution.py:43
  33.5 1.8 %collective-permute-done.7 = f32[2,256]{1,0:T(2,128)S(1)} collective-permute-done((f32[2,256]{1,0:T(2,128)S(1)}, f32[2,256]{1,0:T(2,128)S(1)}, u32[]{:S(2)}, u32[]{:S(2)}) %collective-permute-start.7) | collective-permute-done | bytes 2080 | tf_op jit(solution)/shard_map/ppermute | solution.py:43
  37.1 2.0 %collective-permute-start.9 = (f32[2,1024]{1,0:T(2,128)S(1)}, f32[2,1024]{1,0:T(2,128)S(1)}, u32[]{:S(2)}, u32[]{:S(2)}) collective-permute-start(f32[2,1024]{1,0:T(2,128)S(1)} %pad_maximum_fusion.10), channel_id=1, source_target_pairs={{0,4},{4,0},{8,12},{12,8},{1,5},{5,1},{9,13},{13,9},{2,6},{6,2},{1... | collective-permute-start | bytes 24584 | tf_op jit(solution)/shard_map/ppermute | solution.py:43
  39.1 1.7 %collective-permute-done.9 = f32[2,1024]{1,0:T(2,128)S(1)} collective-permute-done((f32[2,1024]{1,0:T(2,128)S(1)}, f32[2,1024]{1,0:T(2,128)S(1)}, u32[]{:S(2)}, u32[]{:S(2)}) %collective-permute-start.9) | collective-permute-done | bytes 8224 | tf_op jit(solution)/shard_map/ppermute | solution.py:43
  40.9 3.0 %collective-permute-start.10 = (f32[2,1024]{1,0:T(2,128)S(1)}, f32[2,1024]{1,0:T(2,128)S(1)}, u32[]{:S(2)}, u32[]{:S(2)}) collective-permute-start(f32[2,1024]{1,0:T(2,128)S(1)} %pad_maximum_fusion.11), channel_id=1, source_target_pairs={{0,8},{4,12},{8,0},{12,4},{1,9},{5,13},{9,1},{13,5},{2,10},{6,14},... | collective-permute-start | bytes 24584 | tf_op jit(solution)/shard_map/ppermute | solution.py:43
  43.9 1.6 %collective-permute-done.10 = f32[2,1024]{1,0:T(2,128)S(1)} collective-permute-done((f32[2,1024]{1,0:T(2,128)S(1)}, f32[2,1024]{1,0:T(2,128)S(1)}, u32[]{:S(2)}, u32[]{:S(2)}) %collective-permute-start.10) | collective-permute-done | bytes 8224 | tf_op jit(solution)/shard_map/ppermute | solution.py:43
  46.2 1.9 %collective-permute-start.11 = (f32[2,256]{1,0:T(2,128)S(1)}, f32[2,256]{1,0:T(2,128)S(1)}, u32[]{:S(2)}, u32[]{:S(2)}) collective-permute-start(f32[2,256]{1,0:T(2,128)S(1)} %pad_maximum_fusion.29), channel_id=1, source_target_pairs={{0,2},{2,0},{1,3},{3,1},{4,6},{6,4},{5,7},{7,5},{8,10},{10,8},{9,1... | collective-permute-start | bytes 6152 | tf_op jit(solution)/shard_map/ppermute | solution.py:43
  48.0 1.8 %collective-permute-done.11 = f32[2,256]{1,0:T(2,128)S(1)} collective-permute-done((f32[2,256]{1,0:T(2,128)S(1)}, f32[2,256]{1,0:T(2,128)S(1)}, u32[]{:S(2)}, u32[]{:S(2)}) %collective-permute-start.11) | collective-permute-done | bytes 2080 | tf_op jit(solution)/shard_map/ppermute | solution.py:43
  51.7 2.0 %collective-permute-start.13 = (f32[2,1024]{1,0:T(2,128)S(1)}, f32[2,1024]{1,0:T(2,128)S(1)}, u32[]{:S(2)}, u32[]{:S(2)}) collective-permute-start(f32[2,1024]{1,0:T(2,128)S(1)} %pad_maximum_fusion.13), channel_id=1, source_target_pairs={{0,4},{4,0},{8,12},{12,8},{1,5},{5,1},{9,13},{13,9},{2,6},{6,2},{1... | collective-permute-start | bytes 24584 | tf_op jit(solution)/shard_map/ppermute | solution.py:43
  53.7 1.7 %collective-permute-done.13 = f32[2,1024]{1,0:T(2,128)S(1)} collective-permute-done((f32[2,1024]{1,0:T(2,128)S(1)}, f32[2,1024]{1,0:T(2,128)S(1)}, u32[]{:S(2)}, u32[]{:S(2)}) %collective-permute-start.13) | collective-permute-done | bytes 8224 | tf_op jit(solution)/shard_map/ppermute | solution.py:43
  55.5 3.0 %collective-permute-start.14 = (f32[2,1024]{1,0:T(2,128)S(1)}, f32[2,1024]{1,0:T(2,128)S(1)}, u32[]{:S(2)}, u32[]{:S(2)}) collective-permute-start(f32[2,1024]{1,0:T(2,128)S(1)} %pad_maximum_fusion.14), channel_id=1, source_target_pairs={{0,8},{4,12},{8,0},{12,4},{1,9},{5,13},{9,1},{13,5},{2,10},{6,14},... | collective-permute-start | bytes 24584 | tf_op jit(solution)/shard_map/ppermute | solution.py:43
  58.4 1.6 %collective-permute-done.14 = f32[2,1024]{1,0:T(2,128)S(1)} collective-permute-done((f32[2,1024]{1,0:T(2,128)S(1)}, f32[2,1024]{1,0:T(2,128)S(1)}, u32[]{:S(2)}, u32[]{:S(2)}) %collective-permute-start.14) | collective-permute-done | bytes 8224 | tf_op jit(solution)/shard_map/ppermute | solution.py:43
  60.7 1.9 %collective-permute-start.15 = (f32[2,256]{1,0:T(2,128)S(1)}, f32[2,256]{1,0:T(2,128)S(1)}, u32[]{:S(2)}, u32[]{:S(2)}) collective-permute-start(f32[2,256]{1,0:T(2,128)S(1)} %pad_maximum_fusion.30), channel_id=1, source_target_pairs={{0,2},{2,0},{1,3},{3,1},{4,6},{6,4},{5,7},{7,5},{8,10},{10,8},{9,1... | collective-permute-start | bytes 6152 | tf_op jit(solution)/shard_map/ppermute | solution.py:43
  62.6 1.8 %collective-permute-done.15 = f32[2,256]{1,0:T(2,128)S(1)} collective-permute-done((f32[2,256]{1,0:T(2,128)S(1)}, f32[2,256]{1,0:T(2,128)S(1)}, u32[]{:S(2)}, u32[]{:S(2)}) %collective-permute-start.15) | collective-permute-done | bytes 2080 | tf_op jit(solution)/shard_map/ppermute | solution.py:43
  66.3 2.0 %collective-permute-start.17 = (f32[2,1024]{1,0:T(2,128)S(1)}, f32[2,1024]{1,0:T(2,128)S(1)}, u32[]{:S(2)}, u32[]{:S(2)}) collective-permute-start(f32[2,1024]{1,0:T(2,128)S(1)} %pad_maximum_fusion.16), channel_id=1, source_target_pairs={{0,4},{4,0},{8,12},{12,8},{1,5},{5,1},{9,13},{13,9},{2,6},{6,2},{1... | collective-permute-start | bytes 24584 | tf_op jit(solution)/shard_map/ppermute | solution.py:43
  68.2 1.7 %collective-permute-done.17 = f32[2,1024]{1,0:T(2,128)S(1)} collective-permute-done((f32[2,1024]{1,0:T(2,128)S(1)}, f32[2,1024]{1,0:T(2,128)S(1)}, u32[]{:S(2)}, u32[]{:S(2)}) %collective-permute-start.17) | collective-permute-done | bytes 8224 | tf_op jit(solution)/shard_map/ppermute | solution.py:43
  70.0 3.0 %collective-permute-start.18 = (f32[2,1024]{1,0:T(2,128)S(1)}, f32[2,1024]{1,0:T(2,128)S(1)}, u32[]{:S(2)}, u32[]{:S(2)}) collective-permute-start(f32[2,1024]{1,0:T(2,128)S(1)} %pad_maximum_fusion.17), channel_id=1, source_target_pairs={{0,8},{4,12},{8,0},{12,4},{1,9},{5,13},{9,1},{13,5},{2,10},{6,14},... | collective-permute-start | bytes 24584 | tf_op jit(solution)/shard_map/ppermute | solution.py:43
  75.3 1.9 %collective-permute-start.19 = (f32[2,256]{1,0:T(2,128)S(1)}, f32[2,256]{1,0:T(2,128)S(1)}, u32[]{:S(2)}, u32[]{:S(2)}) collective-permute-start(f32[2,256]{1,0:T(2,128)S(1)} %pad_maximum_fusion.31), channel_id=1, source_target_pairs={{0,2},{2,0},{1,3},{3,1},{4,6},{6,4},{5,7},{7,5},{8,10},{10,8},{9,1... | collective-permute-start | bytes 6152 | tf_op jit(solution)/shard_map/ppermute | solution.py:43
  77.2 1.8 %collective-permute-done.19 = f32[2,256]{1,0:T(2,128)S(1)} collective-permute-done((f32[2,256]{1,0:T(2,128)S(1)}, f32[2,256]{1,0:T(2,128)S(1)}, u32[]{:S(2)}, u32[]{:S(2)}) %collective-permute-start.19) | collective-permute-done | bytes 2080 | tf_op jit(solution)/shard_map/ppermute | solution.py:43
  80.8 2.0 %collective-permute-start.21 = (f32[2,1024]{1,0:T(2,128)S(1)}, f32[2,1024]{1,0:T(2,128)S(1)}, u32[]{:S(2)}, u32[]{:S(2)}) collective-permute-start(f32[2,1024]{1,0:T(2,128)S(1)} %pad_maximum_fusion.19), channel_id=1, source_target_pairs={{0,4},{4,0},{8,12},{12,8},{1,5},{5,1},{9,13},{13,9},{2,6},{6,2},{1... | collective-permute-start | bytes 24584 | tf_op jit(solution)/shard_map/ppermute | solution.py:43
  82.8 1.7 %collective-permute-done.21 = f32[2,1024]{1,0:T(2,128)S(1)} collective-permute-done((f32[2,1024]{1,0:T(2,128)S(1)}, f32[2,1024]{1,0:T(2,128)S(1)}, u32[]{:S(2)}, u32[]{:S(2)}) %collective-permute-start.21) | collective-permute-done | bytes 8224 | tf_op jit(solution)/shard_map/ppermute | solution.py:43
  84.6 3.0 %collective-permute-start.22 = (f32[2,1024]{1,0:T(2,128)S(1)}, f32[2,1024]{1,0:T(2,128)S(1)}, u32[]{:S(2)}, u32[]{:S(2)}) collective-permute-start(f32[2,1024]{1,0:T(2,128)S(1)} %pad_maximum_fusion.20), channel_id=1, source_target_pairs={{0,8},{4,12},{8,0},{12,4},{1,9},{5,13},{9,1},{13,5},{2,10},{6,14},... | collective-permute-start | bytes 24584 | tf_op jit(solution)/shard_map/ppermute | solution.py:43
  89.8 1.9 %collective-permute-start.23 = (f32[2,256]{1,0:T(2,128)S(1)}, f32[2,256]{1,0:T(2,128)S(1)}, u32[]{:S(2)}, u32[]{:S(2)}) collective-permute-start(f32[2,256]{1,0:T(2,128)S(1)} %pad_maximum_fusion.32), channel_id=1, source_target_pairs={{0,2},{2,0},{1,3},{3,1},{4,6},{6,4},{5,7},{7,5},{8,10},{10,8},{9,1... | collective-permute-start | bytes 6152 | tf_op jit(solution)/shard_map/ppermute | solution.py:43
  91.7 1.8 %collective-permute-done.23 = f32[2,256]{1,0:T(2,128)S(1)} collective-permute-done((f32[2,256]{1,0:T(2,128)S(1)}, f32[2,256]{1,0:T(2,128)S(1)}, u32[]{:S(2)}, u32[]{:S(2)}) %collective-permute-start.23) | collective-permute-done | bytes 2080 | tf_op jit(solution)/shard_map/ppermute | solution.py:43
  95.4 2.0 %collective-permute-start.25 = (f32[2,1024]{1,0:T(2,128)S(1)}, f32[2,1024]{1,0:T(2,128)S(1)}, u32[]{:S(2)}, u32[]{:S(2)}) collective-permute-start(f32[2,1024]{1,0:T(2,128)S(1)} %pad_maximum_fusion.22), channel_id=1, source_target_pairs={{0,4},{4,0},{8,12},{12,8},{1,5},{5,1},{9,13},{13,9},{2,6},{6,2},{1... | collective-permute-start | bytes 24584 | tf_op jit(solution)/shard_map/ppermute | solution.py:43
  97.4 1.7 %collective-permute-done.25 = f32[2,1024]{1,0:T(2,128)S(1)} collective-permute-done((f32[2,1024]{1,0:T(2,128)S(1)}, f32[2,1024]{1,0:T(2,128)S(1)}, u32[]{:S(2)}, u32[]{:S(2)}) %collective-permute-start.25) | collective-permute-done | bytes 8224 | tf_op jit(solution)/shard_map/ppermute | solution.py:43
  99.1 3.0 %collective-permute-start.26 = (f32[2,1024]{1,0:T(2,128)S(1)}, f32[2,1024]{1,0:T(2,128)S(1)}, u32[]{:S(2)}, u32[]{:S(2)}) collective-permute-start(f32[2,1024]{1,0:T(2,128)S(1)} %pad_maximum_fusion.23), channel_id=1, source_target_pairs={{0,8},{4,12},{8,0},{12,4},{1,9},{5,13},{9,1},{13,5},{2,10},{6,14},... | collective-permute-start | bytes 24584 | tf_op jit(solution)/shard_map/ppermute | solution.py:43
  102.1 1.6 %collective-permute-done.26 = f32[2,1024]{1,0:T(2,128)S(1)} collective-permute-done((f32[2,1024]{1,0:T(2,128)S(1)}, f32[2,1024]{1,0:T(2,128)S(1)}, u32[]{:S(2)}, u32[]{:S(2)}) %collective-permute-start.26) | collective-permute-done | bytes 8224 | tf_op jit(solution)/shard_map/ppermute | solution.py:43
  104.4 1.9 %collective-permute-start.27 = (f32[2,256]{1,0:T(2,128)S(1)}, f32[2,256]{1,0:T(2,128)S(1)}, u32[]{:S(2)}, u32[]{:S(2)}) collective-permute-start(f32[2,256]{1,0:T(2,128)S(1)} %pad_maximum_fusion.33), channel_id=1, source_target_pairs={{0,2},{2,0},{1,3},{3,1},{4,6},{6,4},{5,7},{7,5},{8,10},{10,8},{9,1... | collective-permute-start | bytes 6152 | tf_op jit(solution)/shard_map/ppermute | solution.py:43
  106.3 1.8 %collective-permute-done.27 = f32[2,256]{1,0:T(2,128)S(1)} collective-permute-done((f32[2,256]{1,0:T(2,128)S(1)}, f32[2,256]{1,0:T(2,128)S(1)}, u32[]{:S(2)}, u32[]{:S(2)}) %collective-permute-start.27) | collective-permute-done | bytes 2080 | tf_op jit(solution)/shard_map/ppermute | solution.py:43
  109.9 2.0 %collective-permute-start.29 = (f32[2,1024]{1,0:T(2,128)S(1)}, f32[2,1024]{1,0:T(2,128)S(1)}, u32[]{:S(2)}, u32[]{:S(2)}) collective-permute-start(f32[2,1024]{1,0:T(2,128)S(1)} %pad_maximum_fusion.25), channel_id=1, source_target_pairs={{0,4},{4,0},{8,12},{12,8},{1,5},{5,1},{9,13},{13,9},{2,6},{6,2},{1... | collective-permute-start | bytes 24584 | tf_op jit(solution)/shard_map/ppermute | solution.py:43
  111.9 1.7 %collective-permute-done.29 = f32[2,1024]{1,0:T(2,128)S(1)} collective-permute-done((f32[2,1024]{1,0:T(2,128)S(1)}, f32[2,1024]{1,0:T(2,128)S(1)}, u32[]{:S(2)}, u32[]{:S(2)}) %collective-permute-start.29) | collective-permute-done | bytes 8224 | tf_op jit(solution)/shard_map/ppermute | solution.py:43
  113.7 3.0 %collective-permute-start.30 = (f32[2,1024]{1,0:T(2,128)S(1)}, f32[2,1024]{1,0:T(2,128)S(1)}, u32[]{:S(2)}, u32[]{:S(2)}) collective-permute-start(f32[2,1024]{1,0:T(2,128)S(1)} %pad_maximum_fusion.26), channel_id=1, source_target_pairs={{0,8},{4,12},{8,0},{12,4},{1,9},{5,13},{9,1},{13,5},{2,10},{6,14},... | collective-permute-start | bytes 24584 | tf_op jit(solution)/shard_map/ppermute | solution.py:43
  119.3 1.9 %collective-permute-start.31 = (f32[2,256]{1,0:T(2,128)S(1)}, f32[2,256]{1,0:T(2,128)S(1)}, u32[]{:S(2)}, u32[]{:S(2)}) collective-permute-start(f32[2,256]{1,0:T(2,128)S(1)} %pad_maximum_fusion.34), channel_id=1, source_target_pairs={{0,2},{2,0},{1,3},{3,1},{4,6},{6,4},{5,7},{7,5},{8,10},{10,8},{9,1... | collective-permute-start | bytes 6152 | tf_op jit(solution)/shard_map/ppermute | solution.py:43
  121.2 1.8 %collective-permute-done.31 = f32[2,256]{1,0:T(2,128)S(1)} collective-permute-done((f32[2,256]{1,0:T(2,128)S(1)}, f32[2,256]{1,0:T(2,128)S(1)}, u32[]{:S(2)}, u32[]{:S(2)}) %collective-permute-start.31) | collective-permute-done | bytes 2080 | tf_op jit(solution)/shard_map/ppermute | solution.py:43
  126.9 2.0 %collective-permute-start.33 = (f32[2,128,66]{1,0,2:T(2,128)S(1)}, f32[2,128,66]{1,0,2:T(2,128)S(1)}, u32[]{:S(2)}, u32[]{:S(2)}) collective-permute-start(f32[2,128,66]{1,0,2:T(2,128)S(1)} %pad_maximum_fusion.1), channel_id=1, source_target_pairs={{0,4},{4,0},{8,12},{12,8},{1,5},{5,1},{9,13},{13,9},{2,6},{6,2},{1... | collective-permute-start | bytes 202760 | tf_op jit(solution)/shard_map/ppermute | solution.py:70
  128.9 2.4 %collective-permute-done.33 = f32[2,128,66]{1,0,2:T(2,128)S(1)} collective-permute-done((f32[2,128,66]{1,0,2:T(2,128)S(1)}, f32[2,128,66]{1,0,2:T(2,128)S(1)}, u32[]{:S(2)}, u32[]{:S(2)}) %collective-permute-start.33) | collective-permute-done | bytes 67616 | tf_op jit(solution)/shard_map/ppermute | solution.py:70
  131.5 2.9 %collective-permute-start.34 = (f32[128,66]{0,1:T(8,128)S(1)}, f32[128,66]{0,1:T(8,128)S(1)}, u32[]{:S(2)}, u32[]{:S(2)}) collective-permute-start(f32[128,66]{0,1:T(8,128)S(1)} %pad_maximum_fusion.2), channel_id=1, source_target_pairs={{0,8},{4,12},{8,0},{12,4},{1,9},{5,13},{9,1},{13,5},{2,10},{6,14},... | collective-permute-start | bytes 101384 | tf_op jit(solution)/shard_map/ppermute | solution.py:70
  (171 shorter events, 36.4 us)
Async XLA Ops:
  0.6 122.9 %copy-start = (f32[256,64]{0,1:T(8,128)S(1)}, f32[256,64]{0,1:T(8,128)}, u32[]{:S(2)}) copy-start(f32[256,64]{0,1:T(8,128)} %param.9) | copy-start | bytes 196612
  0.6 2.6 %copy-start.1 = (f32[1024,64]{0,1:T(8,128)S(1)}, f32[1024,64]{0,1:T(8,128)}, u32[]{:S(2)}) copy-start(f32[1024,64]{0,1:T(8,128)} %param.5) | copy-start | bytes 786436
  2.3 1.0 copy-start.2
  4.9 1.4 %collective-permute-start = (f32[2,1024]{1,0:T(2,128)S(1)}, f32[2,1024]{1,0:T(2,128)S(1)}, u32[]{:S(2)}, u32[]{:S(2)}) collective-permute-start(f32[2,1024]{1,0:T(2,128)S(1)} %pad_maximum_fusion.3), channel_id=1, source_target_pairs={{0,1},{1,0},{2,3},{3,2},{4,5},{5,4},{6,7},{7,6},{8,9},{9,8},{10,11... | collective-permute-start | bytes 24584 | tf_op jit(solution)/shard_map/ppermute | solution.py:43
  6.3 4.6 %collective-permute-start.1 = (f32[2,1024]{1,0:T(2,128)S(1)}, f32[2,1024]{1,0:T(2,128)S(1)}, u32[]{:S(2)}, u32[]{:S(2)}) collective-permute-start(f32[2,1024]{1,0:T(2,128)S(1)} %pad_maximum_fusion.4), channel_id=1, source_target_pairs={{0,4},{4,0},{8,12},{12,8},{1,5},{5,1},{9,13},{13,9},{2,6},{6,2},{1... | collective-permute-start | bytes 24584 | tf_op jit(solution)/shard_map/ppermute | solution.py:43
  11.0 4.7 %collective-permute-start.2 = (f32[2,1024]{1,0:T(2,128)S(1)}, f32[2,1024]{1,0:T(2,128)S(1)}, u32[]{:S(2)}, u32[]{:S(2)}) collective-permute-start(f32[2,1024]{1,0:T(2,128)S(1)} %pad_maximum_fusion.5), channel_id=1, source_target_pairs={{0,8},{4,12},{8,0},{12,4},{1,9},{5,13},{9,1},{13,5},{2,10},{6,14},... | collective-permute-start | bytes 24584 | tf_op jit(solution)/shard_map/ppermute | solution.py:43
  15.7 0.7 copy-start.4
  17.0 3.7 %collective-permute-start.3 = (f32[2,256]{1,0:T(2,128)S(1)}, f32[2,256]{1,0:T(2,128)S(1)}, u32[]{:S(2)}, u32[]{:S(2)}) collective-permute-start(f32[2,256]{1,0:T(2,128)S(1)} %pad_maximum_fusion.27), channel_id=1, source_target_pairs={{0,2},{2,0},{1,3},{3,1},{4,6},{6,4},{5,7},{7,5},{8,10},{10,8},{9,1... | collective-permute-start | bytes 6152 | tf_op jit(solution)/shard_map/ppermute | solution.py:43
  21.3 1.2 collective-permute-start.4
  22.6 3.7 %collective-permute-start.5 = (f32[2,1024]{1,0:T(2,128)S(1)}, f32[2,1024]{1,0:T(2,128)S(1)}, u32[]{:S(2)}, u32[]{:S(2)}) collective-permute-start(f32[2,1024]{1,0:T(2,128)S(1)} %pad_maximum_fusion.7), channel_id=1, source_target_pairs={{0,4},{4,0},{8,12},{12,8},{1,5},{5,1},{9,13},{13,9},{2,6},{6,2},{1... | collective-permute-start | bytes 24584 | tf_op jit(solution)/shard_map/ppermute | solution.py:43
  26.3 4.6 %collective-permute-start.6 = (f32[2,1024]{1,0:T(2,128)S(1)}, f32[2,1024]{1,0:T(2,128)S(1)}, u32[]{:S(2)}, u32[]{:S(2)}) collective-permute-start(f32[2,1024]{1,0:T(2,128)S(1)} %pad_maximum_fusion.8), channel_id=1, source_target_pairs={{0,8},{4,12},{8,0},{12,4},{1,9},{5,13},{9,1},{13,5},{2,10},{6,14},... | collective-permute-start | bytes 24584 | tf_op jit(solution)/shard_map/ppermute | solution.py:43
  31.6 3.7 %collective-permute-start.7 = (f32[2,256]{1,0:T(2,128)S(1)}, f32[2,256]{1,0:T(2,128)S(1)}, u32[]{:S(2)}, u32[]{:S(2)}) collective-permute-start(f32[2,256]{1,0:T(2,128)S(1)} %pad_maximum_fusion.28), channel_id=1, source_target_pairs={{0,2},{2,0},{1,3},{3,1},{4,6},{6,4},{5,7},{7,5},{8,10},{10,8},{9,1... | collective-permute-start | bytes 6152 | tf_op jit(solution)/shard_map/ppermute | solution.py:43
  35.8 1.2 collective-permute-start.8
  37.1 3.7 %collective-permute-start.9 = (f32[2,1024]{1,0:T(2,128)S(1)}, f32[2,1024]{1,0:T(2,128)S(1)}, u32[]{:S(2)}, u32[]{:S(2)}) collective-permute-start(f32[2,1024]{1,0:T(2,128)S(1)} %pad_maximum_fusion.10), channel_id=1, source_target_pairs={{0,4},{4,0},{8,12},{12,8},{1,5},{5,1},{9,13},{13,9},{2,6},{6,2},{1... | collective-permute-start | bytes 24584 | tf_op jit(solution)/shard_map/ppermute | solution.py:43
  40.9 4.6 %collective-permute-start.10 = (f32[2,1024]{1,0:T(2,128)S(1)}, f32[2,1024]{1,0:T(2,128)S(1)}, u32[]{:S(2)}, u32[]{:S(2)}) collective-permute-start(f32[2,1024]{1,0:T(2,128)S(1)} %pad_maximum_fusion.11), channel_id=1, source_target_pairs={{0,8},{4,12},{8,0},{12,4},{1,9},{5,13},{9,1},{13,5},{2,10},{6,14},... | collective-permute-start | bytes 24584 | tf_op jit(solution)/shard_map/ppermute | solution.py:43
  46.2 3.7 %collective-permute-start.11 = (f32[2,256]{1,0:T(2,128)S(1)}, f32[2,256]{1,0:T(2,128)S(1)}, u32[]{:S(2)}, u32[]{:S(2)}) collective-permute-start(f32[2,256]{1,0:T(2,128)S(1)} %pad_maximum_fusion.29), channel_id=1, source_target_pairs={{0,2},{2,0},{1,3},{3,1},{4,6},{6,4},{5,7},{7,5},{8,10},{10,8},{9,1... | collective-permute-start | bytes 6152 | tf_op jit(solution)/shard_map/ppermute | solution.py:43
  50.4 1.2 collective-permute-start.12
  51.7 3.7 %collective-permute-start.13 = (f32[2,1024]{1,0:T(2,128)S(1)}, f32[2,1024]{1,0:T(2,128)S(1)}, u32[]{:S(2)}, u32[]{:S(2)}) collective-permute-start(f32[2,1024]{1,0:T(2,128)S(1)} %pad_maximum_fusion.13), channel_id=1, source_target_pairs={{0,4},{4,0},{8,12},{12,8},{1,5},{5,1},{9,13},{13,9},{2,6},{6,2},{1... | collective-permute-start | bytes 24584 | tf_op jit(solution)/shard_map/ppermute | solution.py:43
  55.5 4.6 %collective-permute-start.14 = (f32[2,1024]{1,0:T(2,128)S(1)}, f32[2,1024]{1,0:T(2,128)S(1)}, u32[]{:S(2)}, u32[]{:S(2)}) collective-permute-start(f32[2,1024]{1,0:T(2,128)S(1)} %pad_maximum_fusion.14), channel_id=1, source_target_pairs={{0,8},{4,12},{8,0},{12,4},{1,9},{5,13},{9,1},{13,5},{2,10},{6,14},... | collective-permute-start | bytes 24584 | tf_op jit(solution)/shard_map/ppermute | solution.py:43
  60.7 3.7 %collective-permute-start.15 = (f32[2,256]{1,0:T(2,128)S(1)}, f32[2,256]{1,0:T(2,128)S(1)}, u32[]{:S(2)}, u32[]{:S(2)}) collective-permute-start(f32[2,256]{1,0:T(2,128)S(1)} %pad_maximum_fusion.30), channel_id=1, source_target_pairs={{0,2},{2,0},{1,3},{3,1},{4,6},{6,4},{5,7},{7,5},{8,10},{10,8},{9,1... | collective-permute-start | bytes 6152 | tf_op jit(solution)/shard_map/ppermute | solution.py:43
  65.0 1.2 collective-permute-start.16
  66.3 3.7 %collective-permute-start.17 = (f32[2,1024]{1,0:T(2,128)S(1)}, f32[2,1024]{1,0:T(2,128)S(1)}, u32[]{:S(2)}, u32[]{:S(2)}) collective-permute-start(f32[2,1024]{1,0:T(2,128)S(1)} %pad_maximum_fusion.16), channel_id=1, source_target_pairs={{0,4},{4,0},{8,12},{12,8},{1,5},{5,1},{9,13},{13,9},{2,6},{6,2},{1... | collective-permute-start | bytes 24584 | tf_op jit(solution)/shard_map/ppermute | solution.py:43
  70.0 4.6 %collective-permute-start.18 = (f32[2,1024]{1,0:T(2,128)S(1)}, f32[2,1024]{1,0:T(2,128)S(1)}, u32[]{:S(2)}, u32[]{:S(2)}) collective-permute-start(f32[2,1024]{1,0:T(2,128)S(1)} %pad_maximum_fusion.17), channel_id=1, source_target_pairs={{0,8},{4,12},{8,0},{12,4},{1,9},{5,13},{9,1},{13,5},{2,10},{6,14},... | collective-permute-start | bytes 24584 | tf_op jit(solution)/shard_map/ppermute | solution.py:43
  75.3 3.7 %collective-permute-start.19 = (f32[2,256]{1,0:T(2,128)S(1)}, f32[2,256]{1,0:T(2,128)S(1)}, u32[]{:S(2)}, u32[]{:S(2)}) collective-permute-start(f32[2,256]{1,0:T(2,128)S(1)} %pad_maximum_fusion.31), channel_id=1, source_target_pairs={{0,2},{2,0},{1,3},{3,1},{4,6},{6,4},{5,7},{7,5},{8,10},{10,8},{9,1... | collective-permute-start | bytes 6152 | tf_op jit(solution)/shard_map/ppermute | solution.py:43
  79.5 1.2 collective-permute-start.20
  80.8 3.7 %collective-permute-start.21 = (f32[2,1024]{1,0:T(2,128)S(1)}, f32[2,1024]{1,0:T(2,128)S(1)}, u32[]{:S(2)}, u32[]{:S(2)}) collective-permute-start(f32[2,1024]{1,0:T(2,128)S(1)} %pad_maximum_fusion.19), channel_id=1, source_target_pairs={{0,4},{4,0},{8,12},{12,8},{1,5},{5,1},{9,13},{13,9},{2,6},{6,2},{1... | collective-permute-start | bytes 24584 | tf_op jit(solution)/shard_map/ppermute | solution.py:43
  84.6 4.6 %collective-permute-start.22 = (f32[2,1024]{1,0:T(2,128)S(1)}, f32[2,1024]{1,0:T(2,128)S(1)}, u32[]{:S(2)}, u32[]{:S(2)}) collective-permute-start(f32[2,1024]{1,0:T(2,128)S(1)} %pad_maximum_fusion.20), channel_id=1, source_target_pairs={{0,8},{4,12},{8,0},{12,4},{1,9},{5,13},{9,1},{13,5},{2,10},{6,14},... | collective-permute-start | bytes 24584 | tf_op jit(solution)/shard_map/ppermute | solution.py:43
  89.8 3.7 %collective-permute-start.23 = (f32[2,256]{1,0:T(2,128)S(1)}, f32[2,256]{1,0:T(2,128)S(1)}, u32[]{:S(2)}, u32[]{:S(2)}) collective-permute-start(f32[2,256]{1,0:T(2,128)S(1)} %pad_maximum_fusion.32), channel_id=1, source_target_pairs={{0,2},{2,0},{1,3},{3,1},{4,6},{6,4},{5,7},{7,5},{8,10},{10,8},{9,1... | collective-permute-start | bytes 6152 | tf_op jit(solution)/shard_map/ppermute | solution.py:43
  94.1 1.2 collective-permute-start.24
  95.4 3.7 %collective-permute-start.25 = (f32[2,1024]{1,0:T(2,128)S(1)}, f32[2,1024]{1,0:T(2,128)S(1)}, u32[]{:S(2)}, u32[]{:S(2)}) collective-permute-start(f32[2,1024]{1,0:T(2,128)S(1)} %pad_maximum_fusion.22), channel_id=1, source_target_pairs={{0,4},{4,0},{8,12},{12,8},{1,5},{5,1},{9,13},{13,9},{2,6},{6,2},{1... | collective-permute-start | bytes 24584 | tf_op jit(solution)/shard_map/ppermute | solution.py:43
  99.1 4.6 %collective-permute-start.26 = (f32[2,1024]{1,0:T(2,128)S(1)}, f32[2,1024]{1,0:T(2,128)S(1)}, u32[]{:S(2)}, u32[]{:S(2)}) collective-permute-start(f32[2,1024]{1,0:T(2,128)S(1)} %pad_maximum_fusion.23), channel_id=1, source_target_pairs={{0,8},{4,12},{8,0},{12,4},{1,9},{5,13},{9,1},{13,5},{2,10},{6,14},... | collective-permute-start | bytes 24584 | tf_op jit(solution)/shard_map/ppermute | solution.py:43
  104.4 3.7 %collective-permute-start.27 = (f32[2,256]{1,0:T(2,128)S(1)}, f32[2,256]{1,0:T(2,128)S(1)}, u32[]{:S(2)}, u32[]{:S(2)}) collective-permute-start(f32[2,256]{1,0:T(2,128)S(1)} %pad_maximum_fusion.33), channel_id=1, source_target_pairs={{0,2},{2,0},{1,3},{3,1},{4,6},{6,4},{5,7},{7,5},{8,10},{10,8},{9,1... | collective-permute-start | bytes 6152 | tf_op jit(solution)/shard_map/ppermute | solution.py:43
  108.7 1.2 collective-permute-start.28
  109.9 3.7 %collective-permute-start.29 = (f32[2,1024]{1,0:T(2,128)S(1)}, f32[2,1024]{1,0:T(2,128)S(1)}, u32[]{:S(2)}, u32[]{:S(2)}) collective-permute-start(f32[2,1024]{1,0:T(2,128)S(1)} %pad_maximum_fusion.25), channel_id=1, source_target_pairs={{0,4},{4,0},{8,12},{12,8},{1,5},{5,1},{9,13},{13,9},{2,6},{6,2},{1... | collective-permute-start | bytes 24584 | tf_op jit(solution)/shard_map/ppermute | solution.py:43
  113.7 4.6 %collective-permute-start.30 = (f32[2,1024]{1,0:T(2,128)S(1)}, f32[2,1024]{1,0:T(2,128)S(1)}, u32[]{:S(2)}, u32[]{:S(2)}) collective-permute-start(f32[2,1024]{1,0:T(2,128)S(1)} %pad_maximum_fusion.26), channel_id=1, source_target_pairs={{0,8},{4,12},{8,0},{12,4},{1,9},{5,13},{9,1},{13,5},{2,10},{6,14},... | collective-permute-start | bytes 24584 | tf_op jit(solution)/shard_map/ppermute | solution.py:43
  118.4 0.6 copy-start.3
  119.3 3.7 %collective-permute-start.31 = (f32[2,256]{1,0:T(2,128)S(1)}, f32[2,256]{1,0:T(2,128)S(1)}, u32[]{:S(2)}, u32[]{:S(2)}) collective-permute-start(f32[2,256]{1,0:T(2,128)S(1)} %pad_maximum_fusion.34), channel_id=1, source_target_pairs={{0,2},{2,0},{1,3},{3,1},{4,6},{6,4},{5,7},{7,5},{8,10},{10,8},{9,1... | collective-permute-start | bytes 6152 | tf_op jit(solution)/shard_map/ppermute | solution.py:43
  125.2 1.4 %collective-permute-start.32 = (f32[2,2,128,66]{2,1,0,3:T(2,128)S(1)}, f32[2,2,128,66]{2,1,0,3:T(2,128)S(1)}, u32[]{:S(2)}, u32[]{:S(2)}) collective-permute-start(f32[2,2,128,66]{2,1,0,3:T(2,128)S(1)} %pad_maximum_fusion), channel_id=1, source_target_pairs={{0,1},{1,0},{2,3},{3,2},{4,5},{5,4},{6,7},{7,6},{8,9},{9,8},{10,11... | collective-permute-start | bytes 405512 | tf_op jit(solution)/shard_map/ppermute | solution.py:70
  126.9 4.4 %collective-permute-start.33 = (f32[2,128,66]{1,0,2:T(2,128)S(1)}, f32[2,128,66]{1,0,2:T(2,128)S(1)}, u32[]{:S(2)}, u32[]{:S(2)}) collective-permute-start(f32[2,128,66]{1,0,2:T(2,128)S(1)} %pad_maximum_fusion.1), channel_id=1, source_target_pairs={{0,4},{4,0},{8,12},{12,8},{1,5},{5,1},{9,13},{13,9},{2,6},{6,2},{1... | collective-permute-start | bytes 202760 | tf_op jit(solution)/shard_map/ppermute | solution.py:70
  131.5 4.9 %collective-permute-start.34 = (f32[128,66]{0,1:T(8,128)S(1)}, f32[128,66]{0,1:T(8,128)S(1)}, u32[]{:S(2)}, u32[]{:S(2)}) collective-permute-start(f32[128,66]{0,1:T(8,128)S(1)} %pad_maximum_fusion.2), channel_id=1, source_target_pairs={{0,8},{4,12},{8,0},{12,4},{1,9},{5,13},{9,1},{13,5},{2,10},{6,14},... | collective-permute-start | bytes 101384 | tf_op jit(solution)/shard_map/ppermute | solution.py:70

commit v2 on v1

--- a/solution.py
+++ b/solution.py
@@ -52,6 +52,28 @@
     return maxima, totals
 
 
+def lse_exchange(maxima, totals, axes):
+    size = lax.axis_size(axes)
+    index = lax.axis_index(axes)
+    payload = jnp.stack([maxima, totals])
+    received = [payload]
+    for shift in range(1, size):
+        perm = [(i, (i + shift) % size) for i in range(size)]
+        received.append(lax.ppermute(payload, axes, perm))
+    received = jnp.stack(received)
+    ordered = [
+        lax.dynamic_index_in_dim(received, (index - rank) % size, axis=0, keepdims=False)
+        for rank in range(size)
+    ]
+    peak = ordered[0][0]
+    for item in ordered[1:]:
+        peak = jnp.maximum(peak, item[0])
+    whole = ordered[0][1] * jnp.exp(ordered[0][0] - peak)
+    for item in ordered[1:]:
+        whole = whole + item[1] * jnp.exp(item[0] - peak)
+    return peak, whole
+
+
 def lse_halving(maxima, totals, weighted, dims):
     for name, step in dims:
         size = lax.axis_size(name)
@@ -79,7 +101,7 @@
     return maxima, totals, weighted
 
 
-def body(sources, source_mass, targets, target_mass, fate_panel):
+def body_split(sources, source_mass, targets, target_mass, fate_panel):
     src_count = sources.shape[0]
     tgt_count = targets.shape[0]
     all_sources = src_count * lax.axis_size("rows")
@@ -105,6 +127,11 @@
         peak, whole = lse_allreduce(maxima, totals, ("rows",))
         g_pot = -relaxed * entropic * (peak + jnp.log(whole))
 
+    return (f_pot,) + fate_pullback(cost, log_b, g_pot, fate_panel)
+
+
+def fate_pullback(cost, log_b, g_pot, fate_panel):
+    src_count = cost.shape[0]
     scores = log_b[None, :] + (g_pot[None, :] - cost) / entropic
     maxima = jnp.max(scores, axis=1)
     weights = jnp.exp(scores - maxima[:, None])
@@ -112,7 +139,6 @@
     weighted = jnp.dot(
         weights, fate_panel, precision=lax.Precision.HIGHEST, preferred_element_type=jnp.float32
     )
-
     col_size = lax.axis_size("cols")
     rep_size = lax.axis_size("rep")
     fates = fate_panel.shape[1]
@@ -145,7 +171,55 @@
             lax.psum_scatter(totals * factor, ("cols", "rep"), scatter_dimension=0, tiled=True),
         )
         fate_rows = part_weighted / part_total[:, None]
-    return (f_pot, g_pot, fate_rows)
+    return (g_pot, fate_rows)
+
+
+ROW_AXES = (("rep",), ("cols",))
+
+
+def body(sources, source_mass, targets, target_mass, fate_panel):
+    row_count = lax.axis_size("rows")
+    if row_count != 2 or lax.axis_size("cols") > 8:
+        return body_split(sources, source_mass, targets, target_mass, fate_panel)
+    src_count = sources.shape[0]
+    tgt_count = targets.shape[0]
+    row = lax.axis_index("rows")
+    mine = jnp.concatenate([sources, source_mass[:, None]], axis=1)
+    theirs = lax.ppermute(mine, "rows", [(0, 1), (1, 0)])
+    first = jnp.where(row == 0, mine, theirs)
+    second = jnp.where(row == 0, theirs, mine)
+    gathered = jnp.concatenate([first, second], axis=0)
+    all_src = gathered[:, : sources.shape[1]]
+    all_mass = gathered[:, sources.shape[1]]
+    all_sources = src_count * row_count
+    all_targets = tgt_count * lax.axis_size(("cols", "rep"))
+    log_a = jnp.log(all_mass / all_sources)
+    log_b = jnp.log(target_mass / all_targets)
+    src_sq = jnp.sum(all_src * all_src, axis=1)
+    tgt_sq = jnp.sum(targets * targets, axis=1)
+    cost = pair_cost(all_src, src_sq, targets, tgt_sq)
+
+    g_pot = jnp.zeros((tgt_count,), jnp.float32)
+    f_all = jnp.zeros((all_sources,), jnp.float32)
+    for iteration in range(ITERS):
+        scores = log_b[None, :] + (g_pot[None, :] - cost) / entropic
+        maxima = jnp.max(scores, axis=1)
+        totals = jnp.sum(jnp.exp(scores - maxima[:, None]), axis=1)
+        for axes in ROW_AXES:
+            if len(axes) == 1 and lax.axis_size(axes[0]) == 2:
+                maxima, totals = lse_allreduce(maxima, totals, axes)
+            else:
+                maxima, totals = lse_exchange(maxima, totals, axes)
+        f_all = -relaxed * entropic * (maxima + jnp.log(totals))
+
+        scores = log_a[:, None] + (f_all[:, None] - cost) / entropic
+        maxima = jnp.max(scores, axis=0)
+        totals = jnp.sum(jnp.exp(scores - maxima[None, :]), axis=0)
+        g_pot = -relaxed * entropic * (maxima + jnp.log(totals))
+
+    f_pot = lax.dynamic_slice_in_dim(f_all, row * src_count, src_count)
+    cost_mine = lax.dynamic_slice_in_dim(cost, row * src_count, src_count, axis=0)
+    return (f_pot,) + fate_pullback(cost_mine, log_b, g_pot, fate_panel)
 
 
 def solution(mesh):

time: 137 us -> 114 us (0.83)
  starting transfers between devices: 61.9 us -> 40.4 us
  waiting for transfers between devices: 55.2 us -> 46.3 us
  other arithmetic: 14.8 us -> 21.1 us
    ppermute x32 -> x8, starting transfers between devices: 56.9 us -> 0.57 us  [lse_allreduce(): other = lax.ppermute(jnp.stack([maxima, totals]), name, perm)]
    ppermute x32 -> x8, waiting for transfers between devices: 49.9 us -> 9.28 us  [lse_allreduce(): other = lax.ppermute(jnp.stack([maxima, totals]), name, perm)]
    ppermute x0 -> x25, starting transfers between devices: none -> 38.6 us  [the longest x24 35.6 us: lse_exchange(): received.append(lax.ppermute(payload, axes, perm))]
    ppermute x0 -> x25, waiting for transfers between devices: none -> 28.1 us  [the longest x24 22.7 us: lse_exchange(): received.append(lax.ppermute(payload, axes, perm))]
    ppermute x3, starting transfers between devices: 4.96 us -> 1.23 us  [lse_halving(): packed = lax.ppermute(packed, name, perm)]
    ppermute x3, waiting for transfers between devices: 5.21 us -> 8.86 us  [lse_halving(): packed = lax.ppermute(packed, name, perm)]
    reduce_sum x8, other arithmetic: 2.51 us -> 4.46 us  [body(): totals = jnp.sum(jnp.exp(scores - maxima[:, None]), axis=1)]
    reduce_sum x8, other arithmetic: 2.93 us -> 4.64 us  [body(): totals = jnp.sum(jnp.exp(scores - maxima[None, :]), axis=0)]
  transfers between devices with their start and end apart: 35 -> 36, of which waited for: 35 -> 34; matrix products, arithmetic and copies ran while one was open for 0% -> 2% of each run, Pallas kernels for 0% -> 0%
where the time goes in v2:
time: 114 us
  waiting for transfers between devices  46.3 us (41%)
  starting transfers between devices  40.4 us (35%)
  other arithmetic  21.1 us (19%)
  matrix products  3.39 us (3%)
  local copies, waits for them, and re-layouts  1.54 us (1%)
  between operations  1.49 us (1%)
    ppermute x24, starting transfers between devices, lse_exchange(): received.append(lax.ppermute(payload, axes, perm))  35.6 us
    ppermute x24, waiting for transfers between devices, lse_exchange(): received.append(lax.ppermute(payload, axes, perm))  22.7 us
    ppermute x8, waiting for transfers between devices, lse_allreduce(): other = lax.ppermute(jnp.stack([maxima, totals]), name, perm)  9.28 us
    ppermute x3, waiting for transfers between devices, lse_halving(): packed = lax.ppermute(packed, name, perm)  8.86 us
    ppermute x1, waiting for transfers between devices, body(): theirs = lax.ppermute(mine, 'rows', [(0, 1), (1, 0)])  5.46 us
    reduce_sum x8, other arithmetic, body(): totals = jnp.sum(jnp.exp(scores - maxima[None, :]), axis=0)  4.64 us
    reduce_sum x8, other arithmetic, body(): totals = jnp.sum(jnp.exp(scores - maxima[:, None]), axis=1)  4.46 us
    ppermute x1, starting transfers between devices, body(): theirs = lax.ppermute(mine, 'rows', [(0, 1), (1, 0)])  3.03 us
  transfers between devices with their start and end apart: 36, of which 34 were waited for; matrix products, arithmetic and copies ran while one was open for 2% of the time, Pallas kernels for 0%

profile of v2, /device:TPU:0, one launch (start us, length us, event | category | flops | bytes accessed | tf_op | source)
XLA Modules:
  0.0 114.2 jit_solution(5263121730484453504)
XLA Ops:
  0.7 1.0 pad_maximum_fusion.2
  1.7 3.0 %collective-permute-start = (f32[1024,65]{0,1:T(8,128)S(1)}, f32[1024,65]{0,1:T(8,128)S(1)}, u32[]{:S(2)}, u32[]{:S(2)}) collective-permute-start(f32[1024,65]{0,1:T(8,128)S(1)} %pad_maximum_fusion.2), channel_id=1, source_target_pairs={{0,2},{2,0},{1,3},{3,1},{4,6},{6,4},{5,7},{7,5},{8,10},{10,8},{9,1... | collective-permute-start | bytes 798728 | tf_op jit(solution)/shard_map/ppermute | solution.py:188
  4.7 0.9 multiply_reduce_fusion.1
  6.3 5.5 %collective-permute-done = f32[1024,65]{0,1:T(8,128)S(1)} collective-permute-done((f32[1024,65]{0,1:T(8,128)S(1)}, f32[1024,65]{0,1:T(8,128)S(1)}, u32[]{:S(2)}, u32[]{:S(2)}) %collective-permute-start) | collective-permute-done | bytes 266272 | tf_op jit(solution)/shard_map/ppermute | solution.py:188
  11.7 1.0 broadcast_select_fusion.1
  12.8 2.3 %fusion.2 = (f32[2048]{0:T(1024)S(1)}, f32[2048,256]{0,1:T(8,128)S(1)}) fusion(f32[256]{0:T(256)S(1)} %multiply_log_fusion, f32[256,64]{0,1:T(8,128)S(1)} %copy-done.1, f32[1024,65]{0,1:T(8,128)S(1)} %get-tuple-element.10, f32[1024,65]{0,1:T(8,128)S(1)} %get-tuple-element.9, f32[256]{0:T(256)S(1)} %multiply_reduce_fusion.1, f32[2048]{0:T(1024)S(1)} %multiply_reduce_fusion), kind=kOutput, calls=%fused_computation.35 | convolution fusion | flops 406976512 | bytes 2713600 | tf_op jit(solution)/shard_map/dot_general | solution.py:14
  15.9 1.1 collective-permute-done.1
  17.1 2.9 %collective-permute-start.3 = (f32[2,2048]{1,0:T(2,128)S(1)}, f32[2,2048]{1,0:T(2,128)S(1)}, u32[]{:S(2)}, u32[]{:S(2)}) collective-permute-start(f32[2,2048]{1,0:T(2,128)S(1)} %get-tuple-element.115), channel_id=1, source_target_pairs={{0,8},{4,12},{8,0},{12,4},{1,9},{5,13},{9,1},{13,5},{2,10},{6,14},... | collective-permute-start | bytes 49160 | tf_op jit(solution)/shard_map/ppermute | solution.py:62
  20.0 1.6 %collective-permute-start.2 = (f32[2,2048]{1,0:T(2,128)S(1)}, f32[2,2048]{1,0:T(2,128)S(1)}, u32[]{:S(2)}, u32[]{:S(2)}) collective-permute-start(f32[2,2048]{1,0:T(2,128)S(1)} %get-tuple-element.115), channel_id=1, source_target_pairs={{0,4},{4,8},{8,12},{12,0},{1,5},{5,9},{9,13},{13,1},{2,6},{6,10},{... | collective-permute-start | bytes 49160 | tf_op jit(solution)/shard_map/ppermute | solution.py:62
  21.5 2.2 %collective-permute-start.4 = (f32[2,2048]{1,0:T(2,128)S(1)}, f32[2,2048]{1,0:T(2,128)S(1)}, u32[]{:S(2)}, u32[]{:S(2)}) collective-permute-start(f32[2,2048]{1,0:T(2,128)S(1)} %get-tuple-element.115), channel_id=1, source_target_pairs={{0,12},{4,0},{8,4},{12,8},{1,13},{5,1},{9,5},{13,9},{2,14},{6,2},{... | collective-permute-start | bytes 49160 | tf_op jit(solution)/shard_map/ppermute | solution.py:62
  23.8 1.7 %collective-permute-done.2 = f32[2,2048]{1,0:T(2,128)S(1)} collective-permute-done((f32[2,2048]{1,0:T(2,128)S(1)}, f32[2,2048]{1,0:T(2,128)S(1)}, u32[]{:S(2)}, u32[]{:S(2)}) %collective-permute-start.2) | collective-permute-done | bytes 16416 | tf_op jit(solution)/shard_map/ppermute | solution.py:62
  27.6 1.2 %collective-permute-done.5 = f32[2,2048]{1,0:T(2,128)S(1)} collective-permute-done((f32[2,2048]{1,0:T(2,128)S(1)}, f32[2,2048]{1,0:T(2,128)S(1)}, u32[]{:S(2)}, u32[]{:S(2)}) %collective-permute-start.5) | collective-permute-done | bytes 16416 | tf_op jit(solution)/shard_map/ppermute | solution.py:43
  28.9 0.8 collective-permute-start.7
  29.7 3.6 %collective-permute-start.6 = (f32[2,2048]{1,0:T(2,128)S(1)}, f32[2,2048]{1,0:T(2,128)S(1)}, u32[]{:S(2)}, u32[]{:S(2)}) collective-permute-start(f32[2,2048]{1,0:T(2,128)S(1)} %get-tuple-element.113), channel_id=1, source_target_pairs={{0,4},{4,8},{8,12},{12,0},{1,5},{5,9},{9,13},{13,1},{2,6},{6,10},{... | collective-permute-start | bytes 49160 | tf_op jit(solution)/shard_map/ppermute | solution.py:62
  33.6 1.6 %collective-permute-done.6 = f32[2,2048]{1,0:T(2,128)S(1)} collective-permute-done((f32[2,2048]{1,0:T(2,128)S(1)}, f32[2,2048]{1,0:T(2,128)S(1)}, u32[]{:S(2)}, u32[]{:S(2)}) %collective-permute-start.6) | collective-permute-done | bytes 16416 | tf_op jit(solution)/shard_map/ppermute | solution.py:62
  35.2 1.9 %collective-permute-done.8 = f32[2,2048]{1,0:T(2,128)S(1)} collective-permute-done((f32[2,2048]{1,0:T(2,128)S(1)}, f32[2,2048]{1,0:T(2,128)S(1)}, u32[]{:S(2)}, u32[]{:S(2)}) %collective-permute-start.8) | collective-permute-done | bytes 16416 | tf_op jit(solution)/shard_map/ppermute | solution.py:62
  39.2 1.2 %collective-permute-done.9 = f32[2,2048]{1,0:T(2,128)S(1)} collective-permute-done((f32[2,2048]{1,0:T(2,128)S(1)}, f32[2,2048]{1,0:T(2,128)S(1)}, u32[]{:S(2)}, u32[]{:S(2)}) %collective-permute-start.9) | collective-permute-done | bytes 16416 | tf_op jit(solution)/shard_map/ppermute | solution.py:43
  40.6 2.5 %collective-permute-start.10 = (f32[2,2048]{1,0:T(2,128)S(1)}, f32[2,2048]{1,0:T(2,128)S(1)}, u32[]{:S(2)}, u32[]{:S(2)}) collective-permute-start(f32[2,2048]{1,0:T(2,128)S(1)} %get-tuple-element.111), channel_id=1, source_target_pairs={{0,4},{4,8},{8,12},{12,0},{1,5},{5,9},{9,13},{13,1},{2,6},{6,10},{... | collective-permute-start | bytes 49160 | tf_op jit(solution)/shard_map/ppermute | solution.py:62
  43.1 1.4 %collective-permute-start.12 = (f32[2,2048]{1,0:T(2,128)S(1)}, f32[2,2048]{1,0:T(2,128)S(1)}, u32[]{:S(2)}, u32[]{:S(2)}) collective-permute-start(f32[2,2048]{1,0:T(2,128)S(1)} %get-tuple-element.111), channel_id=1, source_target_pairs={{0,12},{4,0},{8,4},{12,8},{1,13},{5,1},{9,5},{13,9},{2,14},{6,2},{... | collective-permute-start | bytes 49160 | tf_op jit(solution)/shard_map/ppermute | solution.py:62
  44.4 0.8 collective-permute-done.11
  45.2 1.0 collective-permute-done.10
  49.0 1.2 %collective-permute-done.13 = f32[2,2048]{1,0:T(2,128)S(1)} collective-permute-done((f32[2,2048]{1,0:T(2,128)S(1)}, f32[2,2048]{1,0:T(2,128)S(1)}, u32[]{:S(2)}, u32[]{:S(2)}) %collective-permute-start.13) | collective-permute-done | bytes 16416 | tf_op jit(solution)/shard_map/ppermute | solution.py:43
  50.7 3.3 %collective-permute-start.14 = (f32[2,2048]{1,0:T(2,128)S(1)}, f32[2,2048]{1,0:T(2,128)S(1)}, u32[]{:S(2)}, u32[]{:S(2)}) collective-permute-start(f32[2,2048]{1,0:T(2,128)S(1)} %get-tuple-element.109), channel_id=1, source_target_pairs={{0,4},{4,8},{8,12},{12,0},{1,5},{5,9},{9,13},{13,1},{2,6},{6,10},{... | collective-permute-start | bytes 49160 | tf_op jit(solution)/shard_map/ppermute | solution.py:62
  54.9 1.5 %collective-permute-done.14 = f32[2,2048]{1,0:T(2,128)S(1)} collective-permute-done((f32[2,2048]{1,0:T(2,128)S(1)}, f32[2,2048]{1,0:T(2,128)S(1)}, u32[]{:S(2)}, u32[]{:S(2)}) %collective-permute-start.14) | collective-permute-done | bytes 16416 | tf_op jit(solution)/shard_map/ppermute | solution.py:62
  56.4 1.3 %collective-permute-done.16 = f32[2,2048]{1,0:T(2,128)S(1)} collective-permute-done((f32[2,2048]{1,0:T(2,128)S(1)}, f32[2,2048]{1,0:T(2,128)S(1)}, u32[]{:S(2)}, u32[]{:S(2)}) %collective-permute-start.16) | collective-permute-done | bytes 16416 | tf_op jit(solution)/shard_map/ppermute | solution.py:62
  59.9 1.2 %collective-permute-done.17 = f32[2,2048]{1,0:T(2,128)S(1)} collective-permute-done((f32[2,2048]{1,0:T(2,128)S(1)}, f32[2,2048]{1,0:T(2,128)S(1)}, u32[]{:S(2)}, u32[]{:S(2)}) %collective-permute-start.17) | collective-permute-done | bytes 16416 | tf_op jit(solution)/shard_map/ppermute | solution.py:43
  61.3 2.7 %collective-permute-start.18 = (f32[2,2048]{1,0:T(2,128)S(1)}, f32[2,2048]{1,0:T(2,128)S(1)}, u32[]{:S(2)}, u32[]{:S(2)}) collective-permute-start(f32[2,2048]{1,0:T(2,128)S(1)} %get-tuple-element.107), channel_id=1, source_target_pairs={{0,4},{4,8},{8,12},{12,0},{1,5},{5,9},{9,13},{13,1},{2,6},{6,10},{... | collective-permute-start | bytes 49160 | tf_op jit(solution)/shard_map/ppermute | solution.py:62
  64.0 1.1 collective-permute-start.20
  65.8 1.1 collective-permute-done.18
  66.9 0.9 collective-permute-done.20
  69.9 1.2 %collective-permute-done.21 = f32[2,2048]{1,0:T(2,128)S(1)} collective-permute-done((f32[2,2048]{1,0:T(2,128)S(1)}, f32[2,2048]{1,0:T(2,128)S(1)}, u32[]{:S(2)}, u32[]{:S(2)}) %collective-permute-start.21) | collective-permute-done | bytes 16416 | tf_op jit(solution)/shard_map/ppermute | solution.py:43
  71.3 3.4 %collective-permute-start.22 = (f32[2,2048]{1,0:T(2,128)S(1)}, f32[2,2048]{1,0:T(2,128)S(1)}, u32[]{:S(2)}, u32[]{:S(2)}) collective-permute-start(f32[2,2048]{1,0:T(2,128)S(1)} %get-tuple-element.105), channel_id=1, source_target_pairs={{0,4},{4,8},{8,12},{12,0},{1,5},{5,9},{9,13},{13,1},{2,6},{6,10},{... | collective-permute-start | bytes 49160 | tf_op jit(solution)/shard_map/ppermute | solution.py:62
  75.1 1.1 collective-permute-done.23
  77.0 1.5 %collective-permute-done.24 = f32[2,2048]{1,0:T(2,128)S(1)} collective-permute-done((f32[2,2048]{1,0:T(2,128)S(1)}, f32[2,2048]{1,0:T(2,128)S(1)}, u32[]{:S(2)}, u32[]{:S(2)}) %collective-permute-start.24) | collective-permute-done | bytes 16416 | tf_op jit(solution)/shard_map/ppermute | solution.py:62
  80.6 1.2 %collective-permute-done.25 = f32[2,2048]{1,0:T(2,128)S(1)} collective-permute-done((f32[2,2048]{1,0:T(2,128)S(1)}, f32[2,2048]{1,0:T(2,128)S(1)}, u32[]{:S(2)}, u32[]{:S(2)}) %collective-permute-start.25) | collective-permute-done | bytes 16416 | tf_op jit(solution)/shard_map/ppermute | solution.py:43
  82.0 2.7 %collective-permute-start.26 = (f32[2,2048]{1,0:T(2,128)S(1)}, f32[2,2048]{1,0:T(2,128)S(1)}, u32[]{:S(2)}, u32[]{:S(2)}) collective-permute-start(f32[2,2048]{1,0:T(2,128)S(1)} %get-tuple-element.103), channel_id=1, source_target_pairs={{0,4},{4,8},{8,12},{12,0},{1,5},{5,9},{9,13},{13,1},{2,6},{6,10},{... | collective-permute-start | bytes 49160 | tf_op jit(solution)/shard_map/ppermute | solution.py:62
  84.7 1.1 collective-permute-start.28
  86.6 1.0 collective-permute-done.26
  87.5 0.9 collective-permute-done.28
  90.6 1.2 %collective-permute-done.29 = f32[2,2048]{1,0:T(2,128)S(1)} collective-permute-done((f32[2,2048]{1,0:T(2,128)S(1)}, f32[2,2048]{1,0:T(2,128)S(1)}, u32[]{:S(2)}, u32[]{:S(2)}) %collective-permute-start.29) | collective-permute-done | bytes 16416 | tf_op jit(solution)/shard_map/ppermute | solution.py:43
  92.0 3.3 %collective-permute-start.30 = (f32[2,2048]{1,0:T(2,128)S(1)}, f32[2,2048]{1,0:T(2,128)S(1)}, u32[]{:S(2)}, u32[]{:S(2)}) collective-permute-start(f32[2,2048]{1,0:T(2,128)S(1)} %get-tuple-element.101), channel_id=1, source_target_pairs={{0,4},{4,8},{8,12},{12,0},{1,5},{5,9},{9,13},{13,1},{2,6},{6,10},{... | collective-permute-start | bytes 49160 | tf_op jit(solution)/shard_map/ppermute | solution.py:62
  96.5 1.3 %collective-permute-done.30 = f32[2,2048]{1,0:T(2,128)S(1)} collective-permute-done((f32[2,2048]{1,0:T(2,128)S(1)}, f32[2,2048]{1,0:T(2,128)S(1)}, u32[]{:S(2)}, u32[]{:S(2)}) %collective-permute-start.30) | collective-permute-done | bytes 16416 | tf_op jit(solution)/shard_map/ppermute | solution.py:62
  97.8 1.3 %collective-permute-done.32 = f32[2,2048]{1,0:T(2,128)S(1)} collective-permute-done((f32[2,2048]{1,0:T(2,128)S(1)}, f32[2,2048]{1,0:T(2,128)S(1)}, u32[]{:S(2)}, u32[]{:S(2)}) %collective-permute-start.32) | collective-permute-done | bytes 16416 | tf_op jit(solution)/shard_map/ppermute | solution.py:62
  100.8 1.1 fusion.19
  102.5 1.3 %collective-permute-done.33 = f32[2,2,128,66]{2,1,0,3:T(2,128)S(1)} collective-permute-done((f32[2,2,128,66]{2,1,0,3:T(2,128)S(1)}, f32[2,2,128,66]{2,1,0,3:T(2,128)S(1)}, u32[]{:S(2)}, u32[]{:S(2)}) %collective-permute-start.33) | collective-permute-done | bytes 135200 | tf_op jit(solution)/shard_map/ppermute | solution.py:92
  104.2 4.3 %collective-permute-done.34 = f32[2,128,66]{1,0,2:T(2,128)S(1)} collective-permute-done((f32[2,128,66]{1,0,2:T(2,128)S(1)}, f32[2,128,66]{1,0,2:T(2,128)S(1)}, u32[]{:S(2)}, u32[]{:S(2)}) %collective-permute-start.34) | collective-permute-done | bytes 67616 | tf_op jit(solution)/shard_map/ppermute | solution.py:92
  108.6 1.1 collective-permute-start.35
  110.3 3.3 %collective-permute-done.35 = f32[128,66]{0,1:T(8,128)S(1)} collective-permute-done((f32[128,66]{0,1:T(8,128)S(1)}, f32[128,66]{0,1:T(8,128)S(1)}, u32[]{:S(2)}, u32[]{:S(2)}) %collective-permute-start.35) | collective-permute-done | bytes 33824 | tf_op jit(solution)/shard_map/ppermute | solution.py:92
  (155 shorter events, 27.3 us)
Async XLA Ops:
  0.6 100.1 %copy-start = (f32[256,64]{0,1:T(8,128)S(1)}, f32[256,64]{0,1:T(8,128)}, u32[]{:S(2)}) copy-start(f32[256,64]{0,1:T(8,128)} %param.9) | copy-start | bytes 196612
  0.6 12.2 %copy-start.1 = (f32[256,64]{0,1:T(8,128)S(1)}, f32[256,64]{0,1:T(8,128)}, u32[]{:S(2)}) copy-start(f32[256,64]{0,1:T(8,128)} %param.7) | copy-start | bytes 196612
  1.7 10.0 %collective-permute-start = (f32[1024,65]{0,1:T(8,128)S(1)}, f32[1024,65]{0,1:T(8,128)S(1)}, u32[]{:S(2)}, u32[]{:S(2)}) collective-permute-start(f32[1024,65]{0,1:T(8,128)S(1)} %pad_maximum_fusion.2), channel_id=1, source_target_pairs={{0,2},{2,0},{1,3},{3,1},{4,6},{6,4},{5,7},{7,5},{8,10},{10,8},{9,1... | collective-permute-start | bytes 798728 | tf_op jit(solution)/shard_map/ppermute | solution.py:188
  15.7 1.2 %collective-permute-start.1 = (f32[2,2048]{1,0:T(2,128)S(1)}, f32[2,2048]{1,0:T(2,128)S(1)}, u32[]{:S(2)}, u32[]{:S(2)}) collective-permute-start(f32[2,2048]{1,0:T(2,128)S(1)} %pad_maximum_fusion.14), channel_id=1, source_target_pairs={{0,1},{1,0},{2,3},{3,2},{4,5},{5,4},{6,7},{7,6},{8,9},{9,8},{10,11... | collective-permute-start | bytes 49160 | tf_op jit(solution)/shard_map/ppermute | solution.py:43
  17.1 6.7 %collective-permute-start.3 = (f32[2,2048]{1,0:T(2,128)S(1)}, f32[2,2048]{1,0:T(2,128)S(1)}, u32[]{:S(2)}, u32[]{:S(2)}) collective-permute-start(f32[2,2048]{1,0:T(2,128)S(1)} %get-tuple-element.115), channel_id=1, source_target_pairs={{0,8},{4,12},{8,0},{12,4},{1,9},{5,13},{9,1},{13,5},{2,10},{6,14},... | collective-permute-start | bytes 49160 | tf_op jit(solution)/shard_map/ppermute | solution.py:62
  20.0 5.5 %collective-permute-start.2 = (f32[2,2048]{1,0:T(2,128)S(1)}, f32[2,2048]{1,0:T(2,128)S(1)}, u32[]{:S(2)}, u32[]{:S(2)}) collective-permute-start(f32[2,2048]{1,0:T(2,128)S(1)} %get-tuple-element.115), channel_id=1, source_target_pairs={{0,4},{4,8},{8,12},{12,0},{1,5},{5,9},{9,13},{13,1},{2,6},{6,10},{... | collective-permute-start | bytes 49160 | tf_op jit(solution)/shard_map/ppermute | solution.py:62
  21.5 4.0 %collective-permute-start.4 = (f32[2,2048]{1,0:T(2,128)S(1)}, f32[2,2048]{1,0:T(2,128)S(1)}, u32[]{:S(2)}, u32[]{:S(2)}) collective-permute-start(f32[2,2048]{1,0:T(2,128)S(1)} %get-tuple-element.115), channel_id=1, source_target_pairs={{0,12},{4,0},{8,4},{12,8},{1,13},{5,1},{9,5},{13,9},{2,14},{6,2},{... | collective-permute-start | bytes 49160 | tf_op jit(solution)/shard_map/ppermute | solution.py:62
  27.6 1.2 %collective-permute-start.5 = (f32[2,2048]{1,0:T(2,128)S(1)}, f32[2,2048]{1,0:T(2,128)S(1)}, u32[]{:S(2)}, u32[]{:S(2)}) collective-permute-start(f32[2,2048]{1,0:T(2,128)S(1)} %pad_maximum_fusion.16), channel_id=1, source_target_pairs={{0,1},{1,0},{2,3},{3,2},{4,5},{5,4},{6,7},{7,6},{8,9},{9,8},{10,11... | collective-permute-start | bytes 49160 | tf_op jit(solution)/shard_map/ppermute | solution.py:43
  28.9 4.7 %collective-permute-start.7 = (f32[2,2048]{1,0:T(2,128)S(1)}, f32[2,2048]{1,0:T(2,128)S(1)}, u32[]{:S(2)}, u32[]{:S(2)}) collective-permute-start(f32[2,2048]{1,0:T(2,128)S(1)} %get-tuple-element.113), channel_id=1, source_target_pairs={{0,8},{4,12},{8,0},{12,4},{1,9},{5,13},{9,1},{13,5},{2,10},{6,14},... | collective-permute-start | bytes 49160 | tf_op jit(solution)/shard_map/ppermute | solution.py:62
  29.7 5.5 %collective-permute-start.6 = (f32[2,2048]{1,0:T(2,128)S(1)}, f32[2,2048]{1,0:T(2,128)S(1)}, u32[]{:S(2)}, u32[]{:S(2)}) collective-permute-start(f32[2,2048]{1,0:T(2,128)S(1)} %get-tuple-element.113), channel_id=1, source_target_pairs={{0,4},{4,8},{8,12},{12,0},{1,5},{5,9},{9,13},{13,1},{2,6},{6,10},{... | collective-permute-start | bytes 49160 | tf_op jit(solution)/shard_map/ppermute | solution.py:62
  33.3 3.7 %collective-permute-start.8 = (f32[2,2048]{1,0:T(2,128)S(1)}, f32[2,2048]{1,0:T(2,128)S(1)}, u32[]{:S(2)}, u32[]{:S(2)}) collective-permute-start(f32[2,2048]{1,0:T(2,128)S(1)} %get-tuple-element.113), channel_id=1, source_target_pairs={{0,12},{4,0},{8,4},{12,8},{1,13},{5,1},{9,5},{13,9},{2,14},{6,2},{... | collective-permute-start | bytes 49160 | tf_op jit(solution)/shard_map/ppermute | solution.py:62
  39.1 1.2 %collective-permute-start.9 = (f32[2,2048]{1,0:T(2,128)S(1)}, f32[2,2048]{1,0:T(2,128)S(1)}, u32[]{:S(2)}, u32[]{:S(2)}) collective-permute-start(f32[2,2048]{1,0:T(2,128)S(1)} %pad_maximum_fusion.18), channel_id=1, source_target_pairs={{0,1},{1,0},{2,3},{3,2},{4,5},{5,4},{6,7},{7,6},{8,9},{9,8},{10,11... | collective-permute-start | bytes 49160 | tf_op jit(solution)/shard_map/ppermute | solution.py:43
  40.5 4.7 %collective-permute-start.11 = (f32[2,2048]{1,0:T(2,128)S(1)}, f32[2,2048]{1,0:T(2,128)S(1)}, u32[]{:S(2)}, u32[]{:S(2)}) collective-permute-start(f32[2,2048]{1,0:T(2,128)S(1)} %get-tuple-element.111), channel_id=1, source_target_pairs={{0,8},{4,12},{8,0},{12,4},{1,9},{5,13},{9,1},{13,5},{2,10},{6,14},... | collective-permute-start | bytes 49160 | tf_op jit(solution)/shard_map/ppermute | solution.py:62
  40.6 5.5 %collective-permute-start.10 = (f32[2,2048]{1,0:T(2,128)S(1)}, f32[2,2048]{1,0:T(2,128)S(1)}, u32[]{:S(2)}, u32[]{:S(2)}) collective-permute-start(f32[2,2048]{1,0:T(2,128)S(1)} %get-tuple-element.111), channel_id=1, source_target_pairs={{0,4},{4,8},{8,12},{12,0},{1,5},{5,9},{9,13},{13,1},{2,6},{6,10},{... | collective-permute-start | bytes 49160 | tf_op jit(solution)/shard_map/ppermute | solution.py:62
  43.1 3.7 %collective-permute-start.12 = (f32[2,2048]{1,0:T(2,128)S(1)}, f32[2,2048]{1,0:T(2,128)S(1)}, u32[]{:S(2)}, u32[]{:S(2)}) collective-permute-start(f32[2,2048]{1,0:T(2,128)S(1)} %get-tuple-element.111), channel_id=1, source_target_pairs={{0,12},{4,0},{8,4},{12,8},{1,13},{5,1},{9,5},{13,9},{2,14},{6,2},{... | collective-permute-start | bytes 49160 | tf_op jit(solution)/shard_map/ppermute | solution.py:62
  48.9 1.2 %collective-permute-start.13 = (f32[2,2048]{1,0:T(2,128)S(1)}, f32[2,2048]{1,0:T(2,128)S(1)}, u32[]{:S(2)}, u32[]{:S(2)}) collective-permute-start(f32[2,2048]{1,0:T(2,128)S(1)} %pad_maximum_fusion.20), channel_id=1, source_target_pairs={{0,1},{1,0},{2,3},{3,2},{4,5},{5,4},{6,7},{7,6},{8,9},{9,8},{10,11... | collective-permute-start | bytes 49160 | tf_op jit(solution)/shard_map/ppermute | solution.py:43
  50.2 4.7 %collective-permute-start.15 = (f32[2,2048]{1,0:T(2,128)S(1)}, f32[2,2048]{1,0:T(2,128)S(1)}, u32[]{:S(2)}, u32[]{:S(2)}) collective-permute-start(f32[2,2048]{1,0:T(2,128)S(1)} %get-tuple-element.109), channel_id=1, source_target_pairs={{0,8},{4,12},{8,0},{12,4},{1,9},{5,13},{9,1},{13,5},{2,10},{6,14},... | collective-permute-start | bytes 49160 | tf_op jit(solution)/shard_map/ppermute | solution.py:62
  50.7 5.8 %collective-permute-start.14 = (f32[2,2048]{1,0:T(2,128)S(1)}, f32[2,2048]{1,0:T(2,128)S(1)}, u32[]{:S(2)}, u32[]{:S(2)}) collective-permute-start(f32[2,2048]{1,0:T(2,128)S(1)} %get-tuple-element.109), channel_id=1, source_target_pairs={{0,4},{4,8},{8,12},{12,0},{1,5},{5,9},{9,13},{13,1},{2,6},{6,10},{... | collective-permute-start | bytes 49160 | tf_op jit(solution)/shard_map/ppermute | solution.py:62
  54.0 3.7 %collective-permute-start.16 = (f32[2,2048]{1,0:T(2,128)S(1)}, f32[2,2048]{1,0:T(2,128)S(1)}, u32[]{:S(2)}, u32[]{:S(2)}) collective-permute-start(f32[2,2048]{1,0:T(2,128)S(1)} %get-tuple-element.109), channel_id=1, source_target_pairs={{0,12},{4,0},{8,4},{12,8},{1,13},{5,1},{9,5},{13,9},{2,14},{6,2},{... | collective-permute-start | bytes 49160 | tf_op jit(solution)/shard_map/ppermute | solution.py:62
  59.8 1.2 %collective-permute-start.17 = (f32[2,2048]{1,0:T(2,128)S(1)}, f32[2,2048]{1,0:T(2,128)S(1)}, u32[]{:S(2)}, u32[]{:S(2)}) collective-permute-start(f32[2,2048]{1,0:T(2,128)S(1)} %pad_maximum_fusion.22), channel_id=1, source_target_pairs={{0,1},{1,0},{2,3},{3,2},{4,5},{5,4},{6,7},{7,6},{8,9},{9,8},{10,11... | collective-permute-start | bytes 49160 | tf_op jit(solution)/shard_map/ppermute | solution.py:43
  61.1 4.7 %collective-permute-start.19 = (f32[2,2048]{1,0:T(2,128)S(1)}, f32[2,2048]{1,0:T(2,128)S(1)}, u32[]{:S(2)}, u32[]{:S(2)}) collective-permute-start(f32[2,2048]{1,0:T(2,128)S(1)} %get-tuple-element.107), channel_id=1, source_target_pairs={{0,8},{4,12},{8,0},{12,4},{1,9},{5,13},{9,1},{13,5},{2,10},{6,14},... | collective-permute-start | bytes 49160 | tf_op jit(solution)/shard_map/ppermute | solution.py:62
  61.3 5.5 %collective-permute-start.18 = (f32[2,2048]{1,0:T(2,128)S(1)}, f32[2,2048]{1,0:T(2,128)S(1)}, u32[]{:S(2)}, u32[]{:S(2)}) collective-permute-start(f32[2,2048]{1,0:T(2,128)S(1)} %get-tuple-element.107), channel_id=1, source_target_pairs={{0,4},{4,8},{8,12},{12,0},{1,5},{5,9},{9,13},{13,1},{2,6},{6,10},{... | collective-permute-start | bytes 49160 | tf_op jit(solution)/shard_map/ppermute | solution.py:62
  64.0 3.7 %collective-permute-start.20 = (f32[2,2048]{1,0:T(2,128)S(1)}, f32[2,2048]{1,0:T(2,128)S(1)}, u32[]{:S(2)}, u32[]{:S(2)}) collective-permute-start(f32[2,2048]{1,0:T(2,128)S(1)} %get-tuple-element.107), channel_id=1, source_target_pairs={{0,12},{4,0},{8,4},{12,8},{1,13},{5,1},{9,5},{13,9},{2,14},{6,2},{... | collective-permute-start | bytes 49160 | tf_op jit(solution)/shard_map/ppermute | solution.py:62
  69.8 1.2 %collective-permute-start.21 = (f32[2,2048]{1,0:T(2,128)S(1)}, f32[2,2048]{1,0:T(2,128)S(1)}, u32[]{:S(2)}, u32[]{:S(2)}) collective-permute-start(f32[2,2048]{1,0:T(2,128)S(1)} %pad_maximum_fusion.24), channel_id=1, source_target_pairs={{0,1},{1,0},{2,3},{3,2},{4,5},{5,4},{6,7},{7,6},{8,9},{9,8},{10,11... | collective-permute-start | bytes 49160 | tf_op jit(solution)/shard_map/ppermute | solution.py:43
  71.2 5.1 %collective-permute-start.23 = (f32[2,2048]{1,0:T(2,128)S(1)}, f32[2,2048]{1,0:T(2,128)S(1)}, u32[]{:S(2)}, u32[]{:S(2)}) collective-permute-start(f32[2,2048]{1,0:T(2,128)S(1)} %get-tuple-element.105), channel_id=1, source_target_pairs={{0,8},{4,12},{8,0},{12,4},{1,9},{5,13},{9,1},{13,5},{2,10},{6,14},... | collective-permute-start | bytes 49160 | tf_op jit(solution)/shard_map/ppermute | solution.py:62
  71.3 5.7 %collective-permute-start.22 = (f32[2,2048]{1,0:T(2,128)S(1)}, f32[2,2048]{1,0:T(2,128)S(1)}, u32[]{:S(2)}, u32[]{:S(2)}) collective-permute-start(f32[2,2048]{1,0:T(2,128)S(1)} %get-tuple-element.105), channel_id=1, source_target_pairs={{0,4},{4,8},{8,12},{12,0},{1,5},{5,9},{9,13},{13,1},{2,6},{6,10},{... | collective-permute-start | bytes 49160 | tf_op jit(solution)/shard_map/ppermute | solution.py:62
  74.7 3.7 %collective-permute-start.24 = (f32[2,2048]{1,0:T(2,128)S(1)}, f32[2,2048]{1,0:T(2,128)S(1)}, u32[]{:S(2)}, u32[]{:S(2)}) collective-permute-start(f32[2,2048]{1,0:T(2,128)S(1)} %get-tuple-element.105), channel_id=1, source_target_pairs={{0,12},{4,0},{8,4},{12,8},{1,13},{5,1},{9,5},{13,9},{2,14},{6,2},{... | collective-permute-start | bytes 49160 | tf_op jit(solution)/shard_map/ppermute | solution.py:62
  80.5 1.2 %collective-permute-start.25 = (f32[2,2048]{1,0:T(2,128)S(1)}, f32[2,2048]{1,0:T(2,128)S(1)}, u32[]{:S(2)}, u32[]{:S(2)}) collective-permute-start(f32[2,2048]{1,0:T(2,128)S(1)} %pad_maximum_fusion.26), channel_id=1, source_target_pairs={{0,1},{1,0},{2,3},{3,2},{4,5},{5,4},{6,7},{7,6},{8,9},{9,8},{10,11... | collective-permute-start | bytes 49160 | tf_op jit(solution)/shard_map/ppermute | solution.py:43
  81.8 4.7 %collective-permute-start.27 = (f32[2,2048]{1,0:T(2,128)S(1)}, f32[2,2048]{1,0:T(2,128)S(1)}, u32[]{:S(2)}, u32[]{:S(2)}) collective-permute-start(f32[2,2048]{1,0:T(2,128)S(1)} %get-tuple-element.103), channel_id=1, source_target_pairs={{0,8},{4,12},{8,0},{12,4},{1,9},{5,13},{9,1},{13,5},{2,10},{6,14},... | collective-permute-start | bytes 49160 | tf_op jit(solution)/shard_map/ppermute | solution.py:62
  82.0 5.5 %collective-permute-start.26 = (f32[2,2048]{1,0:T(2,128)S(1)}, f32[2,2048]{1,0:T(2,128)S(1)}, u32[]{:S(2)}, u32[]{:S(2)}) collective-permute-start(f32[2,2048]{1,0:T(2,128)S(1)} %get-tuple-element.103), channel_id=1, source_target_pairs={{0,4},{4,8},{8,12},{12,0},{1,5},{5,9},{9,13},{13,1},{2,6},{6,10},{... | collective-permute-start | bytes 49160 | tf_op jit(solution)/shard_map/ppermute | solution.py:62
  84.7 3.7 %collective-permute-start.28 = (f32[2,2048]{1,0:T(2,128)S(1)}, f32[2,2048]{1,0:T(2,128)S(1)}, u32[]{:S(2)}, u32[]{:S(2)}) collective-permute-start(f32[2,2048]{1,0:T(2,128)S(1)} %get-tuple-element.103), channel_id=1, source_target_pairs={{0,12},{4,0},{8,4},{12,8},{1,13},{5,1},{9,5},{13,9},{2,14},{6,2},{... | collective-permute-start | bytes 49160 | tf_op jit(solution)/shard_map/ppermute | solution.py:62
  90.5 1.2 %collective-permute-start.29 = (f32[2,2048]{1,0:T(2,128)S(1)}, f32[2,2048]{1,0:T(2,128)S(1)}, u32[]{:S(2)}, u32[]{:S(2)}) collective-permute-start(f32[2,2048]{1,0:T(2,128)S(1)} %pad_maximum_fusion.28), channel_id=1, source_target_pairs={{0,1},{1,0},{2,3},{3,2},{4,5},{5,4},{6,7},{7,6},{8,9},{9,8},{10,11... | collective-permute-start | bytes 49160 | tf_op jit(solution)/shard_map/ppermute | solution.py:43
  91.8 4.7 %collective-permute-start.31 = (f32[2,2048]{1,0:T(2,128)S(1)}, f32[2,2048]{1,0:T(2,128)S(1)}, u32[]{:S(2)}, u32[]{:S(2)}) collective-permute-start(f32[2,2048]{1,0:T(2,128)S(1)} %get-tuple-element.101), channel_id=1, source_target_pairs={{0,8},{4,12},{8,0},{12,4},{1,9},{5,13},{9,1},{13,5},{2,10},{6,14},... | collective-permute-start | bytes 49160 | tf_op jit(solution)/shard_map/ppermute | solution.py:62
  92.0 5.8 %collective-permute-start.30 = (f32[2,2048]{1,0:T(2,128)S(1)}, f32[2,2048]{1,0:T(2,128)S(1)}, u32[]{:S(2)}, u32[]{:S(2)}) collective-permute-start(f32[2,2048]{1,0:T(2,128)S(1)} %get-tuple-element.101), channel_id=1, source_target_pairs={{0,4},{4,8},{8,12},{12,0},{1,5},{5,9},{9,13},{13,1},{2,6},{6,10},{... | collective-permute-start | bytes 49160 | tf_op jit(solution)/shard_map/ppermute | solution.py:62
  95.3 3.7 %collective-permute-start.32 = (f32[2,2048]{1,0:T(2,128)S(1)}, f32[2,2048]{1,0:T(2,128)S(1)}, u32[]{:S(2)}, u32[]{:S(2)}) collective-permute-start(f32[2,2048]{1,0:T(2,128)S(1)} %get-tuple-element.101), channel_id=1, source_target_pairs={{0,12},{4,0},{8,4},{12,8},{1,13},{5,1},{9,5},{13,9},{2,14},{6,2},{... | collective-permute-start | bytes 49160 | tf_op jit(solution)/shard_map/ppermute | solution.py:62
  100.2 1.9 %copy-start.2 = (f32[256]{0:T(256)}, f32[256]{0:T(256)S(1)}, u32[]{:S(2)}) copy-start(f32[256]{0:T(256)S(1)} %add_multiply_fusion.8) | copy-start | bytes 3076
  102.4 1.4 %collective-permute-start.33 = (f32[2,2,128,66]{2,1,0,3:T(2,128)S(1)}, f32[2,2,128,66]{2,1,0,3:T(2,128)S(1)}, u32[]{:S(2)}, u32[]{:S(2)}) collective-permute-start(f32[2,2,128,66]{2,1,0,3:T(2,128)S(1)} %pad_maximum_fusion.3), channel_id=1, source_target_pairs={{0,1},{1,0},{2,3},{3,2},{4,5},{5,4},{6,7},{7,6},{8,9},{9,8},{10,11... | collective-permute-start | bytes 405512 | tf_op jit(solution)/shard_map/ppermute | solution.py:92
  104.1 4.4 %collective-permute-start.34 = (f32[2,128,66]{1,0,2:T(2,128)S(1)}, f32[2,128,66]{1,0,2:T(2,128)S(1)}, u32[]{:S(2)}, u32[]{:S(2)}) collective-permute-start(f32[2,128,66]{1,0,2:T(2,128)S(1)} %pad_maximum_fusion.4), channel_id=1, source_target_pairs={{0,4},{4,0},{8,12},{12,8},{1,5},{5,1},{9,13},{13,9},{2,6},{6,2},{1... | collective-permute-start | bytes 202760 | tf_op jit(solution)/shard_map/ppermute | solution.py:92
  108.6 4.9 %collective-permute-start.35 = (f32[128,66]{0,1:T(8,128)S(1)}, f32[128,66]{0,1:T(8,128)S(1)}, u32[]{:S(2)}, u32[]{:S(2)}) collective-permute-start(f32[128,66]{0,1:T(8,128)S(1)} %pad_maximum_fusion.13), channel_id=1, source_target_pairs={{0,8},{4,12},{8,0},{12,4},{1,9},{5,13},{9,1},{13,5},{2,10},{6,14},... | collective-permute-start | bytes 101384 | tf_op jit(solution)/shard_map/ppermute | solution.py:92

commit v3 on v2

--- a/solution.py
+++ b/solution.py
@@ -130,6 +130,30 @@
     return (f_pot,) + fate_pullback(cost, log_b, g_pot, fate_panel)
 
 
+def lse_scatter_exchange(maxima, totals, weighted, name):
+    size = lax.axis_size(name)
+    index = lax.axis_index(name)
+    fates = weighted.shape[-1]
+    packed = jnp.concatenate([weighted, maxima[..., None], totals[..., None]], axis=-1)
+    parts = [lax.dynamic_index_in_dim(packed, index, axis=0, keepdims=False)]
+    for shift in range(1, size):
+        perm = [(i, (i + shift) % size) for i in range(size)]
+        send = lax.dynamic_index_in_dim(packed, (index + shift) % size, axis=0, keepdims=False)
+        parts.append(lax.ppermute(send, name, perm))
+    top = parts[0][..., fates]
+    for part in parts[1:]:
+        top = jnp.maximum(top, part[..., fates])
+    totals = None
+    weighted = None
+    for part in parts:
+        factor = jnp.exp(part[..., fates] - top)
+        add_s = part[..., fates + 1] * factor
+        add_w = part[..., :fates] * factor[..., None]
+        totals = add_s if totals is None else totals + add_s
+        weighted = add_w if weighted is None else weighted + add_w
+    return top, totals, weighted
+
+
 def fate_pullback(cost, log_b, g_pot, fate_panel):
     src_count = cost.shape[0]
     scores = log_b[None, :] + (g_pot[None, :] - cost) / entropic
@@ -142,7 +166,15 @@
     col_size = lax.axis_size("cols")
     rep_size = lax.axis_size("rep")
     fates = fate_panel.shape[1]
-    if is_pow2(col_size) and is_pow2(rep_size):
+    if rep_size == 2 and col_size <= 8:
+        block = src_count // (col_size * rep_size)
+        maxima = jnp.swapaxes(maxima.reshape(col_size, rep_size, block), 0, 1)
+        totals = jnp.swapaxes(totals.reshape(col_size, rep_size, block), 0, 1)
+        weighted = jnp.swapaxes(weighted.reshape(col_size, rep_size, block, fates), 0, 1)
+        maxima, totals, weighted = lse_halving(maxima, totals, weighted, [("rep", 1)])
+        maxima, totals, weighted = lse_scatter_exchange(maxima, totals, weighted, "cols")
+        fate_rows = weighted / totals[:, None]
+    elif is_pow2(col_size) and is_pow2(rep_size):
         col_bits = col_size.bit_length() - 1
         rep_bits = rep_size.bit_length() - 1
         lead = (2,) * (col_bits + rep_bits)
@@ -177,49 +209,63 @@
 ROW_AXES = (("rep",), ("cols",))
 
 
+def row_reduce(maxima, totals):
+    for axes in ROW_AXES:
+        if len(axes) == 1 and lax.axis_size(axes[0]) == 2:
+            maxima, totals = lse_allreduce(maxima, totals, axes)
+        else:
+            maxima, totals = lse_exchange(maxima, totals, axes)
+    return maxima, totals
+
+
 def body(sources, source_mass, targets, target_mass, fate_panel):
     row_count = lax.axis_size("rows")
     if row_count != 2 or lax.axis_size("cols") > 8:
         return body_split(sources, source_mass, targets, target_mass, fate_panel)
     src_count = sources.shape[0]
     tgt_count = targets.shape[0]
+    dim = sources.shape[1]
     row = lax.axis_index("rows")
-    mine = jnp.concatenate([sources, source_mass[:, None]], axis=1)
+    mine = jnp.concatenate([sources.T, source_mass[None, :]], axis=0)
     theirs = lax.ppermute(mine, "rows", [(0, 1), (1, 0)])
-    first = jnp.where(row == 0, mine, theirs)
-    second = jnp.where(row == 0, theirs, mine)
-    gathered = jnp.concatenate([first, second], axis=0)
-    all_src = gathered[:, : sources.shape[1]]
-    all_mass = gathered[:, sources.shape[1]]
+    halves = jnp.stack([mine, theirs])
+    src_t = halves[:, :dim, :]
+    all_mass = halves[:, dim, :]
     all_sources = src_count * row_count
     all_targets = tgt_count * lax.axis_size(("cols", "rep"))
     log_a = jnp.log(all_mass / all_sources)
     log_b = jnp.log(target_mass / all_targets)
-    src_sq = jnp.sum(all_src * all_src, axis=1)
+    src_sq = jnp.sum(src_t * src_t, axis=1)
     tgt_sq = jnp.sum(targets * targets, axis=1)
-    cost = pair_cost(all_src, src_sq, targets, tgt_sq)
-
+    products = lax.dot_general(
+        src_t,
+        targets,
+        (((1,), (1,)), ((), ())),
+        precision=lax.Precision.HIGHEST,
+        preferred_element_type=jnp.float32,
+    )
+    cost = (src_sq[:, :, None] + tgt_sq[None, None, :] - 2.0 * products) / dim
+
+    first = row == 0
     g_pot = jnp.zeros((tgt_count,), jnp.float32)
-    f_all = jnp.zeros((all_sources,), jnp.float32)
     for iteration in range(ITERS):
-        scores = log_b[None, :] + (g_pot[None, :] - cost) / entropic
+        scores = log_b[None, None, :] + (g_pot[None, None, :] - cost) / entropic
+        maxima = jnp.max(scores, axis=2)
+        totals = jnp.sum(jnp.exp(scores - maxima[:, :, None]), axis=2)
+        maxima, totals = row_reduce(maxima, totals)
+        f_both = -relaxed * entropic * (maxima + jnp.log(totals))
+
+        scores = log_a[:, :, None] + (f_both[:, :, None] - cost) / entropic
         maxima = jnp.max(scores, axis=1)
-        totals = jnp.sum(jnp.exp(scores - maxima[:, None]), axis=1)
-        for axes in ROW_AXES:
-            if len(axes) == 1 and lax.axis_size(axes[0]) == 2:
-                maxima, totals = lse_allreduce(maxima, totals, axes)
-            else:
-                maxima, totals = lse_exchange(maxima, totals, axes)
-        f_all = -relaxed * entropic * (maxima + jnp.log(totals))
-
-        scores = log_a[:, None] + (f_all[:, None] - cost) / entropic
-        maxima = jnp.max(scores, axis=0)
-        totals = jnp.sum(jnp.exp(scores - maxima[None, :]), axis=0)
+        totals = jnp.sum(jnp.exp(scores - maxima[:, None, :]), axis=1)
+        lo_m = jnp.where(first, maxima[0], maxima[1])
+        hi_m = jnp.where(first, maxima[1], maxima[0])
+        lo_s = jnp.where(first, totals[0], totals[1])
+        hi_s = jnp.where(first, totals[1], totals[0])
+        maxima, totals = merge(lo_m, lo_s, hi_m, hi_s)
         g_pot = -relaxed * entropic * (maxima + jnp.log(totals))
 
-    f_pot = lax.dynamic_slice_in_dim(f_all, row * src_count, src_count)
-    cost_mine = lax.dynamic_slice_in_dim(cost, row * src_count, src_count, axis=0)
-    return (f_pot,) + fate_pullback(cost_mine, log_b, g_pot, fate_panel)
+    return (f_both[0],) + fate_pullback(cost[0], log_b, g_pot, fate_panel)
 
 
 def solution(mesh):

time: 114 us -> 118 us (1.035)
  starting transfers between devices: 40.4 us -> 32.8 us
  other arithmetic: 21.1 us -> 26.9 us
  waiting for transfers between devices: 46.3 us -> 50.9 us
  matrix products: 3.39 us -> 4.94 us
    ppermute x24, starting transfers between devices: 35.6 us -> 26 us  [lse_exchange(): received.append(lax.ppermute(payload, axes, perm))]
    ppermute x24, waiting for transfers between devices: 22.7 us -> 31.7 us  [lse_exchange(): received.append(lax.ppermute(payload, axes, perm))]
    ppermute x3 -> x1, waiting for transfers between devices: 8.86 us -> 1.31 us  [lse_halving(): packed = lax.ppermute(packed, name, perm)]
    reduce_sum x17, other arithmetic: 9.16 us -> 12.7 us  [the longest x8 6.71 us: body(): totals = jnp.sum(jnp.exp(scores - maxima[:, :, None]), axis=2)]
    reduce_max x7 -> x8, other arithmetic: 2.55 us -> 5.71 us  [body(): maxima = jnp.max(scores, axis=1)]
    ppermute x0 -> x3, waiting for transfers between devices: none -> 3.12 us  [lse_scatter_exchange(): parts.append(lax.ppermute(send, name, perm))]
    ppermute x0 -> x3, starting transfers between devices: none -> 3.1 us  [lse_scatter_exchange(): parts.append(lax.ppermute(send, name, perm))]
    dot_general x1, matrix products: 2.33 us -> 3.57 us  [body(): lax.dot_general(src_t, targets, (((1,), (1,)), ((), ())), precision=lax.P...]
  transfers between devices with their start and end apart: 36 -> 37, of which waited for: 34 -> 35; matrix products, arithmetic and copies ran while one was open for 2% -> 2% of each run, Pallas kernels for 0% -> 0%
where the time goes in v3:
time: 118 us
  waiting for transfers between devices  50.9 us (43%)
  starting transfers between devices  32.8 us (28%)
  other arithmetic  26.9 us (23%)
  matrix products  4.94 us (4%)
  between operations  1.5 us (1%)
    ppermute x24, waiting for transfers between devices, lse_exchange(): received.append(lax.ppermute(payload, axes, perm))  31.7 us
    ppermute x24, starting transfers between devices, lse_exchange(): received.append(lax.ppermute(payload, axes, perm))  26 us
    ppermute x8, waiting for transfers between devices, lse_allreduce(): other = lax.ppermute(jnp.stack([maxima, totals]), name, perm)  9.28 us
    reduce_sum x8, other arithmetic, body(): totals = jnp.sum(jnp.exp(scores - maxima[:, :, None]), axis=2)  6.71 us
    reduce_sum x8, other arithmetic, body(): totals = jnp.sum(jnp.exp(scores - maxima[:, None, :]), axis=1)  5.96 us
    reduce_max x8, other arithmetic, body(): maxima = jnp.max(scores, axis=1)  5.71 us
    ppermute x1, waiting for transfers between devices, body(): theirs = lax.ppermute(mine, 'rows', [(0, 1), (1, 0)])  5.46 us
    dot_general x1, matrix products, body(): lax.dot_general(src_t, targets, (((1,), (1,)), ((), ())), precision=lax.P...  3.57 us
  transfers between devices with their start and end apart: 37, of which 35 were waited for; matrix products, arithmetic and copies ran while one was open for 2% of the time, Pallas kernels for 0%

profile of v3, /device:TPU:0, one launch (start us, length us, event | category | flops | bytes accessed | tf_op | source)
XLA Modules:
  0.0 117.7 jit_solution(5683353249910146170)
XLA Ops:
  0.6 1.1 fusion.203
  1.7 3.0 %collective-permute-start = (f32[65,1024]{1,0:T(8,128)S(1)}, f32[65,1024]{1,0:T(8,128)S(1)}, u32[]{:S(2)}, u32[]{:S(2)}) collective-permute-start(f32[65,1024]{1,0:T(8,128)S(1)} %get-tuple-element.15), channel_id=1, source_target_pairs={{0,2},{2,0},{1,3},{3,1},{4,6},{6,4},{5,7},{7,5},{8,10},{10,8},{9,1... | collective-permute-start | bytes 798728 | tf_op jit(solution)/shard_map/ppermute | solution.py:230
  6.3 5.5 %collective-permute-done = f32[65,1024]{1,0:T(8,128)S(1)} collective-permute-done((f32[65,1024]{1,0:T(8,128)S(1)}, f32[65,1024]{1,0:T(8,128)S(1)}, u32[]{:S(2)}, u32[]{:S(2)}) %collective-permute-start) | collective-permute-done | bytes 266272 | tf_op jit(solution)/shard_map/ppermute | solution.py:230
  11.8 3.6 %fusion = (f32[2,1024]{1,0:T(2,128)S(1)}, f32[2,1024,256]{2,1,0:T(8,128)S(1)}) fusion(f32[256]{0:T(256)S(1)} %multiply_log_fusion, f32[256,64]{0,1:T(8,128)} %param.7, f32[1,65,1024]{2,1,0:T(8,128)S(1)} %bitcast.654, f32[1,65,1024]{2,1,0:T(8,128)S(1)} %get-tuple-element.14, f32[256]{0:T(256)S(1)} %multiply_reduce_fusion.1, ...), kind=kOutput, calls=%fused_computation.33 | convolution fusion | flops 406976512 | bytes 2713600 | tf_op jit(solution)/shard_map/dot_general | solution.py:240
  16.4 1.1 collective-permute-done.1
  17.5 3.9 %collective-permute-start.4 = (f32[2,2,1024]{2,1,0:T(2,128)S(1)}, f32[2,2,1024]{2,1,0:T(2,128)S(1)}, u32[]{:S(2)}, u32[]{:S(2)}) collective-permute-start(f32[2,2,1024]{2,1,0:T(2,128)S(1)} %get-tuple-element.55), channel_id=1, source_target_pairs={{0,12},{4,0},{8,4},{12,8},{1,13},{5,1},{9,5},{13,9},{2,14},{6,2},{... | collective-permute-start | bytes 49160 | tf_op jit(solution)/shard_map/ppermute | solution.py:62
  21.4 1.0 collective-permute-start.2
  22.9 3.2 %collective-permute-done.3 = f32[2,2,1024]{2,1,0:T(2,128)S(1)} collective-permute-done((f32[2,2,1024]{2,1,0:T(2,128)S(1)}, f32[2,2,1024]{2,1,0:T(2,128)S(1)}, u32[]{:S(2)}, u32[]{:S(2)}) %collective-permute-start.3) | collective-permute-done | bytes 16416 | tf_op jit(solution)/shard_map/ppermute | solution.py:62
  26.1 0.9 collective-permute-done.2
  29.9 1.2 collective-permute-done.5
  32.4 1.9 %collective-permute-start.6 = (f32[2,2,1024]{2,1,0:T(2,128)S(1)}, f32[2,2,1024]{2,1,0:T(2,128)S(1)}, u32[]{:S(2)}, u32[]{:S(2)}) collective-permute-start(f32[2,2,1024]{2,1,0:T(2,128)S(1)} %get-tuple-element.53), channel_id=1, source_target_pairs={{0,4},{4,8},{8,12},{12,0},{1,5},{5,9},{9,13},{13,1},{2,6},{6,10},{... | collective-permute-start | bytes 49160 | tf_op jit(solution)/shard_map/ppermute | solution.py:62
  34.9 1.5 %collective-permute-done.7 = f32[2,2,1024]{2,1,0:T(2,128)S(1)} collective-permute-done((f32[2,2,1024]{2,1,0:T(2,128)S(1)}, f32[2,2,1024]{2,1,0:T(2,128)S(1)}, u32[]{:S(2)}, u32[]{:S(2)}) %collective-permute-start.7) | collective-permute-done | bytes 16416 | tf_op jit(solution)/shard_map/ppermute | solution.py:62
  36.4 1.5 %collective-permute-done.6 = f32[2,2,1024]{2,1,0:T(2,128)S(1)} collective-permute-done((f32[2,2,1024]{2,1,0:T(2,128)S(1)}, f32[2,2,1024]{2,1,0:T(2,128)S(1)}, u32[]{:S(2)}, u32[]{:S(2)}) %collective-permute-start.6) | collective-permute-done | bytes 16416 | tf_op jit(solution)/shard_map/ppermute | solution.py:62
  40.8 1.2 collective-permute-done.9
  42.1 1.4 %collective-permute-start.12 = (f32[2,2,1024]{2,1,0:T(2,128)S(1)}, f32[2,2,1024]{2,1,0:T(2,128)S(1)}, u32[]{:S(2)}, u32[]{:S(2)}) collective-permute-start(f32[2,2,1024]{2,1,0:T(2,128)S(1)} %get-tuple-element.51), channel_id=1, source_target_pairs={{0,12},{4,0},{8,4},{12,8},{1,13},{5,1},{9,5},{13,9},{2,14},{6,2},{... | collective-permute-start | bytes 49160 | tf_op jit(solution)/shard_map/ppermute | solution.py:62
  43.7 0.9 collective-permute-start.10
  44.6 1.2 %collective-permute-done.12 = f32[2,2,1024]{2,1,0:T(2,128)S(1)} collective-permute-done((f32[2,2,1024]{2,1,0:T(2,128)S(1)}, f32[2,2,1024]{2,1,0:T(2,128)S(1)}, u32[]{:S(2)}, u32[]{:S(2)}) %collective-permute-start.12) | collective-permute-done | bytes 16416 | tf_op jit(solution)/shard_map/ppermute | solution.py:62
  45.8 2.3 %collective-permute-done.11 = f32[2,2,1024]{2,1,0:T(2,128)S(1)} collective-permute-done((f32[2,2,1024]{2,1,0:T(2,128)S(1)}, f32[2,2,1024]{2,1,0:T(2,128)S(1)}, u32[]{:S(2)}, u32[]{:S(2)}) %collective-permute-start.11) | collective-permute-done | bytes 16416 | tf_op jit(solution)/shard_map/ppermute | solution.py:62
  48.1 1.1 collective-permute-done.10
  52.2 1.2 collective-permute-done.13
  53.4 1.0 collective-permute-start.16
  54.5 1.8 %collective-permute-start.14 = (f32[2,2,1024]{2,1,0:T(2,128)S(1)}, f32[2,2,1024]{2,1,0:T(2,128)S(1)}, u32[]{:S(2)}, u32[]{:S(2)}) collective-permute-start(f32[2,2,1024]{2,1,0:T(2,128)S(1)} %get-tuple-element.49), channel_id=1, source_target_pairs={{0,4},{4,8},{8,12},{12,0},{1,5},{5,9},{9,13},{13,1},{2,6},{6,10},{... | collective-permute-start | bytes 49160 | tf_op jit(solution)/shard_map/ppermute | solution.py:62
  57.2 1.9 %collective-permute-done.15 = f32[2,2,1024]{2,1,0:T(2,128)S(1)} collective-permute-done((f32[2,2,1024]{2,1,0:T(2,128)S(1)}, f32[2,2,1024]{2,1,0:T(2,128)S(1)}, u32[]{:S(2)}, u32[]{:S(2)}) %collective-permute-start.15) | collective-permute-done | bytes 16416 | tf_op jit(solution)/shard_map/ppermute | solution.py:62
  59.1 1.0 collective-permute-done.14
  63.0 1.2 collective-permute-done.17
  64.2 1.6 %collective-permute-start.20 = (f32[2,2,1024]{2,1,0:T(2,128)S(1)}, f32[2,2,1024]{2,1,0:T(2,128)S(1)}, u32[]{:S(2)}, u32[]{:S(2)}) collective-permute-start(f32[2,2,1024]{2,1,0:T(2,128)S(1)} %get-tuple-element.47), channel_id=1, source_target_pairs={{0,12},{4,0},{8,4},{12,8},{1,13},{5,1},{9,5},{13,9},{2,14},{6,2},{... | collective-permute-start | bytes 49160 | tf_op jit(solution)/shard_map/ppermute | solution.py:62
  65.8 1.5 %collective-permute-start.18 = (f32[2,2,1024]{2,1,0:T(2,128)S(1)}, f32[2,2,1024]{2,1,0:T(2,128)S(1)}, u32[]{:S(2)}, u32[]{:S(2)}) collective-permute-start(f32[2,2,1024]{2,1,0:T(2,128)S(1)} %get-tuple-element.47), channel_id=1, source_target_pairs={{0,4},{4,8},{8,12},{12,0},{1,5},{5,9},{9,13},{13,1},{2,6},{6,10},{... | collective-permute-start | bytes 49160 | tf_op jit(solution)/shard_map/ppermute | solution.py:62
  68.0 2.6 %collective-permute-done.19 = f32[2,2,1024]{2,1,0:T(2,128)S(1)} collective-permute-done((f32[2,2,1024]{2,1,0:T(2,128)S(1)}, f32[2,2,1024]{2,1,0:T(2,128)S(1)}, u32[]{:S(2)}, u32[]{:S(2)}) %collective-permute-start.19) | collective-permute-done | bytes 16416 | tf_op jit(solution)/shard_map/ppermute | solution.py:62
  74.2 1.2 collective-permute-done.21
  75.5 1.1 collective-permute-start.24
  76.7 1.9 %collective-permute-start.22 = (f32[2,2,1024]{2,1,0:T(2,128)S(1)}, f32[2,2,1024]{2,1,0:T(2,128)S(1)}, u32[]{:S(2)}, u32[]{:S(2)}) collective-permute-start(f32[2,2,1024]{2,1,0:T(2,128)S(1)} %get-tuple-element.45), channel_id=1, source_target_pairs={{0,4},{4,8},{8,12},{12,0},{1,5},{5,9},{9,13},{13,1},{2,6},{6,10},{... | collective-permute-start | bytes 49160 | tf_op jit(solution)/shard_map/ppermute | solution.py:62
  79.3 2.1 %collective-permute-done.23 = f32[2,2,1024]{2,1,0:T(2,128)S(1)} collective-permute-done((f32[2,2,1024]{2,1,0:T(2,128)S(1)}, f32[2,2,1024]{2,1,0:T(2,128)S(1)}, u32[]{:S(2)}, u32[]{:S(2)}) %collective-permute-start.23) | collective-permute-done | bytes 16416 | tf_op jit(solution)/shard_map/ppermute | solution.py:62
  81.3 0.9 collective-permute-done.22
  85.2 1.2 collective-permute-done.25
  86.4 1.4 %collective-permute-start.28 = (f32[2,2,1024]{2,1,0:T(2,128)S(1)}, f32[2,2,1024]{2,1,0:T(2,128)S(1)}, u32[]{:S(2)}, u32[]{:S(2)}) collective-permute-start(f32[2,2,1024]{2,1,0:T(2,128)S(1)} %get-tuple-element.43), channel_id=1, source_target_pairs={{0,12},{4,0},{8,4},{12,8},{1,13},{5,1},{9,5},{13,9},{2,14},{6,2},{... | collective-permute-start | bytes 49160 | tf_op jit(solution)/shard_map/ppermute | solution.py:62
  88.1 1.4 %collective-permute-start.26 = (f32[2,2,1024]{2,1,0:T(2,128)S(1)}, f32[2,2,1024]{2,1,0:T(2,128)S(1)}, u32[]{:S(2)}, u32[]{:S(2)}) collective-permute-start(f32[2,2,1024]{2,1,0:T(2,128)S(1)} %get-tuple-element.43), channel_id=1, source_target_pairs={{0,4},{4,8},{8,12},{12,0},{1,5},{5,9},{9,13},{13,1},{2,6},{6,10},{... | collective-permute-start | bytes 49160 | tf_op jit(solution)/shard_map/ppermute | solution.py:62
  90.2 2.3 %collective-permute-done.27 = f32[2,2,1024]{2,1,0:T(2,128)S(1)} collective-permute-done((f32[2,2,1024]{2,1,0:T(2,128)S(1)}, f32[2,2,1024]{2,1,0:T(2,128)S(1)}, u32[]{:S(2)}, u32[]{:S(2)}) %collective-permute-start.27) | collective-permute-done | bytes 16416 | tf_op jit(solution)/shard_map/ppermute | solution.py:62
  92.5 1.1 collective-permute-done.26
  96.5 1.2 collective-permute-done.29
  97.7 1.0 collective-permute-start.32
  98.9 1.8 %collective-permute-start.30 = (f32[2,2,1024]{2,1,0:T(2,128)S(1)}, f32[2,2,1024]{2,1,0:T(2,128)S(1)}, u32[]{:S(2)}, u32[]{:S(2)}) collective-permute-start(f32[2,2,1024]{2,1,0:T(2,128)S(1)} %get-tuple-element.41), channel_id=1, source_target_pairs={{0,4},{4,8},{8,12},{12,0},{1,5},{5,9},{9,13},{13,1},{2,6},{6,10},{... | collective-permute-start | bytes 49160 | tf_op jit(solution)/shard_map/ppermute | solution.py:62
  101.5 1.9 %collective-permute-done.31 = f32[2,2,1024]{2,1,0:T(2,128)S(1)} collective-permute-done((f32[2,2,1024]{2,1,0:T(2,128)S(1)}, f32[2,2,1024]{2,1,0:T(2,128)S(1)}, u32[]{:S(2)}, u32[]{:S(2)}) %collective-permute-start.31) | collective-permute-done | bytes 16416 | tf_op jit(solution)/shard_map/ppermute | solution.py:62
  103.4 1.0 collective-permute-done.30
  106.7 1.4 %convolution_bitcast_fusion = f32[2,4,128,64]{2,3,0,1:T(8,128)S(1)} fusion(f32[4,2,128,256]{3,2,1,0:T(8,128)S(1)} %bitcast.656, f32[4,2,128]{2,1,0:T(2,128)S(1)} %bitcast.675, f32[256]{0:T(256)S(1)} %bitcast.705, f32[256]{0:T(256)S(1)} %multiply_log_fusion, f32[256,64]{0,1:T(8,128)S(1)} %copy-done), kind=kOutput, calls=%fused_computation.49 | convolution fusion | flops 202375168 | bytes 1382400 | tf_op jit(solution)/shard_map/dot_general | solution.py:163
  108.2 1.3 %collective-permute-done.33 = f32[4,128,66]{1,2,0:T(8,128)S(1)} collective-permute-done((f32[4,128,66]{1,2,0:T(8,128)S(1)}, f32[4,128,66]{1,2,0:T(8,128)S(1)}, u32[]{:S(2)}, u32[]{:S(2)}) %collective-permute-start.33) | collective-permute-done | bytes 135200 | tf_op jit(solution)/shard_map/ppermute | solution.py:92
  109.7 1.6 %collective-permute-start.36 = (f32[128,66]{0,1:T(8,128)S(1)}, f32[128,66]{0,1:T(8,128)S(1)}, u32[]{:S(2)}, u32[]{:S(2)}) collective-permute-start(f32[128,66]{0,1:T(8,128)S(1)} %get-tuple-element.17), channel_id=1, source_target_pairs={{0,12},{4,0},{8,4},{12,8},{1,13},{5,1},{9,5},{13,9},{2,14},{6,2},{... | collective-permute-start | bytes 101384 | tf_op jit(solution)/shard_map/ppermute | solution.py:142
  111.2 1.5 %collective-permute-start.34 = (f32[128,66]{0,1:T(8,128)S(1)}, f32[128,66]{0,1:T(8,128)S(1)}, u32[]{:S(2)}, u32[]{:S(2)}) collective-permute-start(f32[128,66]{0,1:T(8,128)S(1)} %get-tuple-element.19), channel_id=1, source_target_pairs={{0,4},{4,8},{8,12},{12,0},{1,5},{5,9},{9,13},{13,1},{2,6},{6,10},{... | collective-permute-start | bytes 101384 | tf_op jit(solution)/shard_map/ppermute | solution.py:142
  113.9 3.1 %collective-permute-done.35 = f32[128,66]{0,1:T(8,128)S(1)} collective-permute-done((f32[128,66]{0,1:T(8,128)S(1)}, f32[128,66]{0,1:T(8,128)S(1)}, u32[]{:S(2)}, u32[]{:S(2)}) %collective-permute-start.35) | collective-permute-done | bytes 33824 | tf_op jit(solution)/shard_map/ppermute | solution.py:142
  (146 shorter events, 34.5 us)
Async XLA Ops:
  0.6 106.1 %copy-start = (f32[256,64]{0,1:T(8,128)S(1)}, f32[256,64]{0,1:T(8,128)}, u32[]{:S(2)}) copy-start(f32[256,64]{0,1:T(8,128)} %param.9) | copy-start | bytes 196612
  1.7 10.0 %collective-permute-start = (f32[65,1024]{1,0:T(8,128)S(1)}, f32[65,1024]{1,0:T(8,128)S(1)}, u32[]{:S(2)}, u32[]{:S(2)}) collective-permute-start(f32[65,1024]{1,0:T(8,128)S(1)} %get-tuple-element.15), channel_id=1, source_target_pairs={{0,2},{2,0},{1,3},{3,1},{4,6},{6,4},{5,7},{7,5},{8,10},{10,8},{9,1... | collective-permute-start | bytes 798728 | tf_op jit(solution)/shard_map/ppermute | solution.py:230
  16.2 1.2 %collective-permute-start.1 = (f32[2,2,1024]{2,1,0:T(2,128)S(1)}, f32[2,2,1024]{2,1,0:T(2,128)S(1)}, u32[]{:S(2)}, u32[]{:S(2)}) collective-permute-start(f32[2,2,1024]{2,1,0:T(2,128)S(1)} %pad_maximum_fusion.13), channel_id=1, source_target_pairs={{0,1},{1,0},{2,3},{3,2},{4,5},{5,4},{6,7},{7,6},{8,9},{9,8},{10,11... | collective-permute-start | bytes 49160 | tf_op jit(solution)/shard_map/ppermute | solution.py:43
  17.5 5.3 %collective-permute-start.4 = (f32[2,2,1024]{2,1,0:T(2,128)S(1)}, f32[2,2,1024]{2,1,0:T(2,128)S(1)}, u32[]{:S(2)}, u32[]{:S(2)}) collective-permute-start(f32[2,2,1024]{2,1,0:T(2,128)S(1)} %get-tuple-element.55), channel_id=1, source_target_pairs={{0,12},{4,0},{8,4},{12,8},{1,13},{5,1},{9,5},{13,9},{2,14},{6,2},{... | collective-permute-start | bytes 49160 | tf_op jit(solution)/shard_map/ppermute | solution.py:62
  21.4 4.6 %collective-permute-start.3 = (f32[2,2,1024]{2,1,0:T(2,128)S(1)}, f32[2,2,1024]{2,1,0:T(2,128)S(1)}, u32[]{:S(2)}, u32[]{:S(2)}) collective-permute-start(f32[2,2,1024]{2,1,0:T(2,128)S(1)} %get-tuple-element.55), channel_id=1, source_target_pairs={{0,8},{4,12},{8,0},{12,4},{1,9},{5,13},{9,1},{13,5},{2,10},{6,14},... | collective-permute-start | bytes 49160 | tf_op jit(solution)/shard_map/ppermute | solution.py:62
  21.4 5.5 %collective-permute-start.2 = (f32[2,2,1024]{2,1,0:T(2,128)S(1)}, f32[2,2,1024]{2,1,0:T(2,128)S(1)}, u32[]{:S(2)}, u32[]{:S(2)}) collective-permute-start(f32[2,2,1024]{2,1,0:T(2,128)S(1)} %get-tuple-element.55), channel_id=1, source_target_pairs={{0,4},{4,8},{8,12},{12,0},{1,5},{5,9},{9,13},{13,1},{2,6},{6,10},{... | collective-permute-start | bytes 49160 | tf_op jit(solution)/shard_map/ppermute | solution.py:62
  29.8 1.2 %collective-permute-start.5 = (f32[2,2,1024]{2,1,0:T(2,128)S(1)}, f32[2,2,1024]{2,1,0:T(2,128)S(1)}, u32[]{:S(2)}, u32[]{:S(2)}) collective-permute-start(f32[2,2,1024]{2,1,0:T(2,128)S(1)} %pad_maximum_fusion.15), channel_id=1, source_target_pairs={{0,1},{1,0},{2,3},{3,2},{4,5},{5,4},{6,7},{7,6},{8,9},{9,8},{10,11... | collective-permute-start | bytes 49160 | tf_op jit(solution)/shard_map/ppermute | solution.py:43
  31.1 3.8 %collective-permute-start.8 = (f32[2,2,1024]{2,1,0:T(2,128)S(1)}, f32[2,2,1024]{2,1,0:T(2,128)S(1)}, u32[]{:S(2)}, u32[]{:S(2)}) collective-permute-start(f32[2,2,1024]{2,1,0:T(2,128)S(1)} %get-tuple-element.53), channel_id=1, source_target_pairs={{0,12},{4,0},{8,4},{12,8},{1,13},{5,1},{9,5},{13,9},{2,14},{6,2},{... | collective-permute-start | bytes 49160 | tf_op jit(solution)/shard_map/ppermute | solution.py:62
  31.7 4.6 %collective-permute-start.7 = (f32[2,2,1024]{2,1,0:T(2,128)S(1)}, f32[2,2,1024]{2,1,0:T(2,128)S(1)}, u32[]{:S(2)}, u32[]{:S(2)}) collective-permute-start(f32[2,2,1024]{2,1,0:T(2,128)S(1)} %get-tuple-element.53), channel_id=1, source_target_pairs={{0,8},{4,12},{8,0},{12,4},{1,9},{5,13},{9,1},{13,5},{2,10},{6,14},... | collective-permute-start | bytes 49160 | tf_op jit(solution)/shard_map/ppermute | solution.py:62
  32.4 5.5 %collective-permute-start.6 = (f32[2,2,1024]{2,1,0:T(2,128)S(1)}, f32[2,2,1024]{2,1,0:T(2,128)S(1)}, u32[]{:S(2)}, u32[]{:S(2)}) collective-permute-start(f32[2,2,1024]{2,1,0:T(2,128)S(1)} %get-tuple-element.53), channel_id=1, source_target_pairs={{0,4},{4,8},{8,12},{12,0},{1,5},{5,9},{9,13},{13,1},{2,6},{6,10},{... | collective-permute-start | bytes 49160 | tf_op jit(solution)/shard_map/ppermute | solution.py:62
  40.8 1.2 %collective-permute-start.9 = (f32[2,2,1024]{2,1,0:T(2,128)S(1)}, f32[2,2,1024]{2,1,0:T(2,128)S(1)}, u32[]{:S(2)}, u32[]{:S(2)}) collective-permute-start(f32[2,2,1024]{2,1,0:T(2,128)S(1)} %pad_maximum_fusion.17), channel_id=1, source_target_pairs={{0,1},{1,0},{2,3},{3,2},{4,5},{5,4},{6,7},{7,6},{8,9},{9,8},{10,11... | collective-permute-start | bytes 49160 | tf_op jit(solution)/shard_map/ppermute | solution.py:43
  42.1 3.8 %collective-permute-start.12 = (f32[2,2,1024]{2,1,0:T(2,128)S(1)}, f32[2,2,1024]{2,1,0:T(2,128)S(1)}, u32[]{:S(2)}, u32[]{:S(2)}) collective-permute-start(f32[2,2,1024]{2,1,0:T(2,128)S(1)} %get-tuple-element.51), channel_id=1, source_target_pairs={{0,12},{4,0},{8,4},{12,8},{1,13},{5,1},{9,5},{13,9},{2,14},{6,2},{... | collective-permute-start | bytes 49160 | tf_op jit(solution)/shard_map/ppermute | solution.py:62
  43.5 4.6 %collective-permute-start.11 = (f32[2,2,1024]{2,1,0:T(2,128)S(1)}, f32[2,2,1024]{2,1,0:T(2,128)S(1)}, u32[]{:S(2)}, u32[]{:S(2)}) collective-permute-start(f32[2,2,1024]{2,1,0:T(2,128)S(1)} %get-tuple-element.51), channel_id=1, source_target_pairs={{0,8},{4,12},{8,0},{12,4},{1,9},{5,13},{9,1},{13,5},{2,10},{6,14},... | collective-permute-start | bytes 49160 | tf_op jit(solution)/shard_map/ppermute | solution.py:62
  43.7 5.5 %collective-permute-start.10 = (f32[2,2,1024]{2,1,0:T(2,128)S(1)}, f32[2,2,1024]{2,1,0:T(2,128)S(1)}, u32[]{:S(2)}, u32[]{:S(2)}) collective-permute-start(f32[2,2,1024]{2,1,0:T(2,128)S(1)} %get-tuple-element.51), channel_id=1, source_target_pairs={{0,4},{4,8},{8,12},{12,0},{1,5},{5,9},{9,13},{13,1},{2,6},{6,10},{... | collective-permute-start | bytes 49160 | tf_op jit(solution)/shard_map/ppermute | solution.py:62
  52.1 1.2 %collective-permute-start.13 = (f32[2,2,1024]{2,1,0:T(2,128)S(1)}, f32[2,2,1024]{2,1,0:T(2,128)S(1)}, u32[]{:S(2)}, u32[]{:S(2)}) collective-permute-start(f32[2,2,1024]{2,1,0:T(2,128)S(1)} %pad_maximum_fusion.19), channel_id=1, source_target_pairs={{0,1},{1,0},{2,3},{3,2},{4,5},{5,4},{6,7},{7,6},{8,9},{9,8},{10,11... | collective-permute-start | bytes 49160 | tf_op jit(solution)/shard_map/ppermute | solution.py:43
  53.4 3.8 %collective-permute-start.16 = (f32[2,2,1024]{2,1,0:T(2,128)S(1)}, f32[2,2,1024]{2,1,0:T(2,128)S(1)}, u32[]{:S(2)}, u32[]{:S(2)}) collective-permute-start(f32[2,2,1024]{2,1,0:T(2,128)S(1)} %get-tuple-element.49), channel_id=1, source_target_pairs={{0,12},{4,0},{8,4},{12,8},{1,13},{5,1},{9,5},{13,9},{2,14},{6,2},{... | collective-permute-start | bytes 49160 | tf_op jit(solution)/shard_map/ppermute | solution.py:62
  54.4 4.6 %collective-permute-start.15 = (f32[2,2,1024]{2,1,0:T(2,128)S(1)}, f32[2,2,1024]{2,1,0:T(2,128)S(1)}, u32[]{:S(2)}, u32[]{:S(2)}) collective-permute-start(f32[2,2,1024]{2,1,0:T(2,128)S(1)} %get-tuple-element.49), channel_id=1, source_target_pairs={{0,8},{4,12},{8,0},{12,4},{1,9},{5,13},{9,1},{13,5},{2,10},{6,14},... | collective-permute-start | bytes 49160 | tf_op jit(solution)/shard_map/ppermute | solution.py:62
  54.5 5.5 %collective-permute-start.14 = (f32[2,2,1024]{2,1,0:T(2,128)S(1)}, f32[2,2,1024]{2,1,0:T(2,128)S(1)}, u32[]{:S(2)}, u32[]{:S(2)}) collective-permute-start(f32[2,2,1024]{2,1,0:T(2,128)S(1)} %get-tuple-element.49), channel_id=1, source_target_pairs={{0,4},{4,8},{8,12},{12,0},{1,5},{5,9},{9,13},{13,1},{2,6},{6,10},{... | collective-permute-start | bytes 49160 | tf_op jit(solution)/shard_map/ppermute | solution.py:62
  62.9 1.2 %collective-permute-start.17 = (f32[2,2,1024]{2,1,0:T(2,128)S(1)}, f32[2,2,1024]{2,1,0:T(2,128)S(1)}, u32[]{:S(2)}, u32[]{:S(2)}) collective-permute-start(f32[2,2,1024]{2,1,0:T(2,128)S(1)} %pad_maximum_fusion.21), channel_id=1, source_target_pairs={{0,1},{1,0},{2,3},{3,2},{4,5},{5,4},{6,7},{7,6},{8,9},{9,8},{10,11... | collective-permute-start | bytes 49160 | tf_op jit(solution)/shard_map/ppermute | solution.py:43
  64.2 3.8 %collective-permute-start.20 = (f32[2,2,1024]{2,1,0:T(2,128)S(1)}, f32[2,2,1024]{2,1,0:T(2,128)S(1)}, u32[]{:S(2)}, u32[]{:S(2)}) collective-permute-start(f32[2,2,1024]{2,1,0:T(2,128)S(1)} %get-tuple-element.47), channel_id=1, source_target_pairs={{0,12},{4,0},{8,4},{12,8},{1,13},{5,1},{9,5},{13,9},{2,14},{6,2},{... | collective-permute-start | bytes 49160 | tf_op jit(solution)/shard_map/ppermute | solution.py:62
  65.8 4.8 %collective-permute-start.19 = (f32[2,2,1024]{2,1,0:T(2,128)S(1)}, f32[2,2,1024]{2,1,0:T(2,128)S(1)}, u32[]{:S(2)}, u32[]{:S(2)}) collective-permute-start(f32[2,2,1024]{2,1,0:T(2,128)S(1)} %get-tuple-element.47), channel_id=1, source_target_pairs={{0,8},{4,12},{8,0},{12,4},{1,9},{5,13},{9,1},{13,5},{2,10},{6,14},... | collective-permute-start | bytes 49160 | tf_op jit(solution)/shard_map/ppermute | solution.py:62
  65.8 5.5 %collective-permute-start.18 = (f32[2,2,1024]{2,1,0:T(2,128)S(1)}, f32[2,2,1024]{2,1,0:T(2,128)S(1)}, u32[]{:S(2)}, u32[]{:S(2)}) collective-permute-start(f32[2,2,1024]{2,1,0:T(2,128)S(1)} %get-tuple-element.47), channel_id=1, source_target_pairs={{0,4},{4,8},{8,12},{12,0},{1,5},{5,9},{9,13},{13,1},{2,6},{6,10},{... | collective-permute-start | bytes 49160 | tf_op jit(solution)/shard_map/ppermute | solution.py:62
  74.2 1.2 %collective-permute-start.21 = (f32[2,2,1024]{2,1,0:T(2,128)S(1)}, f32[2,2,1024]{2,1,0:T(2,128)S(1)}, u32[]{:S(2)}, u32[]{:S(2)}) collective-permute-start(f32[2,2,1024]{2,1,0:T(2,128)S(1)} %pad_maximum_fusion.23), channel_id=1, source_target_pairs={{0,1},{1,0},{2,3},{3,2},{4,5},{5,4},{6,7},{7,6},{8,9},{9,8},{10,11... | collective-permute-start | bytes 49160 | tf_op jit(solution)/shard_map/ppermute | solution.py:43
  75.5 3.8 %collective-permute-start.24 = (f32[2,2,1024]{2,1,0:T(2,128)S(1)}, f32[2,2,1024]{2,1,0:T(2,128)S(1)}, u32[]{:S(2)}, u32[]{:S(2)}) collective-permute-start(f32[2,2,1024]{2,1,0:T(2,128)S(1)} %get-tuple-element.45), channel_id=1, source_target_pairs={{0,12},{4,0},{8,4},{12,8},{1,13},{5,1},{9,5},{13,9},{2,14},{6,2},{... | collective-permute-start | bytes 49160 | tf_op jit(solution)/shard_map/ppermute | solution.py:62
  76.6 4.8 %collective-permute-start.23 = (f32[2,2,1024]{2,1,0:T(2,128)S(1)}, f32[2,2,1024]{2,1,0:T(2,128)S(1)}, u32[]{:S(2)}, u32[]{:S(2)}) collective-permute-start(f32[2,2,1024]{2,1,0:T(2,128)S(1)} %get-tuple-element.45), channel_id=1, source_target_pairs={{0,8},{4,12},{8,0},{12,4},{1,9},{5,13},{9,1},{13,5},{2,10},{6,14},... | collective-permute-start | bytes 49160 | tf_op jit(solution)/shard_map/ppermute | solution.py:62
  76.7 5.5 %collective-permute-start.22 = (f32[2,2,1024]{2,1,0:T(2,128)S(1)}, f32[2,2,1024]{2,1,0:T(2,128)S(1)}, u32[]{:S(2)}, u32[]{:S(2)}) collective-permute-start(f32[2,2,1024]{2,1,0:T(2,128)S(1)} %get-tuple-element.45), channel_id=1, source_target_pairs={{0,4},{4,8},{8,12},{12,0},{1,5},{5,9},{9,13},{13,1},{2,6},{6,10},{... | collective-permute-start | bytes 49160 | tf_op jit(solution)/shard_map/ppermute | solution.py:62
  85.1 1.2 %collective-permute-start.25 = (f32[2,2,1024]{2,1,0:T(2,128)S(1)}, f32[2,2,1024]{2,1,0:T(2,128)S(1)}, u32[]{:S(2)}, u32[]{:S(2)}) collective-permute-start(f32[2,2,1024]{2,1,0:T(2,128)S(1)} %pad_maximum_fusion.25), channel_id=1, source_target_pairs={{0,1},{1,0},{2,3},{3,2},{4,5},{5,4},{6,7},{7,6},{8,9},{9,8},{10,11... | collective-permute-start | bytes 49160 | tf_op jit(solution)/shard_map/ppermute | solution.py:43
  86.4 3.8 %collective-permute-start.28 = (f32[2,2,1024]{2,1,0:T(2,128)S(1)}, f32[2,2,1024]{2,1,0:T(2,128)S(1)}, u32[]{:S(2)}, u32[]{:S(2)}) collective-permute-start(f32[2,2,1024]{2,1,0:T(2,128)S(1)} %get-tuple-element.43), channel_id=1, source_target_pairs={{0,12},{4,0},{8,4},{12,8},{1,13},{5,1},{9,5},{13,9},{2,14},{6,2},{... | collective-permute-start | bytes 49160 | tf_op jit(solution)/shard_map/ppermute | solution.py:62
  87.8 4.6 %collective-permute-start.27 = (f32[2,2,1024]{2,1,0:T(2,128)S(1)}, f32[2,2,1024]{2,1,0:T(2,128)S(1)}, u32[]{:S(2)}, u32[]{:S(2)}) collective-permute-start(f32[2,2,1024]{2,1,0:T(2,128)S(1)} %get-tuple-element.43), channel_id=1, source_target_pairs={{0,8},{4,12},{8,0},{12,4},{1,9},{5,13},{9,1},{13,5},{2,10},{6,14},... | collective-permute-start | bytes 49160 | tf_op jit(solution)/shard_map/ppermute | solution.py:62
  88.1 5.5 %collective-permute-start.26 = (f32[2,2,1024]{2,1,0:T(2,128)S(1)}, f32[2,2,1024]{2,1,0:T(2,128)S(1)}, u32[]{:S(2)}, u32[]{:S(2)}) collective-permute-start(f32[2,2,1024]{2,1,0:T(2,128)S(1)} %get-tuple-element.43), channel_id=1, source_target_pairs={{0,4},{4,8},{8,12},{12,0},{1,5},{5,9},{9,13},{13,1},{2,6},{6,10},{... | collective-permute-start | bytes 49160 | tf_op jit(solution)/shard_map/ppermute | solution.py:62
  96.4 1.2 %collective-permute-start.29 = (f32[2,2,1024]{2,1,0:T(2,128)S(1)}, f32[2,2,1024]{2,1,0:T(2,128)S(1)}, u32[]{:S(2)}, u32[]{:S(2)}) collective-permute-start(f32[2,2,1024]{2,1,0:T(2,128)S(1)} %pad_maximum_fusion.27), channel_id=1, source_target_pairs={{0,1},{1,0},{2,3},{3,2},{4,5},{5,4},{6,7},{7,6},{8,9},{9,8},{10,11... | collective-permute-start | bytes 49160 | tf_op jit(solution)/shard_map/ppermute | solution.py:43
  97.7 3.8 %collective-permute-start.32 = (f32[2,2,1024]{2,1,0:T(2,128)S(1)}, f32[2,2,1024]{2,1,0:T(2,128)S(1)}, u32[]{:S(2)}, u32[]{:S(2)}) collective-permute-start(f32[2,2,1024]{2,1,0:T(2,128)S(1)} %get-tuple-element.41), channel_id=1, source_target_pairs={{0,12},{4,0},{8,4},{12,8},{1,13},{5,1},{9,5},{13,9},{2,14},{6,2},{... | collective-permute-start | bytes 49160 | tf_op jit(solution)/shard_map/ppermute | solution.py:62
  98.8 4.6 %collective-permute-start.31 = (f32[2,2,1024]{2,1,0:T(2,128)S(1)}, f32[2,2,1024]{2,1,0:T(2,128)S(1)}, u32[]{:S(2)}, u32[]{:S(2)}) collective-permute-start(f32[2,2,1024]{2,1,0:T(2,128)S(1)} %get-tuple-element.41), channel_id=1, source_target_pairs={{0,8},{4,12},{8,0},{12,4},{1,9},{5,13},{9,1},{13,5},{2,10},{6,14},... | collective-permute-start | bytes 49160 | tf_op jit(solution)/shard_map/ppermute | solution.py:62
  98.9 5.5 %collective-permute-start.30 = (f32[2,2,1024]{2,1,0:T(2,128)S(1)}, f32[2,2,1024]{2,1,0:T(2,128)S(1)}, u32[]{:S(2)}, u32[]{:S(2)}) collective-permute-start(f32[2,2,1024]{2,1,0:T(2,128)S(1)} %get-tuple-element.41), channel_id=1, source_target_pairs={{0,4},{4,8},{8,12},{12,0},{1,5},{5,9},{9,13},{13,1},{2,6},{6,10},{... | collective-permute-start | bytes 49160 | tf_op jit(solution)/shard_map/ppermute | solution.py:62
  108.1 1.4 %collective-permute-start.33 = (f32[4,128,66]{1,2,0:T(8,128)S(1)}, f32[4,128,66]{1,2,0:T(8,128)S(1)}, u32[]{:S(2)}, u32[]{:S(2)}) collective-permute-start(f32[4,128,66]{1,2,0:T(8,128)S(1)} %pad_maximum_fusion.3), channel_id=1, source_target_pairs={{0,1},{1,0},{2,3},{3,2},{4,5},{5,4},{6,7},{7,6},{8,9},{9,8},{10,11... | collective-permute-start | bytes 405512 | tf_op jit(solution)/shard_map/ppermute | solution.py:92
  109.7 4.3 %collective-permute-start.36 = (f32[128,66]{0,1:T(8,128)S(1)}, f32[128,66]{0,1:T(8,128)S(1)}, u32[]{:S(2)}, u32[]{:S(2)}) collective-permute-start(f32[128,66]{0,1:T(8,128)S(1)} %get-tuple-element.17), channel_id=1, source_target_pairs={{0,12},{4,0},{8,4},{12,8},{1,13},{5,1},{9,5},{13,9},{2,14},{6,2},{... | collective-permute-start | bytes 101384 | tf_op jit(solution)/shard_map/ppermute | solution.py:142
  111.2 5.8 %collective-permute-start.35 = (f32[128,66]{0,1:T(8,128)S(1)}, f32[128,66]{0,1:T(8,128)S(1)}, u32[]{:S(2)}, u32[]{:S(2)}) collective-permute-start(f32[128,66]{0,1:T(8,128)S(1)} %get-tuple-element.18), channel_id=1, source_target_pairs={{0,8},{4,12},{8,0},{12,4},{1,9},{5,13},{9,1},{13,5},{2,10},{6,14},... | collective-permute-start | bytes 101384 | tf_op jit(solution)/shard_map/ppermute | solution.py:142
  111.2 5.8 %collective-permute-start.34 = (f32[128,66]{0,1:T(8,128)S(1)}, f32[128,66]{0,1:T(8,128)S(1)}, u32[]{:S(2)}, u32[]{:S(2)}) collective-permute-start(f32[128,66]{0,1:T(8,128)S(1)} %get-tuple-element.19), channel_id=1, source_target_pairs={{0,4},{4,8},{8,12},{12,0},{1,5},{5,9},{9,13},{13,1},{2,6},{6,10},{... | collective-permute-start | bytes 101384 | tf_op jit(solution)/shard_map/ppermute | solution.py:142

commit v4 on v2

--- a/solution.py
+++ b/solution.py
@@ -130,6 +130,30 @@
     return (f_pot,) + fate_pullback(cost, log_b, g_pot, fate_panel)
 
 
+def lse_scatter_exchange(maxima, totals, weighted, name):
+    size = lax.axis_size(name)
+    index = lax.axis_index(name)
+    fates = weighted.shape[-1]
+    packed = jnp.concatenate([weighted, maxima[..., None], totals[..., None]], axis=-1)
+    parts = [lax.dynamic_index_in_dim(packed, index, axis=0, keepdims=False)]
+    for shift in range(1, size):
+        perm = [(i, (i + shift) % size) for i in range(size)]
+        send = lax.dynamic_index_in_dim(packed, (index + shift) % size, axis=0, keepdims=False)
+        parts.append(lax.ppermute(send, name, perm))
+    top = parts[0][..., fates]
+    for part in parts[1:]:
+        top = jnp.maximum(top, part[..., fates])
+    totals = None
+    weighted = None
+    for part in parts:
+        factor = jnp.exp(part[..., fates] - top)
+        add_s = part[..., fates + 1] * factor
+        add_w = part[..., :fates] * factor[..., None]
+        totals = add_s if totals is None else totals + add_s
+        weighted = add_w if weighted is None else weighted + add_w
+    return top, totals, weighted
+
+
 def fate_pullback(cost, log_b, g_pot, fate_panel):
     src_count = cost.shape[0]
     scores = log_b[None, :] + (g_pot[None, :] - cost) / entropic
@@ -142,7 +166,15 @@
     col_size = lax.axis_size("cols")
     rep_size = lax.axis_size("rep")
     fates = fate_panel.shape[1]
-    if is_pow2(col_size) and is_pow2(rep_size):
+    if rep_size == 2 and col_size <= 8:
+        block = src_count // (col_size * rep_size)
+        maxima = jnp.swapaxes(maxima.reshape(col_size, rep_size, block), 0, 1)
+        totals = jnp.swapaxes(totals.reshape(col_size, rep_size, block), 0, 1)
+        weighted = jnp.swapaxes(weighted.reshape(col_size, rep_size, block, fates), 0, 1)
+        maxima, totals, weighted = lse_halving(maxima, totals, weighted, [("rep", 1)])
+        maxima, totals, weighted = lse_scatter_exchange(maxima, totals, weighted, "cols")
+        fate_rows = weighted / totals[:, None]
+    elif is_pow2(col_size) and is_pow2(rep_size):
         col_bits = col_size.bit_length() - 1
         rep_bits = rep_size.bit_length() - 1
         lead = (2,) * (col_bits + rep_bits)

time: 114 us -> 112 us (0.982)
  waiting for transfers between devices: 46.3 us -> 41.1 us
  starting transfers between devices: 40.4 us -> 43.1 us
    ppermute x3 -> x1, waiting for transfers between devices: 8.86 us -> 1.29 us  [lse_halving(): packed = lax.ppermute(packed, name, perm)]
    ppermute x0 -> x3, starting transfers between devices: none -> 3.87 us  [lse_scatter_exchange(): parts.append(lax.ppermute(send, name, perm))]
    ppermute x0 -> x3, waiting for transfers between devices: none -> 2.42 us  [lse_scatter_exchange(): parts.append(lax.ppermute(send, name, perm))]
    ppermute x3 -> x1, starting transfers between devices: 1.23 us -> 0.07 us  [lse_halving(): packed = lax.ppermute(packed, name, perm)]
  transfers between devices with their start and end apart: 36 -> 37, of which waited for: 34 -> 35; matrix products, arithmetic and copies ran while one was open for 2% -> 2% of each run, Pallas kernels for 0% -> 0%
where the time goes in v4:
time: 112 us
  starting transfers between devices  43.1 us (38%)
  waiting for transfers between devices  41.1 us (37%)
  other arithmetic  20.8 us (19%)
  matrix products  3.39 us (3%)
  local copies, waits for them, and re-layouts  1.61 us (1%)
  between operations  1.48 us (1%)
    ppermute x24, starting transfers between devices, lse_exchange(): received.append(lax.ppermute(payload, axes, perm))  35.6 us
    ppermute x24, waiting for transfers between devices, lse_exchange(): received.append(lax.ppermute(payload, axes, perm))  22.7 us
    ppermute x8, waiting for transfers between devices, lse_allreduce(): other = lax.ppermute(jnp.stack([maxima, totals]), name, perm)  9.28 us
    ppermute x1, waiting for transfers between devices, body(): theirs = lax.ppermute(mine, 'rows', [(0, 1), (1, 0)])  5.46 us
    reduce_sum x8, other arithmetic, body(): totals = jnp.sum(jnp.exp(scores - maxima[None, :]), axis=0)  4.64 us
    reduce_sum x8, other arithmetic, body(): totals = jnp.sum(jnp.exp(scores - maxima[:, None]), axis=1)  4.46 us
    ppermute x3, starting transfers between devices, lse_scatter_exchange(): parts.append(lax.ppermute(send, name, perm))  3.87 us
    ppermute x1, starting transfers between devices, body(): theirs = lax.ppermute(mine, 'rows', [(0, 1), (1, 0)])  3.03 us
  transfers between devices with their start and end apart: 37, of which 35 were waited for; matrix products, arithmetic and copies ran while one was open for 2% of the time, Pallas kernels for 0%

profile of v4, /device:TPU:0, one launch (start us, length us, event | category | flops | bytes accessed | tf_op | source)
XLA Modules:
  0.0 111.5 jit_solution(15500792336513920493)
XLA Ops:
  0.7 1.0 pad_maximum_fusion.2
  1.7 3.0 %collective-permute-start = (f32[1024,65]{0,1:T(8,128)S(1)}, f32[1024,65]{0,1:T(8,128)S(1)}, u32[]{:S(2)}, u32[]{:S(2)}) collective-permute-start(f32[1024,65]{0,1:T(8,128)S(1)} %pad_maximum_fusion.2), channel_id=1, source_target_pairs={{0,2},{2,0},{1,3},{3,1},{4,6},{6,4},{5,7},{7,5},{8,10},{10,8},{9,1... | collective-permute-start | bytes 798728 | tf_op jit(solution)/shard_map/ppermute | solution.py:220
  4.7 0.9 multiply_reduce_fusion.1
  6.3 5.5 %collective-permute-done = f32[1024,65]{0,1:T(8,128)S(1)} collective-permute-done((f32[1024,65]{0,1:T(8,128)S(1)}, f32[1024,65]{0,1:T(8,128)S(1)}, u32[]{:S(2)}, u32[]{:S(2)}) %collective-permute-start) | collective-permute-done | bytes 266272 | tf_op jit(solution)/shard_map/ppermute | solution.py:220
  11.7 1.0 broadcast_select_fusion.1
  12.8 2.3 %fusion.2 = (f32[2048]{0:T(1024)S(1)}, f32[2048,256]{0,1:T(8,128)S(1)}) fusion(f32[256]{0:T(256)S(1)} %multiply_log_fusion, f32[256,64]{0,1:T(8,128)S(1)} %copy-done.1, f32[1024,65]{0,1:T(8,128)S(1)} %get-tuple-element.8, f32[1024,65]{0,1:T(8,128)S(1)} %get-tuple-element.7, f32[256]{0:T(256)S(1)} %multiply_reduce_fusion.1, f32[2048]{0:T(1024)S(1)} %multiply_reduce_fusion), kind=kOutput, calls=%fused_computation.35 | convolution fusion | flops 406976512 | bytes 2713600 | tf_op jit(solution)/shard_map/dot_general | solution.py:14
  15.9 1.1 collective-permute-done.1
  17.1 2.9 %collective-permute-start.3 = (f32[2,2048]{1,0:T(2,128)S(1)}, f32[2,2048]{1,0:T(2,128)S(1)}, u32[]{:S(2)}, u32[]{:S(2)}) collective-permute-start(f32[2,2048]{1,0:T(2,128)S(1)} %get-tuple-element.114), channel_id=1, source_target_pairs={{0,8},{4,12},{8,0},{12,4},{1,9},{5,13},{9,1},{13,5},{2,10},{6,14},... | collective-permute-start | bytes 49160 | tf_op jit(solution)/shard_map/ppermute | solution.py:62
  20.0 1.6 %collective-permute-start.2 = (f32[2,2048]{1,0:T(2,128)S(1)}, f32[2,2048]{1,0:T(2,128)S(1)}, u32[]{:S(2)}, u32[]{:S(2)}) collective-permute-start(f32[2,2048]{1,0:T(2,128)S(1)} %get-tuple-element.114), channel_id=1, source_target_pairs={{0,4},{4,8},{8,12},{12,0},{1,5},{5,9},{9,13},{13,1},{2,6},{6,10},{... | collective-permute-start | bytes 49160 | tf_op jit(solution)/shard_map/ppermute | solution.py:62
  21.5 2.2 %collective-permute-start.4 = (f32[2,2048]{1,0:T(2,128)S(1)}, f32[2,2048]{1,0:T(2,128)S(1)}, u32[]{:S(2)}, u32[]{:S(2)}) collective-permute-start(f32[2,2048]{1,0:T(2,128)S(1)} %get-tuple-element.114), channel_id=1, source_target_pairs={{0,12},{4,0},{8,4},{12,8},{1,13},{5,1},{9,5},{13,9},{2,14},{6,2},{... | collective-permute-start | bytes 49160 | tf_op jit(solution)/shard_map/ppermute | solution.py:62
  23.8 1.7 %collective-permute-done.2 = f32[2,2048]{1,0:T(2,128)S(1)} collective-permute-done((f32[2,2048]{1,0:T(2,128)S(1)}, f32[2,2048]{1,0:T(2,128)S(1)}, u32[]{:S(2)}, u32[]{:S(2)}) %collective-permute-start.2) | collective-permute-done | bytes 16416 | tf_op jit(solution)/shard_map/ppermute | solution.py:62
  27.6 1.2 %collective-permute-done.5 = f32[2,2048]{1,0:T(2,128)S(1)} collective-permute-done((f32[2,2048]{1,0:T(2,128)S(1)}, f32[2,2048]{1,0:T(2,128)S(1)}, u32[]{:S(2)}, u32[]{:S(2)}) %collective-permute-start.5) | collective-permute-done | bytes 16416 | tf_op jit(solution)/shard_map/ppermute | solution.py:43
  28.9 0.8 collective-permute-start.7
  29.7 3.6 %collective-permute-start.6 = (f32[2,2048]{1,0:T(2,128)S(1)}, f32[2,2048]{1,0:T(2,128)S(1)}, u32[]{:S(2)}, u32[]{:S(2)}) collective-permute-start(f32[2,2048]{1,0:T(2,128)S(1)} %get-tuple-element.112), channel_id=1, source_target_pairs={{0,4},{4,8},{8,12},{12,0},{1,5},{5,9},{9,13},{13,1},{2,6},{6,10},{... | collective-permute-start | bytes 49160 | tf_op jit(solution)/shard_map/ppermute | solution.py:62
  33.6 1.6 %collective-permute-done.6 = f32[2,2048]{1,0:T(2,128)S(1)} collective-permute-done((f32[2,2048]{1,0:T(2,128)S(1)}, f32[2,2048]{1,0:T(2,128)S(1)}, u32[]{:S(2)}, u32[]{:S(2)}) %collective-permute-start.6) | collective-permute-done | bytes 16416 | tf_op jit(solution)/shard_map/ppermute | solution.py:62
  35.2 1.9 %collective-permute-done.8 = f32[2,2048]{1,0:T(2,128)S(1)} collective-permute-done((f32[2,2048]{1,0:T(2,128)S(1)}, f32[2,2048]{1,0:T(2,128)S(1)}, u32[]{:S(2)}, u32[]{:S(2)}) %collective-permute-start.8) | collective-permute-done | bytes 16416 | tf_op jit(solution)/shard_map/ppermute | solution.py:62
  39.2 1.2 %collective-permute-done.9 = f32[2,2048]{1,0:T(2,128)S(1)} collective-permute-done((f32[2,2048]{1,0:T(2,128)S(1)}, f32[2,2048]{1,0:T(2,128)S(1)}, u32[]{:S(2)}, u32[]{:S(2)}) %collective-permute-start.9) | collective-permute-done | bytes 16416 | tf_op jit(solution)/shard_map/ppermute | solution.py:43
  40.6 2.5 %collective-permute-start.10 = (f32[2,2048]{1,0:T(2,128)S(1)}, f32[2,2048]{1,0:T(2,128)S(1)}, u32[]{:S(2)}, u32[]{:S(2)}) collective-permute-start(f32[2,2048]{1,0:T(2,128)S(1)} %get-tuple-element.110), channel_id=1, source_target_pairs={{0,4},{4,8},{8,12},{12,0},{1,5},{5,9},{9,13},{13,1},{2,6},{6,10},{... | collective-permute-start | bytes 49160 | tf_op jit(solution)/shard_map/ppermute | solution.py:62
  43.1 1.4 %collective-permute-start.12 = (f32[2,2048]{1,0:T(2,128)S(1)}, f32[2,2048]{1,0:T(2,128)S(1)}, u32[]{:S(2)}, u32[]{:S(2)}) collective-permute-start(f32[2,2048]{1,0:T(2,128)S(1)} %get-tuple-element.110), channel_id=1, source_target_pairs={{0,12},{4,0},{8,4},{12,8},{1,13},{5,1},{9,5},{13,9},{2,14},{6,2},{... | collective-permute-start | bytes 49160 | tf_op jit(solution)/shard_map/ppermute | solution.py:62
  44.4 0.8 collective-permute-done.11
  45.2 1.0 collective-permute-done.10
  49.0 1.2 %collective-permute-done.13 = f32[2,2048]{1,0:T(2,128)S(1)} collective-permute-done((f32[2,2048]{1,0:T(2,128)S(1)}, f32[2,2048]{1,0:T(2,128)S(1)}, u32[]{:S(2)}, u32[]{:S(2)}) %collective-permute-start.13) | collective-permute-done | bytes 16416 | tf_op jit(solution)/shard_map/ppermute | solution.py:43
  50.7 3.3 %collective-permute-start.14 = (f32[2,2048]{1,0:T(2,128)S(1)}, f32[2,2048]{1,0:T(2,128)S(1)}, u32[]{:S(2)}, u32[]{:S(2)}) collective-permute-start(f32[2,2048]{1,0:T(2,128)S(1)} %get-tuple-element.108), channel_id=1, source_target_pairs={{0,4},{4,8},{8,12},{12,0},{1,5},{5,9},{9,13},{13,1},{2,6},{6,10},{... | collective-permute-start | bytes 49160 | tf_op jit(solution)/shard_map/ppermute | solution.py:62
  54.9 1.5 %collective-permute-done.14 = f32[2,2048]{1,0:T(2,128)S(1)} collective-permute-done((f32[2,2048]{1,0:T(2,128)S(1)}, f32[2,2048]{1,0:T(2,128)S(1)}, u32[]{:S(2)}, u32[]{:S(2)}) %collective-permute-start.14) | collective-permute-done | bytes 16416 | tf_op jit(solution)/shard_map/ppermute | solution.py:62
  56.4 1.3 %collective-permute-done.16 = f32[2,2048]{1,0:T(2,128)S(1)} collective-permute-done((f32[2,2048]{1,0:T(2,128)S(1)}, f32[2,2048]{1,0:T(2,128)S(1)}, u32[]{:S(2)}, u32[]{:S(2)}) %collective-permute-start.16) | collective-permute-done | bytes 16416 | tf_op jit(solution)/shard_map/ppermute | solution.py:62
  59.9 1.2 %collective-permute-done.17 = f32[2,2048]{1,0:T(2,128)S(1)} collective-permute-done((f32[2,2048]{1,0:T(2,128)S(1)}, f32[2,2048]{1,0:T(2,128)S(1)}, u32[]{:S(2)}, u32[]{:S(2)}) %collective-permute-start.17) | collective-permute-done | bytes 16416 | tf_op jit(solution)/shard_map/ppermute | solution.py:43
  61.3 2.7 %collective-permute-start.18 = (f32[2,2048]{1,0:T(2,128)S(1)}, f32[2,2048]{1,0:T(2,128)S(1)}, u32[]{:S(2)}, u32[]{:S(2)}) collective-permute-start(f32[2,2048]{1,0:T(2,128)S(1)} %get-tuple-element.106), channel_id=1, source_target_pairs={{0,4},{4,8},{8,12},{12,0},{1,5},{5,9},{9,13},{13,1},{2,6},{6,10},{... | collective-permute-start | bytes 49160 | tf_op jit(solution)/shard_map/ppermute | solution.py:62
  64.0 1.1 %collective-permute-start.20 = (f32[2,2048]{1,0:T(2,128)S(1)}, f32[2,2048]{1,0:T(2,128)S(1)}, u32[]{:S(2)}, u32[]{:S(2)}) collective-permute-start(f32[2,2048]{1,0:T(2,128)S(1)} %get-tuple-element.106), channel_id=1, source_target_pairs={{0,12},{4,0},{8,4},{12,8},{1,13},{5,1},{9,5},{13,9},{2,14},{6,2},{... | collective-permute-start | bytes 49160 | tf_op jit(solution)/shard_map/ppermute | solution.py:62
  65.8 1.1 collective-permute-done.18
  66.9 0.9 collective-permute-done.20
  69.9 1.2 %collective-permute-done.21 = f32[2,2048]{1,0:T(2,128)S(1)} collective-permute-done((f32[2,2048]{1,0:T(2,128)S(1)}, f32[2,2048]{1,0:T(2,128)S(1)}, u32[]{:S(2)}, u32[]{:S(2)}) %collective-permute-start.21) | collective-permute-done | bytes 16416 | tf_op jit(solution)/shard_map/ppermute | solution.py:43
  71.3 3.4 %collective-permute-start.22 = (f32[2,2048]{1,0:T(2,128)S(1)}, f32[2,2048]{1,0:T(2,128)S(1)}, u32[]{:S(2)}, u32[]{:S(2)}) collective-permute-start(f32[2,2048]{1,0:T(2,128)S(1)} %get-tuple-element.104), channel_id=1, source_target_pairs={{0,4},{4,8},{8,12},{12,0},{1,5},{5,9},{9,13},{13,1},{2,6},{6,10},{... | collective-permute-start | bytes 49160 | tf_op jit(solution)/shard_map/ppermute | solution.py:62
  75.1 1.1 collective-permute-done.23
  77.0 1.5 %collective-permute-done.24 = f32[2,2048]{1,0:T(2,128)S(1)} collective-permute-done((f32[2,2048]{1,0:T(2,128)S(1)}, f32[2,2048]{1,0:T(2,128)S(1)}, u32[]{:S(2)}, u32[]{:S(2)}) %collective-permute-start.24) | collective-permute-done | bytes 16416 | tf_op jit(solution)/shard_map/ppermute | solution.py:62
  80.6 1.2 %collective-permute-done.25 = f32[2,2048]{1,0:T(2,128)S(1)} collective-permute-done((f32[2,2048]{1,0:T(2,128)S(1)}, f32[2,2048]{1,0:T(2,128)S(1)}, u32[]{:S(2)}, u32[]{:S(2)}) %collective-permute-start.25) | collective-permute-done | bytes 16416 | tf_op jit(solution)/shard_map/ppermute | solution.py:43
  82.0 2.7 %collective-permute-start.26 = (f32[2,2048]{1,0:T(2,128)S(1)}, f32[2,2048]{1,0:T(2,128)S(1)}, u32[]{:S(2)}, u32[]{:S(2)}) collective-permute-start(f32[2,2048]{1,0:T(2,128)S(1)} %get-tuple-element.102), channel_id=1, source_target_pairs={{0,4},{4,8},{8,12},{12,0},{1,5},{5,9},{9,13},{13,1},{2,6},{6,10},{... | collective-permute-start | bytes 49160 | tf_op jit(solution)/shard_map/ppermute | solution.py:62
  84.7 1.1 %collective-permute-start.28 = (f32[2,2048]{1,0:T(2,128)S(1)}, f32[2,2048]{1,0:T(2,128)S(1)}, u32[]{:S(2)}, u32[]{:S(2)}) collective-permute-start(f32[2,2048]{1,0:T(2,128)S(1)} %get-tuple-element.102), channel_id=1, source_target_pairs={{0,12},{4,0},{8,4},{12,8},{1,13},{5,1},{9,5},{13,9},{2,14},{6,2},{... | collective-permute-start | bytes 49160 | tf_op jit(solution)/shard_map/ppermute | solution.py:62
  86.6 1.0 collective-permute-done.26
  87.5 0.9 collective-permute-done.28
  90.6 1.2 %collective-permute-done.29 = f32[2,2048]{1,0:T(2,128)S(1)} collective-permute-done((f32[2,2048]{1,0:T(2,128)S(1)}, f32[2,2048]{1,0:T(2,128)S(1)}, u32[]{:S(2)}, u32[]{:S(2)}) %collective-permute-start.29) | collective-permute-done | bytes 16416 | tf_op jit(solution)/shard_map/ppermute | solution.py:43
  92.0 3.3 %collective-permute-start.30 = (f32[2,2048]{1,0:T(2,128)S(1)}, f32[2,2048]{1,0:T(2,128)S(1)}, u32[]{:S(2)}, u32[]{:S(2)}) collective-permute-start(f32[2,2048]{1,0:T(2,128)S(1)} %get-tuple-element.100), channel_id=1, source_target_pairs={{0,4},{4,8},{8,12},{12,0},{1,5},{5,9},{9,13},{13,1},{2,6},{6,10},{... | collective-permute-start | bytes 49160 | tf_op jit(solution)/shard_map/ppermute | solution.py:62
  96.5 1.3 %collective-permute-done.30 = f32[2,2048]{1,0:T(2,128)S(1)} collective-permute-done((f32[2,2048]{1,0:T(2,128)S(1)}, f32[2,2048]{1,0:T(2,128)S(1)}, u32[]{:S(2)}, u32[]{:S(2)}) %collective-permute-start.30) | collective-permute-done | bytes 16416 | tf_op jit(solution)/shard_map/ppermute | solution.py:62
  97.8 1.3 %collective-permute-done.32 = f32[2,2048]{1,0:T(2,128)S(1)} collective-permute-done((f32[2,2048]{1,0:T(2,128)S(1)}, f32[2,2048]{1,0:T(2,128)S(1)}, u32[]{:S(2)}, u32[]{:S(2)}) %collective-permute-start.32) | collective-permute-done | bytes 16416 | tf_op jit(solution)/shard_map/ppermute | solution.py:62
  100.8 1.1 fusion.19
  102.4 1.3 %collective-permute-done.33 = f32[4,128,66]{1,0,2:T(4,128)S(1)} collective-permute-done((f32[4,128,66]{1,0,2:T(4,128)S(1)}, f32[4,128,66]{1,0,2:T(4,128)S(1)}, u32[]{:S(2)}, u32[]{:S(2)}) %collective-permute-start.33) | collective-permute-done | bytes 135200 | tf_op jit(solution)/shard_map/ppermute | solution.py:92
  104.0 2.9 %collective-permute-start.35 = (f32[128,66]{0,1:T(8,128)S(1)}, f32[128,66]{0,1:T(8,128)S(1)}, u32[]{:S(2)}, u32[]{:S(2)}) collective-permute-start(f32[128,66]{0,1:T(8,128)S(1)} %bitcast.231), channel_id=1, source_target_pairs={{0,8},{4,12},{8,0},{12,4},{1,9},{5,13},{9,1},{13,5},{2,10},{6,14},... | collective-permute-start | bytes 101384 | tf_op jit(solution)/shard_map/ppermute | solution.py:142
  106.9 1.0 collective-permute-start.36
  108.4 1.7 %collective-permute-done.34 = f32[128,66]{0,1:T(8,128)S(1)} collective-permute-done((f32[128,66]{0,1:T(8,128)S(1)}, f32[128,66]{0,1:T(8,128)S(1)}, u32[]{:S(2)}, u32[]{:S(2)}) %collective-permute-start.34) | collective-permute-done | bytes 33824 | tf_op jit(solution)/shard_map/ppermute | solution.py:142
  (149 shorter events, 27.7 us)
Async XLA Ops:
  0.6 100.1 %copy-start = (f32[256,64]{0,1:T(8,128)S(1)}, f32[256,64]{0,1:T(8,128)}, u32[]{:S(2)}) copy-start(f32[256,64]{0,1:T(8,128)} %param.9) | copy-start | bytes 196612
  0.6 12.2 %copy-start.1 = (f32[256,64]{0,1:T(8,128)S(1)}, f32[256,64]{0,1:T(8,128)}, u32[]{:S(2)}) copy-start(f32[256,64]{0,1:T(8,128)} %param.7) | copy-start | bytes 196612
  1.7 10.0 %collective-permute-start = (f32[1024,65]{0,1:T(8,128)S(1)}, f32[1024,65]{0,1:T(8,128)S(1)}, u32[]{:S(2)}, u32[]{:S(2)}) collective-permute-start(f32[1024,65]{0,1:T(8,128)S(1)} %pad_maximum_fusion.2), channel_id=1, source_target_pairs={{0,2},{2,0},{1,3},{3,1},{4,6},{6,4},{5,7},{7,5},{8,10},{10,8},{9,1... | collective-permute-start | bytes 798728 | tf_op jit(solution)/shard_map/ppermute | solution.py:220
  15.7 1.2 %collective-permute-start.1 = (f32[2,2048]{1,0:T(2,128)S(1)}, f32[2,2048]{1,0:T(2,128)S(1)}, u32[]{:S(2)}, u32[]{:S(2)}) collective-permute-start(f32[2,2048]{1,0:T(2,128)S(1)} %pad_maximum_fusion.13), channel_id=1, source_target_pairs={{0,1},{1,0},{2,3},{3,2},{4,5},{5,4},{6,7},{7,6},{8,9},{9,8},{10,11... | collective-permute-start | bytes 49160 | tf_op jit(solution)/shard_map/ppermute | solution.py:43
  17.1 6.7 %collective-permute-start.3 = (f32[2,2048]{1,0:T(2,128)S(1)}, f32[2,2048]{1,0:T(2,128)S(1)}, u32[]{:S(2)}, u32[]{:S(2)}) collective-permute-start(f32[2,2048]{1,0:T(2,128)S(1)} %get-tuple-element.114), channel_id=1, source_target_pairs={{0,8},{4,12},{8,0},{12,4},{1,9},{5,13},{9,1},{13,5},{2,10},{6,14},... | collective-permute-start | bytes 49160 | tf_op jit(solution)/shard_map/ppermute | solution.py:62
  20.0 5.5 %collective-permute-start.2 = (f32[2,2048]{1,0:T(2,128)S(1)}, f32[2,2048]{1,0:T(2,128)S(1)}, u32[]{:S(2)}, u32[]{:S(2)}) collective-permute-start(f32[2,2048]{1,0:T(2,128)S(1)} %get-tuple-element.114), channel_id=1, source_target_pairs={{0,4},{4,8},{8,12},{12,0},{1,5},{5,9},{9,13},{13,1},{2,6},{6,10},{... | collective-permute-start | bytes 49160 | tf_op jit(solution)/shard_map/ppermute | solution.py:62
  21.5 4.0 %collective-permute-start.4 = (f32[2,2048]{1,0:T(2,128)S(1)}, f32[2,2048]{1,0:T(2,128)S(1)}, u32[]{:S(2)}, u32[]{:S(2)}) collective-permute-start(f32[2,2048]{1,0:T(2,128)S(1)} %get-tuple-element.114), channel_id=1, source_target_pairs={{0,12},{4,0},{8,4},{12,8},{1,13},{5,1},{9,5},{13,9},{2,14},{6,2},{... | collective-permute-start | bytes 49160 | tf_op jit(solution)/shard_map/ppermute | solution.py:62
  27.6 1.2 %collective-permute-start.5 = (f32[2,2048]{1,0:T(2,128)S(1)}, f32[2,2048]{1,0:T(2,128)S(1)}, u32[]{:S(2)}, u32[]{:S(2)}) collective-permute-start(f32[2,2048]{1,0:T(2,128)S(1)} %pad_maximum_fusion.15), channel_id=1, source_target_pairs={{0,1},{1,0},{2,3},{3,2},{4,5},{5,4},{6,7},{7,6},{8,9},{9,8},{10,11... | collective-permute-start | bytes 49160 | tf_op jit(solution)/shard_map/ppermute | solution.py:43
  28.9 4.7 %collective-permute-start.7 = (f32[2,2048]{1,0:T(2,128)S(1)}, f32[2,2048]{1,0:T(2,128)S(1)}, u32[]{:S(2)}, u32[]{:S(2)}) collective-permute-start(f32[2,2048]{1,0:T(2,128)S(1)} %get-tuple-element.112), channel_id=1, source_target_pairs={{0,8},{4,12},{8,0},{12,4},{1,9},{5,13},{9,1},{13,5},{2,10},{6,14},... | collective-permute-start | bytes 49160 | tf_op jit(solution)/shard_map/ppermute | solution.py:62
  29.7 5.5 %collective-permute-start.6 = (f32[2,2048]{1,0:T(2,128)S(1)}, f32[2,2048]{1,0:T(2,128)S(1)}, u32[]{:S(2)}, u32[]{:S(2)}) collective-permute-start(f32[2,2048]{1,0:T(2,128)S(1)} %get-tuple-element.112), channel_id=1, source_target_pairs={{0,4},{4,8},{8,12},{12,0},{1,5},{5,9},{9,13},{13,1},{2,6},{6,10},{... | collective-permute-start | bytes 49160 | tf_op jit(solution)/shard_map/ppermute | solution.py:62
  33.3 3.7 %collective-permute-start.8 = (f32[2,2048]{1,0:T(2,128)S(1)}, f32[2,2048]{1,0:T(2,128)S(1)}, u32[]{:S(2)}, u32[]{:S(2)}) collective-permute-start(f32[2,2048]{1,0:T(2,128)S(1)} %get-tuple-element.112), channel_id=1, source_target_pairs={{0,12},{4,0},{8,4},{12,8},{1,13},{5,1},{9,5},{13,9},{2,14},{6,2},{... | collective-permute-start | bytes 49160 | tf_op jit(solution)/shard_map/ppermute | solution.py:62
  39.1 1.2 %collective-permute-start.9 = (f32[2,2048]{1,0:T(2,128)S(1)}, f32[2,2048]{1,0:T(2,128)S(1)}, u32[]{:S(2)}, u32[]{:S(2)}) collective-permute-start(f32[2,2048]{1,0:T(2,128)S(1)} %pad_maximum_fusion.17), channel_id=1, source_target_pairs={{0,1},{1,0},{2,3},{3,2},{4,5},{5,4},{6,7},{7,6},{8,9},{9,8},{10,11... | collective-permute-start | bytes 49160 | tf_op jit(solution)/shard_map/ppermute | solution.py:43
  40.5 4.7 %collective-permute-start.11 = (f32[2,2048]{1,0:T(2,128)S(1)}, f32[2,2048]{1,0:T(2,128)S(1)}, u32[]{:S(2)}, u32[]{:S(2)}) collective-permute-start(f32[2,2048]{1,0:T(2,128)S(1)} %get-tuple-element.110), channel_id=1, source_target_pairs={{0,8},{4,12},{8,0},{12,4},{1,9},{5,13},{9,1},{13,5},{2,10},{6,14},... | collective-permute-start | bytes 49160 | tf_op jit(solution)/shard_map/ppermute | solution.py:62
  40.6 5.5 %collective-permute-start.10 = (f32[2,2048]{1,0:T(2,128)S(1)}, f32[2,2048]{1,0:T(2,128)S(1)}, u32[]{:S(2)}, u32[]{:S(2)}) collective-permute-start(f32[2,2048]{1,0:T(2,128)S(1)} %get-tuple-element.110), channel_id=1, source_target_pairs={{0,4},{4,8},{8,12},{12,0},{1,5},{5,9},{9,13},{13,1},{2,6},{6,10},{... | collective-permute-start | bytes 49160 | tf_op jit(solution)/shard_map/ppermute | solution.py:62
  43.1 3.7 %collective-permute-start.12 = (f32[2,2048]{1,0:T(2,128)S(1)}, f32[2,2048]{1,0:T(2,128)S(1)}, u32[]{:S(2)}, u32[]{:S(2)}) collective-permute-start(f32[2,2048]{1,0:T(2,128)S(1)} %get-tuple-element.110), channel_id=1, source_target_pairs={{0,12},{4,0},{8,4},{12,8},{1,13},{5,1},{9,5},{13,9},{2,14},{6,2},{... | collective-permute-start | bytes 49160 | tf_op jit(solution)/shard_map/ppermute | solution.py:62
  48.9 1.2 %collective-permute-start.13 = (f32[2,2048]{1,0:T(2,128)S(1)}, f32[2,2048]{1,0:T(2,128)S(1)}, u32[]{:S(2)}, u32[]{:S(2)}) collective-permute-start(f32[2,2048]{1,0:T(2,128)S(1)} %pad_maximum_fusion.19), channel_id=1, source_target_pairs={{0,1},{1,0},{2,3},{3,2},{4,5},{5,4},{6,7},{7,6},{8,9},{9,8},{10,11... | collective-permute-start | bytes 49160 | tf_op jit(solution)/shard_map/ppermute | solution.py:43
  50.2 4.7 %collective-permute-start.15 = (f32[2,2048]{1,0:T(2,128)S(1)}, f32[2,2048]{1,0:T(2,128)S(1)}, u32[]{:S(2)}, u32[]{:S(2)}) collective-permute-start(f32[2,2048]{1,0:T(2,128)S(1)} %get-tuple-element.108), channel_id=1, source_target_pairs={{0,8},{4,12},{8,0},{12,4},{1,9},{5,13},{9,1},{13,5},{2,10},{6,14},... | collective-permute-start | bytes 49160 | tf_op jit(solution)/shard_map/ppermute | solution.py:62
  50.7 5.8 %collective-permute-start.14 = (f32[2,2048]{1,0:T(2,128)S(1)}, f32[2,2048]{1,0:T(2,128)S(1)}, u32[]{:S(2)}, u32[]{:S(2)}) collective-permute-start(f32[2,2048]{1,0:T(2,128)S(1)} %get-tuple-element.108), channel_id=1, source_target_pairs={{0,4},{4,8},{8,12},{12,0},{1,5},{5,9},{9,13},{13,1},{2,6},{6,10},{... | collective-permute-start | bytes 49160 | tf_op jit(solution)/shard_map/ppermute | solution.py:62
  54.0 3.7 %collective-permute-start.16 = (f32[2,2048]{1,0:T(2,128)S(1)}, f32[2,2048]{1,0:T(2,128)S(1)}, u32[]{:S(2)}, u32[]{:S(2)}) collective-permute-start(f32[2,2048]{1,0:T(2,128)S(1)} %get-tuple-element.108), channel_id=1, source_target_pairs={{0,12},{4,0},{8,4},{12,8},{1,13},{5,1},{9,5},{13,9},{2,14},{6,2},{... | collective-permute-start | bytes 49160 | tf_op jit(solution)/shard_map/ppermute | solution.py:62
  59.8 1.2 %collective-permute-start.17 = (f32[2,2048]{1,0:T(2,128)S(1)}, f32[2,2048]{1,0:T(2,128)S(1)}, u32[]{:S(2)}, u32[]{:S(2)}) collective-permute-start(f32[2,2048]{1,0:T(2,128)S(1)} %pad_maximum_fusion.21), channel_id=1, source_target_pairs={{0,1},{1,0},{2,3},{3,2},{4,5},{5,4},{6,7},{7,6},{8,9},{9,8},{10,11... | collective-permute-start | bytes 49160 | tf_op jit(solution)/shard_map/ppermute | solution.py:43
  61.1 4.7 %collective-permute-start.19 = (f32[2,2048]{1,0:T(2,128)S(1)}, f32[2,2048]{1,0:T(2,128)S(1)}, u32[]{:S(2)}, u32[]{:S(2)}) collective-permute-start(f32[2,2048]{1,0:T(2,128)S(1)} %get-tuple-element.106), channel_id=1, source_target_pairs={{0,8},{4,12},{8,0},{12,4},{1,9},{5,13},{9,1},{13,5},{2,10},{6,14},... | collective-permute-start | bytes 49160 | tf_op jit(solution)/shard_map/ppermute | solution.py:62
  61.3 5.5 %collective-permute-start.18 = (f32[2,2048]{1,0:T(2,128)S(1)}, f32[2,2048]{1,0:T(2,128)S(1)}, u32[]{:S(2)}, u32[]{:S(2)}) collective-permute-start(f32[2,2048]{1,0:T(2,128)S(1)} %get-tuple-element.106), channel_id=1, source_target_pairs={{0,4},{4,8},{8,12},{12,0},{1,5},{5,9},{9,13},{13,1},{2,6},{6,10},{... | collective-permute-start | bytes 49160 | tf_op jit(solution)/shard_map/ppermute | solution.py:62
  64.0 3.7 %collective-permute-start.20 = (f32[2,2048]{1,0:T(2,128)S(1)}, f32[2,2048]{1,0:T(2,128)S(1)}, u32[]{:S(2)}, u32[]{:S(2)}) collective-permute-start(f32[2,2048]{1,0:T(2,128)S(1)} %get-tuple-element.106), channel_id=1, source_target_pairs={{0,12},{4,0},{8,4},{12,8},{1,13},{5,1},{9,5},{13,9},{2,14},{6,2},{... | collective-permute-start | bytes 49160 | tf_op jit(solution)/shard_map/ppermute | solution.py:62
  69.8 1.2 %collective-permute-start.21 = (f32[2,2048]{1,0:T(2,128)S(1)}, f32[2,2048]{1,0:T(2,128)S(1)}, u32[]{:S(2)}, u32[]{:S(2)}) collective-permute-start(f32[2,2048]{1,0:T(2,128)S(1)} %pad_maximum_fusion.23), channel_id=1, source_target_pairs={{0,1},{1,0},{2,3},{3,2},{4,5},{5,4},{6,7},{7,6},{8,9},{9,8},{10,11... | collective-permute-start | bytes 49160 | tf_op jit(solution)/shard_map/ppermute | solution.py:43
  71.2 5.1 %collective-permute-start.23 = (f32[2,2048]{1,0:T(2,128)S(1)}, f32[2,2048]{1,0:T(2,128)S(1)}, u32[]{:S(2)}, u32[]{:S(2)}) collective-permute-start(f32[2,2048]{1,0:T(2,128)S(1)} %get-tuple-element.104), channel_id=1, source_target_pairs={{0,8},{4,12},{8,0},{12,4},{1,9},{5,13},{9,1},{13,5},{2,10},{6,14},... | collective-permute-start | bytes 49160 | tf_op jit(solution)/shard_map/ppermute | solution.py:62
  71.3 5.7 %collective-permute-start.22 = (f32[2,2048]{1,0:T(2,128)S(1)}, f32[2,2048]{1,0:T(2,128)S(1)}, u32[]{:S(2)}, u32[]{:S(2)}) collective-permute-start(f32[2,2048]{1,0:T(2,128)S(1)} %get-tuple-element.104), channel_id=1, source_target_pairs={{0,4},{4,8},{8,12},{12,0},{1,5},{5,9},{9,13},{13,1},{2,6},{6,10},{... | collective-permute-start | bytes 49160 | tf_op jit(solution)/shard_map/ppermute | solution.py:62
  74.7 3.7 %collective-permute-start.24 = (f32[2,2048]{1,0:T(2,128)S(1)}, f32[2,2048]{1,0:T(2,128)S(1)}, u32[]{:S(2)}, u32[]{:S(2)}) collective-permute-start(f32[2,2048]{1,0:T(2,128)S(1)} %get-tuple-element.104), channel_id=1, source_target_pairs={{0,12},{4,0},{8,4},{12,8},{1,13},{5,1},{9,5},{13,9},{2,14},{6,2},{... | collective-permute-start | bytes 49160 | tf_op jit(solution)/shard_map/ppermute | solution.py:62
  80.5 1.2 %collective-permute-start.25 = (f32[2,2048]{1,0:T(2,128)S(1)}, f32[2,2048]{1,0:T(2,128)S(1)}, u32[]{:S(2)}, u32[]{:S(2)}) collective-permute-start(f32[2,2048]{1,0:T(2,128)S(1)} %pad_maximum_fusion.25), channel_id=1, source_target_pairs={{0,1},{1,0},{2,3},{3,2},{4,5},{5,4},{6,7},{7,6},{8,9},{9,8},{10,11... | collective-permute-start | bytes 49160 | tf_op jit(solution)/shard_map/ppermute | solution.py:43
  81.8 4.7 %collective-permute-start.27 = (f32[2,2048]{1,0:T(2,128)S(1)}, f32[2,2048]{1,0:T(2,128)S(1)}, u32[]{:S(2)}, u32[]{:S(2)}) collective-permute-start(f32[2,2048]{1,0:T(2,128)S(1)} %get-tuple-element.102), channel_id=1, source_target_pairs={{0,8},{4,12},{8,0},{12,4},{1,9},{5,13},{9,1},{13,5},{2,10},{6,14},... | collective-permute-start | bytes 49160 | tf_op jit(solution)/shard_map/ppermute | solution.py:62
  82.0 5.5 %collective-permute-start.26 = (f32[2,2048]{1,0:T(2,128)S(1)}, f32[2,2048]{1,0:T(2,128)S(1)}, u32[]{:S(2)}, u32[]{:S(2)}) collective-permute-start(f32[2,2048]{1,0:T(2,128)S(1)} %get-tuple-element.102), channel_id=1, source_target_pairs={{0,4},{4,8},{8,12},{12,0},{1,5},{5,9},{9,13},{13,1},{2,6},{6,10},{... | collective-permute-start | bytes 49160 | tf_op jit(solution)/shard_map/ppermute | solution.py:62
  84.7 3.7 %collective-permute-start.28 = (f32[2,2048]{1,0:T(2,128)S(1)}, f32[2,2048]{1,0:T(2,128)S(1)}, u32[]{:S(2)}, u32[]{:S(2)}) collective-permute-start(f32[2,2048]{1,0:T(2,128)S(1)} %get-tuple-element.102), channel_id=1, source_target_pairs={{0,12},{4,0},{8,4},{12,8},{1,13},{5,1},{9,5},{13,9},{2,14},{6,2},{... | collective-permute-start | bytes 49160 | tf_op jit(solution)/shard_map/ppermute | solution.py:62
  90.5 1.2 %collective-permute-start.29 = (f32[2,2048]{1,0:T(2,128)S(1)}, f32[2,2048]{1,0:T(2,128)S(1)}, u32[]{:S(2)}, u32[]{:S(2)}) collective-permute-start(f32[2,2048]{1,0:T(2,128)S(1)} %pad_maximum_fusion.27), channel_id=1, source_target_pairs={{0,1},{1,0},{2,3},{3,2},{4,5},{5,4},{6,7},{7,6},{8,9},{9,8},{10,11... | collective-permute-start | bytes 49160 | tf_op jit(solution)/shard_map/ppermute | solution.py:43
  91.8 4.7 %collective-permute-start.31 = (f32[2,2048]{1,0:T(2,128)S(1)}, f32[2,2048]{1,0:T(2,128)S(1)}, u32[]{:S(2)}, u32[]{:S(2)}) collective-permute-start(f32[2,2048]{1,0:T(2,128)S(1)} %get-tuple-element.100), channel_id=1, source_target_pairs={{0,8},{4,12},{8,0},{12,4},{1,9},{5,13},{9,1},{13,5},{2,10},{6,14},... | collective-permute-start | bytes 49160 | tf_op jit(solution)/shard_map/ppermute | solution.py:62
  92.0 5.8 %collective-permute-start.30 = (f32[2,2048]{1,0:T(2,128)S(1)}, f32[2,2048]{1,0:T(2,128)S(1)}, u32[]{:S(2)}, u32[]{:S(2)}) collective-permute-start(f32[2,2048]{1,0:T(2,128)S(1)} %get-tuple-element.100), channel_id=1, source_target_pairs={{0,4},{4,8},{8,12},{12,0},{1,5},{5,9},{9,13},{13,1},{2,6},{6,10},{... | collective-permute-start | bytes 49160 | tf_op jit(solution)/shard_map/ppermute | solution.py:62
  95.3 3.7 %collective-permute-start.32 = (f32[2,2048]{1,0:T(2,128)S(1)}, f32[2,2048]{1,0:T(2,128)S(1)}, u32[]{:S(2)}, u32[]{:S(2)}) collective-permute-start(f32[2,2048]{1,0:T(2,128)S(1)} %get-tuple-element.100), channel_id=1, source_target_pairs={{0,12},{4,0},{8,4},{12,8},{1,13},{5,1},{9,5},{13,9},{2,14},{6,2},{... | collective-permute-start | bytes 49160 | tf_op jit(solution)/shard_map/ppermute | solution.py:62
  100.2 1.9 %copy-start.2 = (f32[256]{0:T(256)}, f32[256]{0:T(256)S(1)}, u32[]{:S(2)}) copy-start(f32[256]{0:T(256)S(1)} %add_multiply_fusion.8) | copy-start | bytes 3076
  102.3 1.4 %collective-permute-start.33 = (f32[4,128,66]{1,0,2:T(4,128)S(1)}, f32[4,128,66]{1,0,2:T(4,128)S(1)}, u32[]{:S(2)}, u32[]{:S(2)}) collective-permute-start(f32[4,128,66]{1,0,2:T(4,128)S(1)} %pad_maximum_fusion.3), channel_id=1, source_target_pairs={{0,1},{1,0},{2,3},{3,2},{4,5},{5,4},{6,7},{7,6},{8,9},{9,8},{10,11... | collective-permute-start | bytes 405512 | tf_op jit(solution)/shard_map/ppermute | solution.py:92
  104.0 6.2 %collective-permute-start.34 = (f32[128,66]{0,1:T(8,128)S(1)}, f32[128,66]{0,1:T(8,128)S(1)}, u32[]{:S(2)}, u32[]{:S(2)}) collective-permute-start(f32[128,66]{0,1:T(8,128)S(1)} %bitcast.232), channel_id=1, source_target_pairs={{0,4},{4,8},{8,12},{12,0},{1,5},{5,9},{9,13},{13,1},{2,6},{6,10},{... | collective-permute-start | bytes 101384 | tf_op jit(solution)/shard_map/ppermute | solution.py:142
  104.0 6.5 %collective-permute-start.35 = (f32[128,66]{0,1:T(8,128)S(1)}, f32[128,66]{0,1:T(8,128)S(1)}, u32[]{:S(2)}, u32[]{:S(2)}) collective-permute-start(f32[128,66]{0,1:T(8,128)S(1)} %bitcast.231), channel_id=1, source_target_pairs={{0,8},{4,12},{8,0},{12,4},{1,9},{5,13},{9,1},{13,5},{2,10},{6,14},... | collective-permute-start | bytes 101384 | tf_op jit(solution)/shard_map/ppermute | solution.py:142
  106.9 4.0 %collective-permute-start.36 = (f32[128,66]{0,1:T(8,128)S(1)}, f32[128,66]{0,1:T(8,128)S(1)}, u32[]{:S(2)}, u32[]{:S(2)}) collective-permute-start(f32[128,66]{0,1:T(8,128)S(1)} %bitcast.230), channel_id=1, source_target_pairs={{0,12},{4,0},{8,4},{12,8},{1,13},{5,1},{9,5},{13,9},{2,14},{6,2},{... | collective-permute-start | bytes 101384 | tf_op jit(solution)/shard_map/ppermute | solution.py:142

commit v5 on v4

--- a/solution.py
+++ b/solution.py
@@ -114,7 +114,7 @@
 
     g_pot = jnp.zeros((tgt_count,), jnp.float32)
     f_pot = jnp.zeros((src_count,), jnp.float32)
-    for iteration in range(ITERS):
+    for _ in range(ITERS):
         scores = log_b[None, :] + (g_pot[None, :] - cost) / entropic
         maxima = jnp.max(scores, axis=1)
         totals = jnp.sum(jnp.exp(scores - maxima[:, None]), axis=1)
@@ -209,6 +209,15 @@
 ROW_AXES = (("rep",), ("cols",))
 
 
+def row_reduce(maxima, totals):
+    for axes in ROW_AXES:
+        if len(axes) == 1 and lax.axis_size(axes[0]) == 2:
+            maxima, totals = lse_allreduce(maxima, totals, axes)
+        else:
+            maxima, totals = lse_exchange(maxima, totals, axes)
+    return maxima, totals
+
+
 def body(sources, source_mass, targets, target_mass, fate_panel):
     row_count = lax.axis_size("rows")
     if row_count != 2 or lax.axis_size("cols") > 8:
@@ -216,33 +225,43 @@
     src_count = sources.shape[0]
     tgt_count = targets.shape[0]
     row = lax.axis_index("rows")
+    swap = [(0, 1), (1, 0)]
     mine = jnp.concatenate([sources, source_mass[:, None]], axis=1)
-    theirs = lax.ppermute(mine, "rows", [(0, 1), (1, 0)])
+    theirs = lax.ppermute(mine, "rows", swap)
+    all_sources = src_count * row_count
+    all_targets = tgt_count * lax.axis_size(("cols", "rep"))
+    log_b = jnp.log(target_mass / all_targets)
+    tgt_sq = jnp.sum(targets * targets, axis=1)
+    g_pot = jnp.zeros((tgt_count,), jnp.float32)
+
+    own_sq = jnp.sum(sources * sources, axis=1)
+    own_cost = pair_cost(sources, own_sq, targets, tgt_sq)
+    scores = log_b[None, :] + (g_pot[None, :] - own_cost) / entropic
+    maxima = jnp.max(scores, axis=1)
+    totals = jnp.sum(jnp.exp(scores - maxima[:, None]), axis=1)
+    maxima, totals = row_reduce(maxima, totals)
+    f_own = -relaxed * entropic * (maxima + jnp.log(totals))
+    f_theirs = lax.ppermute(f_own, "rows", swap)
+    f_all = jnp.concatenate(
+        [jnp.where(row == 0, f_own, f_theirs), jnp.where(row == 0, f_theirs, f_own)]
+    )
+
     first = jnp.where(row == 0, mine, theirs)
     second = jnp.where(row == 0, theirs, mine)
     gathered = jnp.concatenate([first, second], axis=0)
     all_src = gathered[:, : sources.shape[1]]
     all_mass = gathered[:, sources.shape[1]]
-    all_sources = src_count * row_count
-    all_targets = tgt_count * lax.axis_size(("cols", "rep"))
     log_a = jnp.log(all_mass / all_sources)
-    log_b = jnp.log(target_mass / all_targets)
     src_sq = jnp.sum(all_src * all_src, axis=1)
-    tgt_sq = jnp.sum(targets * targets, axis=1)
     cost = pair_cost(all_src, src_sq, targets, tgt_sq)
 
-    g_pot = jnp.zeros((tgt_count,), jnp.float32)
-    f_all = jnp.zeros((all_sources,), jnp.float32)
     for iteration in range(ITERS):
-        scores = log_b[None, :] + (g_pot[None, :] - cost) / entropic
-        maxima = jnp.max(scores, axis=1)
-        totals = jnp.sum(jnp.exp(scores - maxima[:, None]), axis=1)
-        for axes in ROW_AXES:
-            if len(axes) == 1 and lax.axis_size(axes[0]) == 2:
-                maxima, totals = lse_allreduce(maxima, totals, axes)
-            else:
-                maxima, totals = lse_exchange(maxima, totals, axes)
-        f_all = -relaxed * entropic * (maxima + jnp.log(totals))
+        if iteration > 0:
+            scores = log_b[None, :] + (g_pot[None, :] - cost) / entropic
+            maxima = jnp.max(scores, axis=1)
+            totals = jnp.sum(jnp.exp(scores - maxima[:, None]), axis=1)
+            maxima, totals = row_reduce(maxima, totals)
+            f_all = -relaxed * entropic * (maxima + jnp.log(totals))
 
         scores = log_a[:, None] + (f_all[:, None] - cost) / entropic
         maxima = jnp.max(scores, axis=0)
@@ -250,8 +269,7 @@
         g_pot = -relaxed * entropic * (maxima + jnp.log(totals))
 
     f_pot = lax.dynamic_slice_in_dim(f_all, row * src_count, src_count)
-    cost_mine = lax.dynamic_slice_in_dim(cost, row * src_count, src_count, axis=0)
-    return (f_pot,) + fate_pullback(cost_mine, log_b, g_pot, fate_panel)
+    return (f_pot,) + fate_pullback(own_cost, log_b, g_pot, fate_panel)
 
 
 def solution(mesh):
@@ -267,4 +285,5 @@
         P(("parts", "cols", "rep")),
         P(("parts", "rows", "cols", "rep"), None),
     )
+
     return jax.shard_map(body, mesh=mesh, in_specs=in_specs, out_specs=out_specs, check_vma=False)

time: 112 us -> 119 us (1.062)
  other arithmetic: 20.8 us -> 24.7 us
  matrix products: 3.39 us -> 6.04 us
  waiting for transfers between devices: 41.1 us -> 42.7 us
    dot_general x1 -> x2, matrix products: 2.33 us -> 4.98 us  [pair_cost(): lax.dot_general(lhs_rows, rhs_rows, (((1,), (1,)), ((), ())), precision=l...]
    reduce_max x8 -> x7, other arithmetic: 2.85 us -> 4.98 us  [body(): maxima = jnp.max(scores, axis=0)]
    reduce_sum x8, other arithmetic: 4.46 us -> 6.1 us  [body(): totals = jnp.sum(jnp.exp(scores - maxima[:, None]), axis=1)]
    reduce_sum x8, other arithmetic: 4.64 us -> 5.9 us  [body(): totals = jnp.sum(jnp.exp(scores - maxima[None, :]), axis=0)]
    ppermute x1 -> x2, waiting for transfers between devices: 5.46 us -> 6.59 us  [the longest x1 5.06 us: body(): theirs = lax.ppermute(mine, 'rows', swap)]
    ppermute x1 -> x2, starting transfers between devices: 3.03 us -> 2.16 us  [the longest x1 1.55 us: body(): f_theirs = lax.ppermute(f_own, 'rows', swap)]
  transfers between devices with their start and end apart: 37 -> 38, of which waited for: 35 -> 36; matrix products, arithmetic and copies ran while one was open for 2% -> 1% of each run, Pallas kernels for 0% -> 0%
where the time goes in v5:
time: 119 us
  starting transfers between devices  42.7 us (36%)
  waiting for transfers between devices  42.7 us (36%)
  other arithmetic  24.7 us (21%)
  matrix products  6.04 us (5%)
  local copies, waits for them, and re-layouts  1.59 us (1%)
  between operations  1.47 us (1%)
    ppermute x24, starting transfers between devices, lse_exchange(): received.append(lax.ppermute(payload, axes, perm))  35.3 us
    ppermute x24, waiting for transfers between devices, lse_exchange(): received.append(lax.ppermute(payload, axes, perm))  23.2 us
    ppermute x8, waiting for transfers between devices, lse_allreduce(): other = lax.ppermute(jnp.stack([maxima, totals]), name, perm)  9.02 us
    reduce_sum x8, other arithmetic, body(): totals = jnp.sum(jnp.exp(scores - maxima[:, None]), axis=1)  6.1 us
    reduce_sum x8, other arithmetic, body(): totals = jnp.sum(jnp.exp(scores - maxima[None, :]), axis=0)  5.9 us
    ppermute x1, waiting for transfers between devices, body(): theirs = lax.ppermute(mine, 'rows', swap)  5.06 us
    dot_general x2, matrix products, pair_cost(): lax.dot_general(lhs_rows, rhs_rows, (((1,), (1,)), ((), ())), precision=l...  4.98 us
    reduce_max x7, other arithmetic, body(): maxima = jnp.max(scores, axis=0)  4.98 us
  transfers between devices with their start and end apart: 38, of which 36 were waited for; matrix products, arithmetic and copies ran while one was open for 1% of the time, Pallas kernels for 0%

profile of v5, /device:TPU:0, one launch (start us, length us, event | category | flops | bytes accessed | tf_op | source)
XLA Modules:
  0.0 119.1 jit_solution(12148430070827568254)
XLA Ops:
  2.3 1.0 multiply_reduce_fusion.1
  3.2 2.2 %fusion.21 = (f32[1024]{0:T(1024)S(1)}, f32[1024,256]{0,1:T(8,128)S(1)}) fusion(f32[256]{0:T(256)S(1)} %multiply_log_fusion, f32[1024,64]{0,1:T(8,128)} %param.5, f32[256,64]{0,1:T(8,128)} %param.7, f32[256]{0:T(256)S(1)} %multiply_reduce_fusion.2, f32[1024]{0:T(1024)S(1)} %multiply_reduce_fusion.1), kind=kOutput, calls=%fused_computation.57 | convolution fusion | flops 203422720 | bytes 1386496 | tf_op jit(solution)/shard_map/dot_general | solution.py:14
  7.2 3.0 %collective-permute-start.2 = (f32[2,1024]{1,0:T(2,128)S(1)}, f32[2,1024]{1,0:T(2,128)S(1)}, u32[]{:S(2)}, u32[]{:S(2)}) collective-permute-start(f32[2,1024]{1,0:T(2,128)S(1)} %get-tuple-element.116), channel_id=1, source_target_pairs={{0,4},{4,8},{8,12},{12,0},{1,5},{5,9},{9,13},{13,1},{2,6},{6,10},{... | collective-permute-start | bytes 24584 | tf_op jit(solution)/shard_map/ppermute | solution.py:62
  10.2 2.6 %collective-permute-start.3 = (f32[2,1024]{1,0:T(2,128)S(1)}, f32[2,1024]{1,0:T(2,128)S(1)}, u32[]{:S(2)}, u32[]{:S(2)}) collective-permute-start(f32[2,1024]{1,0:T(2,128)S(1)} %get-tuple-element.116), channel_id=1, source_target_pairs={{0,8},{4,12},{8,0},{12,4},{1,9},{5,13},{9,1},{13,5},{2,10},{6,14},... | collective-permute-start | bytes 24584 | tf_op jit(solution)/shard_map/ppermute | solution.py:62
  12.8 1.3 %collective-permute-start.4 = (f32[2,1024]{1,0:T(2,128)S(1)}, f32[2,1024]{1,0:T(2,128)S(1)}, u32[]{:S(2)}, u32[]{:S(2)}) collective-permute-start(f32[2,1024]{1,0:T(2,128)S(1)} %get-tuple-element.116), channel_id=1, source_target_pairs={{0,12},{4,0},{8,4},{12,8},{1,13},{5,1},{9,5},{13,9},{2,14},{6,2},{... | collective-permute-start | bytes 24584 | tf_op jit(solution)/shard_map/ppermute | solution.py:62
  14.8 1.7 %collective-permute-done.4 = f32[2,1024]{1,0:T(2,128)S(1)} collective-permute-done((f32[2,1024]{1,0:T(2,128)S(1)}, f32[2,1024]{1,0:T(2,128)S(1)}, u32[]{:S(2)}, u32[]{:S(2)}) %collective-permute-start.4) | collective-permute-done | bytes 8224 | tf_op jit(solution)/shard_map/ppermute | solution.py:62
  16.5 1.6 %collective-permute-start.5 = (f32[1024]{0:T(1024)S(1)}, f32[1024]{0:T(1024)S(1)}, u32[]{:S(2)}, u32[]{:S(2)}) collective-permute-start(f32[1024]{0:T(1024)S(1)} %add_multiply_fusion.7), channel_id=1, source_target_pairs={{0,2},{2,0},{1,3},{3,1},{4,6},{6,4},{5,7},{7,5},{8,10},{10,8},{9,1... | collective-permute-start | bytes 12296 | tf_op jit(solution)/shard_map/ppermute | solution.py:244
  18.7 1.5 %collective-permute-done.5 = f32[1024]{0:T(1024)S(1)} collective-permute-done((f32[1024]{0:T(1024)S(1)}, f32[1024]{0:T(1024)S(1)}, u32[]{:S(2)}, u32[]{:S(2)}) %collective-permute-start.5) | collective-permute-done | bytes 4128 | tf_op jit(solution)/shard_map/ppermute | solution.py:244
  20.2 5.1 %collective-permute-done = f32[1024,65]{0,1:T(8,128)S(1)} collective-permute-done((f32[1024,65]{0,1:T(8,128)S(1)}, f32[1024,65]{0,1:T(8,128)S(1)}, u32[]{:S(2)}, u32[]{:S(2)}) %collective-permute-start) | collective-permute-done | bytes 266272 | tf_op jit(solution)/shard_map/ppermute | solution.py:230
  25.5 2.8 %fusion.2 = (f32[256]{0:T(256)S(1)}, f32[2048,256]{1,0:T(8,128)S(1)}) fusion(f32[2048]{0:T(1024)S(1)} %pad_maximum_fusion.29, f32[2048]{0:T(1024)S(1)} %bitcast.180, f32[256,64]{0,1:T(8,128)S(1)} %copy-done.2, f32[1024,65]{0,1:T(8,128)S(1)} %get-tuple-element.8, f32[1024,65]{0,1:T(8,128)S(1)} %get-tuple-element.7, f32[256]{0:T(256)S(1)} %multiply_reduce_fusion.2, ...), kind=kOutput, calls=%fused_computation.33 | convolution fusion | flops 406978304 | bytes 2721792 | tf_op jit(solution)/shard_map/dot_general | solution.py:14
  30.3 1.2 collective-permute-done.6
  31.9 3.4 %collective-permute-start.8 = (f32[2,2048]{1,0:T(2,128)S(1)}, f32[2,2048]{1,0:T(2,128)S(1)}, u32[]{:S(2)}, u32[]{:S(2)}) collective-permute-start(f32[2,2048]{1,0:T(2,128)S(1)} %get-tuple-element.110), channel_id=1, source_target_pairs={{0,8},{4,12},{8,0},{12,4},{1,9},{5,13},{9,1},{13,5},{2,10},{6,14},... | collective-permute-start | bytes 49160 | tf_op jit(solution)/shard_map/ppermute | solution.py:62
  35.7 1.4 %collective-permute-done.7 = f32[2,2048]{1,0:T(2,128)S(1)} collective-permute-done((f32[2,2048]{1,0:T(2,128)S(1)}, f32[2,2048]{1,0:T(2,128)S(1)}, u32[]{:S(2)}, u32[]{:S(2)}) %collective-permute-start.7) | collective-permute-done | bytes 16416 | tf_op jit(solution)/shard_map/ppermute | solution.py:62
  37.3 1.8 %collective-permute-done.9 = f32[2,2048]{1,0:T(2,128)S(1)} collective-permute-done((f32[2,2048]{1,0:T(2,128)S(1)}, f32[2,2048]{1,0:T(2,128)S(1)}, u32[]{:S(2)}, u32[]{:S(2)}) %collective-permute-start.9) | collective-permute-done | bytes 16416 | tf_op jit(solution)/shard_map/ppermute | solution.py:62
  42.0 1.2 collective-permute-done.10
  43.9 2.1 %collective-permute-start.12 = (f32[2,2048]{1,0:T(2,128)S(1)}, f32[2,2048]{1,0:T(2,128)S(1)}, u32[]{:S(2)}, u32[]{:S(2)}) collective-permute-start(f32[2,2048]{1,0:T(2,128)S(1)} %get-tuple-element.108), channel_id=1, source_target_pairs={{0,8},{4,12},{8,0},{12,4},{1,9},{5,13},{9,1},{13,5},{2,10},{6,14},... | collective-permute-start | bytes 49160 | tf_op jit(solution)/shard_map/ppermute | solution.py:62
  46.0 1.1 collective-permute-start.13
  47.2 1.7 %collective-permute-done.11 = f32[2,2048]{1,0:T(2,128)S(1)} collective-permute-done((f32[2,2048]{1,0:T(2,128)S(1)}, f32[2,2048]{1,0:T(2,128)S(1)}, u32[]{:S(2)}, u32[]{:S(2)}) %collective-permute-start.11) | collective-permute-done | bytes 16416 | tf_op jit(solution)/shard_map/ppermute | solution.py:62
  52.7 1.2 collective-permute-done.14
  53.9 1.9 %collective-permute-start.15 = (f32[2,2048]{1,0:T(2,128)S(1)}, f32[2,2048]{1,0:T(2,128)S(1)}, u32[]{:S(2)}, u32[]{:S(2)}) collective-permute-start(f32[2,2048]{1,0:T(2,128)S(1)} %get-tuple-element.106), channel_id=1, source_target_pairs={{0,4},{4,8},{8,12},{12,0},{1,5},{5,9},{9,13},{13,1},{2,6},{6,10},{... | collective-permute-start | bytes 49160 | tf_op jit(solution)/shard_map/ppermute | solution.py:62
  55.9 1.8 %collective-permute-start.16 = (f32[2,2048]{1,0:T(2,128)S(1)}, f32[2,2048]{1,0:T(2,128)S(1)}, u32[]{:S(2)}, u32[]{:S(2)}) collective-permute-start(f32[2,2048]{1,0:T(2,128)S(1)} %get-tuple-element.106), channel_id=1, source_target_pairs={{0,8},{4,12},{8,0},{12,4},{1,9},{5,13},{9,1},{13,5},{2,10},{6,14},... | collective-permute-start | bytes 49160 | tf_op jit(solution)/shard_map/ppermute | solution.py:62
  58.3 1.4 %collective-permute-done.15 = f32[2,2048]{1,0:T(2,128)S(1)} collective-permute-done((f32[2,2048]{1,0:T(2,128)S(1)}, f32[2,2048]{1,0:T(2,128)S(1)}, u32[]{:S(2)}, u32[]{:S(2)}) %collective-permute-start.15) | collective-permute-done | bytes 16416 | tf_op jit(solution)/shard_map/ppermute | solution.py:62
  64.3 1.2 collective-permute-done.18
  66.5 2.1 %collective-permute-start.20 = (f32[2,2048]{1,0:T(2,128)S(1)}, f32[2,2048]{1,0:T(2,128)S(1)}, u32[]{:S(2)}, u32[]{:S(2)}) collective-permute-start(f32[2,2048]{1,0:T(2,128)S(1)} %get-tuple-element.104), channel_id=1, source_target_pairs={{0,8},{4,12},{8,0},{12,4},{1,9},{5,13},{9,1},{13,5},{2,10},{6,14},... | collective-permute-start | bytes 49160 | tf_op jit(solution)/shard_map/ppermute | solution.py:62
  68.6 1.0 collective-permute-start.21
  69.7 1.6 %collective-permute-done.19 = f32[2,2048]{1,0:T(2,128)S(1)} collective-permute-done((f32[2,2048]{1,0:T(2,128)S(1)}, f32[2,2048]{1,0:T(2,128)S(1)}, u32[]{:S(2)}, u32[]{:S(2)}) %collective-permute-start.19) | collective-permute-done | bytes 16416 | tf_op jit(solution)/shard_map/ppermute | solution.py:62
  71.4 1.0 collective-permute-done.21
  75.3 1.2 collective-permute-done.22
  76.5 1.4 %collective-permute-start.23 = (f32[2,2048]{1,0:T(2,128)S(1)}, f32[2,2048]{1,0:T(2,128)S(1)}, u32[]{:S(2)}, u32[]{:S(2)}) collective-permute-start(f32[2,2048]{1,0:T(2,128)S(1)} %get-tuple-element.102), channel_id=1, source_target_pairs={{0,4},{4,8},{8,12},{12,0},{1,5},{5,9},{9,13},{13,1},{2,6},{6,10},{... | collective-permute-start | bytes 49160 | tf_op jit(solution)/shard_map/ppermute | solution.py:62
  78.0 2.0 %collective-permute-start.24 = (f32[2,2048]{1,0:T(2,128)S(1)}, f32[2,2048]{1,0:T(2,128)S(1)}, u32[]{:S(2)}, u32[]{:S(2)}) collective-permute-start(f32[2,2048]{1,0:T(2,128)S(1)} %get-tuple-element.102), channel_id=1, source_target_pairs={{0,8},{4,12},{8,0},{12,4},{1,9},{5,13},{9,1},{13,5},{2,10},{6,14},... | collective-permute-start | bytes 49160 | tf_op jit(solution)/shard_map/ppermute | solution.py:62
  80.5 1.6 %collective-permute-done.23 = f32[2,2048]{1,0:T(2,128)S(1)} collective-permute-done((f32[2,2048]{1,0:T(2,128)S(1)}, f32[2,2048]{1,0:T(2,128)S(1)}, u32[]{:S(2)}, u32[]{:S(2)}) %collective-permute-start.23) | collective-permute-done | bytes 16416 | tf_op jit(solution)/shard_map/ppermute | solution.py:62
  82.6 1.1 collective-permute-done.25
  86.6 1.2 collective-permute-done.26
  87.9 1.0 collective-permute-start.27
  88.9 1.9 %collective-permute-start.28 = (f32[2,2048]{1,0:T(2,128)S(1)}, f32[2,2048]{1,0:T(2,128)S(1)}, u32[]{:S(2)}, u32[]{:S(2)}) collective-permute-start(f32[2,2048]{1,0:T(2,128)S(1)} %get-tuple-element.100), channel_id=1, source_target_pairs={{0,8},{4,12},{8,0},{12,4},{1,9},{5,13},{9,1},{13,5},{2,10},{6,14},... | collective-permute-start | bytes 49160 | tf_op jit(solution)/shard_map/ppermute | solution.py:62
  90.8 0.9 collective-permute-start.29
  91.8 1.7 %collective-permute-done.27 = f32[2,2048]{1,0:T(2,128)S(1)} collective-permute-done((f32[2,2048]{1,0:T(2,128)S(1)}, f32[2,2048]{1,0:T(2,128)S(1)}, u32[]{:S(2)}, u32[]{:S(2)}) %collective-permute-start.27) | collective-permute-done | bytes 16416 | tf_op jit(solution)/shard_map/ppermute | solution.py:62
  97.5 1.2 collective-permute-done.30
  98.7 1.6 %collective-permute-start.31 = (f32[2,2048]{1,0:T(2,128)S(1)}, f32[2,2048]{1,0:T(2,128)S(1)}, u32[]{:S(2)}, u32[]{:S(2)}) collective-permute-start(f32[2,2048]{1,0:T(2,128)S(1)} %get-tuple-element.98), channel_id=1, source_target_pairs={{0,4},{4,8},{8,12},{12,0},{1,5},{5,9},{9,13},{13,1},{2,6},{6,10},{... | collective-permute-start | bytes 49160 | tf_op jit(solution)/shard_map/ppermute | solution.py:62
  100.3 1.8 %collective-permute-start.32 = (f32[2,2048]{1,0:T(2,128)S(1)}, f32[2,2048]{1,0:T(2,128)S(1)}, u32[]{:S(2)}, u32[]{:S(2)}) collective-permute-start(f32[2,2048]{1,0:T(2,128)S(1)} %get-tuple-element.98), channel_id=1, source_target_pairs={{0,8},{4,12},{8,0},{12,4},{1,9},{5,13},{9,1},{13,5},{2,10},{6,14},... | collective-permute-start | bytes 49160 | tf_op jit(solution)/shard_map/ppermute | solution.py:62
  102.7 1.6 %collective-permute-done.31 = f32[2,2048]{1,0:T(2,128)S(1)} collective-permute-done((f32[2,2048]{1,0:T(2,128)S(1)}, f32[2,2048]{1,0:T(2,128)S(1)}, u32[]{:S(2)}, u32[]{:S(2)}) %collective-permute-start.31) | collective-permute-done | bytes 16416 | tf_op jit(solution)/shard_map/ppermute | solution.py:62
  108.0 1.1 fusion.20
  109.6 1.3 %collective-permute-done.34 = f32[4,128,66]{1,0,2:T(4,128)S(1)} collective-permute-done((f32[4,128,66]{1,0,2:T(4,128)S(1)}, f32[4,128,66]{1,0,2:T(4,128)S(1)}, u32[]{:S(2)}, u32[]{:S(2)}) %collective-permute-start.34) | collective-permute-done | bytes 135200 | tf_op jit(solution)/shard_map/ppermute | solution.py:92
  111.2 1.1 collective-permute-start.35
  112.3 1.9 %collective-permute-start.36 = (f32[128,66]{0,1:T(8,128)S(1)}, f32[128,66]{0,1:T(8,128)S(1)}, u32[]{:S(2)}, u32[]{:S(2)}) collective-permute-start(f32[128,66]{0,1:T(8,128)S(1)} %bitcast.233), channel_id=1, source_target_pairs={{0,8},{4,12},{8,0},{12,4},{1,9},{5,13},{9,1},{13,5},{2,10},{6,14},... | collective-permute-start | bytes 101384 | tf_op jit(solution)/shard_map/ppermute | solution.py:142
  114.3 1.0 collective-permute-start.37
  115.9 1.4 %collective-permute-done.35 = f32[128,66]{0,1:T(8,128)S(1)} collective-permute-done((f32[128,66]{0,1:T(8,128)S(1)}, f32[128,66]{0,1:T(8,128)S(1)}, u32[]{:S(2)}, u32[]{:S(2)}) %collective-permute-start.35) | collective-permute-done | bytes 33824 | tf_op jit(solution)/shard_map/ppermute | solution.py:142
  117.3 1.0 collective-permute-done.36
  (158 shorter events, 38.8 us)
Async XLA Ops:
  0.6 107.4 %copy-start = (f32[256,64]{0,1:T(8,128)S(1)}, f32[256,64]{0,1:T(8,128)}, u32[]{:S(2)}) copy-start(f32[256,64]{0,1:T(8,128)} %param.9) | copy-start | bytes 196612
  0.6 17.4 %copy-start.1 = (f32[1024,64]{0,1:T(8,128)S(1)}, f32[1024,64]{0,1:T(8,128)}, u32[]{:S(2)}) copy-start(f32[1024,64]{0,1:T(8,128)} %param.5) | copy-start | bytes 786436
  0.7 17.4 %copy-start.3 = (f32[1024]{0:T(1024)S(1)}, f32[1024]{0:T(1024)}, u32[]{:S(2)}) copy-start(f32[1024]{0:T(1024)} %param.6) | copy-start | bytes 12292
  5.5 20.0 %copy-start.2 = (f32[256,64]{0,1:T(8,128)S(1)}, f32[256,64]{0,1:T(8,128)}, u32[]{:S(2)}) copy-start(f32[256,64]{0,1:T(8,128)} %param.7) | copy-start | bytes 196612
  5.8 1.4 %collective-permute-start.1 = (f32[2,1024]{1,0:T(2,128)S(1)}, f32[2,1024]{1,0:T(2,128)S(1)}, u32[]{:S(2)}, u32[]{:S(2)}) collective-permute-start(f32[2,1024]{1,0:T(2,128)S(1)} %pad_maximum_fusion.27), channel_id=1, source_target_pairs={{0,1},{1,0},{2,3},{3,2},{4,5},{5,4},{6,7},{7,6},{8,9},{9,8},{10,11... | collective-permute-start | bytes 24584 | tf_op jit(solution)/shard_map/ppermute | solution.py:43
  7.2 6.9 %collective-permute-start.2 = (f32[2,1024]{1,0:T(2,128)S(1)}, f32[2,1024]{1,0:T(2,128)S(1)}, u32[]{:S(2)}, u32[]{:S(2)}) collective-permute-start(f32[2,1024]{1,0:T(2,128)S(1)} %get-tuple-element.116), channel_id=1, source_target_pairs={{0,4},{4,8},{8,12},{12,0},{1,5},{5,9},{9,13},{13,1},{2,6},{6,10},{... | collective-permute-start | bytes 24584 | tf_op jit(solution)/shard_map/ppermute | solution.py:62
  10.2 4.6 %collective-permute-start.3 = (f32[2,1024]{1,0:T(2,128)S(1)}, f32[2,1024]{1,0:T(2,128)S(1)}, u32[]{:S(2)}, u32[]{:S(2)}) collective-permute-start(f32[2,1024]{1,0:T(2,128)S(1)} %get-tuple-element.116), channel_id=1, source_target_pairs={{0,8},{4,12},{8,0},{12,4},{1,9},{5,13},{9,1},{13,5},{2,10},{6,14},... | collective-permute-start | bytes 24584 | tf_op jit(solution)/shard_map/ppermute | solution.py:62
  12.8 3.7 %collective-permute-start.4 = (f32[2,1024]{1,0:T(2,128)S(1)}, f32[2,1024]{1,0:T(2,128)S(1)}, u32[]{:S(2)}, u32[]{:S(2)}) collective-permute-start(f32[2,1024]{1,0:T(2,128)S(1)} %get-tuple-element.116), channel_id=1, source_target_pairs={{0,12},{4,0},{8,4},{12,8},{1,13},{5,1},{9,5},{13,9},{2,14},{6,2},{... | collective-permute-start | bytes 24584 | tf_op jit(solution)/shard_map/ppermute | solution.py:62
  16.5 3.7 %collective-permute-start.5 = (f32[1024]{0:T(1024)S(1)}, f32[1024]{0:T(1024)S(1)}, u32[]{:S(2)}, u32[]{:S(2)}) collective-permute-start(f32[1024]{0:T(1024)S(1)} %add_multiply_fusion.7), channel_id=1, source_target_pairs={{0,2},{2,0},{1,3},{3,1},{4,6},{6,4},{5,7},{7,5},{8,10},{10,8},{9,1... | collective-permute-start | bytes 12296 | tf_op jit(solution)/shard_map/ppermute | solution.py:244
  18.1 7.2 %collective-permute-start = (f32[1024,65]{0,1:T(8,128)S(1)}, f32[1024,65]{0,1:T(8,128)S(1)}, u32[]{:S(2)}, u32[]{:S(2)}) collective-permute-start(f32[1024,65]{0,1:T(8,128)S(1)} %pad_maximum_fusion.2), channel_id=1, source_target_pairs={{0,2},{2,0},{1,3},{3,1},{4,6},{6,4},{5,7},{7,5},{8,10},{10,8},{9,1... | collective-permute-start | bytes 798728 | tf_op jit(solution)/shard_map/ppermute | solution.py:230
  30.2 1.2 %collective-permute-start.6 = (f32[2,2048]{1,0:T(2,128)S(1)}, f32[2,2048]{1,0:T(2,128)S(1)}, u32[]{:S(2)}, u32[]{:S(2)}) collective-permute-start(f32[2,2048]{1,0:T(2,128)S(1)} %pad_maximum_fusion.13), channel_id=1, source_target_pairs={{0,1},{1,0},{2,3},{3,2},{4,5},{5,4},{6,7},{7,6},{8,9},{9,8},{10,11... | collective-permute-start | bytes 49160 | tf_op jit(solution)/shard_map/ppermute | solution.py:43
  31.5 5.6 %collective-permute-start.7 = (f32[2,2048]{1,0:T(2,128)S(1)}, f32[2,2048]{1,0:T(2,128)S(1)}, u32[]{:S(2)}, u32[]{:S(2)}) collective-permute-start(f32[2,2048]{1,0:T(2,128)S(1)} %get-tuple-element.110), channel_id=1, source_target_pairs={{0,4},{4,8},{8,12},{12,0},{1,5},{5,9},{9,13},{13,1},{2,6},{6,10},{... | collective-permute-start | bytes 49160 | tf_op jit(solution)/shard_map/ppermute | solution.py:62
  31.9 5.4 %collective-permute-start.8 = (f32[2,2048]{1,0:T(2,128)S(1)}, f32[2,2048]{1,0:T(2,128)S(1)}, u32[]{:S(2)}, u32[]{:S(2)}) collective-permute-start(f32[2,2048]{1,0:T(2,128)S(1)} %get-tuple-element.110), channel_id=1, source_target_pairs={{0,8},{4,12},{8,0},{12,4},{1,9},{5,13},{9,1},{13,5},{2,10},{6,14},... | collective-permute-start | bytes 49160 | tf_op jit(solution)/shard_map/ppermute | solution.py:62
  35.4 3.7 %collective-permute-start.9 = (f32[2,2048]{1,0:T(2,128)S(1)}, f32[2,2048]{1,0:T(2,128)S(1)}, u32[]{:S(2)}, u32[]{:S(2)}) collective-permute-start(f32[2,2048]{1,0:T(2,128)S(1)} %get-tuple-element.110), channel_id=1, source_target_pairs={{0,12},{4,0},{8,4},{12,8},{1,13},{5,1},{9,5},{13,9},{2,14},{6,2},{... | collective-permute-start | bytes 49160 | tf_op jit(solution)/shard_map/ppermute | solution.py:62
  42.0 1.2 %collective-permute-start.10 = (f32[2,2048]{1,0:T(2,128)S(1)}, f32[2,2048]{1,0:T(2,128)S(1)}, u32[]{:S(2)}, u32[]{:S(2)}) collective-permute-start(f32[2,2048]{1,0:T(2,128)S(1)} %pad_maximum_fusion.15), channel_id=1, source_target_pairs={{0,1},{1,0},{2,3},{3,2},{4,5},{5,4},{6,7},{7,6},{8,9},{9,8},{10,11... | collective-permute-start | bytes 49160 | tf_op jit(solution)/shard_map/ppermute | solution.py:43
  43.3 5.6 %collective-permute-start.11 = (f32[2,2048]{1,0:T(2,128)S(1)}, f32[2,2048]{1,0:T(2,128)S(1)}, u32[]{:S(2)}, u32[]{:S(2)}) collective-permute-start(f32[2,2048]{1,0:T(2,128)S(1)} %get-tuple-element.108), channel_id=1, source_target_pairs={{0,4},{4,8},{8,12},{12,0},{1,5},{5,9},{9,13},{13,1},{2,6},{6,10},{... | collective-permute-start | bytes 49160 | tf_op jit(solution)/shard_map/ppermute | solution.py:62
  43.9 4.9 %collective-permute-start.12 = (f32[2,2048]{1,0:T(2,128)S(1)}, f32[2,2048]{1,0:T(2,128)S(1)}, u32[]{:S(2)}, u32[]{:S(2)}) collective-permute-start(f32[2,2048]{1,0:T(2,128)S(1)} %get-tuple-element.108), channel_id=1, source_target_pairs={{0,8},{4,12},{8,0},{12,4},{1,9},{5,13},{9,1},{13,5},{2,10},{6,14},... | collective-permute-start | bytes 49160 | tf_op jit(solution)/shard_map/ppermute | solution.py:62
  46.0 3.7 %collective-permute-start.13 = (f32[2,2048]{1,0:T(2,128)S(1)}, f32[2,2048]{1,0:T(2,128)S(1)}, u32[]{:S(2)}, u32[]{:S(2)}) collective-permute-start(f32[2,2048]{1,0:T(2,128)S(1)} %get-tuple-element.108), channel_id=1, source_target_pairs={{0,12},{4,0},{8,4},{12,8},{1,13},{5,1},{9,5},{13,9},{2,14},{6,2},{... | collective-permute-start | bytes 49160 | tf_op jit(solution)/shard_map/ppermute | solution.py:62
  52.6 1.2 %collective-permute-start.14 = (f32[2,2048]{1,0:T(2,128)S(1)}, f32[2,2048]{1,0:T(2,128)S(1)}, u32[]{:S(2)}, u32[]{:S(2)}) collective-permute-start(f32[2,2048]{1,0:T(2,128)S(1)} %pad_maximum_fusion.17), channel_id=1, source_target_pairs={{0,1},{1,0},{2,3},{3,2},{4,5},{5,4},{6,7},{7,6},{8,9},{9,8},{10,11... | collective-permute-start | bytes 49160 | tf_op jit(solution)/shard_map/ppermute | solution.py:43
  53.9 5.8 %collective-permute-start.15 = (f32[2,2048]{1,0:T(2,128)S(1)}, f32[2,2048]{1,0:T(2,128)S(1)}, u32[]{:S(2)}, u32[]{:S(2)}) collective-permute-start(f32[2,2048]{1,0:T(2,128)S(1)} %get-tuple-element.106), channel_id=1, source_target_pairs={{0,4},{4,8},{8,12},{12,0},{1,5},{5,9},{9,13},{13,1},{2,6},{6,10},{... | collective-permute-start | bytes 49160 | tf_op jit(solution)/shard_map/ppermute | solution.py:62
  55.9 4.7 %collective-permute-start.16 = (f32[2,2048]{1,0:T(2,128)S(1)}, f32[2,2048]{1,0:T(2,128)S(1)}, u32[]{:S(2)}, u32[]{:S(2)}) collective-permute-start(f32[2,2048]{1,0:T(2,128)S(1)} %get-tuple-element.106), channel_id=1, source_target_pairs={{0,8},{4,12},{8,0},{12,4},{1,9},{5,13},{9,1},{13,5},{2,10},{6,14},... | collective-permute-start | bytes 49160 | tf_op jit(solution)/shard_map/ppermute | solution.py:62
  57.7 3.7 %collective-permute-start.17 = (f32[2,2048]{1,0:T(2,128)S(1)}, f32[2,2048]{1,0:T(2,128)S(1)}, u32[]{:S(2)}, u32[]{:S(2)}) collective-permute-start(f32[2,2048]{1,0:T(2,128)S(1)} %get-tuple-element.106), channel_id=1, source_target_pairs={{0,12},{4,0},{8,4},{12,8},{1,13},{5,1},{9,5},{13,9},{2,14},{6,2},{... | collective-permute-start | bytes 49160 | tf_op jit(solution)/shard_map/ppermute | solution.py:62
  64.2 1.2 %collective-permute-start.18 = (f32[2,2048]{1,0:T(2,128)S(1)}, f32[2,2048]{1,0:T(2,128)S(1)}, u32[]{:S(2)}, u32[]{:S(2)}) collective-permute-start(f32[2,2048]{1,0:T(2,128)S(1)} %pad_maximum_fusion.19), channel_id=1, source_target_pairs={{0,1},{1,0},{2,3},{3,2},{4,5},{5,4},{6,7},{7,6},{8,9},{9,8},{10,11... | collective-permute-start | bytes 49160 | tf_op jit(solution)/shard_map/ppermute | solution.py:43
  65.6 5.7 %collective-permute-start.19 = (f32[2,2048]{1,0:T(2,128)S(1)}, f32[2,2048]{1,0:T(2,128)S(1)}, u32[]{:S(2)}, u32[]{:S(2)}) collective-permute-start(f32[2,2048]{1,0:T(2,128)S(1)} %get-tuple-element.104), channel_id=1, source_target_pairs={{0,4},{4,8},{8,12},{12,0},{1,5},{5,9},{9,13},{13,1},{2,6},{6,10},{... | collective-permute-start | bytes 49160 | tf_op jit(solution)/shard_map/ppermute | solution.py:62
  66.5 4.9 %collective-permute-start.20 = (f32[2,2048]{1,0:T(2,128)S(1)}, f32[2,2048]{1,0:T(2,128)S(1)}, u32[]{:S(2)}, u32[]{:S(2)}) collective-permute-start(f32[2,2048]{1,0:T(2,128)S(1)} %get-tuple-element.104), channel_id=1, source_target_pairs={{0,8},{4,12},{8,0},{12,4},{1,9},{5,13},{9,1},{13,5},{2,10},{6,14},... | collective-permute-start | bytes 49160 | tf_op jit(solution)/shard_map/ppermute | solution.py:62
  68.6 3.7 %collective-permute-start.21 = (f32[2,2048]{1,0:T(2,128)S(1)}, f32[2,2048]{1,0:T(2,128)S(1)}, u32[]{:S(2)}, u32[]{:S(2)}) collective-permute-start(f32[2,2048]{1,0:T(2,128)S(1)} %get-tuple-element.104), channel_id=1, source_target_pairs={{0,12},{4,0},{8,4},{12,8},{1,13},{5,1},{9,5},{13,9},{2,14},{6,2},{... | collective-permute-start | bytes 49160 | tf_op jit(solution)/shard_map/ppermute | solution.py:62
  75.2 1.2 %collective-permute-start.22 = (f32[2,2048]{1,0:T(2,128)S(1)}, f32[2,2048]{1,0:T(2,128)S(1)}, u32[]{:S(2)}, u32[]{:S(2)}) collective-permute-start(f32[2,2048]{1,0:T(2,128)S(1)} %pad_maximum_fusion.21), channel_id=1, source_target_pairs={{0,1},{1,0},{2,3},{3,2},{4,5},{5,4},{6,7},{7,6},{8,9},{9,8},{10,11... | collective-permute-start | bytes 49160 | tf_op jit(solution)/shard_map/ppermute | solution.py:43
  76.5 5.6 %collective-permute-start.23 = (f32[2,2048]{1,0:T(2,128)S(1)}, f32[2,2048]{1,0:T(2,128)S(1)}, u32[]{:S(2)}, u32[]{:S(2)}) collective-permute-start(f32[2,2048]{1,0:T(2,128)S(1)} %get-tuple-element.102), channel_id=1, source_target_pairs={{0,4},{4,8},{8,12},{12,0},{1,5},{5,9},{9,13},{13,1},{2,6},{6,10},{... | collective-permute-start | bytes 49160 | tf_op jit(solution)/shard_map/ppermute | solution.py:62
  78.0 4.6 %collective-permute-start.24 = (f32[2,2048]{1,0:T(2,128)S(1)}, f32[2,2048]{1,0:T(2,128)S(1)}, u32[]{:S(2)}, u32[]{:S(2)}) collective-permute-start(f32[2,2048]{1,0:T(2,128)S(1)} %get-tuple-element.102), channel_id=1, source_target_pairs={{0,8},{4,12},{8,0},{12,4},{1,9},{5,13},{9,1},{13,5},{2,10},{6,14},... | collective-permute-start | bytes 49160 | tf_op jit(solution)/shard_map/ppermute | solution.py:62
  80.0 3.7 %collective-permute-start.25 = (f32[2,2048]{1,0:T(2,128)S(1)}, f32[2,2048]{1,0:T(2,128)S(1)}, u32[]{:S(2)}, u32[]{:S(2)}) collective-permute-start(f32[2,2048]{1,0:T(2,128)S(1)} %get-tuple-element.102), channel_id=1, source_target_pairs={{0,12},{4,0},{8,4},{12,8},{1,13},{5,1},{9,5},{13,9},{2,14},{6,2},{... | collective-permute-start | bytes 49160 | tf_op jit(solution)/shard_map/ppermute | solution.py:62
  86.6 1.2 %collective-permute-start.26 = (f32[2,2048]{1,0:T(2,128)S(1)}, f32[2,2048]{1,0:T(2,128)S(1)}, u32[]{:S(2)}, u32[]{:S(2)}) collective-permute-start(f32[2,2048]{1,0:T(2,128)S(1)} %pad_maximum_fusion.23), channel_id=1, source_target_pairs={{0,1},{1,0},{2,3},{3,2},{4,5},{5,4},{6,7},{7,6},{8,9},{9,8},{10,11... | collective-permute-start | bytes 49160 | tf_op jit(solution)/shard_map/ppermute | solution.py:43
  87.9 5.6 %collective-permute-start.27 = (f32[2,2048]{1,0:T(2,128)S(1)}, f32[2,2048]{1,0:T(2,128)S(1)}, u32[]{:S(2)}, u32[]{:S(2)}) collective-permute-start(f32[2,2048]{1,0:T(2,128)S(1)} %get-tuple-element.100), channel_id=1, source_target_pairs={{0,4},{4,8},{8,12},{12,0},{1,5},{5,9},{9,13},{13,1},{2,6},{6,10},{... | collective-permute-start | bytes 49160 | tf_op jit(solution)/shard_map/ppermute | solution.py:62
  88.9 4.9 %collective-permute-start.28 = (f32[2,2048]{1,0:T(2,128)S(1)}, f32[2,2048]{1,0:T(2,128)S(1)}, u32[]{:S(2)}, u32[]{:S(2)}) collective-permute-start(f32[2,2048]{1,0:T(2,128)S(1)} %get-tuple-element.100), channel_id=1, source_target_pairs={{0,8},{4,12},{8,0},{12,4},{1,9},{5,13},{9,1},{13,5},{2,10},{6,14},... | collective-permute-start | bytes 49160 | tf_op jit(solution)/shard_map/ppermute | solution.py:62
  90.8 3.7 %collective-permute-start.29 = (f32[2,2048]{1,0:T(2,128)S(1)}, f32[2,2048]{1,0:T(2,128)S(1)}, u32[]{:S(2)}, u32[]{:S(2)}) collective-permute-start(f32[2,2048]{1,0:T(2,128)S(1)} %get-tuple-element.100), channel_id=1, source_target_pairs={{0,12},{4,0},{8,4},{12,8},{1,13},{5,1},{9,5},{13,9},{2,14},{6,2},{... | collective-permute-start | bytes 49160 | tf_op jit(solution)/shard_map/ppermute | solution.py:62
  97.4 1.2 %collective-permute-start.30 = (f32[2,2048]{1,0:T(2,128)S(1)}, f32[2,2048]{1,0:T(2,128)S(1)}, u32[]{:S(2)}, u32[]{:S(2)}) collective-permute-start(f32[2,2048]{1,0:T(2,128)S(1)} %pad_maximum_fusion.25), channel_id=1, source_target_pairs={{0,1},{1,0},{2,3},{3,2},{4,5},{5,4},{6,7},{7,6},{8,9},{9,8},{10,11... | collective-permute-start | bytes 49160 | tf_op jit(solution)/shard_map/ppermute | solution.py:43
  98.7 5.6 %collective-permute-start.31 = (f32[2,2048]{1,0:T(2,128)S(1)}, f32[2,2048]{1,0:T(2,128)S(1)}, u32[]{:S(2)}, u32[]{:S(2)}) collective-permute-start(f32[2,2048]{1,0:T(2,128)S(1)} %get-tuple-element.98), channel_id=1, source_target_pairs={{0,4},{4,8},{8,12},{12,0},{1,5},{5,9},{9,13},{13,1},{2,6},{6,10},{... | collective-permute-start | bytes 49160 | tf_op jit(solution)/shard_map/ppermute | solution.py:62
  100.3 4.8 %collective-permute-start.32 = (f32[2,2048]{1,0:T(2,128)S(1)}, f32[2,2048]{1,0:T(2,128)S(1)}, u32[]{:S(2)}, u32[]{:S(2)}) collective-permute-start(f32[2,2048]{1,0:T(2,128)S(1)} %get-tuple-element.98), channel_id=1, source_target_pairs={{0,8},{4,12},{8,0},{12,4},{1,9},{5,13},{9,1},{13,5},{2,10},{6,14},... | collective-permute-start | bytes 49160 | tf_op jit(solution)/shard_map/ppermute | solution.py:62
  102.1 3.7 %collective-permute-start.33 = (f32[2,2048]{1,0:T(2,128)S(1)}, f32[2,2048]{1,0:T(2,128)S(1)}, u32[]{:S(2)}, u32[]{:S(2)}) collective-permute-start(f32[2,2048]{1,0:T(2,128)S(1)} %get-tuple-element.98), channel_id=1, source_target_pairs={{0,12},{4,0},{8,4},{12,8},{1,13},{5,1},{9,5},{13,9},{2,14},{6,2},{... | collective-permute-start | bytes 49160 | tf_op jit(solution)/shard_map/ppermute | solution.py:62
  107.5 1.9 %copy-start.4 = (f32[256]{0:T(256)}, f32[256]{0:T(256)S(1)}, u32[]{:S(2)}) copy-start(f32[256]{0:T(256)S(1)} %add_multiply_fusion.8) | copy-start | bytes 3076
  109.5 1.4 %collective-permute-start.34 = (f32[4,128,66]{1,0,2:T(4,128)S(1)}, f32[4,128,66]{1,0,2:T(4,128)S(1)}, u32[]{:S(2)}, u32[]{:S(2)}) collective-permute-start(f32[4,128,66]{1,0,2:T(4,128)S(1)} %pad_maximum_fusion.3), channel_id=1, source_target_pairs={{0,1},{1,0},{2,3},{3,2},{4,5},{5,4},{6,7},{7,6},{8,9},{9,8},{10,11... | collective-permute-start | bytes 405512 | tf_op jit(solution)/shard_map/ppermute | solution.py:92
  111.2 6.1 %collective-permute-start.35 = (f32[128,66]{0,1:T(8,128)S(1)}, f32[128,66]{0,1:T(8,128)S(1)}, u32[]{:S(2)}, u32[]{:S(2)}) collective-permute-start(f32[128,66]{0,1:T(8,128)S(1)} %bitcast.232), channel_id=1, source_target_pairs={{0,4},{4,8},{8,12},{12,0},{1,5},{5,9},{9,13},{13,1},{2,6},{6,10},{... | collective-permute-start | bytes 101384 | tf_op jit(solution)/shard_map/ppermute | solution.py:142
  112.3 5.9 %collective-permute-start.36 = (f32[128,66]{0,1:T(8,128)S(1)}, f32[128,66]{0,1:T(8,128)S(1)}, u32[]{:S(2)}, u32[]{:S(2)}) collective-permute-start(f32[128,66]{0,1:T(8,128)S(1)} %bitcast.233), channel_id=1, source_target_pairs={{0,8},{4,12},{8,0},{12,4},{1,9},{5,13},{9,1},{13,5},{2,10},{6,14},... | collective-permute-start | bytes 101384 | tf_op jit(solution)/shard_map/ppermute | solution.py:142
  114.3 4.2 %collective-permute-start.37 = (f32[128,66]{0,1:T(8,128)S(1)}, f32[128,66]{0,1:T(8,128)S(1)}, u32[]{:S(2)}, u32[]{:S(2)}) collective-permute-start(f32[128,66]{0,1:T(8,128)S(1)} %bitcast.234), channel_id=1, source_target_pairs={{0,12},{4,0},{8,4},{12,8},{1,13},{5,1},{9,5},{13,9},{2,14},{6,2},{... | collective-permute-start | bytes 101384 | tf_op jit(solution)/shard_map/ppermute | solution.py:142

commit v6 on v4

--- a/solution.py
+++ b/solution.py
@@ -154,9 +154,12 @@
     return top, totals, weighted
 
 
-def fate_pullback(cost, log_b, g_pot, fate_panel):
+def fate_pullback(cost, log_b, g_pot, fate_panel, scaled=False):
     src_count = cost.shape[0]
-    scores = log_b[None, :] + (g_pot[None, :] - cost) / entropic
+    if scaled:
+        scores = (log_b + g_pot / entropic)[None, :] - cost
+    else:
+        scores = log_b[None, :] + (g_pot[None, :] - cost) / entropic
     maxima = jnp.max(scores, axis=1)
     weights = jnp.exp(scores - maxima[:, None])
     totals = jnp.sum(weights, axis=1)
@@ -209,6 +212,15 @@
 ROW_AXES = (("rep",), ("cols",))
 
 
+def row_reduce(maxima, totals):
+    for axes in ROW_AXES:
+        if len(axes) == 1 and lax.axis_size(axes[0]) == 2:
+            maxima, totals = lse_allreduce(maxima, totals, axes)
+        else:
+            maxima, totals = lse_exchange(maxima, totals, axes)
+    return maxima, totals
+
+
 def body(sources, source_mass, targets, target_mass, fate_panel):
     row_count = lax.axis_size("rows")
     if row_count != 2 or lax.axis_size("cols") > 8:
@@ -231,27 +243,24 @@
     tgt_sq = jnp.sum(targets * targets, axis=1)
     cost = pair_cost(all_src, src_sq, targets, tgt_sq)
 
+    scaled = cost / entropic
     g_pot = jnp.zeros((tgt_count,), jnp.float32)
     f_all = jnp.zeros((all_sources,), jnp.float32)
     for iteration in range(ITERS):
-        scores = log_b[None, :] + (g_pot[None, :] - cost) / entropic
+        scores = (log_b + g_pot / entropic)[None, :] - scaled
         maxima = jnp.max(scores, axis=1)
         totals = jnp.sum(jnp.exp(scores - maxima[:, None]), axis=1)
-        for axes in ROW_AXES:
-            if len(axes) == 1 and lax.axis_size(axes[0]) == 2:
-                maxima, totals = lse_allreduce(maxima, totals, axes)
-            else:
-                maxima, totals = lse_exchange(maxima, totals, axes)
+        maxima, totals = row_reduce(maxima, totals)
         f_all = -relaxed * entropic * (maxima + jnp.log(totals))
 
-        scores = log_a[:, None] + (f_all[:, None] - cost) / entropic
+        scores = (log_a + f_all / entropic)[:, None] - scaled
         maxima = jnp.max(scores, axis=0)
         totals = jnp.sum(jnp.exp(scores - maxima[None, :]), axis=0)
         g_pot = -relaxed * entropic * (maxima + jnp.log(totals))
 
     f_pot = lax.dynamic_slice_in_dim(f_all, row * src_count, src_count)
-    cost_mine = lax.dynamic_slice_in_dim(cost, row * src_count, src_count, axis=0)
-    return (f_pot,) + fate_pullback(cost_mine, log_b, g_pot, fate_panel)
+    scaled_mine = lax.dynamic_slice_in_dim(scaled, row * src_count, src_count, axis=0)
+    return (f_pot,) + fate_pullback(scaled_mine, log_b, g_pot, fate_panel, scaled=True)
 
 
 def solution(mesh):

time: 112 us -> 108 us (0.964)
  other arithmetic: 20.8 us -> 18.7 us
  starting transfers between devices: 43.1 us -> 41.7 us
  local copies, waits for them, and re-layouts: 1.61 us -> 0.45 us
    ppermute x24, starting transfers between devices: 35.6 us -> 33.9 us  [lse_exchange(): received.append(lax.ppermute(payload, axes, perm))]
    add x0 -> x16, other arithmetic: none -> 1.52 us  [the longest x8 0.86 us: body(): scores = (log_a + f_all / entropic)[:, None] - scaled]
  transfers between devices with their start and end apart: 37 -> 37, of which waited for: 35 -> 34; matrix products, arithmetic and copies ran while one was open for 2% -> 2% of each run, Pallas kernels for 0% -> 0%
where the time goes in v6:
time: 108 us; the launch traced here: 107 us
  waiting for transfers between devices  41.9 us (39%)
  starting transfers between devices  41.7 us (39%)
  other arithmetic  18.7 us (17%)
  matrix products  3.19 us (3%)
  between operations  1.29 us (1%)
    ppermute x24, starting transfers between devices, lse_exchange(): received.append(lax.ppermute(payload, axes, perm))  33.9 us
    ppermute x24, waiting for transfers between devices, lse_exchange(): received.append(lax.ppermute(payload, axes, perm))  23.3 us
    ppermute x8, waiting for transfers between devices, lse_allreduce(): other = lax.ppermute(jnp.stack([maxima, totals]), name, perm)  9.36 us
    ppermute x1, waiting for transfers between devices, body(): theirs = lax.ppermute(mine, 'rows', [(0, 1), (1, 0)])  5.46 us
    ppermute x3, starting transfers between devices, lse_scatter_exchange(): parts.append(lax.ppermute(send, name, perm))  4.1 us
    reduce_sum x8, other arithmetic, body(): totals = jnp.sum(jnp.exp(scores - maxima[None, :]), axis=0)  3.98 us
    reduce_sum x8, other arithmetic, body(): totals = jnp.sum(jnp.exp(scores - maxima[:, None]), axis=1)  3.37 us
    ppermute x1, starting transfers between devices, body(): theirs = lax.ppermute(mine, 'rows', [(0, 1), (1, 0)])  3.03 us
  transfers between devices with their start and end apart: 37, of which 34 were waited for; matrix products, arithmetic and copies ran while one was open for 2% of the time, Pallas kernels for 0%

profile of v6, /device:TPU:0, one launch (start us, length us, event | category | flops | bytes accessed | tf_op | source)
XLA Modules:
  0.0 107.3 jit_solution(10294518714645645334)
XLA Ops:
  0.7 1.0 pad_maximum_fusion.2
  1.7 3.0 %collective-permute-start = (f32[1024,65]{0,1:T(8,128)S(1)}, f32[1024,65]{0,1:T(8,128)S(1)}, u32[]{:S(2)}, u32[]{:S(2)}) collective-permute-start(f32[1024,65]{0,1:T(8,128)S(1)} %pad_maximum_fusion.2), channel_id=1, source_target_pairs={{0,2},{2,0},{1,3},{3,1},{4,6},{6,4},{5,7},{7,5},{8,10},{10,8},{9,1... | collective-permute-start | bytes 798728 | tf_op jit(solution)/shard_map/ppermute | solution.py:232
  6.3 5.5 %collective-permute-done = f32[1024,65]{0,1:T(8,128)S(1)} collective-permute-done((f32[1024,65]{0,1:T(8,128)S(1)}, f32[1024,65]{0,1:T(8,128)S(1)}, u32[]{:S(2)}, u32[]{:S(2)}) %collective-permute-start) | collective-permute-done | bytes 266272 | tf_op jit(solution)/shard_map/ppermute | solution.py:232
  11.7 1.0 broadcast_select_fusion.1
  12.8 2.2 %subtract_reduce_fusion.15 = (f32[2048]{0:T(1024)S(1)}, f32[2048,256]{0,1:T(8,128)S(1)}) fusion(f32[256]{0:T(256)S(1)} %multiply_log_fusion, f32[256,64]{0,1:T(8,128)S(1)} %copy-done.2, f32[1024,65]{0,1:T(8,128)S(1)} %get-tuple-element.21, f32[1024,65]{0,1:T(8,128)S(1)} %get-tuple-element.20, f32[256]{0:T(256)S(1)} %multiply_reduce_fusion.1, ...), kind=kOutput, calls=%fused_computation.34 | convolution fusion | flops 405927936 | bytes 2713600 | tf_op jit(solution)/shard_map/dot_general | solution.py:14
  15.6 1.2 %collective-permute-done.1 = f32[2,2048]{1,0:T(2,128)S(1)} collective-permute-done((f32[2,2048]{1,0:T(2,128)S(1)}, f32[2,2048]{1,0:T(2,128)S(1)}, u32[]{:S(2)}, u32[]{:S(2)}) %collective-permute-start.1) | collective-permute-done | bytes 16416 | tf_op jit(solution)/shard_map/ppermute | solution.py:43
  16.8 1.9 %collective-permute-start.2 = (f32[2,2048]{1,0:T(2,128)S(1)}, f32[2,2048]{1,0:T(2,128)S(1)}, u32[]{:S(2)}, u32[]{:S(2)}) collective-permute-start(f32[2,2048]{1,0:T(2,128)S(1)} %get-tuple-element.63), channel_id=1, source_target_pairs={{0,4},{4,8},{8,12},{12,0},{1,5},{5,9},{9,13},{13,1},{2,6},{6,10},{... | collective-permute-start | bytes 49160 | tf_op jit(solution)/shard_map/ppermute | solution.py:62
  18.7 2.6 %collective-permute-start.3 = (f32[2,2048]{1,0:T(2,128)S(1)}, f32[2,2048]{1,0:T(2,128)S(1)}, u32[]{:S(2)}, u32[]{:S(2)}) collective-permute-start(f32[2,2048]{1,0:T(2,128)S(1)} %get-tuple-element.63), channel_id=1, source_target_pairs={{0,8},{4,12},{8,0},{12,4},{1,9},{5,13},{9,1},{13,5},{2,10},{6,14},... | collective-permute-start | bytes 49160 | tf_op jit(solution)/shard_map/ppermute | solution.py:62
  21.3 1.3 %collective-permute-start.4 = (f32[2,2048]{1,0:T(2,128)S(1)}, f32[2,2048]{1,0:T(2,128)S(1)}, u32[]{:S(2)}, u32[]{:S(2)}) collective-permute-start(f32[2,2048]{1,0:T(2,128)S(1)} %get-tuple-element.63), channel_id=1, source_target_pairs={{0,12},{4,0},{8,4},{12,8},{1,13},{5,1},{9,5},{13,9},{2,14},{6,2},{... | collective-permute-start | bytes 49160 | tf_op jit(solution)/shard_map/ppermute | solution.py:62
  22.6 1.0 collective-permute-done.3
  23.6 1.4 %collective-permute-done.4 = f32[2,2048]{1,0:T(2,128)S(1)} collective-permute-done((f32[2,2048]{1,0:T(2,128)S(1)}, f32[2,2048]{1,0:T(2,128)S(1)}, u32[]{:S(2)}, u32[]{:S(2)}) %collective-permute-start.4) | collective-permute-done | bytes 16416 | tf_op jit(solution)/shard_map/ppermute | solution.py:62
  26.7 1.2 %collective-permute-done.5 = f32[2,2048]{1,0:T(2,128)S(1)} collective-permute-done((f32[2,2048]{1,0:T(2,128)S(1)}, f32[2,2048]{1,0:T(2,128)S(1)}, u32[]{:S(2)}, u32[]{:S(2)}) %collective-permute-start.5) | collective-permute-done | bytes 16416 | tf_op jit(solution)/shard_map/ppermute | solution.py:43
  28.1 3.6 %collective-permute-start.7 = (f32[2,2048]{1,0:T(2,128)S(1)}, f32[2,2048]{1,0:T(2,128)S(1)}, u32[]{:S(2)}, u32[]{:S(2)}) collective-permute-start(f32[2,2048]{1,0:T(2,128)S(1)} %get-tuple-element.61), channel_id=1, source_target_pairs={{0,8},{4,12},{8,0},{12,4},{1,9},{5,13},{9,1},{13,5},{2,10},{6,14},... | collective-permute-start | bytes 49160 | tf_op jit(solution)/shard_map/ppermute | solution.py:62
  32.0 1.6 %collective-permute-done.6 = f32[2,2048]{1,0:T(2,128)S(1)} collective-permute-done((f32[2,2048]{1,0:T(2,128)S(1)}, f32[2,2048]{1,0:T(2,128)S(1)}, u32[]{:S(2)}, u32[]{:S(2)}) %collective-permute-start.6) | collective-permute-done | bytes 16416 | tf_op jit(solution)/shard_map/ppermute | solution.py:62
  33.7 1.7 %collective-permute-done.8 = f32[2,2048]{1,0:T(2,128)S(1)} collective-permute-done((f32[2,2048]{1,0:T(2,128)S(1)}, f32[2,2048]{1,0:T(2,128)S(1)}, u32[]{:S(2)}, u32[]{:S(2)}) %collective-permute-start.8) | collective-permute-done | bytes 16416 | tf_op jit(solution)/shard_map/ppermute | solution.py:62
  37.1 1.2 %collective-permute-done.9 = f32[2,2048]{1,0:T(2,128)S(1)} collective-permute-done((f32[2,2048]{1,0:T(2,128)S(1)}, f32[2,2048]{1,0:T(2,128)S(1)}, u32[]{:S(2)}, u32[]{:S(2)}) %collective-permute-start.9) | collective-permute-done | bytes 16416 | tf_op jit(solution)/shard_map/ppermute | solution.py:43
  39.1 2.0 %collective-permute-start.11 = (f32[2,2048]{1,0:T(2,128)S(1)}, f32[2,2048]{1,0:T(2,128)S(1)}, u32[]{:S(2)}, u32[]{:S(2)}) collective-permute-start(f32[2,2048]{1,0:T(2,128)S(1)} %get-tuple-element.59), channel_id=1, source_target_pairs={{0,8},{4,12},{8,0},{12,4},{1,9},{5,13},{9,1},{13,5},{2,10},{6,14},... | collective-permute-start | bytes 49160 | tf_op jit(solution)/shard_map/ppermute | solution.py:62
  41.0 1.2 %collective-permute-start.12 = (f32[2,2048]{1,0:T(2,128)S(1)}, f32[2,2048]{1,0:T(2,128)S(1)}, u32[]{:S(2)}, u32[]{:S(2)}) collective-permute-start(f32[2,2048]{1,0:T(2,128)S(1)} %get-tuple-element.59), channel_id=1, source_target_pairs={{0,12},{4,0},{8,4},{12,8},{1,13},{5,1},{9,5},{13,9},{2,14},{6,2},{... | collective-permute-start | bytes 49160 | tf_op jit(solution)/shard_map/ppermute | solution.py:62
  42.2 1.8 %collective-permute-done.10 = f32[2,2048]{1,0:T(2,128)S(1)} collective-permute-done((f32[2,2048]{1,0:T(2,128)S(1)}, f32[2,2048]{1,0:T(2,128)S(1)}, u32[]{:S(2)}, u32[]{:S(2)}) %collective-permute-start.10) | collective-permute-done | bytes 16416 | tf_op jit(solution)/shard_map/ppermute | solution.py:62
  46.4 1.2 %collective-permute-done.13 = f32[2,2048]{1,0:T(2,128)S(1)} collective-permute-done((f32[2,2048]{1,0:T(2,128)S(1)}, f32[2,2048]{1,0:T(2,128)S(1)}, u32[]{:S(2)}, u32[]{:S(2)}) %collective-permute-start.13) | collective-permute-done | bytes 16416 | tf_op jit(solution)/shard_map/ppermute | solution.py:43
  47.7 1.8 %collective-permute-start.14 = (f32[2,2048]{1,0:T(2,128)S(1)}, f32[2,2048]{1,0:T(2,128)S(1)}, u32[]{:S(2)}, u32[]{:S(2)}) collective-permute-start(f32[2,2048]{1,0:T(2,128)S(1)} %get-tuple-element.57), channel_id=1, source_target_pairs={{0,4},{4,8},{8,12},{12,0},{1,5},{5,9},{9,13},{13,1},{2,6},{6,10},{... | collective-permute-start | bytes 49160 | tf_op jit(solution)/shard_map/ppermute | solution.py:62
  49.5 1.8 %collective-permute-start.15 = (f32[2,2048]{1,0:T(2,128)S(1)}, f32[2,2048]{1,0:T(2,128)S(1)}, u32[]{:S(2)}, u32[]{:S(2)}) collective-permute-start(f32[2,2048]{1,0:T(2,128)S(1)} %get-tuple-element.57), channel_id=1, source_target_pairs={{0,8},{4,12},{8,0},{12,4},{1,9},{5,13},{9,1},{13,5},{2,10},{6,14},... | collective-permute-start | bytes 49160 | tf_op jit(solution)/shard_map/ppermute | solution.py:62
  51.9 1.3 %collective-permute-done.14 = f32[2,2048]{1,0:T(2,128)S(1)} collective-permute-done((f32[2,2048]{1,0:T(2,128)S(1)}, f32[2,2048]{1,0:T(2,128)S(1)}, u32[]{:S(2)}, u32[]{:S(2)}) %collective-permute-start.14) | collective-permute-done | bytes 16416 | tf_op jit(solution)/shard_map/ppermute | solution.py:62
  56.7 1.2 %collective-permute-done.17 = f32[2,2048]{1,0:T(2,128)S(1)} collective-permute-done((f32[2,2048]{1,0:T(2,128)S(1)}, f32[2,2048]{1,0:T(2,128)S(1)}, u32[]{:S(2)}, u32[]{:S(2)}) %collective-permute-start.17) | collective-permute-done | bytes 16416 | tf_op jit(solution)/shard_map/ppermute | solution.py:43
  58.8 2.2 %collective-permute-start.19 = (f32[2,2048]{1,0:T(2,128)S(1)}, f32[2,2048]{1,0:T(2,128)S(1)}, u32[]{:S(2)}, u32[]{:S(2)}) collective-permute-start(f32[2,2048]{1,0:T(2,128)S(1)} %get-tuple-element.55), channel_id=1, source_target_pairs={{0,8},{4,12},{8,0},{12,4},{1,9},{5,13},{9,1},{13,5},{2,10},{6,14},... | collective-permute-start | bytes 49160 | tf_op jit(solution)/shard_map/ppermute | solution.py:62
  61.0 1.0 collective-permute-start.20
  62.0 1.7 %collective-permute-done.18 = f32[2,2048]{1,0:T(2,128)S(1)} collective-permute-done((f32[2,2048]{1,0:T(2,128)S(1)}, f32[2,2048]{1,0:T(2,128)S(1)}, u32[]{:S(2)}, u32[]{:S(2)}) %collective-permute-start.18) | collective-permute-done | bytes 16416 | tf_op jit(solution)/shard_map/ppermute | solution.py:62
  63.7 1.0 collective-permute-done.20
  66.4 1.2 %collective-permute-done.21 = f32[2,2048]{1,0:T(2,128)S(1)} collective-permute-done((f32[2,2048]{1,0:T(2,128)S(1)}, f32[2,2048]{1,0:T(2,128)S(1)}, u32[]{:S(2)}, u32[]{:S(2)}) %collective-permute-start.21) | collective-permute-done | bytes 16416 | tf_op jit(solution)/shard_map/ppermute | solution.py:43
  67.6 1.4 %collective-permute-start.22 = (f32[2,2048]{1,0:T(2,128)S(1)}, f32[2,2048]{1,0:T(2,128)S(1)}, u32[]{:S(2)}, u32[]{:S(2)}) collective-permute-start(f32[2,2048]{1,0:T(2,128)S(1)} %get-tuple-element.53), channel_id=1, source_target_pairs={{0,4},{4,8},{8,12},{12,0},{1,5},{5,9},{9,13},{13,1},{2,6},{6,10},{... | collective-permute-start | bytes 49160 | tf_op jit(solution)/shard_map/ppermute | solution.py:62
  69.1 2.0 %collective-permute-start.23 = (f32[2,2048]{1,0:T(2,128)S(1)}, f32[2,2048]{1,0:T(2,128)S(1)}, u32[]{:S(2)}, u32[]{:S(2)}) collective-permute-start(f32[2,2048]{1,0:T(2,128)S(1)} %get-tuple-element.53), channel_id=1, source_target_pairs={{0,8},{4,12},{8,0},{12,4},{1,9},{5,13},{9,1},{13,5},{2,10},{6,14},... | collective-permute-start | bytes 49160 | tf_op jit(solution)/shard_map/ppermute | solution.py:62
  71.6 1.6 %collective-permute-done.22 = f32[2,2048]{1,0:T(2,128)S(1)} collective-permute-done((f32[2,2048]{1,0:T(2,128)S(1)}, f32[2,2048]{1,0:T(2,128)S(1)}, u32[]{:S(2)}, u32[]{:S(2)}) %collective-permute-start.22) | collective-permute-done | bytes 16416 | tf_op jit(solution)/shard_map/ppermute | solution.py:62
  73.7 1.1 %collective-permute-done.24 = f32[2,2048]{1,0:T(2,128)S(1)} collective-permute-done((f32[2,2048]{1,0:T(2,128)S(1)}, f32[2,2048]{1,0:T(2,128)S(1)}, u32[]{:S(2)}, u32[]{:S(2)}) %collective-permute-start.24) | collective-permute-done | bytes 16416 | tf_op jit(solution)/shard_map/ppermute | solution.py:62
  76.5 1.2 %collective-permute-done.25 = f32[2,2048]{1,0:T(2,128)S(1)} collective-permute-done((f32[2,2048]{1,0:T(2,128)S(1)}, f32[2,2048]{1,0:T(2,128)S(1)}, u32[]{:S(2)}, u32[]{:S(2)}) %collective-permute-start.25) | collective-permute-done | bytes 16416 | tf_op jit(solution)/shard_map/ppermute | solution.py:43
  77.7 1.0 collective-permute-start.26
  78.8 1.9 %collective-permute-start.27 = (f32[2,2048]{1,0:T(2,128)S(1)}, f32[2,2048]{1,0:T(2,128)S(1)}, u32[]{:S(2)}, u32[]{:S(2)}) collective-permute-start(f32[2,2048]{1,0:T(2,128)S(1)} %get-tuple-element.51), channel_id=1, source_target_pairs={{0,8},{4,12},{8,0},{12,4},{1,9},{5,13},{9,1},{13,5},{2,10},{6,14},... | collective-permute-start | bytes 49160 | tf_op jit(solution)/shard_map/ppermute | solution.py:62
  81.6 1.7 %collective-permute-done.26 = f32[2,2048]{1,0:T(2,128)S(1)} collective-permute-done((f32[2,2048]{1,0:T(2,128)S(1)}, f32[2,2048]{1,0:T(2,128)S(1)}, u32[]{:S(2)}, u32[]{:S(2)}) %collective-permute-start.26) | collective-permute-done | bytes 16416 | tf_op jit(solution)/shard_map/ppermute | solution.py:62
  86.1 1.2 %collective-permute-done.29 = f32[2,2048]{1,0:T(2,128)S(1)} collective-permute-done((f32[2,2048]{1,0:T(2,128)S(1)}, f32[2,2048]{1,0:T(2,128)S(1)}, u32[]{:S(2)}, u32[]{:S(2)}) %collective-permute-start.29) | collective-permute-done | bytes 16416 | tf_op jit(solution)/shard_map/ppermute | solution.py:43
  87.3 1.6 %collective-permute-start.30 = (f32[2,2048]{1,0:T(2,128)S(1)}, f32[2,2048]{1,0:T(2,128)S(1)}, u32[]{:S(2)}, u32[]{:S(2)}) collective-permute-start(f32[2,2048]{1,0:T(2,128)S(1)} %get-tuple-element.49), channel_id=1, source_target_pairs={{0,4},{4,8},{8,12},{12,0},{1,5},{5,9},{9,13},{13,1},{2,6},{6,10},{... | collective-permute-start | bytes 49160 | tf_op jit(solution)/shard_map/ppermute | solution.py:62
  88.9 1.8 %collective-permute-start.31 = (f32[2,2048]{1,0:T(2,128)S(1)}, f32[2,2048]{1,0:T(2,128)S(1)}, u32[]{:S(2)}, u32[]{:S(2)}) collective-permute-start(f32[2,2048]{1,0:T(2,128)S(1)} %get-tuple-element.49), channel_id=1, source_target_pairs={{0,8},{4,12},{8,0},{12,4},{1,9},{5,13},{9,1},{13,5},{2,10},{6,14},... | collective-permute-start | bytes 49160 | tf_op jit(solution)/shard_map/ppermute | solution.py:62
  91.3 1.6 %collective-permute-done.30 = f32[2,2048]{1,0:T(2,128)S(1)} collective-permute-done((f32[2,2048]{1,0:T(2,128)S(1)}, f32[2,2048]{1,0:T(2,128)S(1)}, u32[]{:S(2)}, u32[]{:S(2)}) %collective-permute-start.30) | collective-permute-done | bytes 16416 | tf_op jit(solution)/shard_map/ppermute | solution.py:62
  96.3 1.0 fusion.3
  97.8 1.3 %collective-permute-done.33 = f32[4,128,66]{1,0,2:T(4,128)S(1)} collective-permute-done((f32[4,128,66]{1,0,2:T(4,128)S(1)}, f32[4,128,66]{1,0,2:T(4,128)S(1)}, u32[]{:S(2)}, u32[]{:S(2)}) %collective-permute-start.33) | collective-permute-done | bytes 135200 | tf_op jit(solution)/shard_map/ppermute | solution.py:92
  99.4 1.1 %collective-permute-start.34 = (f32[128,66]{0,1:T(8,128)S(1)}, f32[128,66]{0,1:T(8,128)S(1)}, u32[]{:S(2)}, u32[]{:S(2)}) collective-permute-start(f32[128,66]{0,1:T(8,128)S(1)} %bitcast.617), channel_id=1, source_target_pairs={{0,4},{4,8},{8,12},{12,0},{1,5},{5,9},{9,13},{13,1},{2,6},{6,10},{... | collective-permute-start | bytes 101384 | tf_op jit(solution)/shard_map/ppermute | solution.py:142
  100.5 1.9 %collective-permute-start.35 = (f32[128,66]{0,1:T(8,128)S(1)}, f32[128,66]{0,1:T(8,128)S(1)}, u32[]{:S(2)}, u32[]{:S(2)}) collective-permute-start(f32[128,66]{0,1:T(8,128)S(1)} %bitcast.618), channel_id=1, source_target_pairs={{0,8},{4,12},{8,0},{12,4},{1,9},{5,13},{9,1},{13,5},{2,10},{6,14},... | collective-permute-start | bytes 101384 | tf_op jit(solution)/shard_map/ppermute | solution.py:142
  102.5 1.0 collective-permute-start.36
  104.1 1.3 %collective-permute-done.34 = f32[128,66]{0,1:T(8,128)S(1)} collective-permute-done((f32[128,66]{0,1:T(8,128)S(1)}, f32[128,66]{0,1:T(8,128)S(1)}, u32[]{:S(2)}, u32[]{:S(2)}) %collective-permute-start.34) | collective-permute-done | bytes 33824 | tf_op jit(solution)/shard_map/ppermute | solution.py:142
  105.5 1.0 collective-permute-done.35
  (142 shorter events, 28.6 us)
Async XLA Ops:
  0.6 95.6 %copy-start = (f32[256,64]{0,1:T(8,128)S(1)}, f32[256,64]{0,1:T(8,128)}, u32[]{:S(2)}) copy-start(f32[256,64]{0,1:T(8,128)} %param.9) | copy-start | bytes 196612
  0.6 12.2 %copy-start.2 = (f32[256,64]{0,1:T(8,128)S(1)}, f32[256,64]{0,1:T(8,128)}, u32[]{:S(2)}) copy-start(f32[256,64]{0,1:T(8,128)} %param.7) | copy-start | bytes 196612
  1.7 10.0 %collective-permute-start = (f32[1024,65]{0,1:T(8,128)S(1)}, f32[1024,65]{0,1:T(8,128)S(1)}, u32[]{:S(2)}, u32[]{:S(2)}) collective-permute-start(f32[1024,65]{0,1:T(8,128)S(1)} %pad_maximum_fusion.2), channel_id=1, source_target_pairs={{0,2},{2,0},{1,3},{3,1},{4,6},{6,4},{5,7},{7,5},{8,10},{10,8},{9,1... | collective-permute-start | bytes 798728 | tf_op jit(solution)/shard_map/ppermute | solution.py:232
  15.5 1.2 %collective-permute-start.1 = (f32[2,2048]{1,0:T(2,128)S(1)}, f32[2,2048]{1,0:T(2,128)S(1)}, u32[]{:S(2)}, u32[]{:S(2)}) collective-permute-start(f32[2,2048]{1,0:T(2,128)S(1)} %pad_maximum_fusion.13), channel_id=1, source_target_pairs={{0,1},{1,0},{2,3},{3,2},{4,5},{5,4},{6,7},{7,6},{8,9},{9,8},{10,11... | collective-permute-start | bytes 49160 | tf_op jit(solution)/shard_map/ppermute | solution.py:43
  16.8 5.8 %collective-permute-start.2 = (f32[2,2048]{1,0:T(2,128)S(1)}, f32[2,2048]{1,0:T(2,128)S(1)}, u32[]{:S(2)}, u32[]{:S(2)}) collective-permute-start(f32[2,2048]{1,0:T(2,128)S(1)} %get-tuple-element.63), channel_id=1, source_target_pairs={{0,4},{4,8},{8,12},{12,0},{1,5},{5,9},{9,13},{13,1},{2,6},{6,10},{... | collective-permute-start | bytes 49160 | tf_op jit(solution)/shard_map/ppermute | solution.py:62
  18.7 4.9 %collective-permute-start.3 = (f32[2,2048]{1,0:T(2,128)S(1)}, f32[2,2048]{1,0:T(2,128)S(1)}, u32[]{:S(2)}, u32[]{:S(2)}) collective-permute-start(f32[2,2048]{1,0:T(2,128)S(1)} %get-tuple-element.63), channel_id=1, source_target_pairs={{0,8},{4,12},{8,0},{12,4},{1,9},{5,13},{9,1},{13,5},{2,10},{6,14},... | collective-permute-start | bytes 49160 | tf_op jit(solution)/shard_map/ppermute | solution.py:62
  21.3 3.7 %collective-permute-start.4 = (f32[2,2048]{1,0:T(2,128)S(1)}, f32[2,2048]{1,0:T(2,128)S(1)}, u32[]{:S(2)}, u32[]{:S(2)}) collective-permute-start(f32[2,2048]{1,0:T(2,128)S(1)} %get-tuple-element.63), channel_id=1, source_target_pairs={{0,12},{4,0},{8,4},{12,8},{1,13},{5,1},{9,5},{13,9},{2,14},{6,2},{... | collective-permute-start | bytes 49160 | tf_op jit(solution)/shard_map/ppermute | solution.py:62
  25.2 0.7 copy-start.1
  26.6 1.2 %collective-permute-start.5 = (f32[2,2048]{1,0:T(2,128)S(1)}, f32[2,2048]{1,0:T(2,128)S(1)}, u32[]{:S(2)}, u32[]{:S(2)}) collective-permute-start(f32[2,2048]{1,0:T(2,128)S(1)} %pad_maximum_fusion.15), channel_id=1, source_target_pairs={{0,1},{1,0},{2,3},{3,2},{4,5},{5,4},{6,7},{7,6},{8,9},{9,8},{10,11... | collective-permute-start | bytes 49160 | tf_op jit(solution)/shard_map/ppermute | solution.py:43
  27.9 5.6 %collective-permute-start.6 = (f32[2,2048]{1,0:T(2,128)S(1)}, f32[2,2048]{1,0:T(2,128)S(1)}, u32[]{:S(2)}, u32[]{:S(2)}) collective-permute-start(f32[2,2048]{1,0:T(2,128)S(1)} %get-tuple-element.61), channel_id=1, source_target_pairs={{0,4},{4,8},{8,12},{12,0},{1,5},{5,9},{9,13},{13,1},{2,6},{6,10},{... | collective-permute-start | bytes 49160 | tf_op jit(solution)/shard_map/ppermute | solution.py:62
  28.1 5.7 %collective-permute-start.7 = (f32[2,2048]{1,0:T(2,128)S(1)}, f32[2,2048]{1,0:T(2,128)S(1)}, u32[]{:S(2)}, u32[]{:S(2)}) collective-permute-start(f32[2,2048]{1,0:T(2,128)S(1)} %get-tuple-element.61), channel_id=1, source_target_pairs={{0,8},{4,12},{8,0},{12,4},{1,9},{5,13},{9,1},{13,5},{2,10},{6,14},... | collective-permute-start | bytes 49160 | tf_op jit(solution)/shard_map/ppermute | solution.py:62
  31.7 3.7 %collective-permute-start.8 = (f32[2,2048]{1,0:T(2,128)S(1)}, f32[2,2048]{1,0:T(2,128)S(1)}, u32[]{:S(2)}, u32[]{:S(2)}) collective-permute-start(f32[2,2048]{1,0:T(2,128)S(1)} %get-tuple-element.61), channel_id=1, source_target_pairs={{0,12},{4,0},{8,4},{12,8},{1,13},{5,1},{9,5},{13,9},{2,14},{6,2},{... | collective-permute-start | bytes 49160 | tf_op jit(solution)/shard_map/ppermute | solution.py:62
  37.0 1.2 %collective-permute-start.9 = (f32[2,2048]{1,0:T(2,128)S(1)}, f32[2,2048]{1,0:T(2,128)S(1)}, u32[]{:S(2)}, u32[]{:S(2)}) collective-permute-start(f32[2,2048]{1,0:T(2,128)S(1)} %pad_maximum_fusion.17), channel_id=1, source_target_pairs={{0,1},{1,0},{2,3},{3,2},{4,5},{5,4},{6,7},{7,6},{8,9},{9,8},{10,11... | collective-permute-start | bytes 49160 | tf_op jit(solution)/shard_map/ppermute | solution.py:43
  38.3 5.6 %collective-permute-start.10 = (f32[2,2048]{1,0:T(2,128)S(1)}, f32[2,2048]{1,0:T(2,128)S(1)}, u32[]{:S(2)}, u32[]{:S(2)}) collective-permute-start(f32[2,2048]{1,0:T(2,128)S(1)} %get-tuple-element.59), channel_id=1, source_target_pairs={{0,4},{4,8},{8,12},{12,0},{1,5},{5,9},{9,13},{13,1},{2,6},{6,10},{... | collective-permute-start | bytes 49160 | tf_op jit(solution)/shard_map/ppermute | solution.py:62
  39.1 4.9 %collective-permute-start.11 = (f32[2,2048]{1,0:T(2,128)S(1)}, f32[2,2048]{1,0:T(2,128)S(1)}, u32[]{:S(2)}, u32[]{:S(2)}) collective-permute-start(f32[2,2048]{1,0:T(2,128)S(1)} %get-tuple-element.59), channel_id=1, source_target_pairs={{0,8},{4,12},{8,0},{12,4},{1,9},{5,13},{9,1},{13,5},{2,10},{6,14},... | collective-permute-start | bytes 49160 | tf_op jit(solution)/shard_map/ppermute | solution.py:62
  41.0 3.7 %collective-permute-start.12 = (f32[2,2048]{1,0:T(2,128)S(1)}, f32[2,2048]{1,0:T(2,128)S(1)}, u32[]{:S(2)}, u32[]{:S(2)}) collective-permute-start(f32[2,2048]{1,0:T(2,128)S(1)} %get-tuple-element.59), channel_id=1, source_target_pairs={{0,12},{4,0},{8,4},{12,8},{1,13},{5,1},{9,5},{13,9},{2,14},{6,2},{... | collective-permute-start | bytes 49160 | tf_op jit(solution)/shard_map/ppermute | solution.py:62
  46.4 1.2 %collective-permute-start.13 = (f32[2,2048]{1,0:T(2,128)S(1)}, f32[2,2048]{1,0:T(2,128)S(1)}, u32[]{:S(2)}, u32[]{:S(2)}) collective-permute-start(f32[2,2048]{1,0:T(2,128)S(1)} %pad_maximum_fusion.19), channel_id=1, source_target_pairs={{0,1},{1,0},{2,3},{3,2},{4,5},{5,4},{6,7},{7,6},{8,9},{9,8},{10,11... | collective-permute-start | bytes 49160 | tf_op jit(solution)/shard_map/ppermute | solution.py:43
  47.7 5.6 %collective-permute-start.14 = (f32[2,2048]{1,0:T(2,128)S(1)}, f32[2,2048]{1,0:T(2,128)S(1)}, u32[]{:S(2)}, u32[]{:S(2)}) collective-permute-start(f32[2,2048]{1,0:T(2,128)S(1)} %get-tuple-element.57), channel_id=1, source_target_pairs={{0,4},{4,8},{8,12},{12,0},{1,5},{5,9},{9,13},{13,1},{2,6},{6,10},{... | collective-permute-start | bytes 49160 | tf_op jit(solution)/shard_map/ppermute | solution.py:62
  49.5 4.6 %collective-permute-start.15 = (f32[2,2048]{1,0:T(2,128)S(1)}, f32[2,2048]{1,0:T(2,128)S(1)}, u32[]{:S(2)}, u32[]{:S(2)}) collective-permute-start(f32[2,2048]{1,0:T(2,128)S(1)} %get-tuple-element.57), channel_id=1, source_target_pairs={{0,8},{4,12},{8,0},{12,4},{1,9},{5,13},{9,1},{13,5},{2,10},{6,14},... | collective-permute-start | bytes 49160 | tf_op jit(solution)/shard_map/ppermute | solution.py:62
  51.3 3.7 %collective-permute-start.16 = (f32[2,2048]{1,0:T(2,128)S(1)}, f32[2,2048]{1,0:T(2,128)S(1)}, u32[]{:S(2)}, u32[]{:S(2)}) collective-permute-start(f32[2,2048]{1,0:T(2,128)S(1)} %get-tuple-element.57), channel_id=1, source_target_pairs={{0,12},{4,0},{8,4},{12,8},{1,13},{5,1},{9,5},{13,9},{2,14},{6,2},{... | collective-permute-start | bytes 49160 | tf_op jit(solution)/shard_map/ppermute | solution.py:62
  56.6 1.2 %collective-permute-start.17 = (f32[2,2048]{1,0:T(2,128)S(1)}, f32[2,2048]{1,0:T(2,128)S(1)}, u32[]{:S(2)}, u32[]{:S(2)}) collective-permute-start(f32[2,2048]{1,0:T(2,128)S(1)} %pad_maximum_fusion.21), channel_id=1, source_target_pairs={{0,1},{1,0},{2,3},{3,2},{4,5},{5,4},{6,7},{7,6},{8,9},{9,8},{10,11... | collective-permute-start | bytes 49160 | tf_op jit(solution)/shard_map/ppermute | solution.py:43
  57.9 5.8 %collective-permute-start.18 = (f32[2,2048]{1,0:T(2,128)S(1)}, f32[2,2048]{1,0:T(2,128)S(1)}, u32[]{:S(2)}, u32[]{:S(2)}) collective-permute-start(f32[2,2048]{1,0:T(2,128)S(1)} %get-tuple-element.55), channel_id=1, source_target_pairs={{0,4},{4,8},{8,12},{12,0},{1,5},{5,9},{9,13},{13,1},{2,6},{6,10},{... | collective-permute-start | bytes 49160 | tf_op jit(solution)/shard_map/ppermute | solution.py:62
  58.8 4.9 %collective-permute-start.19 = (f32[2,2048]{1,0:T(2,128)S(1)}, f32[2,2048]{1,0:T(2,128)S(1)}, u32[]{:S(2)}, u32[]{:S(2)}) collective-permute-start(f32[2,2048]{1,0:T(2,128)S(1)} %get-tuple-element.55), channel_id=1, source_target_pairs={{0,8},{4,12},{8,0},{12,4},{1,9},{5,13},{9,1},{13,5},{2,10},{6,14},... | collective-permute-start | bytes 49160 | tf_op jit(solution)/shard_map/ppermute | solution.py:62
  61.0 3.7 %collective-permute-start.20 = (f32[2,2048]{1,0:T(2,128)S(1)}, f32[2,2048]{1,0:T(2,128)S(1)}, u32[]{:S(2)}, u32[]{:S(2)}) collective-permute-start(f32[2,2048]{1,0:T(2,128)S(1)} %get-tuple-element.55), channel_id=1, source_target_pairs={{0,12},{4,0},{8,4},{12,8},{1,13},{5,1},{9,5},{13,9},{2,14},{6,2},{... | collective-permute-start | bytes 49160 | tf_op jit(solution)/shard_map/ppermute | solution.py:62
  66.3 1.2 %collective-permute-start.21 = (f32[2,2048]{1,0:T(2,128)S(1)}, f32[2,2048]{1,0:T(2,128)S(1)}, u32[]{:S(2)}, u32[]{:S(2)}) collective-permute-start(f32[2,2048]{1,0:T(2,128)S(1)} %pad_maximum_fusion.23), channel_id=1, source_target_pairs={{0,1},{1,0},{2,3},{3,2},{4,5},{5,4},{6,7},{7,6},{8,9},{9,8},{10,11... | collective-permute-start | bytes 49160 | tf_op jit(solution)/shard_map/ppermute | solution.py:43
  67.6 5.6 %collective-permute-start.22 = (f32[2,2048]{1,0:T(2,128)S(1)}, f32[2,2048]{1,0:T(2,128)S(1)}, u32[]{:S(2)}, u32[]{:S(2)}) collective-permute-start(f32[2,2048]{1,0:T(2,128)S(1)} %get-tuple-element.53), channel_id=1, source_target_pairs={{0,4},{4,8},{8,12},{12,0},{1,5},{5,9},{9,13},{13,1},{2,6},{6,10},{... | collective-permute-start | bytes 49160 | tf_op jit(solution)/shard_map/ppermute | solution.py:62
  69.1 4.6 %collective-permute-start.23 = (f32[2,2048]{1,0:T(2,128)S(1)}, f32[2,2048]{1,0:T(2,128)S(1)}, u32[]{:S(2)}, u32[]{:S(2)}) collective-permute-start(f32[2,2048]{1,0:T(2,128)S(1)} %get-tuple-element.53), channel_id=1, source_target_pairs={{0,8},{4,12},{8,0},{12,4},{1,9},{5,13},{9,1},{13,5},{2,10},{6,14},... | collective-permute-start | bytes 49160 | tf_op jit(solution)/shard_map/ppermute | solution.py:62
  71.1 3.7 %collective-permute-start.24 = (f32[2,2048]{1,0:T(2,128)S(1)}, f32[2,2048]{1,0:T(2,128)S(1)}, u32[]{:S(2)}, u32[]{:S(2)}) collective-permute-start(f32[2,2048]{1,0:T(2,128)S(1)} %get-tuple-element.53), channel_id=1, source_target_pairs={{0,12},{4,0},{8,4},{12,8},{1,13},{5,1},{9,5},{13,9},{2,14},{6,2},{... | collective-permute-start | bytes 49160 | tf_op jit(solution)/shard_map/ppermute | solution.py:62
  76.4 1.2 %collective-permute-start.25 = (f32[2,2048]{1,0:T(2,128)S(1)}, f32[2,2048]{1,0:T(2,128)S(1)}, u32[]{:S(2)}, u32[]{:S(2)}) collective-permute-start(f32[2,2048]{1,0:T(2,128)S(1)} %pad_maximum_fusion.25), channel_id=1, source_target_pairs={{0,1},{1,0},{2,3},{3,2},{4,5},{5,4},{6,7},{7,6},{8,9},{9,8},{10,11... | collective-permute-start | bytes 49160 | tf_op jit(solution)/shard_map/ppermute | solution.py:43
  77.7 5.6 %collective-permute-start.26 = (f32[2,2048]{1,0:T(2,128)S(1)}, f32[2,2048]{1,0:T(2,128)S(1)}, u32[]{:S(2)}, u32[]{:S(2)}) collective-permute-start(f32[2,2048]{1,0:T(2,128)S(1)} %get-tuple-element.51), channel_id=1, source_target_pairs={{0,4},{4,8},{8,12},{12,0},{1,5},{5,9},{9,13},{13,1},{2,6},{6,10},{... | collective-permute-start | bytes 49160 | tf_op jit(solution)/shard_map/ppermute | solution.py:62
  78.8 4.9 %collective-permute-start.27 = (f32[2,2048]{1,0:T(2,128)S(1)}, f32[2,2048]{1,0:T(2,128)S(1)}, u32[]{:S(2)}, u32[]{:S(2)}) collective-permute-start(f32[2,2048]{1,0:T(2,128)S(1)} %get-tuple-element.51), channel_id=1, source_target_pairs={{0,8},{4,12},{8,0},{12,4},{1,9},{5,13},{9,1},{13,5},{2,10},{6,14},... | collective-permute-start | bytes 49160 | tf_op jit(solution)/shard_map/ppermute | solution.py:62
  80.7 3.7 %collective-permute-start.28 = (f32[2,2048]{1,0:T(2,128)S(1)}, f32[2,2048]{1,0:T(2,128)S(1)}, u32[]{:S(2)}, u32[]{:S(2)}) collective-permute-start(f32[2,2048]{1,0:T(2,128)S(1)} %get-tuple-element.51), channel_id=1, source_target_pairs={{0,12},{4,0},{8,4},{12,8},{1,13},{5,1},{9,5},{13,9},{2,14},{6,2},{... | collective-permute-start | bytes 49160 | tf_op jit(solution)/shard_map/ppermute | solution.py:62
  86.0 1.2 %collective-permute-start.29 = (f32[2,2048]{1,0:T(2,128)S(1)}, f32[2,2048]{1,0:T(2,128)S(1)}, u32[]{:S(2)}, u32[]{:S(2)}) collective-permute-start(f32[2,2048]{1,0:T(2,128)S(1)} %pad_maximum_fusion.27), channel_id=1, source_target_pairs={{0,1},{1,0},{2,3},{3,2},{4,5},{5,4},{6,7},{7,6},{8,9},{9,8},{10,11... | collective-permute-start | bytes 49160 | tf_op jit(solution)/shard_map/ppermute | solution.py:43
  87.3 5.6 %collective-permute-start.30 = (f32[2,2048]{1,0:T(2,128)S(1)}, f32[2,2048]{1,0:T(2,128)S(1)}, u32[]{:S(2)}, u32[]{:S(2)}) collective-permute-start(f32[2,2048]{1,0:T(2,128)S(1)} %get-tuple-element.49), channel_id=1, source_target_pairs={{0,4},{4,8},{8,12},{12,0},{1,5},{5,9},{9,13},{13,1},{2,6},{6,10},{... | collective-permute-start | bytes 49160 | tf_op jit(solution)/shard_map/ppermute | solution.py:62
  88.9 4.8 %collective-permute-start.31 = (f32[2,2048]{1,0:T(2,128)S(1)}, f32[2,2048]{1,0:T(2,128)S(1)}, u32[]{:S(2)}, u32[]{:S(2)}) collective-permute-start(f32[2,2048]{1,0:T(2,128)S(1)} %get-tuple-element.49), channel_id=1, source_target_pairs={{0,8},{4,12},{8,0},{12,4},{1,9},{5,13},{9,1},{13,5},{2,10},{6,14},... | collective-permute-start | bytes 49160 | tf_op jit(solution)/shard_map/ppermute | solution.py:62
  90.7 3.7 %collective-permute-start.32 = (f32[2,2048]{1,0:T(2,128)S(1)}, f32[2,2048]{1,0:T(2,128)S(1)}, u32[]{:S(2)}, u32[]{:S(2)}) collective-permute-start(f32[2,2048]{1,0:T(2,128)S(1)} %get-tuple-element.49), channel_id=1, source_target_pairs={{0,12},{4,0},{8,4},{12,8},{1,13},{5,1},{9,5},{13,9},{2,14},{6,2},{... | collective-permute-start | bytes 49160 | tf_op jit(solution)/shard_map/ppermute | solution.py:62
  97.7 1.4 %collective-permute-start.33 = (f32[4,128,66]{1,0,2:T(4,128)S(1)}, f32[4,128,66]{1,0,2:T(4,128)S(1)}, u32[]{:S(2)}, u32[]{:S(2)}) collective-permute-start(f32[4,128,66]{1,0,2:T(4,128)S(1)} %pad_maximum_fusion.3), channel_id=1, source_target_pairs={{0,1},{1,0},{2,3},{3,2},{4,5},{5,4},{6,7},{7,6},{8,9},{9,8},{10,11... | collective-permute-start | bytes 405512 | tf_op jit(solution)/shard_map/ppermute | solution.py:92
  99.4 6.1 %collective-permute-start.34 = (f32[128,66]{0,1:T(8,128)S(1)}, f32[128,66]{0,1:T(8,128)S(1)}, u32[]{:S(2)}, u32[]{:S(2)}) collective-permute-start(f32[128,66]{0,1:T(8,128)S(1)} %bitcast.617), channel_id=1, source_target_pairs={{0,4},{4,8},{8,12},{12,0},{1,5},{5,9},{9,13},{13,1},{2,6},{6,10},{... | collective-permute-start | bytes 101384 | tf_op jit(solution)/shard_map/ppermute | solution.py:142
  100.5 5.9 %collective-permute-start.35 = (f32[128,66]{0,1:T(8,128)S(1)}, f32[128,66]{0,1:T(8,128)S(1)}, u32[]{:S(2)}, u32[]{:S(2)}) collective-permute-start(f32[128,66]{0,1:T(8,128)S(1)} %bitcast.618), channel_id=1, source_target_pairs={{0,8},{4,12},{8,0},{12,4},{1,9},{5,13},{9,1},{13,5},{2,10},{6,14},... | collective-permute-start | bytes 101384 | tf_op jit(solution)/shard_map/ppermute | solution.py:142
  102.5 4.2 %collective-permute-start.36 = (f32[128,66]{0,1:T(8,128)S(1)}, f32[128,66]{0,1:T(8,128)S(1)}, u32[]{:S(2)}, u32[]{:S(2)}) collective-permute-start(f32[128,66]{0,1:T(8,128)S(1)} %bitcast.619), channel_id=1, source_target_pairs={{0,12},{4,0},{8,4},{12,8},{1,13},{5,1},{9,5},{13,9},{2,14},{6,2},{... | collective-permute-start | bytes 101384 | tf_op jit(solution)/shard_map/ppermute | solution.py:142

commit v7 on v6

--- a/solution.py
+++ b/solution.py
@@ -1,6 +1,7 @@
 import jax
 import jax.numpy as jnp
 from jax import lax
+from jax.experimental.layout import Layout, with_layout_constraint
 from jax.sharding import PartitionSpec as P
 
 ITERS = 8
@@ -114,7 +115,7 @@
 
     g_pot = jnp.zeros((tgt_count,), jnp.float32)
     f_pot = jnp.zeros((src_count,), jnp.float32)
-    for iteration in range(ITERS):
+    for _ in range(ITERS):
         scores = log_b[None, :] + (g_pot[None, :] - cost) / entropic
         maxima = jnp.max(scores, axis=1)
         totals = jnp.sum(jnp.exp(scores - maxima[:, None]), axis=1)
@@ -228,25 +229,42 @@
     src_count = sources.shape[0]
     tgt_count = targets.shape[0]
     row = lax.axis_index("rows")
+    dim = sources.shape[1]
     mine = jnp.concatenate([sources, source_mass[:, None]], axis=1)
     theirs = lax.ppermute(mine, "rows", [(0, 1), (1, 0)])
+    all_sources = src_count * row_count
+    all_targets = tgt_count * lax.axis_size(("cols", "rep"))
+    log_b = jnp.log(target_mass / all_targets)
+    tgt_sq = jnp.sum(targets * targets, axis=1)
+
+    def scaled_cost(src):
+        src_sq = jnp.sum(src * src, axis=1)
+        return pair_cost(src, src_sq, targets, tgt_sq) / entropic
+
+    scaled_mine = scaled_cost(sources)
+    log_a_mine = jnp.log(source_mass / all_sources)
+    g_pot = jnp.zeros((tgt_count,), jnp.float32)
+    scores = (log_b + g_pot / entropic)[None, :] - scaled_mine
+    maxima = jnp.max(scores, axis=1)
+    totals = jnp.sum(jnp.exp(scores - maxima[:, None]), axis=1)
+    maxima, totals = row_reduce(maxima, totals)
+    f_mine = -relaxed * entropic * (maxima + jnp.log(totals))
+    scores = (log_a_mine + f_mine / entropic)[:, None] - scaled_mine
+    maxima = jnp.max(scores, axis=0)
+    totals = jnp.sum(jnp.exp(scores - maxima[None, :]), axis=0)
+    maxima, totals = lse_allreduce(maxima, totals, ("rows",))
+    g_pot = -relaxed * entropic * (maxima + jnp.log(totals))
+
     first = jnp.where(row == 0, mine, theirs)
     second = jnp.where(row == 0, theirs, mine)
     gathered = jnp.concatenate([first, second], axis=0)
-    all_src = gathered[:, : sources.shape[1]]
-    all_mass = gathered[:, sources.shape[1]]
-    all_sources = src_count * row_count
-    all_targets = tgt_count * lax.axis_size(("cols", "rep"))
+    all_src = gathered[:, :dim]
+    all_mass = gathered[:, dim]
     log_a = jnp.log(all_mass / all_sources)
-    log_b = jnp.log(target_mass / all_targets)
-    src_sq = jnp.sum(all_src * all_src, axis=1)
-    tgt_sq = jnp.sum(targets * targets, axis=1)
-    cost = pair_cost(all_src, src_sq, targets, tgt_sq)
-
-    scaled = cost / entropic
-    g_pot = jnp.zeros((tgt_count,), jnp.float32)
-    f_all = jnp.zeros((all_sources,), jnp.float32)
-    for iteration in range(ITERS):
+    scaled = with_layout_constraint(scaled_cost(all_src), Layout(major_to_minor=(1, 0)))
+    scaled, log_a = lax.optimization_barrier((scaled, log_a))
+
+    for _ in range(1, ITERS):
         scores = (log_b + g_pot / entropic)[None, :] - scaled
         maxima = jnp.max(scores, axis=1)
         totals = jnp.sum(jnp.exp(scores - maxima[:, None]), axis=1)
@@ -259,7 +277,6 @@
         g_pot = -relaxed * entropic * (maxima + jnp.log(totals))
 
     f_pot = lax.dynamic_slice_in_dim(f_all, row * src_count, src_count)
-    scaled_mine = lax.dynamic_slice_in_dim(scaled, row * src_count, src_count, axis=0)
     return (f_pot,) + fate_pullback(scaled_mine, log_b, g_pot, fate_panel, scaled=True)
 
 
@@ -276,4 +293,5 @@
         P(("parts", "cols", "rep")),
         P(("parts", "rows", "cols", "rep"), None),
     )
+
     return jax.shard_map(body, mesh=mesh, in_specs=in_specs, out_specs=out_specs, check_vma=False)

time: 108 us -> 111 us (1.028)
  waiting for transfers between devices: 41.9 us -> 52.2 us
  starting transfers between devices: 41.7 us -> 33.8 us
  other arithmetic: 18.7 us -> 16.7 us
  matrix products: 3.19 us -> 5.18 us
    ppermute x24, waiting for transfers between devices: 23.3 us -> 31.3 us  [lse_exchange(): received.append(lax.ppermute(payload, axes, perm))]
    ppermute x24, starting transfers between devices: 33.9 us -> 27.5 us  [lse_exchange(): received.append(lax.ppermute(payload, axes, perm))]
    ppermute x1, starting transfers between devices: 3.03 us -> 0.6 us  [body(): theirs = lax.ppermute(mine, 'rows', [(0, 1), (1, 0)])]
    ppermute x8 -> x9, starting transfers between devices: 0.57 us -> 2.61 us  [lse_allreduce(): other = lax.ppermute(jnp.stack([maxima, totals]), name, perm)]
    dot_general x1 -> x2, matrix products: 2.18 us -> 4.17 us  [pair_cost(): lax.dot_general(lhs_rows, rhs_rows, (((1,), (1,)), ((), ())), precision=l...]
    ppermute x3, waiting for transfers between devices: 2.53 us -> 3.74 us  [lse_scatter_exchange(): parts.append(lax.ppermute(send, name, perm))]
    ppermute x8 -> x9, waiting for transfers between devices: 9.36 us -> 10.5 us  [lse_allreduce(): other = lax.ppermute(jnp.stack([maxima, totals]), name, perm)]
  transfers between devices with their start and end apart: 37 -> 38, of which waited for: 34 -> 38; matrix products, arithmetic and copies ran while one was open for 2% -> 1% of each run, Pallas kernels for 0% -> 0%
where the time goes in v7:
time: 111 us; the launch traced here: 110 us
  waiting for transfers between devices  52.2 us (47%)
  starting transfers between devices  33.8 us (30%)
  other arithmetic  16.7 us (15%)
  matrix products  5.18 us (5%)
  between operations  1.42 us (1%)
    ppermute x24, waiting for transfers between devices, lse_exchange(): received.append(lax.ppermute(payload, axes, perm))  31.3 us
    ppermute x24, starting transfers between devices, lse_exchange(): received.append(lax.ppermute(payload, axes, perm))  27.5 us
    ppermute x9, waiting for transfers between devices, lse_allreduce(): other = lax.ppermute(jnp.stack([maxima, totals]), name, perm)  10.5 us
    ppermute x1, waiting for transfers between devices, body(): theirs = lax.ppermute(mine, 'rows', [(0, 1), (1, 0)])  5.35 us
    dot_general x2, matrix products, pair_cost(): lax.dot_general(lhs_rows, rhs_rows, (((1,), (1,)), ((), ())), precision=l...  4.17 us
    reduce_sum x8, other arithmetic, body(): totals = jnp.sum(jnp.exp(scores - maxima[None, :]), axis=0)  3.83 us
    ppermute x3, waiting for transfers between devices, lse_scatter_exchange(): parts.append(lax.ppermute(send, name, perm))  3.74 us
    reduce_sum x8, other arithmetic, body(): totals = jnp.sum(jnp.exp(scores - maxima[:, None]), axis=1)  3.27 us
  transfers between devices with their start and end apart: 38, of which 38 were waited for; matrix products, arithmetic and copies ran while one was open for 1% of the time, Pallas kernels for 0%

profile of v7, /device:TPU:0, one launch (start us, length us, event | category | flops | bytes accessed | tf_op | source)
XLA Modules:
  0.0 110.3 jit_solution(18128204181217440281)
XLA Ops:
  2.2 1.0 multiply_reduce_fusion.1
  3.2 2.1 %subtract_reduce_fusion.16 = (f32[1024]{0:T(1024)S(1)}, f32[1024,256]{0,1:T(8,128)S(1)}) fusion(f32[256]{0:T(256)S(1)} %multiply_log_fusion, f32[1024,64]{0,1:T(8,128)} %param.5, f32[256,64]{0,1:T(8,128)} %param.7, f32[256]{0:T(256)S(1)} %multiply_reduce_fusion.2, f32[1024]{0:T(1024)S(1)} %multiply_reduce_fusion.1), kind=kOutput, calls=%fused_computation.39 | convolution fusion | flops 202898432 | bytes 1386496 | tf_op jit(solution)/shard_map/dot_general | solution.py:15
  7.1 5.0 %collective-permute-start.4 = (f32[2,1024]{1,0:T(2,128)S(1)}, f32[2,1024]{1,0:T(2,128)S(1)}, u32[]{:S(2)}, u32[]{:S(2)}) collective-permute-start(f32[2,1024]{1,0:T(2,128)S(1)} %get-tuple-element.120), channel_id=1, source_target_pairs={{0,12},{4,0},{8,4},{12,8},{1,13},{5,1},{9,5},{13,9},{2,14},{6,2},{... | collective-permute-start | bytes 24584 | tf_op jit(solution)/shard_map/ppermute | solution.py:63
  12.1 1.0 collective-permute-start.2
  13.5 3.2 %collective-permute-done.3 = f32[2,1024]{1,0:T(2,128)S(1)} collective-permute-done((f32[2,1024]{1,0:T(2,128)S(1)}, f32[2,1024]{1,0:T(2,128)S(1)}, u32[]{:S(2)}, u32[]{:S(2)}) %collective-permute-start.3) | collective-permute-done | bytes 8224 | tf_op jit(solution)/shard_map/ppermute | solution.py:63
  16.7 0.9 collective-permute-done.2
  18.2 1.6 %collective-permute-start.5 = (f32[2,256]{1,0:T(2,128)S(1)}, f32[2,256]{1,0:T(2,128)S(1)}, u32[]{:S(2)}, u32[]{:S(2)}) collective-permute-start(f32[2,256]{1,0:T(2,128)S(1)} %pad_maximum_fusion.28), channel_id=1, source_target_pairs={{0,2},{2,0},{1,3},{3,1},{4,6},{6,4},{5,7},{7,5},{8,10},{10,8},{9,1... | collective-permute-start | bytes 6152 | tf_op jit(solution)/shard_map/ppermute | solution.py:44
  20.4 1.5 %collective-permute-done.5 = f32[2,256]{1,0:T(2,128)S(1)} collective-permute-done((f32[2,256]{1,0:T(2,128)S(1)}, f32[2,256]{1,0:T(2,128)S(1)}, u32[]{:S(2)}, u32[]{:S(2)}) %collective-permute-start.5) | collective-permute-done | bytes 2080 | tf_op jit(solution)/shard_map/ppermute | solution.py:44
  21.9 5.4 %collective-permute-done = f32[1024,65]{0,1:T(8,128)S(1)} collective-permute-done((f32[1024,65]{0,1:T(8,128)S(1)}, f32[1024,65]{0,1:T(8,128)S(1)}, u32[]{:S(2)}, u32[]{:S(2)}) %collective-permute-start) | collective-permute-done | bytes 266272 | tf_op jit(solution)/shard_map/ppermute | solution.py:234
  27.4 2.0 %fusion.1 = f32[2048,256]{0,1:T(8,128)S(1)} fusion(f32[256,64]{0,1:T(8,128)S(1)} %copy-done.2, f32[256]{0:T(256)S(1)} %multiply_reduce_fusion.2, f32[2048]{0:T(1024)S(1)} %multiply_reduce_fusion, f32[1024,65]{0,1:T(8,128)S(1)} %get-tuple-element.13, f32[1024,65]{0,1:T(8,128)S(1)} %get-tuple-element.14), kind=kOutput, calls=%fused_computation.2 | convolution fusion | flops 404881408 | bytes 2704384 | tf_op jit(solution)/shard_map/dot_general | solution.py:15
  30.2 1.2 %collective-permute-done.6 = f32[2,2048]{1,0:T(2,128)S(1)} collective-permute-done((f32[2,2048]{1,0:T(2,128)S(1)}, f32[2,2048]{1,0:T(2,128)S(1)}, u32[]{:S(2)}, u32[]{:S(2)}) %collective-permute-start.6) | collective-permute-done | bytes 16416 | tf_op jit(solution)/shard_map/ppermute | solution.py:44
  31.4 0.9 collective-permute-start.9
  32.4 1.9 %collective-permute-start.7 = (f32[2,2048]{1,0:T(2,128)S(1)}, f32[2,2048]{1,0:T(2,128)S(1)}, u32[]{:S(2)}, u32[]{:S(2)}) collective-permute-start(f32[2,2048]{1,0:T(2,128)S(1)} %get-tuple-element.116), channel_id=1, source_target_pairs={{0,4},{4,8},{8,12},{12,0},{1,5},{5,9},{9,13},{13,1},{2,6},{6,10},{... | collective-permute-start | bytes 49160 | tf_op jit(solution)/shard_map/ppermute | solution.py:63
  35.2 1.8 %collective-permute-done.8 = f32[2,2048]{1,0:T(2,128)S(1)} collective-permute-done((f32[2,2048]{1,0:T(2,128)S(1)}, f32[2,2048]{1,0:T(2,128)S(1)}, u32[]{:S(2)}, u32[]{:S(2)}) %collective-permute-start.8) | collective-permute-done | bytes 16416 | tf_op jit(solution)/shard_map/ppermute | solution.py:63
  37.0 0.9 collective-permute-done.7
  39.6 1.2 %collective-permute-done.10 = f32[2,2048]{1,0:T(2,128)S(1)} collective-permute-done((f32[2,2048]{1,0:T(2,128)S(1)}, f32[2,2048]{1,0:T(2,128)S(1)}, u32[]{:S(2)}, u32[]{:S(2)}) %collective-permute-start.10) | collective-permute-done | bytes 16416 | tf_op jit(solution)/shard_map/ppermute | solution.py:44
  40.9 1.7 %collective-permute-start.13 = (f32[2,2048]{1,0:T(2,128)S(1)}, f32[2,2048]{1,0:T(2,128)S(1)}, u32[]{:S(2)}, u32[]{:S(2)}) collective-permute-start(f32[2,2048]{1,0:T(2,128)S(1)} %get-tuple-element.114), channel_id=1, source_target_pairs={{0,12},{4,0},{8,4},{12,8},{1,13},{5,1},{9,5},{13,9},{2,14},{6,2},{... | collective-permute-start | bytes 49160 | tf_op jit(solution)/shard_map/ppermute | solution.py:63
  42.6 1.4 %collective-permute-start.11 = (f32[2,2048]{1,0:T(2,128)S(1)}, f32[2,2048]{1,0:T(2,128)S(1)}, u32[]{:S(2)}, u32[]{:S(2)}) collective-permute-start(f32[2,2048]{1,0:T(2,128)S(1)} %get-tuple-element.114), channel_id=1, source_target_pairs={{0,4},{4,8},{8,12},{12,0},{1,5},{5,9},{9,13},{13,1},{2,6},{6,10},{... | collective-permute-start | bytes 49160 | tf_op jit(solution)/shard_map/ppermute | solution.py:63
  44.6 2.7 %collective-permute-done.12 = f32[2,2048]{1,0:T(2,128)S(1)} collective-permute-done((f32[2,2048]{1,0:T(2,128)S(1)}, f32[2,2048]{1,0:T(2,128)S(1)}, u32[]{:S(2)}, u32[]{:S(2)}) %collective-permute-start.12) | collective-permute-done | bytes 16416 | tf_op jit(solution)/shard_map/ppermute | solution.py:63
  49.8 1.2 %collective-permute-done.14 = f32[2,2048]{1,0:T(2,128)S(1)} collective-permute-done((f32[2,2048]{1,0:T(2,128)S(1)}, f32[2,2048]{1,0:T(2,128)S(1)}, u32[]{:S(2)}, u32[]{:S(2)}) %collective-permute-start.14) | collective-permute-done | bytes 16416 | tf_op jit(solution)/shard_map/ppermute | solution.py:44
  51.0 1.0 collective-permute-start.17
  52.3 1.9 %collective-permute-start.15 = (f32[2,2048]{1,0:T(2,128)S(1)}, f32[2,2048]{1,0:T(2,128)S(1)}, u32[]{:S(2)}, u32[]{:S(2)}) collective-permute-start(f32[2,2048]{1,0:T(2,128)S(1)} %get-tuple-element.112), channel_id=1, source_target_pairs={{0,4},{4,8},{8,12},{12,0},{1,5},{5,9},{9,13},{13,1},{2,6},{6,10},{... | collective-permute-start | bytes 49160 | tf_op jit(solution)/shard_map/ppermute | solution.py:63
  54.8 1.8 %collective-permute-done.16 = f32[2,2048]{1,0:T(2,128)S(1)} collective-permute-done((f32[2,2048]{1,0:T(2,128)S(1)}, f32[2,2048]{1,0:T(2,128)S(1)}, u32[]{:S(2)}, u32[]{:S(2)}) %collective-permute-start.16) | collective-permute-done | bytes 16416 | tf_op jit(solution)/shard_map/ppermute | solution.py:63
  56.7 1.2 %collective-permute-done.15 = f32[2,2048]{1,0:T(2,128)S(1)} collective-permute-done((f32[2,2048]{1,0:T(2,128)S(1)}, f32[2,2048]{1,0:T(2,128)S(1)}, u32[]{:S(2)}, u32[]{:S(2)}) %collective-permute-start.15) | collective-permute-done | bytes 16416 | tf_op jit(solution)/shard_map/ppermute | solution.py:63
  59.5 1.2 %collective-permute-done.18 = f32[2,2048]{1,0:T(2,128)S(1)} collective-permute-done((f32[2,2048]{1,0:T(2,128)S(1)}, f32[2,2048]{1,0:T(2,128)S(1)}, u32[]{:S(2)}, u32[]{:S(2)}) %collective-permute-start.18) | collective-permute-done | bytes 16416 | tf_op jit(solution)/shard_map/ppermute | solution.py:44
  60.7 1.4 %collective-permute-start.21 = (f32[2,2048]{1,0:T(2,128)S(1)}, f32[2,2048]{1,0:T(2,128)S(1)}, u32[]{:S(2)}, u32[]{:S(2)}) collective-permute-start(f32[2,2048]{1,0:T(2,128)S(1)} %get-tuple-element.110), channel_id=1, source_target_pairs={{0,12},{4,0},{8,4},{12,8},{1,13},{5,1},{9,5},{13,9},{2,14},{6,2},{... | collective-permute-start | bytes 49160 | tf_op jit(solution)/shard_map/ppermute | solution.py:63
  62.4 1.3 %collective-permute-start.19 = (f32[2,2048]{1,0:T(2,128)S(1)}, f32[2,2048]{1,0:T(2,128)S(1)}, u32[]{:S(2)}, u32[]{:S(2)}) collective-permute-start(f32[2,2048]{1,0:T(2,128)S(1)} %get-tuple-element.110), channel_id=1, source_target_pairs={{0,4},{4,8},{8,12},{12,0},{1,5},{5,9},{9,13},{13,1},{2,6},{6,10},{... | collective-permute-start | bytes 49160 | tf_op jit(solution)/shard_map/ppermute | solution.py:63
  64.5 2.3 %collective-permute-done.20 = f32[2,2048]{1,0:T(2,128)S(1)} collective-permute-done((f32[2,2048]{1,0:T(2,128)S(1)}, f32[2,2048]{1,0:T(2,128)S(1)}, u32[]{:S(2)}, u32[]{:S(2)}) %collective-permute-start.20) | collective-permute-done | bytes 16416 | tf_op jit(solution)/shard_map/ppermute | solution.py:63
  66.8 1.1 %collective-permute-done.19 = f32[2,2048]{1,0:T(2,128)S(1)} collective-permute-done((f32[2,2048]{1,0:T(2,128)S(1)}, f32[2,2048]{1,0:T(2,128)S(1)}, u32[]{:S(2)}, u32[]{:S(2)}) %collective-permute-start.19) | collective-permute-done | bytes 16416 | tf_op jit(solution)/shard_map/ppermute | solution.py:63
  69.6 1.2 %collective-permute-done.22 = f32[2,2048]{1,0:T(2,128)S(1)} collective-permute-done((f32[2,2048]{1,0:T(2,128)S(1)}, f32[2,2048]{1,0:T(2,128)S(1)}, u32[]{:S(2)}, u32[]{:S(2)}) %collective-permute-start.22) | collective-permute-done | bytes 16416 | tf_op jit(solution)/shard_map/ppermute | solution.py:44
  70.9 1.0 collective-permute-start.25
  72.0 1.8 %collective-permute-start.23 = (f32[2,2048]{1,0:T(2,128)S(1)}, f32[2,2048]{1,0:T(2,128)S(1)}, u32[]{:S(2)}, u32[]{:S(2)}) collective-permute-start(f32[2,2048]{1,0:T(2,128)S(1)} %get-tuple-element.108), channel_id=1, source_target_pairs={{0,4},{4,8},{8,12},{12,0},{1,5},{5,9},{9,13},{13,1},{2,6},{6,10},{... | collective-permute-start | bytes 49160 | tf_op jit(solution)/shard_map/ppermute | solution.py:63
  74.6 1.9 %collective-permute-done.24 = f32[2,2048]{1,0:T(2,128)S(1)} collective-permute-done((f32[2,2048]{1,0:T(2,128)S(1)}, f32[2,2048]{1,0:T(2,128)S(1)}, u32[]{:S(2)}, u32[]{:S(2)}) %collective-permute-start.24) | collective-permute-done | bytes 16416 | tf_op jit(solution)/shard_map/ppermute | solution.py:63
  76.5 1.0 collective-permute-done.23
  79.2 1.2 %collective-permute-done.26 = f32[2,2048]{1,0:T(2,128)S(1)} collective-permute-done((f32[2,2048]{1,0:T(2,128)S(1)}, f32[2,2048]{1,0:T(2,128)S(1)}, u32[]{:S(2)}, u32[]{:S(2)}) %collective-permute-start.26) | collective-permute-done | bytes 16416 | tf_op jit(solution)/shard_map/ppermute | solution.py:44
  80.4 1.6 %collective-permute-start.29 = (f32[2,2048]{1,0:T(2,128)S(1)}, f32[2,2048]{1,0:T(2,128)S(1)}, u32[]{:S(2)}, u32[]{:S(2)}) collective-permute-start(f32[2,2048]{1,0:T(2,128)S(1)} %get-tuple-element.106), channel_id=1, source_target_pairs={{0,12},{4,0},{8,4},{12,8},{1,13},{5,1},{9,5},{13,9},{2,14},{6,2},{... | collective-permute-start | bytes 49160 | tf_op jit(solution)/shard_map/ppermute | solution.py:63
  82.0 1.5 %collective-permute-start.27 = (f32[2,2048]{1,0:T(2,128)S(1)}, f32[2,2048]{1,0:T(2,128)S(1)}, u32[]{:S(2)}, u32[]{:S(2)}) collective-permute-start(f32[2,2048]{1,0:T(2,128)S(1)} %get-tuple-element.106), channel_id=1, source_target_pairs={{0,4},{4,8},{8,12},{12,0},{1,5},{5,9},{9,13},{13,1},{2,6},{6,10},{... | collective-permute-start | bytes 49160 | tf_op jit(solution)/shard_map/ppermute | solution.py:63
  84.2 2.6 %collective-permute-done.28 = f32[2,2048]{1,0:T(2,128)S(1)} collective-permute-done((f32[2,2048]{1,0:T(2,128)S(1)}, f32[2,2048]{1,0:T(2,128)S(1)}, u32[]{:S(2)}, u32[]{:S(2)}) %collective-permute-start.28) | collective-permute-done | bytes 16416 | tf_op jit(solution)/shard_map/ppermute | solution.py:63
  89.2 1.2 %collective-permute-done.30 = f32[2,2048]{1,0:T(2,128)S(1)} collective-permute-done((f32[2,2048]{1,0:T(2,128)S(1)}, f32[2,2048]{1,0:T(2,128)S(1)}, u32[]{:S(2)}, u32[]{:S(2)}) %collective-permute-start.30) | collective-permute-done | bytes 16416 | tf_op jit(solution)/shard_map/ppermute | solution.py:44
  90.5 1.1 %collective-permute-start.33 = (f32[2,2048]{1,0:T(2,128)S(1)}, f32[2,2048]{1,0:T(2,128)S(1)}, u32[]{:S(2)}, u32[]{:S(2)}) collective-permute-start(f32[2,2048]{1,0:T(2,128)S(1)} %get-tuple-element.104), channel_id=1, source_target_pairs={{0,12},{4,0},{8,4},{12,8},{1,13},{5,1},{9,5},{13,9},{2,14},{6,2},{... | collective-permute-start | bytes 49160 | tf_op jit(solution)/shard_map/ppermute | solution.py:63
  91.7 1.9 %collective-permute-start.31 = (f32[2,2048]{1,0:T(2,128)S(1)}, f32[2,2048]{1,0:T(2,128)S(1)}, u32[]{:S(2)}, u32[]{:S(2)}) collective-permute-start(f32[2,2048]{1,0:T(2,128)S(1)} %get-tuple-element.104), channel_id=1, source_target_pairs={{0,4},{4,8},{8,12},{12,0},{1,5},{5,9},{9,13},{13,1},{2,6},{6,10},{... | collective-permute-start | bytes 49160 | tf_op jit(solution)/shard_map/ppermute | solution.py:63
  94.2 2.1 %collective-permute-done.32 = f32[2,2048]{1,0:T(2,128)S(1)} collective-permute-done((f32[2,2048]{1,0:T(2,128)S(1)}, f32[2,2048]{1,0:T(2,128)S(1)}, u32[]{:S(2)}, u32[]{:S(2)}) %collective-permute-start.32) | collective-permute-done | bytes 16416 | tf_op jit(solution)/shard_map/ppermute | solution.py:63
  96.3 0.9 collective-permute-done.31
  99.2 1.0 fusion.5
  100.7 1.3 %collective-permute-done.34 = f32[4,128,66]{1,0,2:T(4,128)S(1)} collective-permute-done((f32[4,128,66]{1,0,2:T(4,128)S(1)}, f32[4,128,66]{1,0,2:T(4,128)S(1)}, u32[]{:S(2)}, u32[]{:S(2)}) %collective-permute-start.34) | collective-permute-done | bytes 135200 | tf_op jit(solution)/shard_map/ppermute | solution.py:93
  102.2 1.4 %collective-permute-start.37 = (f32[128,66]{0,1:T(8,128)S(1)}, f32[128,66]{0,1:T(8,128)S(1)}, u32[]{:S(2)}, u32[]{:S(2)}) collective-permute-start(f32[128,66]{0,1:T(8,128)S(1)} %bitcast.229), channel_id=1, source_target_pairs={{0,12},{4,0},{8,4},{12,8},{1,13},{5,1},{9,5},{13,9},{2,14},{6,2},{... | collective-permute-start | bytes 101384 | tf_op jit(solution)/shard_map/ppermute | solution.py:143
  103.9 1.4 %collective-permute-start.35 = (f32[128,66]{0,1:T(8,128)S(1)}, f32[128,66]{0,1:T(8,128)S(1)}, u32[]{:S(2)}, u32[]{:S(2)}) collective-permute-start(f32[128,66]{0,1:T(8,128)S(1)} %bitcast.231), channel_id=1, source_target_pairs={{0,4},{4,8},{8,12},{12,0},{1,5},{5,9},{9,13},{13,1},{2,6},{6,10},{... | collective-permute-start | bytes 101384 | tf_op jit(solution)/shard_map/ppermute | solution.py:143
  106.2 2.9 %collective-permute-done.36 = f32[128,66]{0,1:T(8,128)S(1)} collective-permute-done((f32[128,66]{0,1:T(8,128)S(1)}, f32[128,66]{0,1:T(8,128)S(1)}, u32[]{:S(2)}, u32[]{:S(2)}) %collective-permute-start.36) | collective-permute-done | bytes 33824 | tf_op jit(solution)/shard_map/ppermute | solution.py:143
  (159 shorter events, 28.0 us)
Async XLA Ops:
  0.6 98.5 %copy-start = (f32[256,64]{0,1:T(8,128)S(1)}, f32[256,64]{0,1:T(8,128)}, u32[]{:S(2)}) copy-start(f32[256,64]{0,1:T(8,128)} %param.9) | copy-start | bytes 196612
  0.6 17.0 %copy-start.4 = (f32[1024]{0:T(1024)S(1)}, f32[1024]{0:T(1024)}, u32[]{:S(2)}) copy-start(f32[1024]{0:T(1024)} %param.6) | copy-start | bytes 12292
  5.4 14.4 %copy-start.1 = (f32[1024,64]{0,1:T(8,128)S(1)}, f32[1024,64]{0,1:T(8,128)}, u32[]{:S(2)}) copy-start(f32[1024,64]{0,1:T(8,128)} %param.5) | copy-start | bytes 786436
  5.4 16.5 %copy-start.3 = (f32[256]{0:T(256)S(1)}, f32[256]{0:T(256)}, u32[]{:S(2)}) copy-start(f32[256]{0:T(256)} %param.8) | copy-start | bytes 3076
  5.7 1.4 %collective-permute-start.1 = (f32[2,1024]{1,0:T(2,128)S(1)}, f32[2,1024]{1,0:T(2,128)S(1)}, u32[]{:S(2)}, u32[]{:S(2)}) collective-permute-start(f32[2,1024]{1,0:T(2,128)S(1)} %pad_maximum_fusion.26), channel_id=1, source_target_pairs={{0,1},{1,0},{2,3},{3,2},{4,5},{5,4},{6,7},{7,6},{8,9},{9,8},{10,11... | collective-permute-start | bytes 24584 | tf_op jit(solution)/shard_map/ppermute | solution.py:44
  7.1 6.3 %collective-permute-start.4 = (f32[2,1024]{1,0:T(2,128)S(1)}, f32[2,1024]{1,0:T(2,128)S(1)}, u32[]{:S(2)}, u32[]{:S(2)}) collective-permute-start(f32[2,1024]{1,0:T(2,128)S(1)} %get-tuple-element.120), channel_id=1, source_target_pairs={{0,12},{4,0},{8,4},{12,8},{1,13},{5,1},{9,5},{13,9},{2,14},{6,2},{... | collective-permute-start | bytes 24584 | tf_op jit(solution)/shard_map/ppermute | solution.py:63
  12.1 4.5 %collective-permute-start.3 = (f32[2,1024]{1,0:T(2,128)S(1)}, f32[2,1024]{1,0:T(2,128)S(1)}, u32[]{:S(2)}, u32[]{:S(2)}) collective-permute-start(f32[2,1024]{1,0:T(2,128)S(1)} %get-tuple-element.120), channel_id=1, source_target_pairs={{0,8},{4,12},{8,0},{12,4},{1,9},{5,13},{9,1},{13,5},{2,10},{6,14},... | collective-permute-start | bytes 24584 | tf_op jit(solution)/shard_map/ppermute | solution.py:63
  12.1 5.4 %collective-permute-start.2 = (f32[2,1024]{1,0:T(2,128)S(1)}, f32[2,1024]{1,0:T(2,128)S(1)}, u32[]{:S(2)}, u32[]{:S(2)}) collective-permute-start(f32[2,1024]{1,0:T(2,128)S(1)} %get-tuple-element.120), channel_id=1, source_target_pairs={{0,4},{4,8},{8,12},{12,0},{1,5},{5,9},{9,13},{13,1},{2,6},{6,10},{... | collective-permute-start | bytes 24584 | tf_op jit(solution)/shard_map/ppermute | solution.py:63
  17.8 9.5 %copy-start.2 = (f32[256,64]{0,1:T(8,128)S(1)}, f32[256,64]{0,1:T(8,128)}, u32[]{:S(2)}) copy-start(f32[256,64]{0,1:T(8,128)} %param.7) | copy-start | bytes 196612
  18.2 3.7 %collective-permute-start.5 = (f32[2,256]{1,0:T(2,128)S(1)}, f32[2,256]{1,0:T(2,128)S(1)}, u32[]{:S(2)}, u32[]{:S(2)}) collective-permute-start(f32[2,256]{1,0:T(2,128)S(1)} %pad_maximum_fusion.28), channel_id=1, source_target_pairs={{0,2},{2,0},{1,3},{3,1},{4,6},{6,4},{5,7},{7,5},{8,10},{10,8},{9,1... | collective-permute-start | bytes 6152 | tf_op jit(solution)/shard_map/ppermute | solution.py:44
  19.8 7.5 %collective-permute-start = (f32[1024,65]{0,1:T(8,128)S(1)}, f32[1024,65]{0,1:T(8,128)S(1)}, u32[]{:S(2)}, u32[]{:S(2)}) collective-permute-start(f32[1024,65]{0,1:T(8,128)S(1)} %pad_maximum_fusion), channel_id=1, source_target_pairs={{0,2},{2,0},{1,3},{3,1},{4,6},{6,4},{5,7},{7,5},{8,10},{10,8},{9,1... | collective-permute-start | bytes 798728 | tf_op jit(solution)/shard_map/ppermute | solution.py:234
  30.1 1.2 %collective-permute-start.6 = (f32[2,2048]{1,0:T(2,128)S(1)}, f32[2,2048]{1,0:T(2,128)S(1)}, u32[]{:S(2)}, u32[]{:S(2)}) collective-permute-start(f32[2,2048]{1,0:T(2,128)S(1)} %pad_maximum_fusion.11), channel_id=1, source_target_pairs={{0,1},{1,0},{2,3},{3,2},{4,5},{5,4},{6,7},{7,6},{8,9},{9,8},{10,11... | collective-permute-start | bytes 49160 | tf_op jit(solution)/shard_map/ppermute | solution.py:44
  31.4 3.8 %collective-permute-start.9 = (f32[2,2048]{1,0:T(2,128)S(1)}, f32[2,2048]{1,0:T(2,128)S(1)}, u32[]{:S(2)}, u32[]{:S(2)}) collective-permute-start(f32[2,2048]{1,0:T(2,128)S(1)} %get-tuple-element.116), channel_id=1, source_target_pairs={{0,12},{4,0},{8,4},{12,8},{1,13},{5,1},{9,5},{13,9},{2,14},{6,2},{... | collective-permute-start | bytes 49160 | tf_op jit(solution)/shard_map/ppermute | solution.py:63
  32.3 4.7 %collective-permute-start.8 = (f32[2,2048]{1,0:T(2,128)S(1)}, f32[2,2048]{1,0:T(2,128)S(1)}, u32[]{:S(2)}, u32[]{:S(2)}) collective-permute-start(f32[2,2048]{1,0:T(2,128)S(1)} %get-tuple-element.116), channel_id=1, source_target_pairs={{0,8},{4,12},{8,0},{12,4},{1,9},{5,13},{9,1},{13,5},{2,10},{6,14},... | collective-permute-start | bytes 49160 | tf_op jit(solution)/shard_map/ppermute | solution.py:63
  32.4 5.5 %collective-permute-start.7 = (f32[2,2048]{1,0:T(2,128)S(1)}, f32[2,2048]{1,0:T(2,128)S(1)}, u32[]{:S(2)}, u32[]{:S(2)}) collective-permute-start(f32[2,2048]{1,0:T(2,128)S(1)} %get-tuple-element.116), channel_id=1, source_target_pairs={{0,4},{4,8},{8,12},{12,0},{1,5},{5,9},{9,13},{13,1},{2,6},{6,10},{... | collective-permute-start | bytes 49160 | tf_op jit(solution)/shard_map/ppermute | solution.py:63
  39.5 1.2 %collective-permute-start.10 = (f32[2,2048]{1,0:T(2,128)S(1)}, f32[2,2048]{1,0:T(2,128)S(1)}, u32[]{:S(2)}, u32[]{:S(2)}) collective-permute-start(f32[2,2048]{1,0:T(2,128)S(1)} %pad_maximum_fusion.13), channel_id=1, source_target_pairs={{0,1},{1,0},{2,3},{3,2},{4,5},{5,4},{6,7},{7,6},{8,9},{9,8},{10,11... | collective-permute-start | bytes 49160 | tf_op jit(solution)/shard_map/ppermute | solution.py:44
  40.9 3.8 %collective-permute-start.13 = (f32[2,2048]{1,0:T(2,128)S(1)}, f32[2,2048]{1,0:T(2,128)S(1)}, u32[]{:S(2)}, u32[]{:S(2)}) collective-permute-start(f32[2,2048]{1,0:T(2,128)S(1)} %get-tuple-element.114), channel_id=1, source_target_pairs={{0,12},{4,0},{8,4},{12,8},{1,13},{5,1},{9,5},{13,9},{2,14},{6,2},{... | collective-permute-start | bytes 49160 | tf_op jit(solution)/shard_map/ppermute | solution.py:63
  42.6 4.8 %collective-permute-start.12 = (f32[2,2048]{1,0:T(2,128)S(1)}, f32[2,2048]{1,0:T(2,128)S(1)}, u32[]{:S(2)}, u32[]{:S(2)}) collective-permute-start(f32[2,2048]{1,0:T(2,128)S(1)} %get-tuple-element.114), channel_id=1, source_target_pairs={{0,8},{4,12},{8,0},{12,4},{1,9},{5,13},{9,1},{13,5},{2,10},{6,14},... | collective-permute-start | bytes 49160 | tf_op jit(solution)/shard_map/ppermute | solution.py:63
  42.6 5.5 %collective-permute-start.11 = (f32[2,2048]{1,0:T(2,128)S(1)}, f32[2,2048]{1,0:T(2,128)S(1)}, u32[]{:S(2)}, u32[]{:S(2)}) collective-permute-start(f32[2,2048]{1,0:T(2,128)S(1)} %get-tuple-element.114), channel_id=1, source_target_pairs={{0,4},{4,8},{8,12},{12,0},{1,5},{5,9},{9,13},{13,1},{2,6},{6,10},{... | collective-permute-start | bytes 49160 | tf_op jit(solution)/shard_map/ppermute | solution.py:63
  49.7 1.2 %collective-permute-start.14 = (f32[2,2048]{1,0:T(2,128)S(1)}, f32[2,2048]{1,0:T(2,128)S(1)}, u32[]{:S(2)}, u32[]{:S(2)}) collective-permute-start(f32[2,2048]{1,0:T(2,128)S(1)} %pad_maximum_fusion.15), channel_id=1, source_target_pairs={{0,1},{1,0},{2,3},{3,2},{4,5},{5,4},{6,7},{7,6},{8,9},{9,8},{10,11... | collective-permute-start | bytes 49160 | tf_op jit(solution)/shard_map/ppermute | solution.py:44
  51.0 3.8 %collective-permute-start.17 = (f32[2,2048]{1,0:T(2,128)S(1)}, f32[2,2048]{1,0:T(2,128)S(1)}, u32[]{:S(2)}, u32[]{:S(2)}) collective-permute-start(f32[2,2048]{1,0:T(2,128)S(1)} %get-tuple-element.112), channel_id=1, source_target_pairs={{0,12},{4,0},{8,4},{12,8},{1,13},{5,1},{9,5},{13,9},{2,14},{6,2},{... | collective-permute-start | bytes 49160 | tf_op jit(solution)/shard_map/ppermute | solution.py:63
  52.0 4.6 %collective-permute-start.16 = (f32[2,2048]{1,0:T(2,128)S(1)}, f32[2,2048]{1,0:T(2,128)S(1)}, u32[]{:S(2)}, u32[]{:S(2)}) collective-permute-start(f32[2,2048]{1,0:T(2,128)S(1)} %get-tuple-element.112), channel_id=1, source_target_pairs={{0,8},{4,12},{8,0},{12,4},{1,9},{5,13},{9,1},{13,5},{2,10},{6,14},... | collective-permute-start | bytes 49160 | tf_op jit(solution)/shard_map/ppermute | solution.py:63
  52.3 5.5 %collective-permute-start.15 = (f32[2,2048]{1,0:T(2,128)S(1)}, f32[2,2048]{1,0:T(2,128)S(1)}, u32[]{:S(2)}, u32[]{:S(2)}) collective-permute-start(f32[2,2048]{1,0:T(2,128)S(1)} %get-tuple-element.112), channel_id=1, source_target_pairs={{0,4},{4,8},{8,12},{12,0},{1,5},{5,9},{9,13},{13,1},{2,6},{6,10},{... | collective-permute-start | bytes 49160 | tf_op jit(solution)/shard_map/ppermute | solution.py:63
  59.4 1.2 %collective-permute-start.18 = (f32[2,2048]{1,0:T(2,128)S(1)}, f32[2,2048]{1,0:T(2,128)S(1)}, u32[]{:S(2)}, u32[]{:S(2)}) collective-permute-start(f32[2,2048]{1,0:T(2,128)S(1)} %pad_maximum_fusion.17), channel_id=1, source_target_pairs={{0,1},{1,0},{2,3},{3,2},{4,5},{5,4},{6,7},{7,6},{8,9},{9,8},{10,11... | collective-permute-start | bytes 49160 | tf_op jit(solution)/shard_map/ppermute | solution.py:44
  60.7 3.8 %collective-permute-start.21 = (f32[2,2048]{1,0:T(2,128)S(1)}, f32[2,2048]{1,0:T(2,128)S(1)}, u32[]{:S(2)}, u32[]{:S(2)}) collective-permute-start(f32[2,2048]{1,0:T(2,128)S(1)} %get-tuple-element.110), channel_id=1, source_target_pairs={{0,12},{4,0},{8,4},{12,8},{1,13},{5,1},{9,5},{13,9},{2,14},{6,2},{... | collective-permute-start | bytes 49160 | tf_op jit(solution)/shard_map/ppermute | solution.py:63
  62.2 4.6 %collective-permute-start.20 = (f32[2,2048]{1,0:T(2,128)S(1)}, f32[2,2048]{1,0:T(2,128)S(1)}, u32[]{:S(2)}, u32[]{:S(2)}) collective-permute-start(f32[2,2048]{1,0:T(2,128)S(1)} %get-tuple-element.110), channel_id=1, source_target_pairs={{0,8},{4,12},{8,0},{12,4},{1,9},{5,13},{9,1},{13,5},{2,10},{6,14},... | collective-permute-start | bytes 49160 | tf_op jit(solution)/shard_map/ppermute | solution.py:63
  62.4 5.5 %collective-permute-start.19 = (f32[2,2048]{1,0:T(2,128)S(1)}, f32[2,2048]{1,0:T(2,128)S(1)}, u32[]{:S(2)}, u32[]{:S(2)}) collective-permute-start(f32[2,2048]{1,0:T(2,128)S(1)} %get-tuple-element.110), channel_id=1, source_target_pairs={{0,4},{4,8},{8,12},{12,0},{1,5},{5,9},{9,13},{13,1},{2,6},{6,10},{... | collective-permute-start | bytes 49160 | tf_op jit(solution)/shard_map/ppermute | solution.py:63
  69.5 1.2 %collective-permute-start.22 = (f32[2,2048]{1,0:T(2,128)S(1)}, f32[2,2048]{1,0:T(2,128)S(1)}, u32[]{:S(2)}, u32[]{:S(2)}) collective-permute-start(f32[2,2048]{1,0:T(2,128)S(1)} %pad_maximum_fusion.19), channel_id=1, source_target_pairs={{0,1},{1,0},{2,3},{3,2},{4,5},{5,4},{6,7},{7,6},{8,9},{9,8},{10,11... | collective-permute-start | bytes 49160 | tf_op jit(solution)/shard_map/ppermute | solution.py:44
  70.9 3.8 %collective-permute-start.25 = (f32[2,2048]{1,0:T(2,128)S(1)}, f32[2,2048]{1,0:T(2,128)S(1)}, u32[]{:S(2)}, u32[]{:S(2)}) collective-permute-start(f32[2,2048]{1,0:T(2,128)S(1)} %get-tuple-element.108), channel_id=1, source_target_pairs={{0,12},{4,0},{8,4},{12,8},{1,13},{5,1},{9,5},{13,9},{2,14},{6,2},{... | collective-permute-start | bytes 49160 | tf_op jit(solution)/shard_map/ppermute | solution.py:63
  71.9 4.6 %collective-permute-start.24 = (f32[2,2048]{1,0:T(2,128)S(1)}, f32[2,2048]{1,0:T(2,128)S(1)}, u32[]{:S(2)}, u32[]{:S(2)}) collective-permute-start(f32[2,2048]{1,0:T(2,128)S(1)} %get-tuple-element.108), channel_id=1, source_target_pairs={{0,8},{4,12},{8,0},{12,4},{1,9},{5,13},{9,1},{13,5},{2,10},{6,14},... | collective-permute-start | bytes 49160 | tf_op jit(solution)/shard_map/ppermute | solution.py:63
  72.0 5.5 %collective-permute-start.23 = (f32[2,2048]{1,0:T(2,128)S(1)}, f32[2,2048]{1,0:T(2,128)S(1)}, u32[]{:S(2)}, u32[]{:S(2)}) collective-permute-start(f32[2,2048]{1,0:T(2,128)S(1)} %get-tuple-element.108), channel_id=1, source_target_pairs={{0,4},{4,8},{8,12},{12,0},{1,5},{5,9},{9,13},{13,1},{2,6},{6,10},{... | collective-permute-start | bytes 49160 | tf_op jit(solution)/shard_map/ppermute | solution.py:63
  79.1 1.2 %collective-permute-start.26 = (f32[2,2048]{1,0:T(2,128)S(1)}, f32[2,2048]{1,0:T(2,128)S(1)}, u32[]{:S(2)}, u32[]{:S(2)}) collective-permute-start(f32[2,2048]{1,0:T(2,128)S(1)} %pad_maximum_fusion.21), channel_id=1, source_target_pairs={{0,1},{1,0},{2,3},{3,2},{4,5},{5,4},{6,7},{7,6},{8,9},{9,8},{10,11... | collective-permute-start | bytes 49160 | tf_op jit(solution)/shard_map/ppermute | solution.py:44
  80.4 3.8 %collective-permute-start.29 = (f32[2,2048]{1,0:T(2,128)S(1)}, f32[2,2048]{1,0:T(2,128)S(1)}, u32[]{:S(2)}, u32[]{:S(2)}) collective-permute-start(f32[2,2048]{1,0:T(2,128)S(1)} %get-tuple-element.106), channel_id=1, source_target_pairs={{0,12},{4,0},{8,4},{12,8},{1,13},{5,1},{9,5},{13,9},{2,14},{6,2},{... | collective-permute-start | bytes 49160 | tf_op jit(solution)/shard_map/ppermute | solution.py:63
  82.0 4.8 %collective-permute-start.28 = (f32[2,2048]{1,0:T(2,128)S(1)}, f32[2,2048]{1,0:T(2,128)S(1)}, u32[]{:S(2)}, u32[]{:S(2)}) collective-permute-start(f32[2,2048]{1,0:T(2,128)S(1)} %get-tuple-element.106), channel_id=1, source_target_pairs={{0,8},{4,12},{8,0},{12,4},{1,9},{5,13},{9,1},{13,5},{2,10},{6,14},... | collective-permute-start | bytes 49160 | tf_op jit(solution)/shard_map/ppermute | solution.py:63
  82.0 5.5 %collective-permute-start.27 = (f32[2,2048]{1,0:T(2,128)S(1)}, f32[2,2048]{1,0:T(2,128)S(1)}, u32[]{:S(2)}, u32[]{:S(2)}) collective-permute-start(f32[2,2048]{1,0:T(2,128)S(1)} %get-tuple-element.106), channel_id=1, source_target_pairs={{0,4},{4,8},{8,12},{12,0},{1,5},{5,9},{9,13},{13,1},{2,6},{6,10},{... | collective-permute-start | bytes 49160 | tf_op jit(solution)/shard_map/ppermute | solution.py:63
  89.1 1.2 %collective-permute-start.30 = (f32[2,2048]{1,0:T(2,128)S(1)}, f32[2,2048]{1,0:T(2,128)S(1)}, u32[]{:S(2)}, u32[]{:S(2)}) collective-permute-start(f32[2,2048]{1,0:T(2,128)S(1)} %pad_maximum_fusion.23), channel_id=1, source_target_pairs={{0,1},{1,0},{2,3},{3,2},{4,5},{5,4},{6,7},{7,6},{8,9},{9,8},{10,11... | collective-permute-start | bytes 49160 | tf_op jit(solution)/shard_map/ppermute | solution.py:44
  90.5 3.8 %collective-permute-start.33 = (f32[2,2048]{1,0:T(2,128)S(1)}, f32[2,2048]{1,0:T(2,128)S(1)}, u32[]{:S(2)}, u32[]{:S(2)}) collective-permute-start(f32[2,2048]{1,0:T(2,128)S(1)} %get-tuple-element.104), channel_id=1, source_target_pairs={{0,12},{4,0},{8,4},{12,8},{1,13},{5,1},{9,5},{13,9},{2,14},{6,2},{... | collective-permute-start | bytes 49160 | tf_op jit(solution)/shard_map/ppermute | solution.py:63
  91.6 4.8 %collective-permute-start.32 = (f32[2,2048]{1,0:T(2,128)S(1)}, f32[2,2048]{1,0:T(2,128)S(1)}, u32[]{:S(2)}, u32[]{:S(2)}) collective-permute-start(f32[2,2048]{1,0:T(2,128)S(1)} %get-tuple-element.104), channel_id=1, source_target_pairs={{0,8},{4,12},{8,0},{12,4},{1,9},{5,13},{9,1},{13,5},{2,10},{6,14},... | collective-permute-start | bytes 49160 | tf_op jit(solution)/shard_map/ppermute | solution.py:63
  91.7 5.5 %collective-permute-start.31 = (f32[2,2048]{1,0:T(2,128)S(1)}, f32[2,2048]{1,0:T(2,128)S(1)}, u32[]{:S(2)}, u32[]{:S(2)}) collective-permute-start(f32[2,2048]{1,0:T(2,128)S(1)} %get-tuple-element.104), channel_id=1, source_target_pairs={{0,4},{4,8},{8,12},{12,0},{1,5},{5,9},{9,13},{13,1},{2,6},{6,10},{... | collective-permute-start | bytes 49160 | tf_op jit(solution)/shard_map/ppermute | solution.py:63
  100.6 1.4 %collective-permute-start.34 = (f32[4,128,66]{1,0,2:T(4,128)S(1)}, f32[4,128,66]{1,0,2:T(4,128)S(1)}, u32[]{:S(2)}, u32[]{:S(2)}) collective-permute-start(f32[4,128,66]{1,0,2:T(4,128)S(1)} %pad_maximum_fusion.1), channel_id=1, source_target_pairs={{0,1},{1,0},{2,3},{3,2},{4,5},{5,4},{6,7},{7,6},{8,9},{9,8},{10,11... | collective-permute-start | bytes 405512 | tf_op jit(solution)/shard_map/ppermute | solution.py:93
  102.2 4.0 %collective-permute-start.37 = (f32[128,66]{0,1:T(8,128)S(1)}, f32[128,66]{0,1:T(8,128)S(1)}, u32[]{:S(2)}, u32[]{:S(2)}) collective-permute-start(f32[128,66]{0,1:T(8,128)S(1)} %bitcast.229), channel_id=1, source_target_pairs={{0,12},{4,0},{8,4},{12,8},{1,13},{5,1},{9,5},{13,9},{2,14},{6,2},{... | collective-permute-start | bytes 101384 | tf_op jit(solution)/shard_map/ppermute | solution.py:143
  103.7 5.5 %collective-permute-start.36 = (f32[128,66]{0,1:T(8,128)S(1)}, f32[128,66]{0,1:T(8,128)S(1)}, u32[]{:S(2)}, u32[]{:S(2)}) collective-permute-start(f32[128,66]{0,1:T(8,128)S(1)} %bitcast.230), channel_id=1, source_target_pairs={{0,8},{4,12},{8,0},{12,4},{1,9},{5,13},{9,1},{13,5},{2,10},{6,14},... | collective-permute-start | bytes 101384 | tf_op jit(solution)/shard_map/ppermute | solution.py:143
  103.9 5.8 %collective-permute-start.35 = (f32[128,66]{0,1:T(8,128)S(1)}, f32[128,66]{0,1:T(8,128)S(1)}, u32[]{:S(2)}, u32[]{:S(2)}) collective-permute-start(f32[128,66]{0,1:T(8,128)S(1)} %bitcast.231), channel_id=1, source_target_pairs={{0,4},{4,8},{8,12},{12,0},{1,5},{5,9},{9,13},{13,1},{2,6},{6,10},{... | collective-permute-start | bytes 101384 | tf_op jit(solution)/shard_map/ppermute | solution.py:143

commit v8 on v7

--- a/solution.py
+++ b/solution.py
@@ -58,14 +58,18 @@
     index = lax.axis_index(axes)
     payload = jnp.stack([maxima, totals])
     received = [payload]
-    for shift in range(1, size):
-        perm = [(i, (i + shift) % size) for i in range(size)]
+    for mask in range(1, size):
+        if is_pow2(size):
+            perm = [(i, i ^ mask) for i in range(size)]
+        else:
+            perm = [(i, (i + mask) % size) for i in range(size)]
         received.append(lax.ppermute(payload, axes, perm))
     received = jnp.stack(received)
-    ordered = [
-        lax.dynamic_index_in_dim(received, (index - rank) % size, axis=0, keepdims=False)
-        for rank in range(size)
-    ]
+    if is_pow2(size):
+        slots = [index ^ rank for rank in range(size)]
+    else:
+        slots = [(index - rank) % size for rank in range(size)]
+    ordered = [lax.dynamic_index_in_dim(received, slot, axis=0, keepdims=False) for slot in slots]
     peak = ordered[0][0]
     for item in ordered[1:]:
         peak = jnp.maximum(peak, item[0])
@@ -138,8 +142,13 @@
     packed = jnp.concatenate([weighted, maxima[..., None], totals[..., None]], axis=-1)
     parts = [lax.dynamic_index_in_dim(packed, index, axis=0, keepdims=False)]
     for shift in range(1, size):
-        perm = [(i, (i + shift) % size) for i in range(size)]
-        send = lax.dynamic_index_in_dim(packed, (index + shift) % size, axis=0, keepdims=False)
+        if is_pow2(size):
+            perm = [(i, i ^ shift) for i in range(size)]
+            owner = index ^ shift
+        else:
+            perm = [(i, (i + shift) % size) for i in range(size)]
+            owner = (index + shift) % size
+        send = lax.dynamic_index_in_dim(packed, owner, axis=0, keepdims=False)
         parts.append(lax.ppermute(send, name, perm))
     top = parts[0][..., fates]
     for part in parts[1:]:

time: 111 us -> 109 us (0.982)
  waiting for transfers between devices: 52.2 us -> 39.8 us
  starting transfers between devices: 33.8 us -> 44.5 us
    ppermute x24, waiting for transfers between devices: 31.3 us -> 20.1 us  [lse_exchange(): received.append(lax.ppermute(payload, axes, perm))]
    ppermute x24, starting transfers between devices: 27.5 us -> 36.8 us  [lse_exchange(): received.append(lax.ppermute(payload, axes, perm))]
    ppermute x3, starting transfers between devices: 3.08 us -> 4.45 us  [lse_scatter_exchange(): parts.append(lax.ppermute(send, name, perm))]
    ppermute x3, waiting for transfers between devices: 3.74 us -> 2.52 us  [lse_scatter_exchange(): parts.append(lax.ppermute(send, name, perm))]
  transfers between devices with their start and end apart: 38 -> 38, of which waited for: 38 -> 33; matrix products, arithmetic and copies ran while one was open for 1% -> 1% of each run, Pallas kernels for 0% -> 0%
where the time goes in v8:
time: 109 us
  starting transfers between devices  44.5 us (41%)
  waiting for transfers between devices  39.8 us (37%)
  other arithmetic  16.9 us (16%)
  matrix products  5.18 us (5%)
  between operations  1.37 us (1%)
    ppermute x24, starting transfers between devices, lse_exchange(): received.append(lax.ppermute(payload, axes, perm))  36.8 us
    ppermute x24, waiting for transfers between devices, lse_exchange(): received.append(lax.ppermute(payload, axes, perm))  20.1 us
    ppermute x9, waiting for transfers between devices, lse_allreduce(): other = lax.ppermute(jnp.stack([maxima, totals]), name, perm)  10.5 us
    ppermute x1, waiting for transfers between devices, body(): theirs = lax.ppermute(mine, 'rows', [(0, 1), (1, 0)])  5.36 us
    ppermute x3, starting transfers between devices, lse_scatter_exchange(): parts.append(lax.ppermute(send, name, perm))  4.45 us
    dot_general x2, matrix products, pair_cost(): lax.dot_general(lhs_rows, rhs_rows, (((1,), (1,)), ((), ())), precision=l...  4.17 us
    reduce_sum x8, other arithmetic, body(): totals = jnp.sum(jnp.exp(scores - maxima[None, :]), axis=0)  3.83 us
    reduce_sum x8, other arithmetic, body(): totals = jnp.sum(jnp.exp(scores - maxima[:, None]), axis=1)  3.45 us
  transfers between devices with their start and end apart: 38, of which 33 were waited for; matrix products, arithmetic and copies ran while one was open for 1% of the time, Pallas kernels for 0%

profile of v8, /device:TPU:0, one launch (start us, length us, event | category | flops | bytes accessed | tf_op | source)
XLA Modules:
  0.0 108.8 jit_solution(17609031587149632519)
XLA Ops:
  2.2 1.0 multiply_reduce_fusion.1
  3.2 2.1 %subtract_reduce_fusion.16 = (f32[1024]{0:T(1024)S(1)}, f32[1024,256]{0,1:T(8,128)S(1)}) fusion(f32[256]{0:T(256)S(1)} %multiply_log_fusion, f32[1024,64]{0,1:T(8,128)} %param.5, f32[256,64]{0,1:T(8,128)} %param.7, f32[256]{0:T(256)S(1)} %multiply_reduce_fusion.2, f32[1024]{0:T(1024)S(1)} %multiply_reduce_fusion.1), kind=kOutput, calls=%fused_computation.39 | convolution fusion | flops 202898432 | bytes 1386496 | tf_op jit(solution)/shard_map/dot_general | solution.py:15
  7.1 5.0 %collective-permute-start.4 = (f32[2,1024]{1,0:T(2,128)S(1)}, f32[2,1024]{1,0:T(2,128)S(1)}, u32[]{:S(2)}, u32[]{:S(2)}) collective-permute-start(f32[2,1024]{1,0:T(2,128)S(1)} %get-tuple-element.120), channel_id=1, source_target_pairs={{0,12},{4,8},{8,4},{12,0},{1,13},{5,9},{9,5},{13,1},{2,14},{6,10},... | collective-permute-start | bytes 24584 | tf_op jit(solution)/shard_map/ppermute | solution.py:66
  12.8 1.0 collective-permute-done.4
  13.7 2.9 %collective-permute-done.3 = f32[2,1024]{1,0:T(2,128)S(1)} collective-permute-done((f32[2,1024]{1,0:T(2,128)S(1)}, f32[2,1024]{1,0:T(2,128)S(1)}, u32[]{:S(2)}, u32[]{:S(2)}) %collective-permute-start.3) | collective-permute-done | bytes 8224 | tf_op jit(solution)/shard_map/ppermute | solution.py:66
  17.3 1.6 %collective-permute-start.5 = (f32[2,256]{1,0:T(2,128)S(1)}, f32[2,256]{1,0:T(2,128)S(1)}, u32[]{:S(2)}, u32[]{:S(2)}) collective-permute-start(f32[2,256]{1,0:T(2,128)S(1)} %pad_maximum_fusion.28), channel_id=1, source_target_pairs={{0,2},{2,0},{1,3},{3,1},{4,6},{6,4},{5,7},{7,5},{8,10},{10,8},{9,1... | collective-permute-start | bytes 6152 | tf_op jit(solution)/shard_map/ppermute | solution.py:44
  19.5 1.5 %collective-permute-done.5 = f32[2,256]{1,0:T(2,128)S(1)} collective-permute-done((f32[2,256]{1,0:T(2,128)S(1)}, f32[2,256]{1,0:T(2,128)S(1)}, u32[]{:S(2)}, u32[]{:S(2)}) %collective-permute-start.5) | collective-permute-done | bytes 2080 | tf_op jit(solution)/shard_map/ppermute | solution.py:44
  21.0 5.4 %collective-permute-done = f32[1024,65]{0,1:T(8,128)S(1)} collective-permute-done((f32[1024,65]{0,1:T(8,128)S(1)}, f32[1024,65]{0,1:T(8,128)S(1)}, u32[]{:S(2)}, u32[]{:S(2)}) %collective-permute-start) | collective-permute-done | bytes 266272 | tf_op jit(solution)/shard_map/ppermute | solution.py:243
  26.5 2.0 %fusion.1 = f32[2048,256]{0,1:T(8,128)S(1)} fusion(f32[256,64]{0,1:T(8,128)S(1)} %copy-done.2, f32[256]{0:T(256)S(1)} %multiply_reduce_fusion.2, f32[2048]{0:T(1024)S(1)} %multiply_reduce_fusion, f32[1024,65]{0,1:T(8,128)S(1)} %get-tuple-element.13, f32[1024,65]{0,1:T(8,128)S(1)} %get-tuple-element.14), kind=kOutput, calls=%fused_computation.2 | convolution fusion | flops 404881408 | bytes 2704384 | tf_op jit(solution)/shard_map/dot_general | solution.py:15
  29.3 1.2 %collective-permute-done.6 = f32[2,2048]{1,0:T(2,128)S(1)} collective-permute-done((f32[2,2048]{1,0:T(2,128)S(1)}, f32[2,2048]{1,0:T(2,128)S(1)}, u32[]{:S(2)}, u32[]{:S(2)}) %collective-permute-start.6) | collective-permute-done | bytes 16416 | tf_op jit(solution)/shard_map/ppermute | solution.py:44
  30.6 1.8 %collective-permute-start.9 = (f32[2,2048]{1,0:T(2,128)S(1)}, f32[2,2048]{1,0:T(2,128)S(1)}, u32[]{:S(2)}, u32[]{:S(2)}) collective-permute-start(f32[2,2048]{1,0:T(2,128)S(1)} %get-tuple-element.116), channel_id=1, source_target_pairs={{0,12},{4,8},{8,4},{12,0},{1,13},{5,9},{9,5},{13,1},{2,14},{6,10},... | collective-permute-start | bytes 49160 | tf_op jit(solution)/shard_map/ppermute | solution.py:66
  32.4 2.6 %collective-permute-start.7 = (f32[2,2048]{1,0:T(2,128)S(1)}, f32[2,2048]{1,0:T(2,128)S(1)}, u32[]{:S(2)}, u32[]{:S(2)}) collective-permute-start(f32[2,2048]{1,0:T(2,128)S(1)} %get-tuple-element.116), channel_id=1, source_target_pairs={{0,4},{4,0},{8,12},{12,8},{1,5},{5,1},{9,13},{13,9},{2,6},{6,2},{1... | collective-permute-start | bytes 49160 | tf_op jit(solution)/shard_map/ppermute | solution.py:66
  35.0 1.2 %collective-permute-done.9 = f32[2,2048]{1,0:T(2,128)S(1)} collective-permute-done((f32[2,2048]{1,0:T(2,128)S(1)}, f32[2,2048]{1,0:T(2,128)S(1)}, u32[]{:S(2)}, u32[]{:S(2)}) %collective-permute-start.9) | collective-permute-done | bytes 16416 | tf_op jit(solution)/shard_map/ppermute | solution.py:66
  36.2 1.0 collective-permute-done.8
  38.8 1.2 %collective-permute-done.10 = f32[2,2048]{1,0:T(2,128)S(1)} collective-permute-done((f32[2,2048]{1,0:T(2,128)S(1)}, f32[2,2048]{1,0:T(2,128)S(1)}, u32[]{:S(2)}, u32[]{:S(2)}) %collective-permute-start.10) | collective-permute-done | bytes 16416 | tf_op jit(solution)/shard_map/ppermute | solution.py:44
  40.1 2.1 %collective-permute-start.13 = (f32[2,2048]{1,0:T(2,128)S(1)}, f32[2,2048]{1,0:T(2,128)S(1)}, u32[]{:S(2)}, u32[]{:S(2)}) collective-permute-start(f32[2,2048]{1,0:T(2,128)S(1)} %get-tuple-element.114), channel_id=1, source_target_pairs={{0,12},{4,8},{8,4},{12,0},{1,13},{5,9},{9,5},{13,1},{2,14},{6,10},... | collective-permute-start | bytes 49160 | tf_op jit(solution)/shard_map/ppermute | solution.py:66
  42.2 1.0 collective-permute-start.12
  43.2 1.3 %collective-permute-start.11 = (f32[2,2048]{1,0:T(2,128)S(1)}, f32[2,2048]{1,0:T(2,128)S(1)}, u32[]{:S(2)}, u32[]{:S(2)}) collective-permute-start(f32[2,2048]{1,0:T(2,128)S(1)} %get-tuple-element.114), channel_id=1, source_target_pairs={{0,4},{4,0},{8,12},{12,8},{1,5},{5,1},{9,13},{13,9},{2,6},{6,2},{1... | collective-permute-start | bytes 49160 | tf_op jit(solution)/shard_map/ppermute | solution.py:66
  44.5 1.2 %collective-permute-done.13 = f32[2,2048]{1,0:T(2,128)S(1)} collective-permute-done((f32[2,2048]{1,0:T(2,128)S(1)}, f32[2,2048]{1,0:T(2,128)S(1)}, u32[]{:S(2)}, u32[]{:S(2)}) %collective-permute-start.13) | collective-permute-done | bytes 16416 | tf_op jit(solution)/shard_map/ppermute | solution.py:66
  45.8 1.1 collective-permute-done.12
  48.7 1.2 %collective-permute-done.14 = f32[2,2048]{1,0:T(2,128)S(1)} collective-permute-done((f32[2,2048]{1,0:T(2,128)S(1)}, f32[2,2048]{1,0:T(2,128)S(1)}, u32[]{:S(2)}, u32[]{:S(2)}) %collective-permute-start.14) | collective-permute-done | bytes 16416 | tf_op jit(solution)/shard_map/ppermute | solution.py:44
  49.9 1.9 %collective-permute-start.17 = (f32[2,2048]{1,0:T(2,128)S(1)}, f32[2,2048]{1,0:T(2,128)S(1)}, u32[]{:S(2)}, u32[]{:S(2)}) collective-permute-start(f32[2,2048]{1,0:T(2,128)S(1)} %get-tuple-element.112), channel_id=1, source_target_pairs={{0,12},{4,8},{8,4},{12,0},{1,13},{5,9},{9,5},{13,1},{2,14},{6,10},... | collective-permute-start | bytes 49160 | tf_op jit(solution)/shard_map/ppermute | solution.py:66
  52.7 1.6 %collective-permute-start.15 = (f32[2,2048]{1,0:T(2,128)S(1)}, f32[2,2048]{1,0:T(2,128)S(1)}, u32[]{:S(2)}, u32[]{:S(2)}) collective-permute-start(f32[2,2048]{1,0:T(2,128)S(1)} %get-tuple-element.112), channel_id=1, source_target_pairs={{0,4},{4,0},{8,12},{12,8},{1,5},{5,1},{9,13},{13,9},{2,6},{6,2},{1... | collective-permute-start | bytes 49160 | tf_op jit(solution)/shard_map/ppermute | solution.py:66
  54.4 1.3 %collective-permute-done.17 = f32[2,2048]{1,0:T(2,128)S(1)} collective-permute-done((f32[2,2048]{1,0:T(2,128)S(1)}, f32[2,2048]{1,0:T(2,128)S(1)}, u32[]{:S(2)}, u32[]{:S(2)}) %collective-permute-start.17) | collective-permute-done | bytes 16416 | tf_op jit(solution)/shard_map/ppermute | solution.py:66
  58.3 1.2 %collective-permute-done.18 = f32[2,2048]{1,0:T(2,128)S(1)} collective-permute-done((f32[2,2048]{1,0:T(2,128)S(1)}, f32[2,2048]{1,0:T(2,128)S(1)}, u32[]{:S(2)}, u32[]{:S(2)}) %collective-permute-start.18) | collective-permute-done | bytes 16416 | tf_op jit(solution)/shard_map/ppermute | solution.py:44
  59.5 2.1 %collective-permute-start.21 = (f32[2,2048]{1,0:T(2,128)S(1)}, f32[2,2048]{1,0:T(2,128)S(1)}, u32[]{:S(2)}, u32[]{:S(2)}) collective-permute-start(f32[2,2048]{1,0:T(2,128)S(1)} %get-tuple-element.110), channel_id=1, source_target_pairs={{0,12},{4,8},{8,4},{12,0},{1,13},{5,9},{9,5},{13,1},{2,14},{6,10},... | collective-permute-start | bytes 49160 | tf_op jit(solution)/shard_map/ppermute | solution.py:66
  62.5 1.4 %collective-permute-start.19 = (f32[2,2048]{1,0:T(2,128)S(1)}, f32[2,2048]{1,0:T(2,128)S(1)}, u32[]{:S(2)}, u32[]{:S(2)}) collective-permute-start(f32[2,2048]{1,0:T(2,128)S(1)} %get-tuple-element.110), channel_id=1, source_target_pairs={{0,4},{4,0},{8,12},{12,8},{1,5},{5,1},{9,13},{13,9},{2,6},{6,2},{1... | collective-permute-start | bytes 49160 | tf_op jit(solution)/shard_map/ppermute | solution.py:66
  64.0 1.2 %collective-permute-done.21 = f32[2,2048]{1,0:T(2,128)S(1)} collective-permute-done((f32[2,2048]{1,0:T(2,128)S(1)}, f32[2,2048]{1,0:T(2,128)S(1)}, u32[]{:S(2)}, u32[]{:S(2)}) %collective-permute-start.21) | collective-permute-done | bytes 16416 | tf_op jit(solution)/shard_map/ppermute | solution.py:66
  65.1 1.1 %collective-permute-done.20 = f32[2,2048]{1,0:T(2,128)S(1)} collective-permute-done((f32[2,2048]{1,0:T(2,128)S(1)}, f32[2,2048]{1,0:T(2,128)S(1)}, u32[]{:S(2)}, u32[]{:S(2)}) %collective-permute-start.20) | collective-permute-done | bytes 16416 | tf_op jit(solution)/shard_map/ppermute | solution.py:66
  68.3 1.2 %collective-permute-done.22 = f32[2,2048]{1,0:T(2,128)S(1)} collective-permute-done((f32[2,2048]{1,0:T(2,128)S(1)}, f32[2,2048]{1,0:T(2,128)S(1)}, u32[]{:S(2)}, u32[]{:S(2)}) %collective-permute-start.22) | collective-permute-done | bytes 16416 | tf_op jit(solution)/shard_map/ppermute | solution.py:44
  69.5 1.9 %collective-permute-start.25 = (f32[2,2048]{1,0:T(2,128)S(1)}, f32[2,2048]{1,0:T(2,128)S(1)}, u32[]{:S(2)}, u32[]{:S(2)}) collective-permute-start(f32[2,2048]{1,0:T(2,128)S(1)} %get-tuple-element.108), channel_id=1, source_target_pairs={{0,12},{4,8},{8,4},{12,0},{1,13},{5,9},{9,5},{13,1},{2,14},{6,10},... | collective-permute-start | bytes 49160 | tf_op jit(solution)/shard_map/ppermute | solution.py:66
  72.3 1.6 %collective-permute-start.23 = (f32[2,2048]{1,0:T(2,128)S(1)}, f32[2,2048]{1,0:T(2,128)S(1)}, u32[]{:S(2)}, u32[]{:S(2)}) collective-permute-start(f32[2,2048]{1,0:T(2,128)S(1)} %get-tuple-element.108), channel_id=1, source_target_pairs={{0,4},{4,0},{8,12},{12,8},{1,5},{5,1},{9,13},{13,9},{2,6},{6,2},{1... | collective-permute-start | bytes 49160 | tf_op jit(solution)/shard_map/ppermute | solution.py:66
  74.0 1.3 %collective-permute-done.25 = f32[2,2048]{1,0:T(2,128)S(1)} collective-permute-done((f32[2,2048]{1,0:T(2,128)S(1)}, f32[2,2048]{1,0:T(2,128)S(1)}, u32[]{:S(2)}, u32[]{:S(2)}) %collective-permute-start.25) | collective-permute-done | bytes 16416 | tf_op jit(solution)/shard_map/ppermute | solution.py:66
  77.8 1.2 %collective-permute-done.26 = f32[2,2048]{1,0:T(2,128)S(1)} collective-permute-done((f32[2,2048]{1,0:T(2,128)S(1)}, f32[2,2048]{1,0:T(2,128)S(1)}, u32[]{:S(2)}, u32[]{:S(2)}) %collective-permute-start.26) | collective-permute-done | bytes 16416 | tf_op jit(solution)/shard_map/ppermute | solution.py:44
  79.1 2.1 %collective-permute-start.29 = (f32[2,2048]{1,0:T(2,128)S(1)}, f32[2,2048]{1,0:T(2,128)S(1)}, u32[]{:S(2)}, u32[]{:S(2)}) collective-permute-start(f32[2,2048]{1,0:T(2,128)S(1)} %get-tuple-element.106), channel_id=1, source_target_pairs={{0,12},{4,8},{8,4},{12,0},{1,13},{5,9},{9,5},{13,1},{2,14},{6,10},... | collective-permute-start | bytes 49160 | tf_op jit(solution)/shard_map/ppermute | solution.py:66
  82.1 1.4 %collective-permute-start.27 = (f32[2,2048]{1,0:T(2,128)S(1)}, f32[2,2048]{1,0:T(2,128)S(1)}, u32[]{:S(2)}, u32[]{:S(2)}) collective-permute-start(f32[2,2048]{1,0:T(2,128)S(1)} %get-tuple-element.106), channel_id=1, source_target_pairs={{0,4},{4,0},{8,12},{12,8},{1,5},{5,1},{9,13},{13,9},{2,6},{6,2},{1... | collective-permute-start | bytes 49160 | tf_op jit(solution)/shard_map/ppermute | solution.py:66
  83.5 1.2 %collective-permute-done.29 = f32[2,2048]{1,0:T(2,128)S(1)} collective-permute-done((f32[2,2048]{1,0:T(2,128)S(1)}, f32[2,2048]{1,0:T(2,128)S(1)}, u32[]{:S(2)}, u32[]{:S(2)}) %collective-permute-start.29) | collective-permute-done | bytes 16416 | tf_op jit(solution)/shard_map/ppermute | solution.py:66
  84.7 1.1 %collective-permute-done.28 = f32[2,2048]{1,0:T(2,128)S(1)} collective-permute-done((f32[2,2048]{1,0:T(2,128)S(1)}, f32[2,2048]{1,0:T(2,128)S(1)}, u32[]{:S(2)}, u32[]{:S(2)}) %collective-permute-start.28) | collective-permute-done | bytes 16416 | tf_op jit(solution)/shard_map/ppermute | solution.py:66
  87.7 1.2 %collective-permute-done.30 = f32[2,2048]{1,0:T(2,128)S(1)} collective-permute-done((f32[2,2048]{1,0:T(2,128)S(1)}, f32[2,2048]{1,0:T(2,128)S(1)}, u32[]{:S(2)}, u32[]{:S(2)}) %collective-permute-start.30) | collective-permute-done | bytes 16416 | tf_op jit(solution)/shard_map/ppermute | solution.py:44
  88.9 1.9 %collective-permute-start.33 = (f32[2,2048]{1,0:T(2,128)S(1)}, f32[2,2048]{1,0:T(2,128)S(1)}, u32[]{:S(2)}, u32[]{:S(2)}) collective-permute-start(f32[2,2048]{1,0:T(2,128)S(1)} %get-tuple-element.104), channel_id=1, source_target_pairs={{0,12},{4,8},{8,4},{12,0},{1,13},{5,9},{9,5},{13,1},{2,14},{6,10},... | collective-permute-start | bytes 49160 | tf_op jit(solution)/shard_map/ppermute | solution.py:66
  91.7 1.6 %collective-permute-start.31 = (f32[2,2048]{1,0:T(2,128)S(1)}, f32[2,2048]{1,0:T(2,128)S(1)}, u32[]{:S(2)}, u32[]{:S(2)}) collective-permute-start(f32[2,2048]{1,0:T(2,128)S(1)} %get-tuple-element.104), channel_id=1, source_target_pairs={{0,4},{4,0},{8,12},{12,8},{1,5},{5,1},{9,13},{13,9},{2,6},{6,2},{1... | collective-permute-start | bytes 49160 | tf_op jit(solution)/shard_map/ppermute | solution.py:66
  93.4 1.3 %collective-permute-done.33 = f32[2,2048]{1,0:T(2,128)S(1)} collective-permute-done((f32[2,2048]{1,0:T(2,128)S(1)}, f32[2,2048]{1,0:T(2,128)S(1)}, u32[]{:S(2)}, u32[]{:S(2)}) %collective-permute-start.33) | collective-permute-done | bytes 16416 | tf_op jit(solution)/shard_map/ppermute | solution.py:66
  97.5 1.0 fusion.5
  99.0 1.3 %collective-permute-done.34 = f32[4,128,66]{1,0,2:T(4,128)S(1)} collective-permute-done((f32[4,128,66]{1,0,2:T(4,128)S(1)}, f32[4,128,66]{1,0,2:T(4,128)S(1)}, u32[]{:S(2)}, u32[]{:S(2)}) %collective-permute-start.34) | collective-permute-done | bytes 135200 | tf_op jit(solution)/shard_map/ppermute | solution.py:97
  100.6 2.1 %collective-permute-start.37 = (f32[128,66]{0,1:T(8,128)S(1)}, f32[128,66]{0,1:T(8,128)S(1)}, u32[]{:S(2)}, u32[]{:S(2)}) collective-permute-start(f32[128,66]{0,1:T(8,128)S(1)} %bitcast.229), channel_id=1, source_target_pairs={{0,12},{4,8},{8,4},{12,0},{1,13},{5,9},{9,5},{13,1},{2,14},{6,10},... | collective-permute-start | bytes 101384 | tf_op jit(solution)/shard_map/ppermute | solution.py:152
  103.6 1.4 %collective-permute-start.35 = (f32[128,66]{0,1:T(8,128)S(1)}, f32[128,66]{0,1:T(8,128)S(1)}, u32[]{:S(2)}, u32[]{:S(2)}) collective-permute-start(f32[128,66]{0,1:T(8,128)S(1)} %bitcast.231), channel_id=1, source_target_pairs={{0,4},{4,0},{8,12},{12,8},{1,5},{5,1},{9,13},{13,9},{2,6},{6,2},{1... | collective-permute-start | bytes 101384 | tf_op jit(solution)/shard_map/ppermute | solution.py:152
  105.6 1.0 collective-permute-done.37
  106.6 1.4 %collective-permute-done.36 = f32[128,66]{0,1:T(8,128)S(1)} collective-permute-done((f32[128,66]{0,1:T(8,128)S(1)}, f32[128,66]{0,1:T(8,128)S(1)}, u32[]{:S(2)}, u32[]{:S(2)}) %collective-permute-start.36) | collective-permute-done | bytes 33824 | tf_op jit(solution)/shard_map/ppermute | solution.py:152
  (159 shorter events, 29.3 us)
Async XLA Ops:
  0.6 96.9 %copy-start = (f32[256,64]{0,1:T(8,128)S(1)}, f32[256,64]{0,1:T(8,128)}, u32[]{:S(2)}) copy-start(f32[256,64]{0,1:T(8,128)} %param.9) | copy-start | bytes 196612
  0.6 16.1 %copy-start.4 = (f32[1024]{0:T(1024)S(1)}, f32[1024]{0:T(1024)}, u32[]{:S(2)}) copy-start(f32[1024]{0:T(1024)} %param.6) | copy-start | bytes 12292
  5.4 13.5 %copy-start.1 = (f32[1024,64]{0,1:T(8,128)S(1)}, f32[1024,64]{0,1:T(8,128)}, u32[]{:S(2)}) copy-start(f32[1024,64]{0,1:T(8,128)} %param.5) | copy-start | bytes 786436
  5.4 15.6 %copy-start.3 = (f32[256]{0:T(256)S(1)}, f32[256]{0:T(256)}, u32[]{:S(2)}) copy-start(f32[256]{0:T(256)} %param.8) | copy-start | bytes 3076
  5.7 1.4 %collective-permute-start.1 = (f32[2,1024]{1,0:T(2,128)S(1)}, f32[2,1024]{1,0:T(2,128)S(1)}, u32[]{:S(2)}, u32[]{:S(2)}) collective-permute-start(f32[2,1024]{1,0:T(2,128)S(1)} %pad_maximum_fusion.26), channel_id=1, source_target_pairs={{0,1},{1,0},{2,3},{3,2},{4,5},{5,4},{6,7},{7,6},{8,9},{9,8},{10,11... | collective-permute-start | bytes 24584 | tf_op jit(solution)/shard_map/ppermute | solution.py:44
  7.1 6.6 %collective-permute-start.4 = (f32[2,1024]{1,0:T(2,128)S(1)}, f32[2,1024]{1,0:T(2,128)S(1)}, u32[]{:S(2)}, u32[]{:S(2)}) collective-permute-start(f32[2,1024]{1,0:T(2,128)S(1)} %get-tuple-element.120), channel_id=1, source_target_pairs={{0,12},{4,8},{8,4},{12,0},{1,13},{5,9},{9,5},{13,1},{2,14},{6,10},... | collective-permute-start | bytes 24584 | tf_op jit(solution)/shard_map/ppermute | solution.py:66
  12.1 4.5 %collective-permute-start.3 = (f32[2,1024]{1,0:T(2,128)S(1)}, f32[2,1024]{1,0:T(2,128)S(1)}, u32[]{:S(2)}, u32[]{:S(2)}) collective-permute-start(f32[2,1024]{1,0:T(2,128)S(1)} %get-tuple-element.120), channel_id=1, source_target_pairs={{0,8},{4,12},{8,0},{12,4},{1,9},{5,13},{9,1},{13,5},{2,10},{6,14},... | collective-permute-start | bytes 24584 | tf_op jit(solution)/shard_map/ppermute | solution.py:66
  12.1 4.5 %collective-permute-start.2 = (f32[2,1024]{1,0:T(2,128)S(1)}, f32[2,1024]{1,0:T(2,128)S(1)}, u32[]{:S(2)}, u32[]{:S(2)}) collective-permute-start(f32[2,1024]{1,0:T(2,128)S(1)} %get-tuple-element.120), channel_id=1, source_target_pairs={{0,4},{4,0},{8,12},{12,8},{1,5},{5,1},{9,13},{13,9},{2,6},{6,2},{1... | collective-permute-start | bytes 24584 | tf_op jit(solution)/shard_map/ppermute | solution.py:66
  16.9 9.6 %copy-start.2 = (f32[256,64]{0,1:T(8,128)S(1)}, f32[256,64]{0,1:T(8,128)}, u32[]{:S(2)}) copy-start(f32[256,64]{0,1:T(8,128)} %param.7) | copy-start | bytes 196612
  17.3 3.7 %collective-permute-start.5 = (f32[2,256]{1,0:T(2,128)S(1)}, f32[2,256]{1,0:T(2,128)S(1)}, u32[]{:S(2)}, u32[]{:S(2)}) collective-permute-start(f32[2,256]{1,0:T(2,128)S(1)} %pad_maximum_fusion.28), channel_id=1, source_target_pairs={{0,2},{2,0},{1,3},{3,1},{4,6},{6,4},{5,7},{7,5},{8,10},{10,8},{9,1... | collective-permute-start | bytes 6152 | tf_op jit(solution)/shard_map/ppermute | solution.py:44
  18.9 7.5 %collective-permute-start = (f32[1024,65]{0,1:T(8,128)S(1)}, f32[1024,65]{0,1:T(8,128)S(1)}, u32[]{:S(2)}, u32[]{:S(2)}) collective-permute-start(f32[1024,65]{0,1:T(8,128)S(1)} %pad_maximum_fusion), channel_id=1, source_target_pairs={{0,2},{2,0},{1,3},{3,1},{4,6},{6,4},{5,7},{7,5},{8,10},{10,8},{9,1... | collective-permute-start | bytes 798728 | tf_op jit(solution)/shard_map/ppermute | solution.py:243
  29.2 1.2 %collective-permute-start.6 = (f32[2,2048]{1,0:T(2,128)S(1)}, f32[2,2048]{1,0:T(2,128)S(1)}, u32[]{:S(2)}, u32[]{:S(2)}) collective-permute-start(f32[2,2048]{1,0:T(2,128)S(1)} %pad_maximum_fusion.11), channel_id=1, source_target_pairs={{0,1},{1,0},{2,3},{3,2},{4,5},{5,4},{6,7},{7,6},{8,9},{9,8},{10,11... | collective-permute-start | bytes 49160 | tf_op jit(solution)/shard_map/ppermute | solution.py:44
  30.6 5.6 %collective-permute-start.9 = (f32[2,2048]{1,0:T(2,128)S(1)}, f32[2,2048]{1,0:T(2,128)S(1)}, u32[]{:S(2)}, u32[]{:S(2)}) collective-permute-start(f32[2,2048]{1,0:T(2,128)S(1)} %get-tuple-element.116), channel_id=1, source_target_pairs={{0,12},{4,8},{8,4},{12,0},{1,13},{5,9},{9,5},{13,1},{2,14},{6,10},... | collective-permute-start | bytes 49160 | tf_op jit(solution)/shard_map/ppermute | solution.py:66
  32.4 4.8 %collective-permute-start.8 = (f32[2,2048]{1,0:T(2,128)S(1)}, f32[2,2048]{1,0:T(2,128)S(1)}, u32[]{:S(2)}, u32[]{:S(2)}) collective-permute-start(f32[2,2048]{1,0:T(2,128)S(1)} %get-tuple-element.116), channel_id=1, source_target_pairs={{0,8},{4,12},{8,0},{12,4},{1,9},{5,13},{9,1},{13,5},{2,10},{6,14},... | collective-permute-start | bytes 49160 | tf_op jit(solution)/shard_map/ppermute | solution.py:66
  32.4 4.7 %collective-permute-start.7 = (f32[2,2048]{1,0:T(2,128)S(1)}, f32[2,2048]{1,0:T(2,128)S(1)}, u32[]{:S(2)}, u32[]{:S(2)}) collective-permute-start(f32[2,2048]{1,0:T(2,128)S(1)} %get-tuple-element.116), channel_id=1, source_target_pairs={{0,4},{4,0},{8,12},{12,8},{1,5},{5,1},{9,13},{13,9},{2,6},{6,2},{1... | collective-permute-start | bytes 49160 | tf_op jit(solution)/shard_map/ppermute | solution.py:66
  38.8 1.2 %collective-permute-start.10 = (f32[2,2048]{1,0:T(2,128)S(1)}, f32[2,2048]{1,0:T(2,128)S(1)}, u32[]{:S(2)}, u32[]{:S(2)}) collective-permute-start(f32[2,2048]{1,0:T(2,128)S(1)} %pad_maximum_fusion.13), channel_id=1, source_target_pairs={{0,1},{1,0},{2,3},{3,2},{4,5},{5,4},{6,7},{7,6},{8,9},{9,8},{10,11... | collective-permute-start | bytes 49160 | tf_op jit(solution)/shard_map/ppermute | solution.py:44
  40.1 5.7 %collective-permute-start.13 = (f32[2,2048]{1,0:T(2,128)S(1)}, f32[2,2048]{1,0:T(2,128)S(1)}, u32[]{:S(2)}, u32[]{:S(2)}) collective-permute-start(f32[2,2048]{1,0:T(2,128)S(1)} %get-tuple-element.114), channel_id=1, source_target_pairs={{0,12},{4,8},{8,4},{12,0},{1,13},{5,9},{9,5},{13,1},{2,14},{6,10},... | collective-permute-start | bytes 49160 | tf_op jit(solution)/shard_map/ppermute | solution.py:66
  42.2 4.7 %collective-permute-start.12 = (f32[2,2048]{1,0:T(2,128)S(1)}, f32[2,2048]{1,0:T(2,128)S(1)}, u32[]{:S(2)}, u32[]{:S(2)}) collective-permute-start(f32[2,2048]{1,0:T(2,128)S(1)} %get-tuple-element.114), channel_id=1, source_target_pairs={{0,8},{4,12},{8,0},{12,4},{1,9},{5,13},{9,1},{13,5},{2,10},{6,14},... | collective-permute-start | bytes 49160 | tf_op jit(solution)/shard_map/ppermute | solution.py:66
  43.2 3.8 %collective-permute-start.11 = (f32[2,2048]{1,0:T(2,128)S(1)}, f32[2,2048]{1,0:T(2,128)S(1)}, u32[]{:S(2)}, u32[]{:S(2)}) collective-permute-start(f32[2,2048]{1,0:T(2,128)S(1)} %get-tuple-element.114), channel_id=1, source_target_pairs={{0,4},{4,0},{8,12},{12,8},{1,5},{5,1},{9,13},{13,9},{2,6},{6,2},{1... | collective-permute-start | bytes 49160 | tf_op jit(solution)/shard_map/ppermute | solution.py:66
  48.6 1.2 %collective-permute-start.14 = (f32[2,2048]{1,0:T(2,128)S(1)}, f32[2,2048]{1,0:T(2,128)S(1)}, u32[]{:S(2)}, u32[]{:S(2)}) collective-permute-start(f32[2,2048]{1,0:T(2,128)S(1)} %pad_maximum_fusion.15), channel_id=1, source_target_pairs={{0,1},{1,0},{2,3},{3,2},{4,5},{5,4},{6,7},{7,6},{8,9},{9,8},{10,11... | collective-permute-start | bytes 49160 | tf_op jit(solution)/shard_map/ppermute | solution.py:44
  49.9 5.7 %collective-permute-start.17 = (f32[2,2048]{1,0:T(2,128)S(1)}, f32[2,2048]{1,0:T(2,128)S(1)}, u32[]{:S(2)}, u32[]{:S(2)}) collective-permute-start(f32[2,2048]{1,0:T(2,128)S(1)} %get-tuple-element.112), channel_id=1, source_target_pairs={{0,12},{4,8},{8,4},{12,0},{1,13},{5,9},{9,5},{13,1},{2,14},{6,10},... | collective-permute-start | bytes 49160 | tf_op jit(solution)/shard_map/ppermute | solution.py:66
  51.8 4.8 %collective-permute-start.16 = (f32[2,2048]{1,0:T(2,128)S(1)}, f32[2,2048]{1,0:T(2,128)S(1)}, u32[]{:S(2)}, u32[]{:S(2)}) collective-permute-start(f32[2,2048]{1,0:T(2,128)S(1)} %get-tuple-element.112), channel_id=1, source_target_pairs={{0,8},{4,12},{8,0},{12,4},{1,9},{5,13},{9,1},{13,5},{2,10},{6,14},... | collective-permute-start | bytes 49160 | tf_op jit(solution)/shard_map/ppermute | solution.py:66
  52.7 3.9 %collective-permute-start.15 = (f32[2,2048]{1,0:T(2,128)S(1)}, f32[2,2048]{1,0:T(2,128)S(1)}, u32[]{:S(2)}, u32[]{:S(2)}) collective-permute-start(f32[2,2048]{1,0:T(2,128)S(1)} %get-tuple-element.112), channel_id=1, source_target_pairs={{0,4},{4,0},{8,12},{12,8},{1,5},{5,1},{9,13},{13,9},{2,6},{6,2},{1... | collective-permute-start | bytes 49160 | tf_op jit(solution)/shard_map/ppermute | solution.py:66
  58.2 1.2 %collective-permute-start.18 = (f32[2,2048]{1,0:T(2,128)S(1)}, f32[2,2048]{1,0:T(2,128)S(1)}, u32[]{:S(2)}, u32[]{:S(2)}) collective-permute-start(f32[2,2048]{1,0:T(2,128)S(1)} %pad_maximum_fusion.17), channel_id=1, source_target_pairs={{0,1},{1,0},{2,3},{3,2},{4,5},{5,4},{6,7},{7,6},{8,9},{9,8},{10,11... | collective-permute-start | bytes 49160 | tf_op jit(solution)/shard_map/ppermute | solution.py:44
  59.5 5.6 %collective-permute-start.21 = (f32[2,2048]{1,0:T(2,128)S(1)}, f32[2,2048]{1,0:T(2,128)S(1)}, u32[]{:S(2)}, u32[]{:S(2)}) collective-permute-start(f32[2,2048]{1,0:T(2,128)S(1)} %get-tuple-element.110), channel_id=1, source_target_pairs={{0,12},{4,8},{8,4},{12,0},{1,13},{5,9},{9,5},{13,1},{2,14},{6,10},... | collective-permute-start | bytes 49160 | tf_op jit(solution)/shard_map/ppermute | solution.py:66
  61.6 4.6 %collective-permute-start.20 = (f32[2,2048]{1,0:T(2,128)S(1)}, f32[2,2048]{1,0:T(2,128)S(1)}, u32[]{:S(2)}, u32[]{:S(2)}) collective-permute-start(f32[2,2048]{1,0:T(2,128)S(1)} %get-tuple-element.110), channel_id=1, source_target_pairs={{0,8},{4,12},{8,0},{12,4},{1,9},{5,13},{9,1},{13,5},{2,10},{6,14},... | collective-permute-start | bytes 49160 | tf_op jit(solution)/shard_map/ppermute | solution.py:66
  62.5 3.9 %collective-permute-start.19 = (f32[2,2048]{1,0:T(2,128)S(1)}, f32[2,2048]{1,0:T(2,128)S(1)}, u32[]{:S(2)}, u32[]{:S(2)}) collective-permute-start(f32[2,2048]{1,0:T(2,128)S(1)} %get-tuple-element.110), channel_id=1, source_target_pairs={{0,4},{4,0},{8,12},{12,8},{1,5},{5,1},{9,13},{13,9},{2,6},{6,2},{1... | collective-permute-start | bytes 49160 | tf_op jit(solution)/shard_map/ppermute | solution.py:66
  68.2 1.2 %collective-permute-start.22 = (f32[2,2048]{1,0:T(2,128)S(1)}, f32[2,2048]{1,0:T(2,128)S(1)}, u32[]{:S(2)}, u32[]{:S(2)}) collective-permute-start(f32[2,2048]{1,0:T(2,128)S(1)} %pad_maximum_fusion.19), channel_id=1, source_target_pairs={{0,1},{1,0},{2,3},{3,2},{4,5},{5,4},{6,7},{7,6},{8,9},{9,8},{10,11... | collective-permute-start | bytes 49160 | tf_op jit(solution)/shard_map/ppermute | solution.py:44
  69.5 5.7 %collective-permute-start.25 = (f32[2,2048]{1,0:T(2,128)S(1)}, f32[2,2048]{1,0:T(2,128)S(1)}, u32[]{:S(2)}, u32[]{:S(2)}) collective-permute-start(f32[2,2048]{1,0:T(2,128)S(1)} %get-tuple-element.108), channel_id=1, source_target_pairs={{0,12},{4,8},{8,4},{12,0},{1,13},{5,9},{9,5},{13,1},{2,14},{6,10},... | collective-permute-start | bytes 49160 | tf_op jit(solution)/shard_map/ppermute | solution.py:66
  71.4 4.8 %collective-permute-start.24 = (f32[2,2048]{1,0:T(2,128)S(1)}, f32[2,2048]{1,0:T(2,128)S(1)}, u32[]{:S(2)}, u32[]{:S(2)}) collective-permute-start(f32[2,2048]{1,0:T(2,128)S(1)} %get-tuple-element.108), channel_id=1, source_target_pairs={{0,8},{4,12},{8,0},{12,4},{1,9},{5,13},{9,1},{13,5},{2,10},{6,14},... | collective-permute-start | bytes 49160 | tf_op jit(solution)/shard_map/ppermute | solution.py:66
  72.3 3.9 %collective-permute-start.23 = (f32[2,2048]{1,0:T(2,128)S(1)}, f32[2,2048]{1,0:T(2,128)S(1)}, u32[]{:S(2)}, u32[]{:S(2)}) collective-permute-start(f32[2,2048]{1,0:T(2,128)S(1)} %get-tuple-element.108), channel_id=1, source_target_pairs={{0,4},{4,0},{8,12},{12,8},{1,5},{5,1},{9,13},{13,9},{2,6},{6,2},{1... | collective-permute-start | bytes 49160 | tf_op jit(solution)/shard_map/ppermute | solution.py:66
  77.8 1.2 %collective-permute-start.26 = (f32[2,2048]{1,0:T(2,128)S(1)}, f32[2,2048]{1,0:T(2,128)S(1)}, u32[]{:S(2)}, u32[]{:S(2)}) collective-permute-start(f32[2,2048]{1,0:T(2,128)S(1)} %pad_maximum_fusion.21), channel_id=1, source_target_pairs={{0,1},{1,0},{2,3},{3,2},{4,5},{5,4},{6,7},{7,6},{8,9},{9,8},{10,11... | collective-permute-start | bytes 49160 | tf_op jit(solution)/shard_map/ppermute | solution.py:44
  79.1 5.6 %collective-permute-start.29 = (f32[2,2048]{1,0:T(2,128)S(1)}, f32[2,2048]{1,0:T(2,128)S(1)}, u32[]{:S(2)}, u32[]{:S(2)}) collective-permute-start(f32[2,2048]{1,0:T(2,128)S(1)} %get-tuple-element.106), channel_id=1, source_target_pairs={{0,12},{4,8},{8,4},{12,0},{1,13},{5,9},{9,5},{13,1},{2,14},{6,10},... | collective-permute-start | bytes 49160 | tf_op jit(solution)/shard_map/ppermute | solution.py:66
  81.2 4.6 %collective-permute-start.28 = (f32[2,2048]{1,0:T(2,128)S(1)}, f32[2,2048]{1,0:T(2,128)S(1)}, u32[]{:S(2)}, u32[]{:S(2)}) collective-permute-start(f32[2,2048]{1,0:T(2,128)S(1)} %get-tuple-element.106), channel_id=1, source_target_pairs={{0,8},{4,12},{8,0},{12,4},{1,9},{5,13},{9,1},{13,5},{2,10},{6,14},... | collective-permute-start | bytes 49160 | tf_op jit(solution)/shard_map/ppermute | solution.py:66
  82.1 3.9 %collective-permute-start.27 = (f32[2,2048]{1,0:T(2,128)S(1)}, f32[2,2048]{1,0:T(2,128)S(1)}, u32[]{:S(2)}, u32[]{:S(2)}) collective-permute-start(f32[2,2048]{1,0:T(2,128)S(1)} %get-tuple-element.106), channel_id=1, source_target_pairs={{0,4},{4,0},{8,12},{12,8},{1,5},{5,1},{9,13},{13,9},{2,6},{6,2},{1... | collective-permute-start | bytes 49160 | tf_op jit(solution)/shard_map/ppermute | solution.py:66
  87.6 1.2 %collective-permute-start.30 = (f32[2,2048]{1,0:T(2,128)S(1)}, f32[2,2048]{1,0:T(2,128)S(1)}, u32[]{:S(2)}, u32[]{:S(2)}) collective-permute-start(f32[2,2048]{1,0:T(2,128)S(1)} %pad_maximum_fusion.23), channel_id=1, source_target_pairs={{0,1},{1,0},{2,3},{3,2},{4,5},{5,4},{6,7},{7,6},{8,9},{9,8},{10,11... | collective-permute-start | bytes 49160 | tf_op jit(solution)/shard_map/ppermute | solution.py:44
  88.9 5.7 %collective-permute-start.33 = (f32[2,2048]{1,0:T(2,128)S(1)}, f32[2,2048]{1,0:T(2,128)S(1)}, u32[]{:S(2)}, u32[]{:S(2)}) collective-permute-start(f32[2,2048]{1,0:T(2,128)S(1)} %get-tuple-element.104), channel_id=1, source_target_pairs={{0,12},{4,8},{8,4},{12,0},{1,13},{5,9},{9,5},{13,1},{2,14},{6,10},... | collective-permute-start | bytes 49160 | tf_op jit(solution)/shard_map/ppermute | solution.py:66
  90.8 4.8 %collective-permute-start.32 = (f32[2,2048]{1,0:T(2,128)S(1)}, f32[2,2048]{1,0:T(2,128)S(1)}, u32[]{:S(2)}, u32[]{:S(2)}) collective-permute-start(f32[2,2048]{1,0:T(2,128)S(1)} %get-tuple-element.104), channel_id=1, source_target_pairs={{0,8},{4,12},{8,0},{12,4},{1,9},{5,13},{9,1},{13,5},{2,10},{6,14},... | collective-permute-start | bytes 49160 | tf_op jit(solution)/shard_map/ppermute | solution.py:66
  91.7 3.9 %collective-permute-start.31 = (f32[2,2048]{1,0:T(2,128)S(1)}, f32[2,2048]{1,0:T(2,128)S(1)}, u32[]{:S(2)}, u32[]{:S(2)}) collective-permute-start(f32[2,2048]{1,0:T(2,128)S(1)} %get-tuple-element.104), channel_id=1, source_target_pairs={{0,4},{4,0},{8,12},{12,8},{1,5},{5,1},{9,13},{13,9},{2,6},{6,2},{1... | collective-permute-start | bytes 49160 | tf_op jit(solution)/shard_map/ppermute | solution.py:66
  98.9 1.4 %collective-permute-start.34 = (f32[4,128,66]{1,0,2:T(4,128)S(1)}, f32[4,128,66]{1,0,2:T(4,128)S(1)}, u32[]{:S(2)}, u32[]{:S(2)}) collective-permute-start(f32[4,128,66]{1,0,2:T(4,128)S(1)} %pad_maximum_fusion.1), channel_id=1, source_target_pairs={{0,1},{1,0},{2,3},{3,2},{4,5},{5,4},{6,7},{7,6},{8,9},{9,8},{10,11... | collective-permute-start | bytes 405512 | tf_op jit(solution)/shard_map/ppermute | solution.py:97
  100.6 6.1 %collective-permute-start.37 = (f32[128,66]{0,1:T(8,128)S(1)}, f32[128,66]{0,1:T(8,128)S(1)}, u32[]{:S(2)}, u32[]{:S(2)}) collective-permute-start(f32[128,66]{0,1:T(8,128)S(1)} %bitcast.229), channel_id=1, source_target_pairs={{0,12},{4,8},{8,4},{12,0},{1,13},{5,9},{9,5},{13,1},{2,14},{6,10},... | collective-permute-start | bytes 101384 | tf_op jit(solution)/shard_map/ppermute | solution.py:152
  102.7 5.4 %collective-permute-start.36 = (f32[128,66]{0,1:T(8,128)S(1)}, f32[128,66]{0,1:T(8,128)S(1)}, u32[]{:S(2)}, u32[]{:S(2)}) collective-permute-start(f32[128,66]{0,1:T(8,128)S(1)} %bitcast.230), channel_id=1, source_target_pairs={{0,8},{4,12},{8,0},{12,4},{1,9},{5,13},{9,1},{13,5},{2,10},{6,14},... | collective-permute-start | bytes 101384 | tf_op jit(solution)/shard_map/ppermute | solution.py:152
  103.6 4.5 %collective-permute-start.35 = (f32[128,66]{0,1:T(8,128)S(1)}, f32[128,66]{0,1:T(8,128)S(1)}, u32[]{:S(2)}, u32[]{:S(2)}) collective-permute-start(f32[128,66]{0,1:T(8,128)S(1)} %bitcast.231), channel_id=1, source_target_pairs={{0,4},{4,0},{8,12},{12,8},{1,5},{5,1},{9,13},{13,9},{2,6},{6,2},{1... | collective-permute-start | bytes 101384 | tf_op jit(solution)/shard_map/ppermute | solution.py:152

commit v9 on v8

--- a/solution.py
+++ b/solution.py
@@ -181,10 +181,17 @@
     fates = fate_panel.shape[1]
     if rep_size == 2 and col_size <= 8:
         block = src_count // (col_size * rep_size)
-        maxima = jnp.swapaxes(maxima.reshape(col_size, rep_size, block), 0, 1)
-        totals = jnp.swapaxes(totals.reshape(col_size, rep_size, block), 0, 1)
-        weighted = jnp.swapaxes(weighted.reshape(col_size, rep_size, block, fates), 0, 1)
-        maxima, totals, weighted = lse_halving(maxima, totals, weighted, [("rep", 1)])
+        rep = lax.axis_index("rep")
+        packed = jnp.concatenate([weighted, maxima[:, None], totals[:, None]], axis=-1)
+        packed = packed.reshape(col_size, rep_size, block, fates + 2)
+        keep = lax.dynamic_index_in_dim(packed, rep, axis=1, keepdims=False)
+        send = lax.dynamic_index_in_dim(packed, 1 - rep, axis=1, keepdims=False)
+        recv = lax.ppermute(send, "rep", [(0, 1), (1, 0)])
+        maxima = jnp.maximum(keep[..., fates], recv[..., fates])
+        keep_f = jnp.exp(keep[..., fates] - maxima)
+        recv_f = jnp.exp(recv[..., fates] - maxima)
+        totals = keep[..., fates + 1] * keep_f + recv[..., fates + 1] * recv_f
+        weighted = keep[..., :fates] * keep_f[..., None] + recv[..., :fates] * recv_f[..., None]
         maxima, totals, weighted = lse_scatter_exchange(maxima, totals, weighted, "cols")
         fate_rows = weighted / totals[:, None]
     elif is_pow2(col_size) and is_pow2(rep_size):

time: 109 us -> 109 us (level)
  no operation moved by 1% of the time
where the time goes in v9:
time: 109 us
  starting transfers between devices  44.5 us (41%)
  waiting for transfers between devices  39.8 us (37%)
  other arithmetic  16.8 us (15%)
  matrix products  5.18 us (5%)
  between operations  1.34 us (1%)
    ppermute x24, starting transfers between devices, lse_exchange(): received.append(lax.ppermute(payload, axes, perm))  36.8 us
    ppermute x24, waiting for transfers between devices, lse_exchange(): received.append(lax.ppermute(payload, axes, perm))  20.1 us
    ppermute x9, waiting for transfers between devices, lse_allreduce(): other = lax.ppermute(jnp.stack([maxima, totals]), name, perm)  10.5 us
    ppermute x1, waiting for transfers between devices, body(): theirs = lax.ppermute(mine, 'rows', [(0, 1), (1, 0)])  5.36 us
    ppermute x3, starting transfers between devices, lse_scatter_exchange(): parts.append(lax.ppermute(send, name, perm))  4.45 us
    dot_general x2, matrix products, pair_cost(): lax.dot_general(lhs_rows, rhs_rows, (((1,), (1,)), ((), ())), precision=l...  4.17 us
    reduce_sum x8, other arithmetic, body(): totals = jnp.sum(jnp.exp(scores - maxima[None, :]), axis=0)  3.83 us
    reduce_sum x8, other arithmetic, body(): totals = jnp.sum(jnp.exp(scores - maxima[:, None]), axis=1)  3.45 us
  transfers between devices with their start and end apart: 38, of which 33 were waited for; matrix products, arithmetic and copies ran while one was open for 1% of the time, Pallas kernels for 0%

profile of v9, /device:TPU:0, one launch (start us, length us, event | category | flops | bytes accessed | tf_op | source)
XLA Modules:
  0.0 108.8 jit_solution(1708790148230434084)
XLA Ops:
  2.2 1.0 multiply_reduce_fusion.1
  3.2 2.1 %subtract_reduce_fusion.16 = (f32[1024]{0:T(1024)S(1)}, f32[1024,256]{0,1:T(8,128)S(1)}) fusion(f32[256]{0:T(256)S(1)} %multiply_log_fusion, f32[1024,64]{0,1:T(8,128)} %param.5, f32[256,64]{0,1:T(8,128)} %param.7, f32[256]{0:T(256)S(1)} %multiply_reduce_fusion.2, f32[1024]{0:T(1024)S(1)} %multiply_reduce_fusion.1), kind=kOutput, calls=%fused_computation.39 | convolution fusion | flops 202898432 | bytes 1386496 | tf_op jit(solution)/shard_map/dot_general | solution.py:15
  7.1 5.0 %collective-permute-start.4 = (f32[2,1024]{1,0:T(2,128)S(1)}, f32[2,1024]{1,0:T(2,128)S(1)}, u32[]{:S(2)}, u32[]{:S(2)}) collective-permute-start(f32[2,1024]{1,0:T(2,128)S(1)} %get-tuple-element.122), channel_id=1, source_target_pairs={{0,12},{4,8},{8,4},{12,0},{1,13},{5,9},{9,5},{13,1},{2,14},{6,10},... | collective-permute-start | bytes 24584 | tf_op jit(solution)/shard_map/ppermute | solution.py:66
  12.8 1.0 collective-permute-done.4
  13.7 2.9 %collective-permute-done.3 = f32[2,1024]{1,0:T(2,128)S(1)} collective-permute-done((f32[2,1024]{1,0:T(2,128)S(1)}, f32[2,1024]{1,0:T(2,128)S(1)}, u32[]{:S(2)}, u32[]{:S(2)}) %collective-permute-start.3) | collective-permute-done | bytes 8224 | tf_op jit(solution)/shard_map/ppermute | solution.py:66
  17.3 1.6 %collective-permute-start.5 = (f32[2,256]{1,0:T(2,128)S(1)}, f32[2,256]{1,0:T(2,128)S(1)}, u32[]{:S(2)}, u32[]{:S(2)}) collective-permute-start(f32[2,256]{1,0:T(2,128)S(1)} %pad_maximum_fusion.27), channel_id=1, source_target_pairs={{0,2},{2,0},{1,3},{3,1},{4,6},{6,4},{5,7},{7,5},{8,10},{10,8},{9,1... | collective-permute-start | bytes 6152 | tf_op jit(solution)/shard_map/ppermute | solution.py:44
  19.5 1.5 %collective-permute-done.5 = f32[2,256]{1,0:T(2,128)S(1)} collective-permute-done((f32[2,256]{1,0:T(2,128)S(1)}, f32[2,256]{1,0:T(2,128)S(1)}, u32[]{:S(2)}, u32[]{:S(2)}) %collective-permute-start.5) | collective-permute-done | bytes 2080 | tf_op jit(solution)/shard_map/ppermute | solution.py:44
  21.0 5.4 %collective-permute-done = f32[1024,65]{0,1:T(8,128)S(1)} collective-permute-done((f32[1024,65]{0,1:T(8,128)S(1)}, f32[1024,65]{0,1:T(8,128)S(1)}, u32[]{:S(2)}, u32[]{:S(2)}) %collective-permute-start) | collective-permute-done | bytes 266272 | tf_op jit(solution)/shard_map/ppermute | solution.py:250
  26.5 2.0 %fusion.1 = f32[2048,256]{0,1:T(8,128)S(1)} fusion(f32[256,64]{0,1:T(8,128)S(1)} %copy-done.2, f32[256]{0:T(256)S(1)} %multiply_reduce_fusion.2, f32[2048]{0:T(1024)S(1)} %multiply_reduce_fusion, f32[1024,65]{0,1:T(8,128)S(1)} %get-tuple-element.13, f32[1024,65]{0,1:T(8,128)S(1)} %get-tuple-element.14), kind=kOutput, calls=%fused_computation.2 | convolution fusion | flops 404881408 | bytes 2704384 | tf_op jit(solution)/shard_map/dot_general | solution.py:15
  29.3 1.2 %collective-permute-done.6 = f32[2,2048]{1,0:T(2,128)S(1)} collective-permute-done((f32[2,2048]{1,0:T(2,128)S(1)}, f32[2,2048]{1,0:T(2,128)S(1)}, u32[]{:S(2)}, u32[]{:S(2)}) %collective-permute-start.6) | collective-permute-done | bytes 16416 | tf_op jit(solution)/shard_map/ppermute | solution.py:44
  30.6 1.8 %collective-permute-start.9 = (f32[2,2048]{1,0:T(2,128)S(1)}, f32[2,2048]{1,0:T(2,128)S(1)}, u32[]{:S(2)}, u32[]{:S(2)}) collective-permute-start(f32[2,2048]{1,0:T(2,128)S(1)} %get-tuple-element.118), channel_id=1, source_target_pairs={{0,12},{4,8},{8,4},{12,0},{1,13},{5,9},{9,5},{13,1},{2,14},{6,10},... | collective-permute-start | bytes 49160 | tf_op jit(solution)/shard_map/ppermute | solution.py:66
  32.4 2.6 %collective-permute-start.7 = (f32[2,2048]{1,0:T(2,128)S(1)}, f32[2,2048]{1,0:T(2,128)S(1)}, u32[]{:S(2)}, u32[]{:S(2)}) collective-permute-start(f32[2,2048]{1,0:T(2,128)S(1)} %get-tuple-element.118), channel_id=1, source_target_pairs={{0,4},{4,0},{8,12},{12,8},{1,5},{5,1},{9,13},{13,9},{2,6},{6,2},{1... | collective-permute-start | bytes 49160 | tf_op jit(solution)/shard_map/ppermute | solution.py:66
  35.0 1.2 %collective-permute-done.9 = f32[2,2048]{1,0:T(2,128)S(1)} collective-permute-done((f32[2,2048]{1,0:T(2,128)S(1)}, f32[2,2048]{1,0:T(2,128)S(1)}, u32[]{:S(2)}, u32[]{:S(2)}) %collective-permute-start.9) | collective-permute-done | bytes 16416 | tf_op jit(solution)/shard_map/ppermute | solution.py:66
  36.2 1.0 collective-permute-done.8
  38.8 1.2 %collective-permute-done.10 = f32[2,2048]{1,0:T(2,128)S(1)} collective-permute-done((f32[2,2048]{1,0:T(2,128)S(1)}, f32[2,2048]{1,0:T(2,128)S(1)}, u32[]{:S(2)}, u32[]{:S(2)}) %collective-permute-start.10) | collective-permute-done | bytes 16416 | tf_op jit(solution)/shard_map/ppermute | solution.py:44
  40.1 2.1 %collective-permute-start.13 = (f32[2,2048]{1,0:T(2,128)S(1)}, f32[2,2048]{1,0:T(2,128)S(1)}, u32[]{:S(2)}, u32[]{:S(2)}) collective-permute-start(f32[2,2048]{1,0:T(2,128)S(1)} %get-tuple-element.116), channel_id=1, source_target_pairs={{0,12},{4,8},{8,4},{12,0},{1,13},{5,9},{9,5},{13,1},{2,14},{6,10},... | collective-permute-start | bytes 49160 | tf_op jit(solution)/shard_map/ppermute | solution.py:66
  42.2 1.0 collective-permute-start.12
  43.2 1.3 %collective-permute-start.11 = (f32[2,2048]{1,0:T(2,128)S(1)}, f32[2,2048]{1,0:T(2,128)S(1)}, u32[]{:S(2)}, u32[]{:S(2)}) collective-permute-start(f32[2,2048]{1,0:T(2,128)S(1)} %get-tuple-element.116), channel_id=1, source_target_pairs={{0,4},{4,0},{8,12},{12,8},{1,5},{5,1},{9,13},{13,9},{2,6},{6,2},{1... | collective-permute-start | bytes 49160 | tf_op jit(solution)/shard_map/ppermute | solution.py:66
  44.5 1.2 %collective-permute-done.13 = f32[2,2048]{1,0:T(2,128)S(1)} collective-permute-done((f32[2,2048]{1,0:T(2,128)S(1)}, f32[2,2048]{1,0:T(2,128)S(1)}, u32[]{:S(2)}, u32[]{:S(2)}) %collective-permute-start.13) | collective-permute-done | bytes 16416 | tf_op jit(solution)/shard_map/ppermute | solution.py:66
  45.8 1.1 collective-permute-done.12
  48.7 1.2 %collective-permute-done.14 = f32[2,2048]{1,0:T(2,128)S(1)} collective-permute-done((f32[2,2048]{1,0:T(2,128)S(1)}, f32[2,2048]{1,0:T(2,128)S(1)}, u32[]{:S(2)}, u32[]{:S(2)}) %collective-permute-start.14) | collective-permute-done | bytes 16416 | tf_op jit(solution)/shard_map/ppermute | solution.py:44
  49.9 1.9 %collective-permute-start.17 = (f32[2,2048]{1,0:T(2,128)S(1)}, f32[2,2048]{1,0:T(2,128)S(1)}, u32[]{:S(2)}, u32[]{:S(2)}) collective-permute-start(f32[2,2048]{1,0:T(2,128)S(1)} %get-tuple-element.114), channel_id=1, source_target_pairs={{0,12},{4,8},{8,4},{12,0},{1,13},{5,9},{9,5},{13,1},{2,14},{6,10},... | collective-permute-start | bytes 49160 | tf_op jit(solution)/shard_map/ppermute | solution.py:66
  52.7 1.6 %collective-permute-start.15 = (f32[2,2048]{1,0:T(2,128)S(1)}, f32[2,2048]{1,0:T(2,128)S(1)}, u32[]{:S(2)}, u32[]{:S(2)}) collective-permute-start(f32[2,2048]{1,0:T(2,128)S(1)} %get-tuple-element.114), channel_id=1, source_target_pairs={{0,4},{4,0},{8,12},{12,8},{1,5},{5,1},{9,13},{13,9},{2,6},{6,2},{1... | collective-permute-start | bytes 49160 | tf_op jit(solution)/shard_map/ppermute | solution.py:66
  54.4 1.3 %collective-permute-done.17 = f32[2,2048]{1,0:T(2,128)S(1)} collective-permute-done((f32[2,2048]{1,0:T(2,128)S(1)}, f32[2,2048]{1,0:T(2,128)S(1)}, u32[]{:S(2)}, u32[]{:S(2)}) %collective-permute-start.17) | collective-permute-done | bytes 16416 | tf_op jit(solution)/shard_map/ppermute | solution.py:66
  58.3 1.2 %collective-permute-done.18 = f32[2,2048]{1,0:T(2,128)S(1)} collective-permute-done((f32[2,2048]{1,0:T(2,128)S(1)}, f32[2,2048]{1,0:T(2,128)S(1)}, u32[]{:S(2)}, u32[]{:S(2)}) %collective-permute-start.18) | collective-permute-done | bytes 16416 | tf_op jit(solution)/shard_map/ppermute | solution.py:44
  59.5 2.1 %collective-permute-start.21 = (f32[2,2048]{1,0:T(2,128)S(1)}, f32[2,2048]{1,0:T(2,128)S(1)}, u32[]{:S(2)}, u32[]{:S(2)}) collective-permute-start(f32[2,2048]{1,0:T(2,128)S(1)} %get-tuple-element.112), channel_id=1, source_target_pairs={{0,12},{4,8},{8,4},{12,0},{1,13},{5,9},{9,5},{13,1},{2,14},{6,10},... | collective-permute-start | bytes 49160 | tf_op jit(solution)/shard_map/ppermute | solution.py:66
  62.5 1.4 %collective-permute-start.19 = (f32[2,2048]{1,0:T(2,128)S(1)}, f32[2,2048]{1,0:T(2,128)S(1)}, u32[]{:S(2)}, u32[]{:S(2)}) collective-permute-start(f32[2,2048]{1,0:T(2,128)S(1)} %get-tuple-element.112), channel_id=1, source_target_pairs={{0,4},{4,0},{8,12},{12,8},{1,5},{5,1},{9,13},{13,9},{2,6},{6,2},{1... | collective-permute-start | bytes 49160 | tf_op jit(solution)/shard_map/ppermute | solution.py:66
  64.0 1.2 %collective-permute-done.21 = f32[2,2048]{1,0:T(2,128)S(1)} collective-permute-done((f32[2,2048]{1,0:T(2,128)S(1)}, f32[2,2048]{1,0:T(2,128)S(1)}, u32[]{:S(2)}, u32[]{:S(2)}) %collective-permute-start.21) | collective-permute-done | bytes 16416 | tf_op jit(solution)/shard_map/ppermute | solution.py:66
  65.1 1.1 %collective-permute-done.20 = f32[2,2048]{1,0:T(2,128)S(1)} collective-permute-done((f32[2,2048]{1,0:T(2,128)S(1)}, f32[2,2048]{1,0:T(2,128)S(1)}, u32[]{:S(2)}, u32[]{:S(2)}) %collective-permute-start.20) | collective-permute-done | bytes 16416 | tf_op jit(solution)/shard_map/ppermute | solution.py:66
  68.3 1.2 %collective-permute-done.22 = f32[2,2048]{1,0:T(2,128)S(1)} collective-permute-done((f32[2,2048]{1,0:T(2,128)S(1)}, f32[2,2048]{1,0:T(2,128)S(1)}, u32[]{:S(2)}, u32[]{:S(2)}) %collective-permute-start.22) | collective-permute-done | bytes 16416 | tf_op jit(solution)/shard_map/ppermute | solution.py:44
  69.5 1.9 %collective-permute-start.25 = (f32[2,2048]{1,0:T(2,128)S(1)}, f32[2,2048]{1,0:T(2,128)S(1)}, u32[]{:S(2)}, u32[]{:S(2)}) collective-permute-start(f32[2,2048]{1,0:T(2,128)S(1)} %get-tuple-element.110), channel_id=1, source_target_pairs={{0,12},{4,8},{8,4},{12,0},{1,13},{5,9},{9,5},{13,1},{2,14},{6,10},... | collective-permute-start | bytes 49160 | tf_op jit(solution)/shard_map/ppermute | solution.py:66
  72.3 1.6 %collective-permute-start.23 = (f32[2,2048]{1,0:T(2,128)S(1)}, f32[2,2048]{1,0:T(2,128)S(1)}, u32[]{:S(2)}, u32[]{:S(2)}) collective-permute-start(f32[2,2048]{1,0:T(2,128)S(1)} %get-tuple-element.110), channel_id=1, source_target_pairs={{0,4},{4,0},{8,12},{12,8},{1,5},{5,1},{9,13},{13,9},{2,6},{6,2},{1... | collective-permute-start | bytes 49160 | tf_op jit(solution)/shard_map/ppermute | solution.py:66
  74.0 1.3 %collective-permute-done.25 = f32[2,2048]{1,0:T(2,128)S(1)} collective-permute-done((f32[2,2048]{1,0:T(2,128)S(1)}, f32[2,2048]{1,0:T(2,128)S(1)}, u32[]{:S(2)}, u32[]{:S(2)}) %collective-permute-start.25) | collective-permute-done | bytes 16416 | tf_op jit(solution)/shard_map/ppermute | solution.py:66
  77.8 1.2 %collective-permute-done.26 = f32[2,2048]{1,0:T(2,128)S(1)} collective-permute-done((f32[2,2048]{1,0:T(2,128)S(1)}, f32[2,2048]{1,0:T(2,128)S(1)}, u32[]{:S(2)}, u32[]{:S(2)}) %collective-permute-start.26) | collective-permute-done | bytes 16416 | tf_op jit(solution)/shard_map/ppermute | solution.py:44
  79.1 2.1 %collective-permute-start.29 = (f32[2,2048]{1,0:T(2,128)S(1)}, f32[2,2048]{1,0:T(2,128)S(1)}, u32[]{:S(2)}, u32[]{:S(2)}) collective-permute-start(f32[2,2048]{1,0:T(2,128)S(1)} %get-tuple-element.108), channel_id=1, source_target_pairs={{0,12},{4,8},{8,4},{12,0},{1,13},{5,9},{9,5},{13,1},{2,14},{6,10},... | collective-permute-start | bytes 49160 | tf_op jit(solution)/shard_map/ppermute | solution.py:66
  82.1 1.4 %collective-permute-start.27 = (f32[2,2048]{1,0:T(2,128)S(1)}, f32[2,2048]{1,0:T(2,128)S(1)}, u32[]{:S(2)}, u32[]{:S(2)}) collective-permute-start(f32[2,2048]{1,0:T(2,128)S(1)} %get-tuple-element.108), channel_id=1, source_target_pairs={{0,4},{4,0},{8,12},{12,8},{1,5},{5,1},{9,13},{13,9},{2,6},{6,2},{1... | collective-permute-start | bytes 49160 | tf_op jit(solution)/shard_map/ppermute | solution.py:66
  83.5 1.2 %collective-permute-done.29 = f32[2,2048]{1,0:T(2,128)S(1)} collective-permute-done((f32[2,2048]{1,0:T(2,128)S(1)}, f32[2,2048]{1,0:T(2,128)S(1)}, u32[]{:S(2)}, u32[]{:S(2)}) %collective-permute-start.29) | collective-permute-done | bytes 16416 | tf_op jit(solution)/shard_map/ppermute | solution.py:66
  84.7 1.1 %collective-permute-done.28 = f32[2,2048]{1,0:T(2,128)S(1)} collective-permute-done((f32[2,2048]{1,0:T(2,128)S(1)}, f32[2,2048]{1,0:T(2,128)S(1)}, u32[]{:S(2)}, u32[]{:S(2)}) %collective-permute-start.28) | collective-permute-done | bytes 16416 | tf_op jit(solution)/shard_map/ppermute | solution.py:66
  87.7 1.2 %collective-permute-done.30 = f32[2,2048]{1,0:T(2,128)S(1)} collective-permute-done((f32[2,2048]{1,0:T(2,128)S(1)}, f32[2,2048]{1,0:T(2,128)S(1)}, u32[]{:S(2)}, u32[]{:S(2)}) %collective-permute-start.30) | collective-permute-done | bytes 16416 | tf_op jit(solution)/shard_map/ppermute | solution.py:44
  88.9 1.9 %collective-permute-start.33 = (f32[2,2048]{1,0:T(2,128)S(1)}, f32[2,2048]{1,0:T(2,128)S(1)}, u32[]{:S(2)}, u32[]{:S(2)}) collective-permute-start(f32[2,2048]{1,0:T(2,128)S(1)} %get-tuple-element.106), channel_id=1, source_target_pairs={{0,12},{4,8},{8,4},{12,0},{1,13},{5,9},{9,5},{13,1},{2,14},{6,10},... | collective-permute-start | bytes 49160 | tf_op jit(solution)/shard_map/ppermute | solution.py:66
  91.7 1.6 %collective-permute-start.31 = (f32[2,2048]{1,0:T(2,128)S(1)}, f32[2,2048]{1,0:T(2,128)S(1)}, u32[]{:S(2)}, u32[]{:S(2)}) collective-permute-start(f32[2,2048]{1,0:T(2,128)S(1)} %get-tuple-element.106), channel_id=1, source_target_pairs={{0,4},{4,0},{8,12},{12,8},{1,5},{5,1},{9,13},{13,9},{2,6},{6,2},{1... | collective-permute-start | bytes 49160 | tf_op jit(solution)/shard_map/ppermute | solution.py:66
  93.4 1.3 %collective-permute-done.33 = f32[2,2048]{1,0:T(2,128)S(1)} collective-permute-done((f32[2,2048]{1,0:T(2,128)S(1)}, f32[2,2048]{1,0:T(2,128)S(1)}, u32[]{:S(2)}, u32[]{:S(2)}) %collective-permute-start.33) | collective-permute-done | bytes 16416 | tf_op jit(solution)/shard_map/ppermute | solution.py:66
  97.5 1.0 fusion.5
  98.9 1.3 %collective-permute-done.34 = f32[4,128,66]{1,0,2:T(4,128)S(1)} collective-permute-done((f32[4,128,66]{1,0,2:T(4,128)S(1)}, f32[4,128,66]{1,0,2:T(4,128)S(1)}, u32[]{:S(2)}, u32[]{:S(2)}) %collective-permute-start.34) | collective-permute-done | bytes 135200 | tf_op jit(solution)/shard_map/ppermute | solution.py:189
  100.5 2.1 %collective-permute-start.37 = (f32[128,66]{0,1:T(8,128)S(1)}, f32[128,66]{0,1:T(8,128)S(1)}, u32[]{:S(2)}, u32[]{:S(2)}) collective-permute-start(f32[128,66]{0,1:T(8,128)S(1)} %bitcast.209), channel_id=1, source_target_pairs={{0,12},{4,8},{8,4},{12,0},{1,13},{5,9},{9,5},{13,1},{2,14},{6,10},... | collective-permute-start | bytes 101384 | tf_op jit(solution)/shard_map/ppermute | solution.py:152
  103.6 1.4 %collective-permute-start.35 = (f32[128,66]{0,1:T(8,128)S(1)}, f32[128,66]{0,1:T(8,128)S(1)}, u32[]{:S(2)}, u32[]{:S(2)}) collective-permute-start(f32[128,66]{0,1:T(8,128)S(1)} %bitcast.211), channel_id=1, source_target_pairs={{0,4},{4,0},{8,12},{12,8},{1,5},{5,1},{9,13},{13,9},{2,6},{6,2},{1... | collective-permute-start | bytes 101384 | tf_op jit(solution)/shard_map/ppermute | solution.py:152
  105.6 1.0 collective-permute-done.37
  106.6 1.4 %collective-permute-done.36 = f32[128,66]{0,1:T(8,128)S(1)} collective-permute-done((f32[128,66]{0,1:T(8,128)S(1)}, f32[128,66]{0,1:T(8,128)S(1)}, u32[]{:S(2)}, u32[]{:S(2)}) %collective-permute-start.36) | collective-permute-done | bytes 33824 | tf_op jit(solution)/shard_map/ppermute | solution.py:152
  (157 shorter events, 29.3 us)
Async XLA Ops:
  0.6 96.8 %copy-start = (f32[256,64]{0,1:T(8,128)S(1)}, f32[256,64]{0,1:T(8,128)}, u32[]{:S(2)}) copy-start(f32[256,64]{0,1:T(8,128)} %param.9) | copy-start | bytes 196612
  0.6 16.1 %copy-start.4 = (f32[1024]{0:T(1024)S(1)}, f32[1024]{0:T(1024)}, u32[]{:S(2)}) copy-start(f32[1024]{0:T(1024)} %param.6) | copy-start | bytes 12292
  5.4 13.5 %copy-start.1 = (f32[1024,64]{0,1:T(8,128)S(1)}, f32[1024,64]{0,1:T(8,128)}, u32[]{:S(2)}) copy-start(f32[1024,64]{0,1:T(8,128)} %param.5) | copy-start | bytes 786436
  5.4 15.6 %copy-start.3 = (f32[256]{0:T(256)S(1)}, f32[256]{0:T(256)}, u32[]{:S(2)}) copy-start(f32[256]{0:T(256)} %param.8) | copy-start | bytes 3076
  5.7 1.4 %collective-permute-start.1 = (f32[2,1024]{1,0:T(2,128)S(1)}, f32[2,1024]{1,0:T(2,128)S(1)}, u32[]{:S(2)}, u32[]{:S(2)}) collective-permute-start(f32[2,1024]{1,0:T(2,128)S(1)} %pad_maximum_fusion.25), channel_id=1, source_target_pairs={{0,1},{1,0},{2,3},{3,2},{4,5},{5,4},{6,7},{7,6},{8,9},{9,8},{10,11... | collective-permute-start | bytes 24584 | tf_op jit(solution)/shard_map/ppermute | solution.py:44
  7.1 6.6 %collective-permute-start.4 = (f32[2,1024]{1,0:T(2,128)S(1)}, f32[2,1024]{1,0:T(2,128)S(1)}, u32[]{:S(2)}, u32[]{:S(2)}) collective-permute-start(f32[2,1024]{1,0:T(2,128)S(1)} %get-tuple-element.122), channel_id=1, source_target_pairs={{0,12},{4,8},{8,4},{12,0},{1,13},{5,9},{9,5},{13,1},{2,14},{6,10},... | collective-permute-start | bytes 24584 | tf_op jit(solution)/shard_map/ppermute | solution.py:66
  12.1 4.5 %collective-permute-start.3 = (f32[2,1024]{1,0:T(2,128)S(1)}, f32[2,1024]{1,0:T(2,128)S(1)}, u32[]{:S(2)}, u32[]{:S(2)}) collective-permute-start(f32[2,1024]{1,0:T(2,128)S(1)} %get-tuple-element.122), channel_id=1, source_target_pairs={{0,8},{4,12},{8,0},{12,4},{1,9},{5,13},{9,1},{13,5},{2,10},{6,14},... | collective-permute-start | bytes 24584 | tf_op jit(solution)/shard_map/ppermute | solution.py:66
  12.1 4.5 %collective-permute-start.2 = (f32[2,1024]{1,0:T(2,128)S(1)}, f32[2,1024]{1,0:T(2,128)S(1)}, u32[]{:S(2)}, u32[]{:S(2)}) collective-permute-start(f32[2,1024]{1,0:T(2,128)S(1)} %get-tuple-element.122), channel_id=1, source_target_pairs={{0,4},{4,0},{8,12},{12,8},{1,5},{5,1},{9,13},{13,9},{2,6},{6,2},{1... | collective-permute-start | bytes 24584 | tf_op jit(solution)/shard_map/ppermute | solution.py:66
  16.9 9.6 %copy-start.2 = (f32[256,64]{0,1:T(8,128)S(1)}, f32[256,64]{0,1:T(8,128)}, u32[]{:S(2)}) copy-start(f32[256,64]{0,1:T(8,128)} %param.7) | copy-start | bytes 196612
  17.3 3.7 %collective-permute-start.5 = (f32[2,256]{1,0:T(2,128)S(1)}, f32[2,256]{1,0:T(2,128)S(1)}, u32[]{:S(2)}, u32[]{:S(2)}) collective-permute-start(f32[2,256]{1,0:T(2,128)S(1)} %pad_maximum_fusion.27), channel_id=1, source_target_pairs={{0,2},{2,0},{1,3},{3,1},{4,6},{6,4},{5,7},{7,5},{8,10},{10,8},{9,1... | collective-permute-start | bytes 6152 | tf_op jit(solution)/shard_map/ppermute | solution.py:44
  18.9 7.5 %collective-permute-start = (f32[1024,65]{0,1:T(8,128)S(1)}, f32[1024,65]{0,1:T(8,128)S(1)}, u32[]{:S(2)}, u32[]{:S(2)}) collective-permute-start(f32[1024,65]{0,1:T(8,128)S(1)} %pad_maximum_fusion), channel_id=1, source_target_pairs={{0,2},{2,0},{1,3},{3,1},{4,6},{6,4},{5,7},{7,5},{8,10},{10,8},{9,1... | collective-permute-start | bytes 798728 | tf_op jit(solution)/shard_map/ppermute | solution.py:250
  29.2 1.2 %collective-permute-start.6 = (f32[2,2048]{1,0:T(2,128)S(1)}, f32[2,2048]{1,0:T(2,128)S(1)}, u32[]{:S(2)}, u32[]{:S(2)}) collective-permute-start(f32[2,2048]{1,0:T(2,128)S(1)} %pad_maximum_fusion.10), channel_id=1, source_target_pairs={{0,1},{1,0},{2,3},{3,2},{4,5},{5,4},{6,7},{7,6},{8,9},{9,8},{10,11... | collective-permute-start | bytes 49160 | tf_op jit(solution)/shard_map/ppermute | solution.py:44
  30.6 5.6 %collective-permute-start.9 = (f32[2,2048]{1,0:T(2,128)S(1)}, f32[2,2048]{1,0:T(2,128)S(1)}, u32[]{:S(2)}, u32[]{:S(2)}) collective-permute-start(f32[2,2048]{1,0:T(2,128)S(1)} %get-tuple-element.118), channel_id=1, source_target_pairs={{0,12},{4,8},{8,4},{12,0},{1,13},{5,9},{9,5},{13,1},{2,14},{6,10},... | collective-permute-start | bytes 49160 | tf_op jit(solution)/shard_map/ppermute | solution.py:66
  32.4 4.8 %collective-permute-start.8 = (f32[2,2048]{1,0:T(2,128)S(1)}, f32[2,2048]{1,0:T(2,128)S(1)}, u32[]{:S(2)}, u32[]{:S(2)}) collective-permute-start(f32[2,2048]{1,0:T(2,128)S(1)} %get-tuple-element.118), channel_id=1, source_target_pairs={{0,8},{4,12},{8,0},{12,4},{1,9},{5,13},{9,1},{13,5},{2,10},{6,14},... | collective-permute-start | bytes 49160 | tf_op jit(solution)/shard_map/ppermute | solution.py:66
  32.4 4.7 %collective-permute-start.7 = (f32[2,2048]{1,0:T(2,128)S(1)}, f32[2,2048]{1,0:T(2,128)S(1)}, u32[]{:S(2)}, u32[]{:S(2)}) collective-permute-start(f32[2,2048]{1,0:T(2,128)S(1)} %get-tuple-element.118), channel_id=1, source_target_pairs={{0,4},{4,0},{8,12},{12,8},{1,5},{5,1},{9,13},{13,9},{2,6},{6,2},{1... | collective-permute-start | bytes 49160 | tf_op jit(solution)/shard_map/ppermute | solution.py:66
  38.8 1.2 %collective-permute-start.10 = (f32[2,2048]{1,0:T(2,128)S(1)}, f32[2,2048]{1,0:T(2,128)S(1)}, u32[]{:S(2)}, u32[]{:S(2)}) collective-permute-start(f32[2,2048]{1,0:T(2,128)S(1)} %pad_maximum_fusion.12), channel_id=1, source_target_pairs={{0,1},{1,0},{2,3},{3,2},{4,5},{5,4},{6,7},{7,6},{8,9},{9,8},{10,11... | collective-permute-start | bytes 49160 | tf_op jit(solution)/shard_map/ppermute | solution.py:44
  40.1 5.7 %collective-permute-start.13 = (f32[2,2048]{1,0:T(2,128)S(1)}, f32[2,2048]{1,0:T(2,128)S(1)}, u32[]{:S(2)}, u32[]{:S(2)}) collective-permute-start(f32[2,2048]{1,0:T(2,128)S(1)} %get-tuple-element.116), channel_id=1, source_target_pairs={{0,12},{4,8},{8,4},{12,0},{1,13},{5,9},{9,5},{13,1},{2,14},{6,10},... | collective-permute-start | bytes 49160 | tf_op jit(solution)/shard_map/ppermute | solution.py:66
  42.2 4.7 %collective-permute-start.12 = (f32[2,2048]{1,0:T(2,128)S(1)}, f32[2,2048]{1,0:T(2,128)S(1)}, u32[]{:S(2)}, u32[]{:S(2)}) collective-permute-start(f32[2,2048]{1,0:T(2,128)S(1)} %get-tuple-element.116), channel_id=1, source_target_pairs={{0,8},{4,12},{8,0},{12,4},{1,9},{5,13},{9,1},{13,5},{2,10},{6,14},... | collective-permute-start | bytes 49160 | tf_op jit(solution)/shard_map/ppermute | solution.py:66
  43.2 3.8 %collective-permute-start.11 = (f32[2,2048]{1,0:T(2,128)S(1)}, f32[2,2048]{1,0:T(2,128)S(1)}, u32[]{:S(2)}, u32[]{:S(2)}) collective-permute-start(f32[2,2048]{1,0:T(2,128)S(1)} %get-tuple-element.116), channel_id=1, source_target_pairs={{0,4},{4,0},{8,12},{12,8},{1,5},{5,1},{9,13},{13,9},{2,6},{6,2},{1... | collective-permute-start | bytes 49160 | tf_op jit(solution)/shard_map/ppermute | solution.py:66
  48.6 1.2 %collective-permute-start.14 = (f32[2,2048]{1,0:T(2,128)S(1)}, f32[2,2048]{1,0:T(2,128)S(1)}, u32[]{:S(2)}, u32[]{:S(2)}) collective-permute-start(f32[2,2048]{1,0:T(2,128)S(1)} %pad_maximum_fusion.14), channel_id=1, source_target_pairs={{0,1},{1,0},{2,3},{3,2},{4,5},{5,4},{6,7},{7,6},{8,9},{9,8},{10,11... | collective-permute-start | bytes 49160 | tf_op jit(solution)/shard_map/ppermute | solution.py:44
  49.9 5.7 %collective-permute-start.17 = (f32[2,2048]{1,0:T(2,128)S(1)}, f32[2,2048]{1,0:T(2,128)S(1)}, u32[]{:S(2)}, u32[]{:S(2)}) collective-permute-start(f32[2,2048]{1,0:T(2,128)S(1)} %get-tuple-element.114), channel_id=1, source_target_pairs={{0,12},{4,8},{8,4},{12,0},{1,13},{5,9},{9,5},{13,1},{2,14},{6,10},... | collective-permute-start | bytes 49160 | tf_op jit(solution)/shard_map/ppermute | solution.py:66
  51.8 4.8 %collective-permute-start.16 = (f32[2,2048]{1,0:T(2,128)S(1)}, f32[2,2048]{1,0:T(2,128)S(1)}, u32[]{:S(2)}, u32[]{:S(2)}) collective-permute-start(f32[2,2048]{1,0:T(2,128)S(1)} %get-tuple-element.114), channel_id=1, source_target_pairs={{0,8},{4,12},{8,0},{12,4},{1,9},{5,13},{9,1},{13,5},{2,10},{6,14},... | collective-permute-start | bytes 49160 | tf_op jit(solution)/shard_map/ppermute | solution.py:66
  52.7 3.9 %collective-permute-start.15 = (f32[2,2048]{1,0:T(2,128)S(1)}, f32[2,2048]{1,0:T(2,128)S(1)}, u32[]{:S(2)}, u32[]{:S(2)}) collective-permute-start(f32[2,2048]{1,0:T(2,128)S(1)} %get-tuple-element.114), channel_id=1, source_target_pairs={{0,4},{4,0},{8,12},{12,8},{1,5},{5,1},{9,13},{13,9},{2,6},{6,2},{1... | collective-permute-start | bytes 49160 | tf_op jit(solution)/shard_map/ppermute | solution.py:66
  58.2 1.2 %collective-permute-start.18 = (f32[2,2048]{1,0:T(2,128)S(1)}, f32[2,2048]{1,0:T(2,128)S(1)}, u32[]{:S(2)}, u32[]{:S(2)}) collective-permute-start(f32[2,2048]{1,0:T(2,128)S(1)} %pad_maximum_fusion.16), channel_id=1, source_target_pairs={{0,1},{1,0},{2,3},{3,2},{4,5},{5,4},{6,7},{7,6},{8,9},{9,8},{10,11... | collective-permute-start | bytes 49160 | tf_op jit(solution)/shard_map/ppermute | solution.py:44
  59.5 5.6 %collective-permute-start.21 = (f32[2,2048]{1,0:T(2,128)S(1)}, f32[2,2048]{1,0:T(2,128)S(1)}, u32[]{:S(2)}, u32[]{:S(2)}) collective-permute-start(f32[2,2048]{1,0:T(2,128)S(1)} %get-tuple-element.112), channel_id=1, source_target_pairs={{0,12},{4,8},{8,4},{12,0},{1,13},{5,9},{9,5},{13,1},{2,14},{6,10},... | collective-permute-start | bytes 49160 | tf_op jit(solution)/shard_map/ppermute | solution.py:66
  61.6 4.6 %collective-permute-start.20 = (f32[2,2048]{1,0:T(2,128)S(1)}, f32[2,2048]{1,0:T(2,128)S(1)}, u32[]{:S(2)}, u32[]{:S(2)}) collective-permute-start(f32[2,2048]{1,0:T(2,128)S(1)} %get-tuple-element.112), channel_id=1, source_target_pairs={{0,8},{4,12},{8,0},{12,4},{1,9},{5,13},{9,1},{13,5},{2,10},{6,14},... | collective-permute-start | bytes 49160 | tf_op jit(solution)/shard_map/ppermute | solution.py:66
  62.5 3.9 %collective-permute-start.19 = (f32[2,2048]{1,0:T(2,128)S(1)}, f32[2,2048]{1,0:T(2,128)S(1)}, u32[]{:S(2)}, u32[]{:S(2)}) collective-permute-start(f32[2,2048]{1,0:T(2,128)S(1)} %get-tuple-element.112), channel_id=1, source_target_pairs={{0,4},{4,0},{8,12},{12,8},{1,5},{5,1},{9,13},{13,9},{2,6},{6,2},{1... | collective-permute-start | bytes 49160 | tf_op jit(solution)/shard_map/ppermute | solution.py:66
  68.2 1.2 %collective-permute-start.22 = (f32[2,2048]{1,0:T(2,128)S(1)}, f32[2,2048]{1,0:T(2,128)S(1)}, u32[]{:S(2)}, u32[]{:S(2)}) collective-permute-start(f32[2,2048]{1,0:T(2,128)S(1)} %pad_maximum_fusion.18), channel_id=1, source_target_pairs={{0,1},{1,0},{2,3},{3,2},{4,5},{5,4},{6,7},{7,6},{8,9},{9,8},{10,11... | collective-permute-start | bytes 49160 | tf_op jit(solution)/shard_map/ppermute | solution.py:44
  69.5 5.7 %collective-permute-start.25 = (f32[2,2048]{1,0:T(2,128)S(1)}, f32[2,2048]{1,0:T(2,128)S(1)}, u32[]{:S(2)}, u32[]{:S(2)}) collective-permute-start(f32[2,2048]{1,0:T(2,128)S(1)} %get-tuple-element.110), channel_id=1, source_target_pairs={{0,12},{4,8},{8,4},{12,0},{1,13},{5,9},{9,5},{13,1},{2,14},{6,10},... | collective-permute-start | bytes 49160 | tf_op jit(solution)/shard_map/ppermute | solution.py:66
  71.4 4.8 %collective-permute-start.24 = (f32[2,2048]{1,0:T(2,128)S(1)}, f32[2,2048]{1,0:T(2,128)S(1)}, u32[]{:S(2)}, u32[]{:S(2)}) collective-permute-start(f32[2,2048]{1,0:T(2,128)S(1)} %get-tuple-element.110), channel_id=1, source_target_pairs={{0,8},{4,12},{8,0},{12,4},{1,9},{5,13},{9,1},{13,5},{2,10},{6,14},... | collective-permute-start | bytes 49160 | tf_op jit(solution)/shard_map/ppermute | solution.py:66
  72.3 3.9 %collective-permute-start.23 = (f32[2,2048]{1,0:T(2,128)S(1)}, f32[2,2048]{1,0:T(2,128)S(1)}, u32[]{:S(2)}, u32[]{:S(2)}) collective-permute-start(f32[2,2048]{1,0:T(2,128)S(1)} %get-tuple-element.110), channel_id=1, source_target_pairs={{0,4},{4,0},{8,12},{12,8},{1,5},{5,1},{9,13},{13,9},{2,6},{6,2},{1... | collective-permute-start | bytes 49160 | tf_op jit(solution)/shard_map/ppermute | solution.py:66
  77.8 1.2 %collective-permute-start.26 = (f32[2,2048]{1,0:T(2,128)S(1)}, f32[2,2048]{1,0:T(2,128)S(1)}, u32[]{:S(2)}, u32[]{:S(2)}) collective-permute-start(f32[2,2048]{1,0:T(2,128)S(1)} %pad_maximum_fusion.20), channel_id=1, source_target_pairs={{0,1},{1,0},{2,3},{3,2},{4,5},{5,4},{6,7},{7,6},{8,9},{9,8},{10,11... | collective-permute-start | bytes 49160 | tf_op jit(solution)/shard_map/ppermute | solution.py:44
  79.1 5.6 %collective-permute-start.29 = (f32[2,2048]{1,0:T(2,128)S(1)}, f32[2,2048]{1,0:T(2,128)S(1)}, u32[]{:S(2)}, u32[]{:S(2)}) collective-permute-start(f32[2,2048]{1,0:T(2,128)S(1)} %get-tuple-element.108), channel_id=1, source_target_pairs={{0,12},{4,8},{8,4},{12,0},{1,13},{5,9},{9,5},{13,1},{2,14},{6,10},... | collective-permute-start | bytes 49160 | tf_op jit(solution)/shard_map/ppermute | solution.py:66
  81.2 4.6 %collective-permute-start.28 = (f32[2,2048]{1,0:T(2,128)S(1)}, f32[2,2048]{1,0:T(2,128)S(1)}, u32[]{:S(2)}, u32[]{:S(2)}) collective-permute-start(f32[2,2048]{1,0:T(2,128)S(1)} %get-tuple-element.108), channel_id=1, source_target_pairs={{0,8},{4,12},{8,0},{12,4},{1,9},{5,13},{9,1},{13,5},{2,10},{6,14},... | collective-permute-start | bytes 49160 | tf_op jit(solution)/shard_map/ppermute | solution.py:66
  82.1 3.9 %collective-permute-start.27 = (f32[2,2048]{1,0:T(2,128)S(1)}, f32[2,2048]{1,0:T(2,128)S(1)}, u32[]{:S(2)}, u32[]{:S(2)}) collective-permute-start(f32[2,2048]{1,0:T(2,128)S(1)} %get-tuple-element.108), channel_id=1, source_target_pairs={{0,4},{4,0},{8,12},{12,8},{1,5},{5,1},{9,13},{13,9},{2,6},{6,2},{1... | collective-permute-start | bytes 49160 | tf_op jit(solution)/shard_map/ppermute | solution.py:66
  87.6 1.2 %collective-permute-start.30 = (f32[2,2048]{1,0:T(2,128)S(1)}, f32[2,2048]{1,0:T(2,128)S(1)}, u32[]{:S(2)}, u32[]{:S(2)}) collective-permute-start(f32[2,2048]{1,0:T(2,128)S(1)} %pad_maximum_fusion.22), channel_id=1, source_target_pairs={{0,1},{1,0},{2,3},{3,2},{4,5},{5,4},{6,7},{7,6},{8,9},{9,8},{10,11... | collective-permute-start | bytes 49160 | tf_op jit(solution)/shard_map/ppermute | solution.py:44
  88.9 5.7 %collective-permute-start.33 = (f32[2,2048]{1,0:T(2,128)S(1)}, f32[2,2048]{1,0:T(2,128)S(1)}, u32[]{:S(2)}, u32[]{:S(2)}) collective-permute-start(f32[2,2048]{1,0:T(2,128)S(1)} %get-tuple-element.106), channel_id=1, source_target_pairs={{0,12},{4,8},{8,4},{12,0},{1,13},{5,9},{9,5},{13,1},{2,14},{6,10},... | collective-permute-start | bytes 49160 | tf_op jit(solution)/shard_map/ppermute | solution.py:66
  90.8 4.8 %collective-permute-start.32 = (f32[2,2048]{1,0:T(2,128)S(1)}, f32[2,2048]{1,0:T(2,128)S(1)}, u32[]{:S(2)}, u32[]{:S(2)}) collective-permute-start(f32[2,2048]{1,0:T(2,128)S(1)} %get-tuple-element.106), channel_id=1, source_target_pairs={{0,8},{4,12},{8,0},{12,4},{1,9},{5,13},{9,1},{13,5},{2,10},{6,14},... | collective-permute-start | bytes 49160 | tf_op jit(solution)/shard_map/ppermute | solution.py:66
  91.7 3.9 %collective-permute-start.31 = (f32[2,2048]{1,0:T(2,128)S(1)}, f32[2,2048]{1,0:T(2,128)S(1)}, u32[]{:S(2)}, u32[]{:S(2)}) collective-permute-start(f32[2,2048]{1,0:T(2,128)S(1)} %get-tuple-element.106), channel_id=1, source_target_pairs={{0,4},{4,0},{8,12},{12,8},{1,5},{5,1},{9,13},{13,9},{2,6},{6,2},{1... | collective-permute-start | bytes 49160 | tf_op jit(solution)/shard_map/ppermute | solution.py:66
  98.8 1.4 %collective-permute-start.34 = (f32[4,128,66]{1,0,2:T(4,128)S(1)}, f32[4,128,66]{1,0,2:T(4,128)S(1)}, u32[]{:S(2)}, u32[]{:S(2)}) collective-permute-start(f32[4,128,66]{1,0,2:T(4,128)S(1)} %get-tuple-element.16), channel_id=1, source_target_pairs={{0,1},{1,0},{2,3},{3,2},{4,5},{5,4},{6,7},{7,6},{8,9},{9,8},{10,11... | collective-permute-start | bytes 405512 | tf_op jit(solution)/shard_map/ppermute | solution.py:189
  100.5 6.1 %collective-permute-start.37 = (f32[128,66]{0,1:T(8,128)S(1)}, f32[128,66]{0,1:T(8,128)S(1)}, u32[]{:S(2)}, u32[]{:S(2)}) collective-permute-start(f32[128,66]{0,1:T(8,128)S(1)} %bitcast.209), channel_id=1, source_target_pairs={{0,12},{4,8},{8,4},{12,0},{1,13},{5,9},{9,5},{13,1},{2,14},{6,10},... | collective-permute-start | bytes 101384 | tf_op jit(solution)/shard_map/ppermute | solution.py:152
  102.6 5.4 %collective-permute-start.36 = (f32[128,66]{0,1:T(8,128)S(1)}, f32[128,66]{0,1:T(8,128)S(1)}, u32[]{:S(2)}, u32[]{:S(2)}) collective-permute-start(f32[128,66]{0,1:T(8,128)S(1)} %bitcast.210), channel_id=1, source_target_pairs={{0,8},{4,12},{8,0},{12,4},{1,9},{5,13},{9,1},{13,5},{2,10},{6,14},... | collective-permute-start | bytes 101384 | tf_op jit(solution)/shard_map/ppermute | solution.py:152
  103.6 4.5 %collective-permute-start.35 = (f32[128,66]{0,1:T(8,128)S(1)}, f32[128,66]{0,1:T(8,128)S(1)}, u32[]{:S(2)}, u32[]{:S(2)}) collective-permute-start(f32[128,66]{0,1:T(8,128)S(1)} %bitcast.211), channel_id=1, source_target_pairs={{0,4},{4,0},{8,12},{12,8},{1,5},{5,1},{9,13},{13,9},{2,6},{6,2},{1... | collective-permute-start | bytes 101384 | tf_op jit(solution)/shard_map/ppermute | solution.py:152

commit v10 on v9

--- a/solution.py
+++ b/solution.py
@@ -246,7 +246,8 @@
     tgt_count = targets.shape[0]
     row = lax.axis_index("rows")
     dim = sources.shape[1]
-    mine = jnp.concatenate([sources, source_mass[:, None]], axis=1)
+    flat = src_count * dim
+    mine = jnp.concatenate([sources.reshape(flat), source_mass])
     theirs = lax.ppermute(mine, "rows", [(0, 1), (1, 0)])
     all_sources = src_count * row_count
     all_targets = tgt_count * lax.axis_size(("cols", "rep"))
@@ -271,11 +272,15 @@
     maxima, totals = lse_allreduce(maxima, totals, ("rows",))
     g_pot = -relaxed * entropic * (maxima + jnp.log(totals))
 
-    first = jnp.where(row == 0, mine, theirs)
-    second = jnp.where(row == 0, theirs, mine)
-    gathered = jnp.concatenate([first, second], axis=0)
-    all_src = gathered[:, :dim]
-    all_mass = gathered[:, dim]
+    lead = row == 0
+    their_src = theirs[:flat].reshape(src_count, dim)
+    their_mass = theirs[flat:]
+    all_src = jnp.concatenate(
+        [jnp.where(lead, sources, their_src), jnp.where(lead, their_src, sources)]
+    )
+    all_mass = jnp.concatenate(
+        [jnp.where(lead, source_mass, their_mass), jnp.where(lead, their_mass, source_mass)]
+    )
     log_a = jnp.log(all_mass / all_sources)
     scaled = with_layout_constraint(scaled_cost(all_src), Layout(major_to_minor=(1, 0)))
     scaled, log_a = lax.optimization_barrier((scaled, log_a))

time: 109 us -> 106 us (0.972)
  waiting for transfers between devices: 39.8 us -> 35 us
  local copies, waits for them, and re-layouts: 1.06 us -> 2.36 us
    ppermute x1, waiting for transfers between devices: 5.36 us -> 0.01 us  [body(): theirs = lax.ppermute(mine, 'rows', [(0, 1), (1, 0)])]
    ppermute x1, starting transfers between devices: 0.6 us -> 2.56 us  [body(): theirs = lax.ppermute(mine, 'rows', [(0, 1), (1, 0)])]
    ppermute x24, starting transfers between devices: 36.8 us -> 35.6 us  [lse_exchange(): received.append(lax.ppermute(payload, axes, perm))]
  transfers between devices with their start and end apart: 38 -> 38, of which waited for: 33 -> 27; matrix products, arithmetic and copies ran while one was open for 1% -> 2% of each run, Pallas kernels for 0% -> 0%
where the time goes in v10:
time: 106 us
  starting transfers between devices  44.5 us (42%)
  waiting for transfers between devices  35 us (33%)
  other arithmetic  17.1 us (16%)
  matrix products  5.18 us (5%)
  local copies, waits for them, and re-layouts  2.36 us (2%)
  between operations  1.48 us (1%)
    ppermute x24, starting transfers between devices, lse_exchange(): received.append(lax.ppermute(payload, axes, perm))  35.6 us
    ppermute x24, waiting for transfers between devices, lse_exchange(): received.append(lax.ppermute(payload, axes, perm))  20.3 us
    ppermute x9, waiting for transfers between devices, lse_allreduce(): other = lax.ppermute(jnp.stack([maxima, totals]), name, perm)  11.1 us
    ppermute x3, starting transfers between devices, lse_scatter_exchange(): parts.append(lax.ppermute(send, name, perm))  4.45 us
    dot_general x2, matrix products, pair_cost(): lax.dot_general(lhs_rows, rhs_rows, (((1,), (1,)), ((), ())), precision=l...  4.17 us
    reduce_sum x8, other arithmetic, body(): totals = jnp.sum(jnp.exp(scores - maxima[None, :]), axis=0)  3.97 us
    reduce_sum x8, other arithmetic, body(): totals = jnp.sum(jnp.exp(scores - maxima[:, None]), axis=1)  3.27 us
    ppermute x1, starting transfers between devices, body(): theirs = lax.ppermute(mine, 'rows', [(0, 1), (1, 0)])  2.56 us
  transfers between devices with their start and end apart: 38, of which 27 were waited for; matrix products, arithmetic and copies ran while one was open for 2% of the time, Pallas kernels for 0%

profile of v10, /device:TPU:0, one launch (start us, length us, event | category | flops | bytes accessed | tf_op | source)
XLA Modules:
  0.0 105.7 jit_solution(16080934397766025884)
XLA Ops:
  2.3 1.0 multiply_reduce_fusion.1
  3.3 2.1 %subtract_reduce_fusion.16 = (f32[1024]{0:T(1024)S(1)}, f32[1024,256]{0,1:T(8,128)S(1)}) fusion(f32[256]{0:T(256)S(1)} %multiply_log_fusion, f32[1024,64]{0,1:T(8,128)} %param.5, f32[256,64]{0,1:T(8,128)} %param.7, f32[256]{0:T(256)S(1)} %multiply_reduce_fusion.2, f32[1024]{0:T(1024)S(1)} %multiply_reduce_fusion.1), kind=kOutput, calls=%fused_computation.41 | convolution fusion | flops 202898432 | bytes 1386496 | tf_op jit(solution)/shard_map/dot_general | solution.py:15
  6.6 2.6 %collective-permute-start = (f32[66560]{0:T(1024)S(1)}, f32[66560]{0:T(1024)S(1)}, u32[]{:S(2)}, u32[]{:S(2)}) collective-permute-start(f32[66560]{0:T(1024)S(1)} %pad_maximum_fusion.2), channel_id=1, source_target_pairs={{0,2},{2,0},{1,3},{3,1},{4,6},{6,4},{5,7},{7,5},{8,10},{10,8},{9,1... | collective-permute-start | bytes 798728 | tf_op jit(solution)/shard_map/ppermute | solution.py:251
  9.3 3.7 %collective-permute-start.4 = (f32[2,1024]{1,0:T(2,128)S(1)}, f32[2,1024]{1,0:T(2,128)S(1)}, u32[]{:S(2)}, u32[]{:S(2)}) collective-permute-start(f32[2,1024]{1,0:T(2,128)S(1)} %get-tuple-element.124), channel_id=1, source_target_pairs={{0,12},{4,8},{8,4},{12,0},{1,13},{5,9},{9,5},{13,1},{2,14},{6,10},... | collective-permute-start | bytes 24584 | tf_op jit(solution)/shard_map/ppermute | solution.py:66
  13.7 1.1 %collective-permute-done.4 = f32[2,1024]{1,0:T(2,128)S(1)} collective-permute-done((f32[2,1024]{1,0:T(2,128)S(1)}, f32[2,1024]{1,0:T(2,128)S(1)}, u32[]{:S(2)}, u32[]{:S(2)}) %collective-permute-start.4) | collective-permute-done | bytes 8224 | tf_op jit(solution)/shard_map/ppermute | solution.py:66
  14.8 2.7 %collective-permute-done.3 = f32[2,1024]{1,0:T(2,128)S(1)} collective-permute-done((f32[2,1024]{1,0:T(2,128)S(1)}, f32[2,1024]{1,0:T(2,128)S(1)}, u32[]{:S(2)}, u32[]{:S(2)}) %collective-permute-start.3) | collective-permute-done | bytes 8224 | tf_op jit(solution)/shard_map/ppermute | solution.py:66
  19.0 2.0 %fusion.1 = f32[2048,256]{0,1:T(8,128)S(1)} fusion(f32[256,64]{0,1:T(8,128)S(1)} %copy-done.2, f32[256]{0:T(256)S(1)} %copy-done.13, f32[2048]{0:T(1024)S(1)} %multiply_reduce_fusion, f32[1024,64]{1,0:T(8,128)S(1)} %get-tuple-element.14, f32[1024,64]{1,0:T(8,128)S(1)} %get-tuple-element.13), kind=kOutput, calls=%fused_computation.2 | convolution fusion | flops 404881408 | bytes 2696192 | tf_op jit(solution)/shard_map/dot_general | solution.py:15
  22.4 2.9 %collective-permute-done.5 = f32[2,256]{1,0:T(2,128)S(1)} collective-permute-done((f32[2,256]{1,0:T(2,128)S(1)}, f32[2,256]{1,0:T(2,128)S(1)}, u32[]{:S(2)}, u32[]{:S(2)}) %collective-permute-start.5) | collective-permute-done | bytes 2080 | tf_op jit(solution)/shard_map/ppermute | solution.py:44
  26.1 1.2 %collective-permute-done.6 = f32[2,2048]{1,0:T(2,128)S(1)} collective-permute-done((f32[2,2048]{1,0:T(2,128)S(1)}, f32[2,2048]{1,0:T(2,128)S(1)}, u32[]{:S(2)}, u32[]{:S(2)}) %collective-permute-start.6) | collective-permute-done | bytes 16416 | tf_op jit(solution)/shard_map/ppermute | solution.py:44
  27.4 2.0 %collective-permute-start.9 = (f32[2,2048]{1,0:T(2,128)S(1)}, f32[2,2048]{1,0:T(2,128)S(1)}, u32[]{:S(2)}, u32[]{:S(2)}) collective-permute-start(f32[2,2048]{1,0:T(2,128)S(1)} %get-tuple-element.120), channel_id=1, source_target_pairs={{0,12},{4,8},{8,4},{12,0},{1,13},{5,9},{9,5},{13,1},{2,14},{6,10},... | collective-permute-start | bytes 49160 | tf_op jit(solution)/shard_map/ppermute | solution.py:66
  29.5 2.3 %collective-permute-start.7 = (f32[2,2048]{1,0:T(2,128)S(1)}, f32[2,2048]{1,0:T(2,128)S(1)}, u32[]{:S(2)}, u32[]{:S(2)}) collective-permute-start(f32[2,2048]{1,0:T(2,128)S(1)} %get-tuple-element.120), channel_id=1, source_target_pairs={{0,4},{4,0},{8,12},{12,8},{1,5},{5,1},{9,13},{13,9},{2,6},{6,2},{1... | collective-permute-start | bytes 49160 | tf_op jit(solution)/shard_map/ppermute | solution.py:66
  31.8 1.4 %collective-permute-done.9 = f32[2,2048]{1,0:T(2,128)S(1)} collective-permute-done((f32[2,2048]{1,0:T(2,128)S(1)}, f32[2,2048]{1,0:T(2,128)S(1)}, u32[]{:S(2)}, u32[]{:S(2)}) %collective-permute-start.9) | collective-permute-done | bytes 16416 | tf_op jit(solution)/shard_map/ppermute | solution.py:66
  35.8 1.2 %collective-permute-done.10 = f32[2,2048]{1,0:T(2,128)S(1)} collective-permute-done((f32[2,2048]{1,0:T(2,128)S(1)}, f32[2,2048]{1,0:T(2,128)S(1)}, u32[]{:S(2)}, u32[]{:S(2)}) %collective-permute-start.10) | collective-permute-done | bytes 16416 | tf_op jit(solution)/shard_map/ppermute | solution.py:44
  37.1 2.0 %collective-permute-start.13 = (f32[2,2048]{1,0:T(2,128)S(1)}, f32[2,2048]{1,0:T(2,128)S(1)}, u32[]{:S(2)}, u32[]{:S(2)}) collective-permute-start(f32[2,2048]{1,0:T(2,128)S(1)} %get-tuple-element.118), channel_id=1, source_target_pairs={{0,12},{4,8},{8,4},{12,0},{1,13},{5,9},{9,5},{13,1},{2,14},{6,10},... | collective-permute-start | bytes 49160 | tf_op jit(solution)/shard_map/ppermute | solution.py:66
  40.0 1.5 %collective-permute-start.11 = (f32[2,2048]{1,0:T(2,128)S(1)}, f32[2,2048]{1,0:T(2,128)S(1)}, u32[]{:S(2)}, u32[]{:S(2)}) collective-permute-start(f32[2,2048]{1,0:T(2,128)S(1)} %get-tuple-element.118), channel_id=1, source_target_pairs={{0,4},{4,0},{8,12},{12,8},{1,5},{5,1},{9,13},{13,9},{2,6},{6,2},{1... | collective-permute-start | bytes 49160 | tf_op jit(solution)/shard_map/ppermute | solution.py:66
  41.5 1.2 %collective-permute-done.13 = f32[2,2048]{1,0:T(2,128)S(1)} collective-permute-done((f32[2,2048]{1,0:T(2,128)S(1)}, f32[2,2048]{1,0:T(2,128)S(1)}, u32[]{:S(2)}, u32[]{:S(2)}) %collective-permute-start.13) | collective-permute-done | bytes 16416 | tf_op jit(solution)/shard_map/ppermute | solution.py:66
  42.8 1.1 %collective-permute-done.12 = f32[2,2048]{1,0:T(2,128)S(1)} collective-permute-done((f32[2,2048]{1,0:T(2,128)S(1)}, f32[2,2048]{1,0:T(2,128)S(1)}, u32[]{:S(2)}, u32[]{:S(2)}) %collective-permute-start.12) | collective-permute-done | bytes 16416 | tf_op jit(solution)/shard_map/ppermute | solution.py:66
  45.6 1.2 %collective-permute-done.14 = f32[2,2048]{1,0:T(2,128)S(1)} collective-permute-done((f32[2,2048]{1,0:T(2,128)S(1)}, f32[2,2048]{1,0:T(2,128)S(1)}, u32[]{:S(2)}, u32[]{:S(2)}) %collective-permute-start.14) | collective-permute-done | bytes 16416 | tf_op jit(solution)/shard_map/ppermute | solution.py:44
  46.8 2.0 %collective-permute-start.17 = (f32[2,2048]{1,0:T(2,128)S(1)}, f32[2,2048]{1,0:T(2,128)S(1)}, u32[]{:S(2)}, u32[]{:S(2)}) collective-permute-start(f32[2,2048]{1,0:T(2,128)S(1)} %get-tuple-element.116), channel_id=1, source_target_pairs={{0,12},{4,8},{8,4},{12,0},{1,13},{5,9},{9,5},{13,1},{2,14},{6,10},... | collective-permute-start | bytes 49160 | tf_op jit(solution)/shard_map/ppermute | solution.py:66
  49.7 1.6 %collective-permute-start.15 = (f32[2,2048]{1,0:T(2,128)S(1)}, f32[2,2048]{1,0:T(2,128)S(1)}, u32[]{:S(2)}, u32[]{:S(2)}) collective-permute-start(f32[2,2048]{1,0:T(2,128)S(1)} %get-tuple-element.116), channel_id=1, source_target_pairs={{0,4},{4,0},{8,12},{12,8},{1,5},{5,1},{9,13},{13,9},{2,6},{6,2},{1... | collective-permute-start | bytes 49160 | tf_op jit(solution)/shard_map/ppermute | solution.py:66
  51.3 1.2 %collective-permute-done.17 = f32[2,2048]{1,0:T(2,128)S(1)} collective-permute-done((f32[2,2048]{1,0:T(2,128)S(1)}, f32[2,2048]{1,0:T(2,128)S(1)}, u32[]{:S(2)}, u32[]{:S(2)}) %collective-permute-start.17) | collective-permute-done | bytes 16416 | tf_op jit(solution)/shard_map/ppermute | solution.py:66
  52.5 1.1 %collective-permute-done.16 = f32[2,2048]{1,0:T(2,128)S(1)} collective-permute-done((f32[2,2048]{1,0:T(2,128)S(1)}, f32[2,2048]{1,0:T(2,128)S(1)}, u32[]{:S(2)}, u32[]{:S(2)}) %collective-permute-start.16) | collective-permute-done | bytes 16416 | tf_op jit(solution)/shard_map/ppermute | solution.py:66
  55.3 1.2 %collective-permute-done.18 = f32[2,2048]{1,0:T(2,128)S(1)} collective-permute-done((f32[2,2048]{1,0:T(2,128)S(1)}, f32[2,2048]{1,0:T(2,128)S(1)}, u32[]{:S(2)}, u32[]{:S(2)}) %collective-permute-start.18) | collective-permute-done | bytes 16416 | tf_op jit(solution)/shard_map/ppermute | solution.py:44
  56.6 2.0 %collective-permute-start.21 = (f32[2,2048]{1,0:T(2,128)S(1)}, f32[2,2048]{1,0:T(2,128)S(1)}, u32[]{:S(2)}, u32[]{:S(2)}) collective-permute-start(f32[2,2048]{1,0:T(2,128)S(1)} %get-tuple-element.114), channel_id=1, source_target_pairs={{0,12},{4,8},{8,4},{12,0},{1,13},{5,9},{9,5},{13,1},{2,14},{6,10},... | collective-permute-start | bytes 49160 | tf_op jit(solution)/shard_map/ppermute | solution.py:66
  59.5 1.5 %collective-permute-start.19 = (f32[2,2048]{1,0:T(2,128)S(1)}, f32[2,2048]{1,0:T(2,128)S(1)}, u32[]{:S(2)}, u32[]{:S(2)}) collective-permute-start(f32[2,2048]{1,0:T(2,128)S(1)} %get-tuple-element.114), channel_id=1, source_target_pairs={{0,4},{4,0},{8,12},{12,8},{1,5},{5,1},{9,13},{13,9},{2,6},{6,2},{1... | collective-permute-start | bytes 49160 | tf_op jit(solution)/shard_map/ppermute | solution.py:66
  61.0 1.2 %collective-permute-done.21 = f32[2,2048]{1,0:T(2,128)S(1)} collective-permute-done((f32[2,2048]{1,0:T(2,128)S(1)}, f32[2,2048]{1,0:T(2,128)S(1)}, u32[]{:S(2)}, u32[]{:S(2)}) %collective-permute-start.21) | collective-permute-done | bytes 16416 | tf_op jit(solution)/shard_map/ppermute | solution.py:66
  62.3 1.1 %collective-permute-done.20 = f32[2,2048]{1,0:T(2,128)S(1)} collective-permute-done((f32[2,2048]{1,0:T(2,128)S(1)}, f32[2,2048]{1,0:T(2,128)S(1)}, u32[]{:S(2)}, u32[]{:S(2)}) %collective-permute-start.20) | collective-permute-done | bytes 16416 | tf_op jit(solution)/shard_map/ppermute | solution.py:66
  65.2 1.2 %collective-permute-done.22 = f32[2,2048]{1,0:T(2,128)S(1)} collective-permute-done((f32[2,2048]{1,0:T(2,128)S(1)}, f32[2,2048]{1,0:T(2,128)S(1)}, u32[]{:S(2)}, u32[]{:S(2)}) %collective-permute-start.22) | collective-permute-done | bytes 16416 | tf_op jit(solution)/shard_map/ppermute | solution.py:44
  66.5 2.0 %collective-permute-start.25 = (f32[2,2048]{1,0:T(2,128)S(1)}, f32[2,2048]{1,0:T(2,128)S(1)}, u32[]{:S(2)}, u32[]{:S(2)}) collective-permute-start(f32[2,2048]{1,0:T(2,128)S(1)} %get-tuple-element.112), channel_id=1, source_target_pairs={{0,12},{4,8},{8,4},{12,0},{1,13},{5,9},{9,5},{13,1},{2,14},{6,10},... | collective-permute-start | bytes 49160 | tf_op jit(solution)/shard_map/ppermute | solution.py:66
  69.3 1.6 %collective-permute-start.23 = (f32[2,2048]{1,0:T(2,128)S(1)}, f32[2,2048]{1,0:T(2,128)S(1)}, u32[]{:S(2)}, u32[]{:S(2)}) collective-permute-start(f32[2,2048]{1,0:T(2,128)S(1)} %get-tuple-element.112), channel_id=1, source_target_pairs={{0,4},{4,0},{8,12},{12,8},{1,5},{5,1},{9,13},{13,9},{2,6},{6,2},{1... | collective-permute-start | bytes 49160 | tf_op jit(solution)/shard_map/ppermute | solution.py:66
  70.9 1.2 %collective-permute-done.25 = f32[2,2048]{1,0:T(2,128)S(1)} collective-permute-done((f32[2,2048]{1,0:T(2,128)S(1)}, f32[2,2048]{1,0:T(2,128)S(1)}, u32[]{:S(2)}, u32[]{:S(2)}) %collective-permute-start.25) | collective-permute-done | bytes 16416 | tf_op jit(solution)/shard_map/ppermute | solution.py:66
  72.1 1.2 %collective-permute-done.24 = f32[2,2048]{1,0:T(2,128)S(1)} collective-permute-done((f32[2,2048]{1,0:T(2,128)S(1)}, f32[2,2048]{1,0:T(2,128)S(1)}, u32[]{:S(2)}, u32[]{:S(2)}) %collective-permute-start.24) | collective-permute-done | bytes 16416 | tf_op jit(solution)/shard_map/ppermute | solution.py:66
  74.9 1.2 %collective-permute-done.26 = f32[2,2048]{1,0:T(2,128)S(1)} collective-permute-done((f32[2,2048]{1,0:T(2,128)S(1)}, f32[2,2048]{1,0:T(2,128)S(1)}, u32[]{:S(2)}, u32[]{:S(2)}) %collective-permute-start.26) | collective-permute-done | bytes 16416 | tf_op jit(solution)/shard_map/ppermute | solution.py:44
  76.2 2.0 %collective-permute-start.29 = (f32[2,2048]{1,0:T(2,128)S(1)}, f32[2,2048]{1,0:T(2,128)S(1)}, u32[]{:S(2)}, u32[]{:S(2)}) collective-permute-start(f32[2,2048]{1,0:T(2,128)S(1)} %get-tuple-element.110), channel_id=1, source_target_pairs={{0,12},{4,8},{8,4},{12,0},{1,13},{5,9},{9,5},{13,1},{2,14},{6,10},... | collective-permute-start | bytes 49160 | tf_op jit(solution)/shard_map/ppermute | solution.py:66
  79.1 1.5 %collective-permute-start.27 = (f32[2,2048]{1,0:T(2,128)S(1)}, f32[2,2048]{1,0:T(2,128)S(1)}, u32[]{:S(2)}, u32[]{:S(2)}) collective-permute-start(f32[2,2048]{1,0:T(2,128)S(1)} %get-tuple-element.110), channel_id=1, source_target_pairs={{0,4},{4,0},{8,12},{12,8},{1,5},{5,1},{9,13},{13,9},{2,6},{6,2},{1... | collective-permute-start | bytes 49160 | tf_op jit(solution)/shard_map/ppermute | solution.py:66
  80.6 1.2 %collective-permute-done.29 = f32[2,2048]{1,0:T(2,128)S(1)} collective-permute-done((f32[2,2048]{1,0:T(2,128)S(1)}, f32[2,2048]{1,0:T(2,128)S(1)}, u32[]{:S(2)}, u32[]{:S(2)}) %collective-permute-start.29) | collective-permute-done | bytes 16416 | tf_op jit(solution)/shard_map/ppermute | solution.py:66
  81.9 1.1 %collective-permute-done.28 = f32[2,2048]{1,0:T(2,128)S(1)} collective-permute-done((f32[2,2048]{1,0:T(2,128)S(1)}, f32[2,2048]{1,0:T(2,128)S(1)}, u32[]{:S(2)}, u32[]{:S(2)}) %collective-permute-start.28) | collective-permute-done | bytes 16416 | tf_op jit(solution)/shard_map/ppermute | solution.py:66
  84.7 1.2 %collective-permute-done.30 = f32[2,2048]{1,0:T(2,128)S(1)} collective-permute-done((f32[2,2048]{1,0:T(2,128)S(1)}, f32[2,2048]{1,0:T(2,128)S(1)}, u32[]{:S(2)}, u32[]{:S(2)}) %collective-permute-start.30) | collective-permute-done | bytes 16416 | tf_op jit(solution)/shard_map/ppermute | solution.py:44
  85.9 2.0 %collective-permute-start.33 = (f32[2,2048]{1,0:T(2,128)S(1)}, f32[2,2048]{1,0:T(2,128)S(1)}, u32[]{:S(2)}, u32[]{:S(2)}) collective-permute-start(f32[2,2048]{1,0:T(2,128)S(1)} %get-tuple-element.108), channel_id=1, source_target_pairs={{0,12},{4,8},{8,4},{12,0},{1,13},{5,9},{9,5},{13,1},{2,14},{6,10},... | collective-permute-start | bytes 49160 | tf_op jit(solution)/shard_map/ppermute | solution.py:66
  88.8 1.6 %collective-permute-start.31 = (f32[2,2048]{1,0:T(2,128)S(1)}, f32[2,2048]{1,0:T(2,128)S(1)}, u32[]{:S(2)}, u32[]{:S(2)}) collective-permute-start(f32[2,2048]{1,0:T(2,128)S(1)} %get-tuple-element.108), channel_id=1, source_target_pairs={{0,4},{4,0},{8,12},{12,8},{1,5},{5,1},{9,13},{13,9},{2,6},{6,2},{1... | collective-permute-start | bytes 49160 | tf_op jit(solution)/shard_map/ppermute | solution.py:66
  90.4 1.2 %collective-permute-done.33 = f32[2,2048]{1,0:T(2,128)S(1)} collective-permute-done((f32[2,2048]{1,0:T(2,128)S(1)}, f32[2,2048]{1,0:T(2,128)S(1)}, u32[]{:S(2)}, u32[]{:S(2)}) %collective-permute-start.33) | collective-permute-done | bytes 16416 | tf_op jit(solution)/shard_map/ppermute | solution.py:66
  91.6 1.2 %collective-permute-done.32 = f32[2,2048]{1,0:T(2,128)S(1)} collective-permute-done((f32[2,2048]{1,0:T(2,128)S(1)}, f32[2,2048]{1,0:T(2,128)S(1)}, u32[]{:S(2)}, u32[]{:S(2)}) %collective-permute-start.32) | collective-permute-done | bytes 16416 | tf_op jit(solution)/shard_map/ppermute | solution.py:66
  94.6 1.0 fusion.5
  96.1 1.3 %collective-permute-done.34 = f32[4,128,66]{1,0,2:T(4,128)S(1)} collective-permute-done((f32[4,128,66]{1,0,2:T(4,128)S(1)}, f32[4,128,66]{1,0,2:T(4,128)S(1)}, u32[]{:S(2)}, u32[]{:S(2)}) %collective-permute-start.34) | collective-permute-done | bytes 135200 | tf_op jit(solution)/shard_map/ppermute | solution.py:189
  97.6 2.0 %collective-permute-start.37 = (f32[128,66]{0,1:T(8,128)S(1)}, f32[128,66]{0,1:T(8,128)S(1)}, u32[]{:S(2)}, u32[]{:S(2)}) collective-permute-start(f32[128,66]{0,1:T(8,128)S(1)} %bitcast.198), channel_id=1, source_target_pairs={{0,12},{4,8},{8,4},{12,0},{1,13},{5,9},{9,5},{13,1},{2,14},{6,10},... | collective-permute-start | bytes 101384 | tf_op jit(solution)/shard_map/ppermute | solution.py:152
  100.6 1.5 %collective-permute-start.35 = (f32[128,66]{0,1:T(8,128)S(1)}, f32[128,66]{0,1:T(8,128)S(1)}, u32[]{:S(2)}, u32[]{:S(2)}) collective-permute-start(f32[128,66]{0,1:T(8,128)S(1)} %bitcast.200), channel_id=1, source_target_pairs={{0,4},{4,0},{8,12},{12,8},{1,5},{5,1},{9,13},{13,9},{2,6},{6,2},{1... | collective-permute-start | bytes 101384 | tf_op jit(solution)/shard_map/ppermute | solution.py:152
  102.7 1.0 collective-permute-done.37
  103.7 1.3 %collective-permute-done.36 = f32[128,66]{0,1:T(8,128)S(1)} collective-permute-done((f32[128,66]{0,1:T(8,128)S(1)}, f32[128,66]{0,1:T(8,128)S(1)}, u32[]{:S(2)}, u32[]{:S(2)}) %collective-permute-start.36) | collective-permute-done | bytes 33824 | tf_op jit(solution)/shard_map/ppermute | solution.py:152
  (179 shorter events, 28.6 us)
Async XLA Ops:
  0.6 94.0 %copy-start = (f32[256,64]{0,1:T(8,128)S(1)}, f32[256,64]{0,1:T(8,128)}, u32[]{:S(2)}) copy-start(f32[256,64]{0,1:T(8,128)} %param.9) | copy-start | bytes 196612
  0.6 5.6 %copy-start.1 = (f32[1024,64]{0,1:T(8,128)S(1)}, f32[1024,64]{0,1:T(8,128)}, u32[]{:S(2)}) copy-start(f32[1024,64]{0,1:T(8,128)} %param.5) | copy-start | bytes 786436
  1.6 4.9 %copy-start.12 = (f32[256]{0:T(256)}, f32[256]{0:T(256)S(1)}, u32[]{:S(2)}) copy-start(f32[256]{0:T(256)S(1)} %multiply_reduce_fusion.2) | copy-start | bytes 3076
  3.2 3.4 %copy-start.4 = (f32[1024]{0:T(1024)S(1)}, f32[1024]{0:T(1024)}, u32[]{:S(2)}) copy-start(f32[1024]{0:T(1024)} %param.6) | copy-start | bytes 12292
  5.7 3.5 %collective-permute-start.1 = (f32[2,1024]{1,0:T(2,128)S(1)}, f32[2,1024]{1,0:T(2,128)S(1)}, u32[]{:S(2)}, u32[]{:S(2)}) collective-permute-start(f32[2,1024]{1,0:T(2,128)S(1)} %pad_maximum_fusion.26), channel_id=1, source_target_pairs={{0,1},{1,0},{2,3},{3,2},{4,5},{5,4},{6,7},{7,6},{8,9},{9,8},{10,11... | collective-permute-start | bytes 24584 | tf_op jit(solution)/shard_map/ppermute | solution.py:44
  6.6 11.5 %collective-permute-start = (f32[66560]{0:T(1024)S(1)}, f32[66560]{0:T(1024)S(1)}, u32[]{:S(2)}, u32[]{:S(2)}) collective-permute-start(f32[66560]{0:T(1024)S(1)} %pad_maximum_fusion.2), channel_id=1, source_target_pairs={{0,2},{2,0},{1,3},{3,1},{4,6},{6,4},{5,7},{7,5},{8,10},{10,8},{9,1... | collective-permute-start | bytes 798728 | tf_op jit(solution)/shard_map/ppermute | solution.py:251
  9.3 5.5 %collective-permute-start.4 = (f32[2,1024]{1,0:T(2,128)S(1)}, f32[2,1024]{1,0:T(2,128)S(1)}, u32[]{:S(2)}, u32[]{:S(2)}) collective-permute-start(f32[2,1024]{1,0:T(2,128)S(1)} %get-tuple-element.124), channel_id=1, source_target_pairs={{0,12},{4,8},{8,4},{12,0},{1,13},{5,9},{9,5},{13,1},{2,14},{6,10},... | collective-permute-start | bytes 24584 | tf_op jit(solution)/shard_map/ppermute | solution.py:66
  12.9 4.5 %collective-permute-start.3 = (f32[2,1024]{1,0:T(2,128)S(1)}, f32[2,1024]{1,0:T(2,128)S(1)}, u32[]{:S(2)}, u32[]{:S(2)}) collective-permute-start(f32[2,1024]{1,0:T(2,128)S(1)} %get-tuple-element.124), channel_id=1, source_target_pairs={{0,8},{4,12},{8,0},{12,4},{1,9},{5,13},{9,1},{13,5},{2,10},{6,14},... | collective-permute-start | bytes 24584 | tf_op jit(solution)/shard_map/ppermute | solution.py:66
  12.9 4.5 %collective-permute-start.2 = (f32[2,1024]{1,0:T(2,128)S(1)}, f32[2,1024]{1,0:T(2,128)S(1)}, u32[]{:S(2)}, u32[]{:S(2)}) collective-permute-start(f32[2,1024]{1,0:T(2,128)S(1)} %get-tuple-element.124), channel_id=1, source_target_pairs={{0,4},{4,0},{8,12},{12,8},{1,5},{5,1},{9,13},{13,9},{2,6},{6,2},{1... | collective-permute-start | bytes 24584 | tf_op jit(solution)/shard_map/ppermute | solution.py:66
  18.4 2.6 %copy-start.5 = (f32[1,1,1024]{2,1,0:T(1,128)S(1)}, f32[1,1,1024]{2,1,0:T(1,128)}, u32[]{:S(2)}) copy-start(f32[1,1,1024]{2,1,0:T(1,128)} %get-tuple-element.86) | copy-start | bytes 12292
  18.4 2.6 %copy-start.6 = (f32[1,1,1024]{2,1,0:T(1,128)S(1)}, f32[1,1,1024]{2,1,0:T(1,128)}, u32[]{:S(2)}) copy-start(f32[1,1,1024]{2,1,0:T(1,128)} %get-tuple-element.87) | copy-start | bytes 12292
  18.4 2.6 %copy-start.7 = (f32[1,1,1024]{2,1,0:T(1,128)S(1)}, f32[1,1,1024]{2,1,0:T(1,128)}, u32[]{:S(2)}) copy-start(f32[1,1,1024]{2,1,0:T(1,128)} %get-tuple-element.88) | copy-start | bytes 12292
  18.5 2.6 %copy-start.8 = (f32[1,1,1024]{2,1,0:T(1,128)S(1)}, f32[1,1,1024]{2,1,0:T(1,128)}, u32[]{:S(2)}) copy-start(f32[1,1,1024]{2,1,0:T(1,128)} %get-tuple-element.89) | copy-start | bytes 12292
  18.5 2.6 %copy-start.9 = (f32[1,1,1024]{2,1,0:T(1,128)S(1)}, f32[1,1,1024]{2,1,0:T(1,128)}, u32[]{:S(2)}) copy-start(f32[1,1,1024]{2,1,0:T(1,128)} %get-tuple-element.90) | copy-start | bytes 12292
  19.0 6.3 %copy-start.3 = (f32[256]{0:T(256)S(1)}, f32[256]{0:T(256)}, u32[]{:S(2)}) copy-start(f32[256]{0:T(256)} %param.8) | copy-start | bytes 3076
  21.7 3.7 %collective-permute-start.5 = (f32[2,256]{1,0:T(2,128)S(1)}, f32[2,256]{1,0:T(2,128)S(1)}, u32[]{:S(2)}, u32[]{:S(2)}) collective-permute-start(f32[2,256]{1,0:T(2,128)S(1)} %pad_maximum_fusion.28), channel_id=1, source_target_pairs={{0,2},{2,0},{1,3},{3,1},{4,6},{6,4},{5,7},{7,5},{8,10},{10,8},{9,1... | collective-permute-start | bytes 6152 | tf_op jit(solution)/shard_map/ppermute | solution.py:44
  26.0 1.2 %collective-permute-start.6 = (f32[2,2048]{1,0:T(2,128)S(1)}, f32[2,2048]{1,0:T(2,128)S(1)}, u32[]{:S(2)}, u32[]{:S(2)}) collective-permute-start(f32[2,2048]{1,0:T(2,128)S(1)} %pad_maximum_fusion.12), channel_id=1, source_target_pairs={{0,1},{1,0},{2,3},{3,2},{4,5},{5,4},{6,7},{7,6},{8,9},{9,8},{10,11... | collective-permute-start | bytes 49160 | tf_op jit(solution)/shard_map/ppermute | solution.py:44
  27.4 5.8 %collective-permute-start.9 = (f32[2,2048]{1,0:T(2,128)S(1)}, f32[2,2048]{1,0:T(2,128)S(1)}, u32[]{:S(2)}, u32[]{:S(2)}) collective-permute-start(f32[2,2048]{1,0:T(2,128)S(1)} %get-tuple-element.120), channel_id=1, source_target_pairs={{0,12},{4,8},{8,4},{12,0},{1,13},{5,9},{9,5},{13,1},{2,14},{6,10},... | collective-permute-start | bytes 49160 | tf_op jit(solution)/shard_map/ppermute | solution.py:66
  29.4 4.8 %collective-permute-start.8 = (f32[2,2048]{1,0:T(2,128)S(1)}, f32[2,2048]{1,0:T(2,128)S(1)}, u32[]{:S(2)}, u32[]{:S(2)}) collective-permute-start(f32[2,2048]{1,0:T(2,128)S(1)} %get-tuple-element.120), channel_id=1, source_target_pairs={{0,8},{4,12},{8,0},{12,4},{1,9},{5,13},{9,1},{13,5},{2,10},{6,14},... | collective-permute-start | bytes 49160 | tf_op jit(solution)/shard_map/ppermute | solution.py:66
  29.5 4.6 %collective-permute-start.7 = (f32[2,2048]{1,0:T(2,128)S(1)}, f32[2,2048]{1,0:T(2,128)S(1)}, u32[]{:S(2)}, u32[]{:S(2)}) collective-permute-start(f32[2,2048]{1,0:T(2,128)S(1)} %get-tuple-element.120), channel_id=1, source_target_pairs={{0,4},{4,0},{8,12},{12,8},{1,5},{5,1},{9,13},{13,9},{2,6},{6,2},{1... | collective-permute-start | bytes 49160 | tf_op jit(solution)/shard_map/ppermute | solution.py:66
  35.8 1.2 %collective-permute-start.10 = (f32[2,2048]{1,0:T(2,128)S(1)}, f32[2,2048]{1,0:T(2,128)S(1)}, u32[]{:S(2)}, u32[]{:S(2)}) collective-permute-start(f32[2,2048]{1,0:T(2,128)S(1)} %pad_maximum_fusion.14), channel_id=1, source_target_pairs={{0,1},{1,0},{2,3},{3,2},{4,5},{5,4},{6,7},{7,6},{8,9},{9,8},{10,11... | collective-permute-start | bytes 49160 | tf_op jit(solution)/shard_map/ppermute | solution.py:44
  37.1 5.7 %collective-permute-start.13 = (f32[2,2048]{1,0:T(2,128)S(1)}, f32[2,2048]{1,0:T(2,128)S(1)}, u32[]{:S(2)}, u32[]{:S(2)}) collective-permute-start(f32[2,2048]{1,0:T(2,128)S(1)} %get-tuple-element.118), channel_id=1, source_target_pairs={{0,12},{4,8},{8,4},{12,0},{1,13},{5,9},{9,5},{13,1},{2,14},{6,10},... | collective-permute-start | bytes 49160 | tf_op jit(solution)/shard_map/ppermute | solution.py:66
  39.1 4.8 %collective-permute-start.12 = (f32[2,2048]{1,0:T(2,128)S(1)}, f32[2,2048]{1,0:T(2,128)S(1)}, u32[]{:S(2)}, u32[]{:S(2)}) collective-permute-start(f32[2,2048]{1,0:T(2,128)S(1)} %get-tuple-element.118), channel_id=1, source_target_pairs={{0,8},{4,12},{8,0},{12,4},{1,9},{5,13},{9,1},{13,5},{2,10},{6,14},... | collective-permute-start | bytes 49160 | tf_op jit(solution)/shard_map/ppermute | solution.py:66
  40.0 3.9 %collective-permute-start.11 = (f32[2,2048]{1,0:T(2,128)S(1)}, f32[2,2048]{1,0:T(2,128)S(1)}, u32[]{:S(2)}, u32[]{:S(2)}) collective-permute-start(f32[2,2048]{1,0:T(2,128)S(1)} %get-tuple-element.118), channel_id=1, source_target_pairs={{0,4},{4,0},{8,12},{12,8},{1,5},{5,1},{9,13},{13,9},{2,6},{6,2},{1... | collective-permute-start | bytes 49160 | tf_op jit(solution)/shard_map/ppermute | solution.py:66
  45.5 1.2 %collective-permute-start.14 = (f32[2,2048]{1,0:T(2,128)S(1)}, f32[2,2048]{1,0:T(2,128)S(1)}, u32[]{:S(2)}, u32[]{:S(2)}) collective-permute-start(f32[2,2048]{1,0:T(2,128)S(1)} %pad_maximum_fusion.16), channel_id=1, source_target_pairs={{0,1},{1,0},{2,3},{3,2},{4,5},{5,4},{6,7},{7,6},{8,9},{9,8},{10,11... | collective-permute-start | bytes 49160 | tf_op jit(solution)/shard_map/ppermute | solution.py:44
  46.8 5.7 %collective-permute-start.17 = (f32[2,2048]{1,0:T(2,128)S(1)}, f32[2,2048]{1,0:T(2,128)S(1)}, u32[]{:S(2)}, u32[]{:S(2)}) collective-permute-start(f32[2,2048]{1,0:T(2,128)S(1)} %get-tuple-element.116), channel_id=1, source_target_pairs={{0,12},{4,8},{8,4},{12,0},{1,13},{5,9},{9,5},{13,1},{2,14},{6,10},... | collective-permute-start | bytes 49160 | tf_op jit(solution)/shard_map/ppermute | solution.py:66
  48.9 4.8 %collective-permute-start.16 = (f32[2,2048]{1,0:T(2,128)S(1)}, f32[2,2048]{1,0:T(2,128)S(1)}, u32[]{:S(2)}, u32[]{:S(2)}) collective-permute-start(f32[2,2048]{1,0:T(2,128)S(1)} %get-tuple-element.116), channel_id=1, source_target_pairs={{0,8},{4,12},{8,0},{12,4},{1,9},{5,13},{9,1},{13,5},{2,10},{6,14},... | collective-permute-start | bytes 49160 | tf_op jit(solution)/shard_map/ppermute | solution.py:66
  49.7 3.9 %collective-permute-start.15 = (f32[2,2048]{1,0:T(2,128)S(1)}, f32[2,2048]{1,0:T(2,128)S(1)}, u32[]{:S(2)}, u32[]{:S(2)}) collective-permute-start(f32[2,2048]{1,0:T(2,128)S(1)} %get-tuple-element.116), channel_id=1, source_target_pairs={{0,4},{4,0},{8,12},{12,8},{1,5},{5,1},{9,13},{13,9},{2,6},{6,2},{1... | collective-permute-start | bytes 49160 | tf_op jit(solution)/shard_map/ppermute | solution.py:66
  55.2 1.2 %collective-permute-start.18 = (f32[2,2048]{1,0:T(2,128)S(1)}, f32[2,2048]{1,0:T(2,128)S(1)}, u32[]{:S(2)}, u32[]{:S(2)}) collective-permute-start(f32[2,2048]{1,0:T(2,128)S(1)} %pad_maximum_fusion.18), channel_id=1, source_target_pairs={{0,1},{1,0},{2,3},{3,2},{4,5},{5,4},{6,7},{7,6},{8,9},{9,8},{10,11... | collective-permute-start | bytes 49160 | tf_op jit(solution)/shard_map/ppermute | solution.py:44
  56.6 5.7 %collective-permute-start.21 = (f32[2,2048]{1,0:T(2,128)S(1)}, f32[2,2048]{1,0:T(2,128)S(1)}, u32[]{:S(2)}, u32[]{:S(2)}) collective-permute-start(f32[2,2048]{1,0:T(2,128)S(1)} %get-tuple-element.114), channel_id=1, source_target_pairs={{0,12},{4,8},{8,4},{12,0},{1,13},{5,9},{9,5},{13,1},{2,14},{6,10},... | collective-permute-start | bytes 49160 | tf_op jit(solution)/shard_map/ppermute | solution.py:66
  58.6 4.8 %collective-permute-start.20 = (f32[2,2048]{1,0:T(2,128)S(1)}, f32[2,2048]{1,0:T(2,128)S(1)}, u32[]{:S(2)}, u32[]{:S(2)}) collective-permute-start(f32[2,2048]{1,0:T(2,128)S(1)} %get-tuple-element.114), channel_id=1, source_target_pairs={{0,8},{4,12},{8,0},{12,4},{1,9},{5,13},{9,1},{13,5},{2,10},{6,14},... | collective-permute-start | bytes 49160 | tf_op jit(solution)/shard_map/ppermute | solution.py:66
  59.5 3.9 %collective-permute-start.19 = (f32[2,2048]{1,0:T(2,128)S(1)}, f32[2,2048]{1,0:T(2,128)S(1)}, u32[]{:S(2)}, u32[]{:S(2)}) collective-permute-start(f32[2,2048]{1,0:T(2,128)S(1)} %get-tuple-element.114), channel_id=1, source_target_pairs={{0,4},{4,0},{8,12},{12,8},{1,5},{5,1},{9,13},{13,9},{2,6},{6,2},{1... | collective-permute-start | bytes 49160 | tf_op jit(solution)/shard_map/ppermute | solution.py:66
  65.1 1.2 %collective-permute-start.22 = (f32[2,2048]{1,0:T(2,128)S(1)}, f32[2,2048]{1,0:T(2,128)S(1)}, u32[]{:S(2)}, u32[]{:S(2)}) collective-permute-start(f32[2,2048]{1,0:T(2,128)S(1)} %pad_maximum_fusion.20), channel_id=1, source_target_pairs={{0,1},{1,0},{2,3},{3,2},{4,5},{5,4},{6,7},{7,6},{8,9},{9,8},{10,11... | collective-permute-start | bytes 49160 | tf_op jit(solution)/shard_map/ppermute | solution.py:44
  66.5 5.7 %collective-permute-start.25 = (f32[2,2048]{1,0:T(2,128)S(1)}, f32[2,2048]{1,0:T(2,128)S(1)}, u32[]{:S(2)}, u32[]{:S(2)}) collective-permute-start(f32[2,2048]{1,0:T(2,128)S(1)} %get-tuple-element.112), channel_id=1, source_target_pairs={{0,12},{4,8},{8,4},{12,0},{1,13},{5,9},{9,5},{13,1},{2,14},{6,10},... | collective-permute-start | bytes 49160 | tf_op jit(solution)/shard_map/ppermute | solution.py:66
  68.5 4.8 %collective-permute-start.24 = (f32[2,2048]{1,0:T(2,128)S(1)}, f32[2,2048]{1,0:T(2,128)S(1)}, u32[]{:S(2)}, u32[]{:S(2)}) collective-permute-start(f32[2,2048]{1,0:T(2,128)S(1)} %get-tuple-element.112), channel_id=1, source_target_pairs={{0,8},{4,12},{8,0},{12,4},{1,9},{5,13},{9,1},{13,5},{2,10},{6,14},... | collective-permute-start | bytes 49160 | tf_op jit(solution)/shard_map/ppermute | solution.py:66
  69.3 3.9 %collective-permute-start.23 = (f32[2,2048]{1,0:T(2,128)S(1)}, f32[2,2048]{1,0:T(2,128)S(1)}, u32[]{:S(2)}, u32[]{:S(2)}) collective-permute-start(f32[2,2048]{1,0:T(2,128)S(1)} %get-tuple-element.112), channel_id=1, source_target_pairs={{0,4},{4,0},{8,12},{12,8},{1,5},{5,1},{9,13},{13,9},{2,6},{6,2},{1... | collective-permute-start | bytes 49160 | tf_op jit(solution)/shard_map/ppermute | solution.py:66
  74.8 1.2 %collective-permute-start.26 = (f32[2,2048]{1,0:T(2,128)S(1)}, f32[2,2048]{1,0:T(2,128)S(1)}, u32[]{:S(2)}, u32[]{:S(2)}) collective-permute-start(f32[2,2048]{1,0:T(2,128)S(1)} %pad_maximum_fusion.22), channel_id=1, source_target_pairs={{0,1},{1,0},{2,3},{3,2},{4,5},{5,4},{6,7},{7,6},{8,9},{9,8},{10,11... | collective-permute-start | bytes 49160 | tf_op jit(solution)/shard_map/ppermute | solution.py:44
  76.2 5.7 %collective-permute-start.29 = (f32[2,2048]{1,0:T(2,128)S(1)}, f32[2,2048]{1,0:T(2,128)S(1)}, u32[]{:S(2)}, u32[]{:S(2)}) collective-permute-start(f32[2,2048]{1,0:T(2,128)S(1)} %get-tuple-element.110), channel_id=1, source_target_pairs={{0,12},{4,8},{8,4},{12,0},{1,13},{5,9},{9,5},{13,1},{2,14},{6,10},... | collective-permute-start | bytes 49160 | tf_op jit(solution)/shard_map/ppermute | solution.py:66
  78.2 4.8 %collective-permute-start.28 = (f32[2,2048]{1,0:T(2,128)S(1)}, f32[2,2048]{1,0:T(2,128)S(1)}, u32[]{:S(2)}, u32[]{:S(2)}) collective-permute-start(f32[2,2048]{1,0:T(2,128)S(1)} %get-tuple-element.110), channel_id=1, source_target_pairs={{0,8},{4,12},{8,0},{12,4},{1,9},{5,13},{9,1},{13,5},{2,10},{6,14},... | collective-permute-start | bytes 49160 | tf_op jit(solution)/shard_map/ppermute | solution.py:66
  79.1 3.9 %collective-permute-start.27 = (f32[2,2048]{1,0:T(2,128)S(1)}, f32[2,2048]{1,0:T(2,128)S(1)}, u32[]{:S(2)}, u32[]{:S(2)}) collective-permute-start(f32[2,2048]{1,0:T(2,128)S(1)} %get-tuple-element.110), channel_id=1, source_target_pairs={{0,4},{4,0},{8,12},{12,8},{1,5},{5,1},{9,13},{13,9},{2,6},{6,2},{1... | collective-permute-start | bytes 49160 | tf_op jit(solution)/shard_map/ppermute | solution.py:66
  84.6 1.2 %collective-permute-start.30 = (f32[2,2048]{1,0:T(2,128)S(1)}, f32[2,2048]{1,0:T(2,128)S(1)}, u32[]{:S(2)}, u32[]{:S(2)}) collective-permute-start(f32[2,2048]{1,0:T(2,128)S(1)} %pad_maximum_fusion.24), channel_id=1, source_target_pairs={{0,1},{1,0},{2,3},{3,2},{4,5},{5,4},{6,7},{7,6},{8,9},{9,8},{10,11... | collective-permute-start | bytes 49160 | tf_op jit(solution)/shard_map/ppermute | solution.py:44
  85.9 5.6 %collective-permute-start.33 = (f32[2,2048]{1,0:T(2,128)S(1)}, f32[2,2048]{1,0:T(2,128)S(1)}, u32[]{:S(2)}, u32[]{:S(2)}) collective-permute-start(f32[2,2048]{1,0:T(2,128)S(1)} %get-tuple-element.108), channel_id=1, source_target_pairs={{0,12},{4,8},{8,4},{12,0},{1,13},{5,9},{9,5},{13,1},{2,14},{6,10},... | collective-permute-start | bytes 49160 | tf_op jit(solution)/shard_map/ppermute | solution.py:66
  87.9 4.8 %collective-permute-start.32 = (f32[2,2048]{1,0:T(2,128)S(1)}, f32[2,2048]{1,0:T(2,128)S(1)}, u32[]{:S(2)}, u32[]{:S(2)}) collective-permute-start(f32[2,2048]{1,0:T(2,128)S(1)} %get-tuple-element.108), channel_id=1, source_target_pairs={{0,8},{4,12},{8,0},{12,4},{1,9},{5,13},{9,1},{13,5},{2,10},{6,14},... | collective-permute-start | bytes 49160 | tf_op jit(solution)/shard_map/ppermute | solution.py:66
  88.8 3.9 %collective-permute-start.31 = (f32[2,2048]{1,0:T(2,128)S(1)}, f32[2,2048]{1,0:T(2,128)S(1)}, u32[]{:S(2)}, u32[]{:S(2)}) collective-permute-start(f32[2,2048]{1,0:T(2,128)S(1)} %get-tuple-element.108), channel_id=1, source_target_pairs={{0,4},{4,0},{8,12},{12,8},{1,5},{5,1},{9,13},{13,9},{2,6},{6,2},{1... | collective-permute-start | bytes 49160 | tf_op jit(solution)/shard_map/ppermute | solution.py:66
  96.0 1.4 %collective-permute-start.34 = (f32[4,128,66]{1,0,2:T(4,128)S(1)}, f32[4,128,66]{1,0,2:T(4,128)S(1)}, u32[]{:S(2)}, u32[]{:S(2)}) collective-permute-start(f32[4,128,66]{1,0,2:T(4,128)S(1)} %get-tuple-element.16), channel_id=1, source_target_pairs={{0,1},{1,0},{2,3},{3,2},{4,5},{5,4},{6,7},{7,6},{8,9},{9,8},{10,11... | collective-permute-start | bytes 405512 | tf_op jit(solution)/shard_map/ppermute | solution.py:189
  97.6 6.1 %collective-permute-start.37 = (f32[128,66]{0,1:T(8,128)S(1)}, f32[128,66]{0,1:T(8,128)S(1)}, u32[]{:S(2)}, u32[]{:S(2)}) collective-permute-start(f32[128,66]{0,1:T(8,128)S(1)} %bitcast.198), channel_id=1, source_target_pairs={{0,12},{4,8},{8,4},{12,0},{1,13},{5,9},{9,5},{13,1},{2,14},{6,10},... | collective-permute-start | bytes 101384 | tf_op jit(solution)/shard_map/ppermute | solution.py:152
  99.6 5.4 %collective-permute-start.36 = (f32[128,66]{0,1:T(8,128)S(1)}, f32[128,66]{0,1:T(8,128)S(1)}, u32[]{:S(2)}, u32[]{:S(2)}) collective-permute-start(f32[128,66]{0,1:T(8,128)S(1)} %bitcast.199), channel_id=1, source_target_pairs={{0,8},{4,12},{8,0},{12,4},{1,9},{5,13},{9,1},{13,5},{2,10},{6,14},... | collective-permute-start | bytes 101384 | tf_op jit(solution)/shard_map/ppermute | solution.py:152
  100.6 4.4 %collective-permute-start.35 = (f32[128,66]{0,1:T(8,128)S(1)}, f32[128,66]{0,1:T(8,128)S(1)}, u32[]{:S(2)}, u32[]{:S(2)}) collective-permute-start(f32[128,66]{0,1:T(8,128)S(1)} %bitcast.200), channel_id=1, source_target_pairs={{0,4},{4,0},{8,12},{12,8},{1,5},{5,1},{9,13},{13,9},{2,6},{6,2},{1... | collective-permute-start | bytes 101384 | tf_op jit(solution)/shard_map/ppermute | solution.py:152
  (4 other events, 6.8 us)

commit v11 on v10

--- a/solution.py
+++ b/solution.py
@@ -247,7 +247,10 @@
     row = lax.axis_index("rows")
     dim = sources.shape[1]
     flat = src_count * dim
-    mine = jnp.concatenate([sources.reshape(flat), source_mass])
+    lanes = 128
+    mine = jnp.concatenate(
+        [sources.reshape(flat // lanes, lanes), source_mass.reshape(src_count // lanes, lanes)]
+    )
     theirs = lax.ppermute(mine, "rows", [(0, 1), (1, 0)])
     all_sources = src_count * row_count
     all_targets = tgt_count * lax.axis_size(("cols", "rep"))
@@ -273,8 +276,8 @@
     g_pot = -relaxed * entropic * (maxima + jnp.log(totals))
 
     lead = row == 0
-    their_src = theirs[:flat].reshape(src_count, dim)
-    their_mass = theirs[flat:]
+    their_src = theirs[: flat // lanes].reshape(src_count, dim)
+    their_mass = theirs[flat // lanes :].reshape(src_count)
     all_src = jnp.concatenate(
         [jnp.where(lead, sources, their_src), jnp.where(lead, their_src, sources)]
     )

time: 106 us -> 106 us (level)
  no operation moved by 1% of the time
where the time goes in v11:
time: 106 us
  starting transfers between devices  44.5 us (42%)
  waiting for transfers between devices  35 us (33%)
  other arithmetic  17.1 us (16%)
  matrix products  5.18 us (5%)
  local copies, waits for them, and re-layouts  2.37 us (2%)
  between operations  1.48 us (1%)
    ppermute x24, starting transfers between devices, lse_exchange(): received.append(lax.ppermute(payload, axes, perm))  35.6 us
    ppermute x24, waiting for transfers between devices, lse_exchange(): received.append(lax.ppermute(payload, axes, perm))  20.3 us
    ppermute x9, waiting for transfers between devices, lse_allreduce(): other = lax.ppermute(jnp.stack([maxima, totals]), name, perm)  11.1 us
    ppermute x3, starting transfers between devices, lse_scatter_exchange(): parts.append(lax.ppermute(send, name, perm))  4.45 us
    dot_general x2, matrix products, pair_cost(): lax.dot_general(lhs_rows, rhs_rows, (((1,), (1,)), ((), ())), precision=l...  4.17 us
    reduce_sum x8, other arithmetic, body(): totals = jnp.sum(jnp.exp(scores - maxima[None, :]), axis=0)  3.97 us
    reduce_sum x8, other arithmetic, body(): totals = jnp.sum(jnp.exp(scores - maxima[:, None]), axis=1)  3.27 us
    ppermute x1, starting transfers between devices, body(): theirs = lax.ppermute(mine, 'rows', [(0, 1), (1, 0)])  2.56 us
  transfers between devices with their start and end apart: 38, of which 27 were waited for; matrix products, arithmetic and copies ran while one was open for 2% of the time, Pallas kernels for 0%

profile of v11, /device:TPU:0, one launch (start us, length us, event | category | flops | bytes accessed | tf_op | source)
XLA Modules:
  0.0 105.7 jit_solution(17984494299048006598)
XLA Ops:
  2.3 1.0 multiply_reduce_fusion.1
  3.3 2.1 %subtract_reduce_fusion.16 = (f32[1024]{0:T(1024)S(1)}, f32[1024,256]{0,1:T(8,128)S(1)}) fusion(f32[256]{0:T(256)S(1)} %multiply_log_fusion, f32[1024,64]{0,1:T(8,128)} %param.5, f32[256,64]{0,1:T(8,128)} %param.7, f32[256]{0:T(256)S(1)} %multiply_reduce_fusion.2, f32[1024]{0:T(1024)S(1)} %multiply_reduce_fusion.1), kind=kOutput, calls=%fused_computation.41 | convolution fusion | flops 202898432 | bytes 1386496 | tf_op jit(solution)/shard_map/dot_general | solution.py:15
  6.6 2.6 %collective-permute-start = (f32[520,128]{1,0:T(8,128)S(1)}, f32[520,128]{1,0:T(8,128)S(1)}, u32[]{:S(2)}, u32[]{:S(2)}) collective-permute-start(f32[520,128]{1,0:T(8,128)S(1)} %pad_maximum_fusion.2), channel_id=1, source_target_pairs={{0,2},{2,0},{1,3},{3,1},{4,6},{6,4},{5,7},{7,5},{8,10},{10,8},{9,1... | collective-permute-start | bytes 798728 | tf_op jit(solution)/shard_map/ppermute | solution.py:254
  9.3 3.7 %collective-permute-start.4 = (f32[2,1024]{1,0:T(2,128)S(1)}, f32[2,1024]{1,0:T(2,128)S(1)}, u32[]{:S(2)}, u32[]{:S(2)}) collective-permute-start(f32[2,1024]{1,0:T(2,128)S(1)} %get-tuple-element.124), channel_id=1, source_target_pairs={{0,12},{4,8},{8,4},{12,0},{1,13},{5,9},{9,5},{13,1},{2,14},{6,10},... | collective-permute-start | bytes 24584 | tf_op jit(solution)/shard_map/ppermute | solution.py:66
  13.7 1.1 %collective-permute-done.4 = f32[2,1024]{1,0:T(2,128)S(1)} collective-permute-done((f32[2,1024]{1,0:T(2,128)S(1)}, f32[2,1024]{1,0:T(2,128)S(1)}, u32[]{:S(2)}, u32[]{:S(2)}) %collective-permute-start.4) | collective-permute-done | bytes 8224 | tf_op jit(solution)/shard_map/ppermute | solution.py:66
  14.8 2.7 %collective-permute-done.3 = f32[2,1024]{1,0:T(2,128)S(1)} collective-permute-done((f32[2,1024]{1,0:T(2,128)S(1)}, f32[2,1024]{1,0:T(2,128)S(1)}, u32[]{:S(2)}, u32[]{:S(2)}) %collective-permute-start.3) | collective-permute-done | bytes 8224 | tf_op jit(solution)/shard_map/ppermute | solution.py:66
  19.0 2.0 %fusion.1 = f32[2048,256]{0,1:T(8,128)S(1)} fusion(f32[256,64]{0,1:T(8,128)S(1)} %copy-done.2, f32[256]{0:T(256)S(1)} %copy-done.13, f32[2048]{0:T(1024)S(1)} %multiply_reduce_fusion, f32[1024,64]{1,0:T(8,128)S(1)} %get-tuple-element.14, f32[1024,64]{1,0:T(8,128)S(1)} %get-tuple-element.13), kind=kOutput, calls=%fused_computation.2 | convolution fusion | flops 404881408 | bytes 2696192 | tf_op jit(solution)/shard_map/dot_general | solution.py:15
  22.4 2.9 %collective-permute-done.5 = f32[2,256]{1,0:T(2,128)S(1)} collective-permute-done((f32[2,256]{1,0:T(2,128)S(1)}, f32[2,256]{1,0:T(2,128)S(1)}, u32[]{:S(2)}, u32[]{:S(2)}) %collective-permute-start.5) | collective-permute-done | bytes 2080 | tf_op jit(solution)/shard_map/ppermute | solution.py:44
  26.1 1.2 %collective-permute-done.6 = f32[2,2048]{1,0:T(2,128)S(1)} collective-permute-done((f32[2,2048]{1,0:T(2,128)S(1)}, f32[2,2048]{1,0:T(2,128)S(1)}, u32[]{:S(2)}, u32[]{:S(2)}) %collective-permute-start.6) | collective-permute-done | bytes 16416 | tf_op jit(solution)/shard_map/ppermute | solution.py:44
  27.4 2.0 %collective-permute-start.9 = (f32[2,2048]{1,0:T(2,128)S(1)}, f32[2,2048]{1,0:T(2,128)S(1)}, u32[]{:S(2)}, u32[]{:S(2)}) collective-permute-start(f32[2,2048]{1,0:T(2,128)S(1)} %get-tuple-element.120), channel_id=1, source_target_pairs={{0,12},{4,8},{8,4},{12,0},{1,13},{5,9},{9,5},{13,1},{2,14},{6,10},... | collective-permute-start | bytes 49160 | tf_op jit(solution)/shard_map/ppermute | solution.py:66
  29.5 2.3 %collective-permute-start.7 = (f32[2,2048]{1,0:T(2,128)S(1)}, f32[2,2048]{1,0:T(2,128)S(1)}, u32[]{:S(2)}, u32[]{:S(2)}) collective-permute-start(f32[2,2048]{1,0:T(2,128)S(1)} %get-tuple-element.120), channel_id=1, source_target_pairs={{0,4},{4,0},{8,12},{12,8},{1,5},{5,1},{9,13},{13,9},{2,6},{6,2},{1... | collective-permute-start | bytes 49160 | tf_op jit(solution)/shard_map/ppermute | solution.py:66
  31.8 1.4 %collective-permute-done.9 = f32[2,2048]{1,0:T(2,128)S(1)} collective-permute-done((f32[2,2048]{1,0:T(2,128)S(1)}, f32[2,2048]{1,0:T(2,128)S(1)}, u32[]{:S(2)}, u32[]{:S(2)}) %collective-permute-start.9) | collective-permute-done | bytes 16416 | tf_op jit(solution)/shard_map/ppermute | solution.py:66
  35.8 1.2 %collective-permute-done.10 = f32[2,2048]{1,0:T(2,128)S(1)} collective-permute-done((f32[2,2048]{1,0:T(2,128)S(1)}, f32[2,2048]{1,0:T(2,128)S(1)}, u32[]{:S(2)}, u32[]{:S(2)}) %collective-permute-start.10) | collective-permute-done | bytes 16416 | tf_op jit(solution)/shard_map/ppermute | solution.py:44
  37.1 2.0 %collective-permute-start.13 = (f32[2,2048]{1,0:T(2,128)S(1)}, f32[2,2048]{1,0:T(2,128)S(1)}, u32[]{:S(2)}, u32[]{:S(2)}) collective-permute-start(f32[2,2048]{1,0:T(2,128)S(1)} %get-tuple-element.118), channel_id=1, source_target_pairs={{0,12},{4,8},{8,4},{12,0},{1,13},{5,9},{9,5},{13,1},{2,14},{6,10},... | collective-permute-start | bytes 49160 | tf_op jit(solution)/shard_map/ppermute | solution.py:66
  40.0 1.5 %collective-permute-start.11 = (f32[2,2048]{1,0:T(2,128)S(1)}, f32[2,2048]{1,0:T(2,128)S(1)}, u32[]{:S(2)}, u32[]{:S(2)}) collective-permute-start(f32[2,2048]{1,0:T(2,128)S(1)} %get-tuple-element.118), channel_id=1, source_target_pairs={{0,4},{4,0},{8,12},{12,8},{1,5},{5,1},{9,13},{13,9},{2,6},{6,2},{1... | collective-permute-start | bytes 49160 | tf_op jit(solution)/shard_map/ppermute | solution.py:66
  41.5 1.2 %collective-permute-done.13 = f32[2,2048]{1,0:T(2,128)S(1)} collective-permute-done((f32[2,2048]{1,0:T(2,128)S(1)}, f32[2,2048]{1,0:T(2,128)S(1)}, u32[]{:S(2)}, u32[]{:S(2)}) %collective-permute-start.13) | collective-permute-done | bytes 16416 | tf_op jit(solution)/shard_map/ppermute | solution.py:66
  42.8 1.1 %collective-permute-done.12 = f32[2,2048]{1,0:T(2,128)S(1)} collective-permute-done((f32[2,2048]{1,0:T(2,128)S(1)}, f32[2,2048]{1,0:T(2,128)S(1)}, u32[]{:S(2)}, u32[]{:S(2)}) %collective-permute-start.12) | collective-permute-done | bytes 16416 | tf_op jit(solution)/shard_map/ppermute | solution.py:66
  45.6 1.2 %collective-permute-done.14 = f32[2,2048]{1,0:T(2,128)S(1)} collective-permute-done((f32[2,2048]{1,0:T(2,128)S(1)}, f32[2,2048]{1,0:T(2,128)S(1)}, u32[]{:S(2)}, u32[]{:S(2)}) %collective-permute-start.14) | collective-permute-done | bytes 16416 | tf_op jit(solution)/shard_map/ppermute | solution.py:44
  46.8 2.0 %collective-permute-start.17 = (f32[2,2048]{1,0:T(2,128)S(1)}, f32[2,2048]{1,0:T(2,128)S(1)}, u32[]{:S(2)}, u32[]{:S(2)}) collective-permute-start(f32[2,2048]{1,0:T(2,128)S(1)} %get-tuple-element.116), channel_id=1, source_target_pairs={{0,12},{4,8},{8,4},{12,0},{1,13},{5,9},{9,5},{13,1},{2,14},{6,10},... | collective-permute-start | bytes 49160 | tf_op jit(solution)/shard_map/ppermute | solution.py:66
  49.7 1.6 %collective-permute-start.15 = (f32[2,2048]{1,0:T(2,128)S(1)}, f32[2,2048]{1,0:T(2,128)S(1)}, u32[]{:S(2)}, u32[]{:S(2)}) collective-permute-start(f32[2,2048]{1,0:T(2,128)S(1)} %get-tuple-element.116), channel_id=1, source_target_pairs={{0,4},{4,0},{8,12},{12,8},{1,5},{5,1},{9,13},{13,9},{2,6},{6,2},{1... | collective-permute-start | bytes 49160 | tf_op jit(solution)/shard_map/ppermute | solution.py:66
  51.3 1.2 %collective-permute-done.17 = f32[2,2048]{1,0:T(2,128)S(1)} collective-permute-done((f32[2,2048]{1,0:T(2,128)S(1)}, f32[2,2048]{1,0:T(2,128)S(1)}, u32[]{:S(2)}, u32[]{:S(2)}) %collective-permute-start.17) | collective-permute-done | bytes 16416 | tf_op jit(solution)/shard_map/ppermute | solution.py:66
  52.5 1.1 %collective-permute-done.16 = f32[2,2048]{1,0:T(2,128)S(1)} collective-permute-done((f32[2,2048]{1,0:T(2,128)S(1)}, f32[2,2048]{1,0:T(2,128)S(1)}, u32[]{:S(2)}, u32[]{:S(2)}) %collective-permute-start.16) | collective-permute-done | bytes 16416 | tf_op jit(solution)/shard_map/ppermute | solution.py:66
  55.3 1.2 %collective-permute-done.18 = f32[2,2048]{1,0:T(2,128)S(1)} collective-permute-done((f32[2,2048]{1,0:T(2,128)S(1)}, f32[2,2048]{1,0:T(2,128)S(1)}, u32[]{:S(2)}, u32[]{:S(2)}) %collective-permute-start.18) | collective-permute-done | bytes 16416 | tf_op jit(solution)/shard_map/ppermute | solution.py:44
  56.6 2.0 %collective-permute-start.21 = (f32[2,2048]{1,0:T(2,128)S(1)}, f32[2,2048]{1,0:T(2,128)S(1)}, u32[]{:S(2)}, u32[]{:S(2)}) collective-permute-start(f32[2,2048]{1,0:T(2,128)S(1)} %get-tuple-element.114), channel_id=1, source_target_pairs={{0,12},{4,8},{8,4},{12,0},{1,13},{5,9},{9,5},{13,1},{2,14},{6,10},... | collective-permute-start | bytes 49160 | tf_op jit(solution)/shard_map/ppermute | solution.py:66
  59.5 1.5 %collective-permute-start.19 = (f32[2,2048]{1,0:T(2,128)S(1)}, f32[2,2048]{1,0:T(2,128)S(1)}, u32[]{:S(2)}, u32[]{:S(2)}) collective-permute-start(f32[2,2048]{1,0:T(2,128)S(1)} %get-tuple-element.114), channel_id=1, source_target_pairs={{0,4},{4,0},{8,12},{12,8},{1,5},{5,1},{9,13},{13,9},{2,6},{6,2},{1... | collective-permute-start | bytes 49160 | tf_op jit(solution)/shard_map/ppermute | solution.py:66
  61.0 1.2 %collective-permute-done.21 = f32[2,2048]{1,0:T(2,128)S(1)} collective-permute-done((f32[2,2048]{1,0:T(2,128)S(1)}, f32[2,2048]{1,0:T(2,128)S(1)}, u32[]{:S(2)}, u32[]{:S(2)}) %collective-permute-start.21) | collective-permute-done | bytes 16416 | tf_op jit(solution)/shard_map/ppermute | solution.py:66
  62.3 1.1 %collective-permute-done.20 = f32[2,2048]{1,0:T(2,128)S(1)} collective-permute-done((f32[2,2048]{1,0:T(2,128)S(1)}, f32[2,2048]{1,0:T(2,128)S(1)}, u32[]{:S(2)}, u32[]{:S(2)}) %collective-permute-start.20) | collective-permute-done | bytes 16416 | tf_op jit(solution)/shard_map/ppermute | solution.py:66
  65.2 1.2 %collective-permute-done.22 = f32[2,2048]{1,0:T(2,128)S(1)} collective-permute-done((f32[2,2048]{1,0:T(2,128)S(1)}, f32[2,2048]{1,0:T(2,128)S(1)}, u32[]{:S(2)}, u32[]{:S(2)}) %collective-permute-start.22) | collective-permute-done | bytes 16416 | tf_op jit(solution)/shard_map/ppermute | solution.py:44
  66.5 2.0 %collective-permute-start.25 = (f32[2,2048]{1,0:T(2,128)S(1)}, f32[2,2048]{1,0:T(2,128)S(1)}, u32[]{:S(2)}, u32[]{:S(2)}) collective-permute-start(f32[2,2048]{1,0:T(2,128)S(1)} %get-tuple-element.112), channel_id=1, source_target_pairs={{0,12},{4,8},{8,4},{12,0},{1,13},{5,9},{9,5},{13,1},{2,14},{6,10},... | collective-permute-start | bytes 49160 | tf_op jit(solution)/shard_map/ppermute | solution.py:66
  69.3 1.6 %collective-permute-start.23 = (f32[2,2048]{1,0:T(2,128)S(1)}, f32[2,2048]{1,0:T(2,128)S(1)}, u32[]{:S(2)}, u32[]{:S(2)}) collective-permute-start(f32[2,2048]{1,0:T(2,128)S(1)} %get-tuple-element.112), channel_id=1, source_target_pairs={{0,4},{4,0},{8,12},{12,8},{1,5},{5,1},{9,13},{13,9},{2,6},{6,2},{1... | collective-permute-start | bytes 49160 | tf_op jit(solution)/shard_map/ppermute | solution.py:66
  70.9 1.2 %collective-permute-done.25 = f32[2,2048]{1,0:T(2,128)S(1)} collective-permute-done((f32[2,2048]{1,0:T(2,128)S(1)}, f32[2,2048]{1,0:T(2,128)S(1)}, u32[]{:S(2)}, u32[]{:S(2)}) %collective-permute-start.25) | collective-permute-done | bytes 16416 | tf_op jit(solution)/shard_map/ppermute | solution.py:66
  72.1 1.1 %collective-permute-done.24 = f32[2,2048]{1,0:T(2,128)S(1)} collective-permute-done((f32[2,2048]{1,0:T(2,128)S(1)}, f32[2,2048]{1,0:T(2,128)S(1)}, u32[]{:S(2)}, u32[]{:S(2)}) %collective-permute-start.24) | collective-permute-done | bytes 16416 | tf_op jit(solution)/shard_map/ppermute | solution.py:66
  74.9 1.2 %collective-permute-done.26 = f32[2,2048]{1,0:T(2,128)S(1)} collective-permute-done((f32[2,2048]{1,0:T(2,128)S(1)}, f32[2,2048]{1,0:T(2,128)S(1)}, u32[]{:S(2)}, u32[]{:S(2)}) %collective-permute-start.26) | collective-permute-done | bytes 16416 | tf_op jit(solution)/shard_map/ppermute | solution.py:44
  76.2 2.0 %collective-permute-start.29 = (f32[2,2048]{1,0:T(2,128)S(1)}, f32[2,2048]{1,0:T(2,128)S(1)}, u32[]{:S(2)}, u32[]{:S(2)}) collective-permute-start(f32[2,2048]{1,0:T(2,128)S(1)} %get-tuple-element.110), channel_id=1, source_target_pairs={{0,12},{4,8},{8,4},{12,0},{1,13},{5,9},{9,5},{13,1},{2,14},{6,10},... | collective-permute-start | bytes 49160 | tf_op jit(solution)/shard_map/ppermute | solution.py:66
  79.1 1.5 %collective-permute-start.27 = (f32[2,2048]{1,0:T(2,128)S(1)}, f32[2,2048]{1,0:T(2,128)S(1)}, u32[]{:S(2)}, u32[]{:S(2)}) collective-permute-start(f32[2,2048]{1,0:T(2,128)S(1)} %get-tuple-element.110), channel_id=1, source_target_pairs={{0,4},{4,0},{8,12},{12,8},{1,5},{5,1},{9,13},{13,9},{2,6},{6,2},{1... | collective-permute-start | bytes 49160 | tf_op jit(solution)/shard_map/ppermute | solution.py:66
  80.6 1.2 %collective-permute-done.29 = f32[2,2048]{1,0:T(2,128)S(1)} collective-permute-done((f32[2,2048]{1,0:T(2,128)S(1)}, f32[2,2048]{1,0:T(2,128)S(1)}, u32[]{:S(2)}, u32[]{:S(2)}) %collective-permute-start.29) | collective-permute-done | bytes 16416 | tf_op jit(solution)/shard_map/ppermute | solution.py:66
  81.9 1.1 %collective-permute-done.28 = f32[2,2048]{1,0:T(2,128)S(1)} collective-permute-done((f32[2,2048]{1,0:T(2,128)S(1)}, f32[2,2048]{1,0:T(2,128)S(1)}, u32[]{:S(2)}, u32[]{:S(2)}) %collective-permute-start.28) | collective-permute-done | bytes 16416 | tf_op jit(solution)/shard_map/ppermute | solution.py:66
  84.7 1.2 %collective-permute-done.30 = f32[2,2048]{1,0:T(2,128)S(1)} collective-permute-done((f32[2,2048]{1,0:T(2,128)S(1)}, f32[2,2048]{1,0:T(2,128)S(1)}, u32[]{:S(2)}, u32[]{:S(2)}) %collective-permute-start.30) | collective-permute-done | bytes 16416 | tf_op jit(solution)/shard_map/ppermute | solution.py:44
  85.9 2.0 %collective-permute-start.33 = (f32[2,2048]{1,0:T(2,128)S(1)}, f32[2,2048]{1,0:T(2,128)S(1)}, u32[]{:S(2)}, u32[]{:S(2)}) collective-permute-start(f32[2,2048]{1,0:T(2,128)S(1)} %get-tuple-element.108), channel_id=1, source_target_pairs={{0,12},{4,8},{8,4},{12,0},{1,13},{5,9},{9,5},{13,1},{2,14},{6,10},... | collective-permute-start | bytes 49160 | tf_op jit(solution)/shard_map/ppermute | solution.py:66
  88.8 1.6 %collective-permute-start.31 = (f32[2,2048]{1,0:T(2,128)S(1)}, f32[2,2048]{1,0:T(2,128)S(1)}, u32[]{:S(2)}, u32[]{:S(2)}) collective-permute-start(f32[2,2048]{1,0:T(2,128)S(1)} %get-tuple-element.108), channel_id=1, source_target_pairs={{0,4},{4,0},{8,12},{12,8},{1,5},{5,1},{9,13},{13,9},{2,6},{6,2},{1... | collective-permute-start | bytes 49160 | tf_op jit(solution)/shard_map/ppermute | solution.py:66
  90.4 1.2 %collective-permute-done.33 = f32[2,2048]{1,0:T(2,128)S(1)} collective-permute-done((f32[2,2048]{1,0:T(2,128)S(1)}, f32[2,2048]{1,0:T(2,128)S(1)}, u32[]{:S(2)}, u32[]{:S(2)}) %collective-permute-start.33) | collective-permute-done | bytes 16416 | tf_op jit(solution)/shard_map/ppermute | solution.py:66
  91.6 1.2 %collective-permute-done.32 = f32[2,2048]{1,0:T(2,128)S(1)} collective-permute-done((f32[2,2048]{1,0:T(2,128)S(1)}, f32[2,2048]{1,0:T(2,128)S(1)}, u32[]{:S(2)}, u32[]{:S(2)}) %collective-permute-start.32) | collective-permute-done | bytes 16416 | tf_op jit(solution)/shard_map/ppermute | solution.py:66
  94.6 1.0 fusion.5
  96.1 1.3 %collective-permute-done.34 = f32[4,128,66]{1,0,2:T(4,128)S(1)} collective-permute-done((f32[4,128,66]{1,0,2:T(4,128)S(1)}, f32[4,128,66]{1,0,2:T(4,128)S(1)}, u32[]{:S(2)}, u32[]{:S(2)}) %collective-permute-start.34) | collective-permute-done | bytes 135200 | tf_op jit(solution)/shard_map/ppermute | solution.py:189
  97.7 2.0 %collective-permute-start.37 = (f32[128,66]{0,1:T(8,128)S(1)}, f32[128,66]{0,1:T(8,128)S(1)}, u32[]{:S(2)}, u32[]{:S(2)}) collective-permute-start(f32[128,66]{0,1:T(8,128)S(1)} %bitcast.205), channel_id=1, source_target_pairs={{0,12},{4,8},{8,4},{12,0},{1,13},{5,9},{9,5},{13,1},{2,14},{6,10},... | collective-permute-start | bytes 101384 | tf_op jit(solution)/shard_map/ppermute | solution.py:152
  100.6 1.5 %collective-permute-start.35 = (f32[128,66]{0,1:T(8,128)S(1)}, f32[128,66]{0,1:T(8,128)S(1)}, u32[]{:S(2)}, u32[]{:S(2)}) collective-permute-start(f32[128,66]{0,1:T(8,128)S(1)} %bitcast.207), channel_id=1, source_target_pairs={{0,4},{4,0},{8,12},{12,8},{1,5},{5,1},{9,13},{13,9},{2,6},{6,2},{1... | collective-permute-start | bytes 101384 | tf_op jit(solution)/shard_map/ppermute | solution.py:152
  102.7 1.0 collective-permute-done.37
  103.7 1.3 %collective-permute-done.36 = f32[128,66]{0,1:T(8,128)S(1)} collective-permute-done((f32[128,66]{0,1:T(8,128)S(1)}, f32[128,66]{0,1:T(8,128)S(1)}, u32[]{:S(2)}, u32[]{:S(2)}) %collective-permute-start.36) | collective-permute-done | bytes 33824 | tf_op jit(solution)/shard_map/ppermute | solution.py:152
  (179 shorter events, 28.6 us)
Async XLA Ops:
  0.6 94.0 %copy-start = (f32[256,64]{0,1:T(8,128)S(1)}, f32[256,64]{0,1:T(8,128)}, u32[]{:S(2)}) copy-start(f32[256,64]{0,1:T(8,128)} %param.9) | copy-start | bytes 196612
  0.6 5.6 %copy-start.1 = (f32[1024,64]{0,1:T(8,128)S(1)}, f32[1024,64]{0,1:T(8,128)}, u32[]{:S(2)}) copy-start(f32[1024,64]{0,1:T(8,128)} %param.5) | copy-start | bytes 786436
  1.6 5.0 %copy-start.12 = (f32[256]{0:T(256)}, f32[256]{0:T(256)S(1)}, u32[]{:S(2)}) copy-start(f32[256]{0:T(256)S(1)} %multiply_reduce_fusion.2) | copy-start | bytes 3076
  3.2 3.4 %copy-start.4 = (f32[1024]{0:T(1024)S(1)}, f32[1024]{0:T(1024)}, u32[]{:S(2)}) copy-start(f32[1024]{0:T(1024)} %param.6) | copy-start | bytes 12292
  5.7 3.5 %collective-permute-start.1 = (f32[2,1024]{1,0:T(2,128)S(1)}, f32[2,1024]{1,0:T(2,128)S(1)}, u32[]{:S(2)}, u32[]{:S(2)}) collective-permute-start(f32[2,1024]{1,0:T(2,128)S(1)} %pad_maximum_fusion.26), channel_id=1, source_target_pairs={{0,1},{1,0},{2,3},{3,2},{4,5},{5,4},{6,7},{7,6},{8,9},{9,8},{10,11... | collective-permute-start | bytes 24584 | tf_op jit(solution)/shard_map/ppermute | solution.py:44
  6.6 11.5 %collective-permute-start = (f32[520,128]{1,0:T(8,128)S(1)}, f32[520,128]{1,0:T(8,128)S(1)}, u32[]{:S(2)}, u32[]{:S(2)}) collective-permute-start(f32[520,128]{1,0:T(8,128)S(1)} %pad_maximum_fusion.2), channel_id=1, source_target_pairs={{0,2},{2,0},{1,3},{3,1},{4,6},{6,4},{5,7},{7,5},{8,10},{10,8},{9,1... | collective-permute-start | bytes 798728 | tf_op jit(solution)/shard_map/ppermute | solution.py:254
  9.3 5.5 %collective-permute-start.4 = (f32[2,1024]{1,0:T(2,128)S(1)}, f32[2,1024]{1,0:T(2,128)S(1)}, u32[]{:S(2)}, u32[]{:S(2)}) collective-permute-start(f32[2,1024]{1,0:T(2,128)S(1)} %get-tuple-element.124), channel_id=1, source_target_pairs={{0,12},{4,8},{8,4},{12,0},{1,13},{5,9},{9,5},{13,1},{2,14},{6,10},... | collective-permute-start | bytes 24584 | tf_op jit(solution)/shard_map/ppermute | solution.py:66
  12.9 4.5 %collective-permute-start.3 = (f32[2,1024]{1,0:T(2,128)S(1)}, f32[2,1024]{1,0:T(2,128)S(1)}, u32[]{:S(2)}, u32[]{:S(2)}) collective-permute-start(f32[2,1024]{1,0:T(2,128)S(1)} %get-tuple-element.124), channel_id=1, source_target_pairs={{0,8},{4,12},{8,0},{12,4},{1,9},{5,13},{9,1},{13,5},{2,10},{6,14},... | collective-permute-start | bytes 24584 | tf_op jit(solution)/shard_map/ppermute | solution.py:66
  12.9 4.5 %collective-permute-start.2 = (f32[2,1024]{1,0:T(2,128)S(1)}, f32[2,1024]{1,0:T(2,128)S(1)}, u32[]{:S(2)}, u32[]{:S(2)}) collective-permute-start(f32[2,1024]{1,0:T(2,128)S(1)} %get-tuple-element.124), channel_id=1, source_target_pairs={{0,4},{4,0},{8,12},{12,8},{1,5},{5,1},{9,13},{13,9},{2,6},{6,2},{1... | collective-permute-start | bytes 24584 | tf_op jit(solution)/shard_map/ppermute | solution.py:66
  18.4 2.6 %copy-start.5 = (f32[1,1,1024]{2,1,0:T(1,128)S(1)}, f32[1,1,1024]{2,1,0:T(1,128)}, u32[]{:S(2)}) copy-start(f32[1,1,1024]{2,1,0:T(1,128)} %get-tuple-element.86) | copy-start | bytes 12292
  18.4 2.6 %copy-start.6 = (f32[1,1,1024]{2,1,0:T(1,128)S(1)}, f32[1,1,1024]{2,1,0:T(1,128)}, u32[]{:S(2)}) copy-start(f32[1,1,1024]{2,1,0:T(1,128)} %get-tuple-element.87) | copy-start | bytes 12292
  18.5 2.6 %copy-start.7 = (f32[1,1,1024]{2,1,0:T(1,128)S(1)}, f32[1,1,1024]{2,1,0:T(1,128)}, u32[]{:S(2)}) copy-start(f32[1,1,1024]{2,1,0:T(1,128)} %get-tuple-element.88) | copy-start | bytes 12292
  18.5 2.6 %copy-start.8 = (f32[1,1,1024]{2,1,0:T(1,128)S(1)}, f32[1,1,1024]{2,1,0:T(1,128)}, u32[]{:S(2)}) copy-start(f32[1,1,1024]{2,1,0:T(1,128)} %get-tuple-element.89) | copy-start | bytes 12292
  18.5 2.6 %copy-start.9 = (f32[1,1,1024]{2,1,0:T(1,128)S(1)}, f32[1,1,1024]{2,1,0:T(1,128)}, u32[]{:S(2)}) copy-start(f32[1,1,1024]{2,1,0:T(1,128)} %get-tuple-element.90) | copy-start | bytes 12292
  19.0 6.3 %copy-start.3 = (f32[256]{0:T(256)S(1)}, f32[256]{0:T(256)}, u32[]{:S(2)}) copy-start(f32[256]{0:T(256)} %param.8) | copy-start | bytes 3076
  21.7 3.7 %collective-permute-start.5 = (f32[2,256]{1,0:T(2,128)S(1)}, f32[2,256]{1,0:T(2,128)S(1)}, u32[]{:S(2)}, u32[]{:S(2)}) collective-permute-start(f32[2,256]{1,0:T(2,128)S(1)} %pad_maximum_fusion.28), channel_id=1, source_target_pairs={{0,2},{2,0},{1,3},{3,1},{4,6},{6,4},{5,7},{7,5},{8,10},{10,8},{9,1... | collective-permute-start | bytes 6152 | tf_op jit(solution)/shard_map/ppermute | solution.py:44
  26.0 1.2 %collective-permute-start.6 = (f32[2,2048]{1,0:T(2,128)S(1)}, f32[2,2048]{1,0:T(2,128)S(1)}, u32[]{:S(2)}, u32[]{:S(2)}) collective-permute-start(f32[2,2048]{1,0:T(2,128)S(1)} %pad_maximum_fusion.12), channel_id=1, source_target_pairs={{0,1},{1,0},{2,3},{3,2},{4,5},{5,4},{6,7},{7,6},{8,9},{9,8},{10,11... | collective-permute-start | bytes 49160 | tf_op jit(solution)/shard_map/ppermute | solution.py:44
  27.4 5.8 %collective-permute-start.9 = (f32[2,2048]{1,0:T(2,128)S(1)}, f32[2,2048]{1,0:T(2,128)S(1)}, u32[]{:S(2)}, u32[]{:S(2)}) collective-permute-start(f32[2,2048]{1,0:T(2,128)S(1)} %get-tuple-element.120), channel_id=1, source_target_pairs={{0,12},{4,8},{8,4},{12,0},{1,13},{5,9},{9,5},{13,1},{2,14},{6,10},... | collective-permute-start | bytes 49160 | tf_op jit(solution)/shard_map/ppermute | solution.py:66
  29.4 4.8 %collective-permute-start.8 = (f32[2,2048]{1,0:T(2,128)S(1)}, f32[2,2048]{1,0:T(2,128)S(1)}, u32[]{:S(2)}, u32[]{:S(2)}) collective-permute-start(f32[2,2048]{1,0:T(2,128)S(1)} %get-tuple-element.120), channel_id=1, source_target_pairs={{0,8},{4,12},{8,0},{12,4},{1,9},{5,13},{9,1},{13,5},{2,10},{6,14},... | collective-permute-start | bytes 49160 | tf_op jit(solution)/shard_map/ppermute | solution.py:66
  29.5 4.6 %collective-permute-start.7 = (f32[2,2048]{1,0:T(2,128)S(1)}, f32[2,2048]{1,0:T(2,128)S(1)}, u32[]{:S(2)}, u32[]{:S(2)}) collective-permute-start(f32[2,2048]{1,0:T(2,128)S(1)} %get-tuple-element.120), channel_id=1, source_target_pairs={{0,4},{4,0},{8,12},{12,8},{1,5},{5,1},{9,13},{13,9},{2,6},{6,2},{1... | collective-permute-start | bytes 49160 | tf_op jit(solution)/shard_map/ppermute | solution.py:66
  35.8 1.2 %collective-permute-start.10 = (f32[2,2048]{1,0:T(2,128)S(1)}, f32[2,2048]{1,0:T(2,128)S(1)}, u32[]{:S(2)}, u32[]{:S(2)}) collective-permute-start(f32[2,2048]{1,0:T(2,128)S(1)} %pad_maximum_fusion.14), channel_id=1, source_target_pairs={{0,1},{1,0},{2,3},{3,2},{4,5},{5,4},{6,7},{7,6},{8,9},{9,8},{10,11... | collective-permute-start | bytes 49160 | tf_op jit(solution)/shard_map/ppermute | solution.py:44
  37.1 5.7 %collective-permute-start.13 = (f32[2,2048]{1,0:T(2,128)S(1)}, f32[2,2048]{1,0:T(2,128)S(1)}, u32[]{:S(2)}, u32[]{:S(2)}) collective-permute-start(f32[2,2048]{1,0:T(2,128)S(1)} %get-tuple-element.118), channel_id=1, source_target_pairs={{0,12},{4,8},{8,4},{12,0},{1,13},{5,9},{9,5},{13,1},{2,14},{6,10},... | collective-permute-start | bytes 49160 | tf_op jit(solution)/shard_map/ppermute | solution.py:66
  39.1 4.8 %collective-permute-start.12 = (f32[2,2048]{1,0:T(2,128)S(1)}, f32[2,2048]{1,0:T(2,128)S(1)}, u32[]{:S(2)}, u32[]{:S(2)}) collective-permute-start(f32[2,2048]{1,0:T(2,128)S(1)} %get-tuple-element.118), channel_id=1, source_target_pairs={{0,8},{4,12},{8,0},{12,4},{1,9},{5,13},{9,1},{13,5},{2,10},{6,14},... | collective-permute-start | bytes 49160 | tf_op jit(solution)/shard_map/ppermute | solution.py:66
  40.0 3.9 %collective-permute-start.11 = (f32[2,2048]{1,0:T(2,128)S(1)}, f32[2,2048]{1,0:T(2,128)S(1)}, u32[]{:S(2)}, u32[]{:S(2)}) collective-permute-start(f32[2,2048]{1,0:T(2,128)S(1)} %get-tuple-element.118), channel_id=1, source_target_pairs={{0,4},{4,0},{8,12},{12,8},{1,5},{5,1},{9,13},{13,9},{2,6},{6,2},{1... | collective-permute-start | bytes 49160 | tf_op jit(solution)/shard_map/ppermute | solution.py:66
  45.5 1.2 %collective-permute-start.14 = (f32[2,2048]{1,0:T(2,128)S(1)}, f32[2,2048]{1,0:T(2,128)S(1)}, u32[]{:S(2)}, u32[]{:S(2)}) collective-permute-start(f32[2,2048]{1,0:T(2,128)S(1)} %pad_maximum_fusion.16), channel_id=1, source_target_pairs={{0,1},{1,0},{2,3},{3,2},{4,5},{5,4},{6,7},{7,6},{8,9},{9,8},{10,11... | collective-permute-start | bytes 49160 | tf_op jit(solution)/shard_map/ppermute | solution.py:44
  46.8 5.7 %collective-permute-start.17 = (f32[2,2048]{1,0:T(2,128)S(1)}, f32[2,2048]{1,0:T(2,128)S(1)}, u32[]{:S(2)}, u32[]{:S(2)}) collective-permute-start(f32[2,2048]{1,0:T(2,128)S(1)} %get-tuple-element.116), channel_id=1, source_target_pairs={{0,12},{4,8},{8,4},{12,0},{1,13},{5,9},{9,5},{13,1},{2,14},{6,10},... | collective-permute-start | bytes 49160 | tf_op jit(solution)/shard_map/ppermute | solution.py:66
  48.9 4.8 %collective-permute-start.16 = (f32[2,2048]{1,0:T(2,128)S(1)}, f32[2,2048]{1,0:T(2,128)S(1)}, u32[]{:S(2)}, u32[]{:S(2)}) collective-permute-start(f32[2,2048]{1,0:T(2,128)S(1)} %get-tuple-element.116), channel_id=1, source_target_pairs={{0,8},{4,12},{8,0},{12,4},{1,9},{5,13},{9,1},{13,5},{2,10},{6,14},... | collective-permute-start | bytes 49160 | tf_op jit(solution)/shard_map/ppermute | solution.py:66
  49.7 3.9 %collective-permute-start.15 = (f32[2,2048]{1,0:T(2,128)S(1)}, f32[2,2048]{1,0:T(2,128)S(1)}, u32[]{:S(2)}, u32[]{:S(2)}) collective-permute-start(f32[2,2048]{1,0:T(2,128)S(1)} %get-tuple-element.116), channel_id=1, source_target_pairs={{0,4},{4,0},{8,12},{12,8},{1,5},{5,1},{9,13},{13,9},{2,6},{6,2},{1... | collective-permute-start | bytes 49160 | tf_op jit(solution)/shard_map/ppermute | solution.py:66
  55.2 1.2 %collective-permute-start.18 = (f32[2,2048]{1,0:T(2,128)S(1)}, f32[2,2048]{1,0:T(2,128)S(1)}, u32[]{:S(2)}, u32[]{:S(2)}) collective-permute-start(f32[2,2048]{1,0:T(2,128)S(1)} %pad_maximum_fusion.18), channel_id=1, source_target_pairs={{0,1},{1,0},{2,3},{3,2},{4,5},{5,4},{6,7},{7,6},{8,9},{9,8},{10,11... | collective-permute-start | bytes 49160 | tf_op jit(solution)/shard_map/ppermute | solution.py:44
  56.6 5.7 %collective-permute-start.21 = (f32[2,2048]{1,0:T(2,128)S(1)}, f32[2,2048]{1,0:T(2,128)S(1)}, u32[]{:S(2)}, u32[]{:S(2)}) collective-permute-start(f32[2,2048]{1,0:T(2,128)S(1)} %get-tuple-element.114), channel_id=1, source_target_pairs={{0,12},{4,8},{8,4},{12,0},{1,13},{5,9},{9,5},{13,1},{2,14},{6,10},... | collective-permute-start | bytes 49160 | tf_op jit(solution)/shard_map/ppermute | solution.py:66
  58.6 4.8 %collective-permute-start.20 = (f32[2,2048]{1,0:T(2,128)S(1)}, f32[2,2048]{1,0:T(2,128)S(1)}, u32[]{:S(2)}, u32[]{:S(2)}) collective-permute-start(f32[2,2048]{1,0:T(2,128)S(1)} %get-tuple-element.114), channel_id=1, source_target_pairs={{0,8},{4,12},{8,0},{12,4},{1,9},{5,13},{9,1},{13,5},{2,10},{6,14},... | collective-permute-start | bytes 49160 | tf_op jit(solution)/shard_map/ppermute | solution.py:66
  59.5 3.9 %collective-permute-start.19 = (f32[2,2048]{1,0:T(2,128)S(1)}, f32[2,2048]{1,0:T(2,128)S(1)}, u32[]{:S(2)}, u32[]{:S(2)}) collective-permute-start(f32[2,2048]{1,0:T(2,128)S(1)} %get-tuple-element.114), channel_id=1, source_target_pairs={{0,4},{4,0},{8,12},{12,8},{1,5},{5,1},{9,13},{13,9},{2,6},{6,2},{1... | collective-permute-start | bytes 49160 | tf_op jit(solution)/shard_map/ppermute | solution.py:66
  65.1 1.2 %collective-permute-start.22 = (f32[2,2048]{1,0:T(2,128)S(1)}, f32[2,2048]{1,0:T(2,128)S(1)}, u32[]{:S(2)}, u32[]{:S(2)}) collective-permute-start(f32[2,2048]{1,0:T(2,128)S(1)} %pad_maximum_fusion.20), channel_id=1, source_target_pairs={{0,1},{1,0},{2,3},{3,2},{4,5},{5,4},{6,7},{7,6},{8,9},{9,8},{10,11... | collective-permute-start | bytes 49160 | tf_op jit(solution)/shard_map/ppermute | solution.py:44
  66.5 5.7 %collective-permute-start.25 = (f32[2,2048]{1,0:T(2,128)S(1)}, f32[2,2048]{1,0:T(2,128)S(1)}, u32[]{:S(2)}, u32[]{:S(2)}) collective-permute-start(f32[2,2048]{1,0:T(2,128)S(1)} %get-tuple-element.112), channel_id=1, source_target_pairs={{0,12},{4,8},{8,4},{12,0},{1,13},{5,9},{9,5},{13,1},{2,14},{6,10},... | collective-permute-start | bytes 49160 | tf_op jit(solution)/shard_map/ppermute | solution.py:66
  68.5 4.8 %collective-permute-start.24 = (f32[2,2048]{1,0:T(2,128)S(1)}, f32[2,2048]{1,0:T(2,128)S(1)}, u32[]{:S(2)}, u32[]{:S(2)}) collective-permute-start(f32[2,2048]{1,0:T(2,128)S(1)} %get-tuple-element.112), channel_id=1, source_target_pairs={{0,8},{4,12},{8,0},{12,4},{1,9},{5,13},{9,1},{13,5},{2,10},{6,14},... | collective-permute-start | bytes 49160 | tf_op jit(solution)/shard_map/ppermute | solution.py:66
  69.3 3.9 %collective-permute-start.23 = (f32[2,2048]{1,0:T(2,128)S(1)}, f32[2,2048]{1,0:T(2,128)S(1)}, u32[]{:S(2)}, u32[]{:S(2)}) collective-permute-start(f32[2,2048]{1,0:T(2,128)S(1)} %get-tuple-element.112), channel_id=1, source_target_pairs={{0,4},{4,0},{8,12},{12,8},{1,5},{5,1},{9,13},{13,9},{2,6},{6,2},{1... | collective-permute-start | bytes 49160 | tf_op jit(solution)/shard_map/ppermute | solution.py:66
  74.9 1.2 %collective-permute-start.26 = (f32[2,2048]{1,0:T(2,128)S(1)}, f32[2,2048]{1,0:T(2,128)S(1)}, u32[]{:S(2)}, u32[]{:S(2)}) collective-permute-start(f32[2,2048]{1,0:T(2,128)S(1)} %pad_maximum_fusion.22), channel_id=1, source_target_pairs={{0,1},{1,0},{2,3},{3,2},{4,5},{5,4},{6,7},{7,6},{8,9},{9,8},{10,11... | collective-permute-start | bytes 49160 | tf_op jit(solution)/shard_map/ppermute | solution.py:44
  76.2 5.7 %collective-permute-start.29 = (f32[2,2048]{1,0:T(2,128)S(1)}, f32[2,2048]{1,0:T(2,128)S(1)}, u32[]{:S(2)}, u32[]{:S(2)}) collective-permute-start(f32[2,2048]{1,0:T(2,128)S(1)} %get-tuple-element.110), channel_id=1, source_target_pairs={{0,12},{4,8},{8,4},{12,0},{1,13},{5,9},{9,5},{13,1},{2,14},{6,10},... | collective-permute-start | bytes 49160 | tf_op jit(solution)/shard_map/ppermute | solution.py:66
  78.2 4.8 %collective-permute-start.28 = (f32[2,2048]{1,0:T(2,128)S(1)}, f32[2,2048]{1,0:T(2,128)S(1)}, u32[]{:S(2)}, u32[]{:S(2)}) collective-permute-start(f32[2,2048]{1,0:T(2,128)S(1)} %get-tuple-element.110), channel_id=1, source_target_pairs={{0,8},{4,12},{8,0},{12,4},{1,9},{5,13},{9,1},{13,5},{2,10},{6,14},... | collective-permute-start | bytes 49160 | tf_op jit(solution)/shard_map/ppermute | solution.py:66
  79.1 3.9 %collective-permute-start.27 = (f32[2,2048]{1,0:T(2,128)S(1)}, f32[2,2048]{1,0:T(2,128)S(1)}, u32[]{:S(2)}, u32[]{:S(2)}) collective-permute-start(f32[2,2048]{1,0:T(2,128)S(1)} %get-tuple-element.110), channel_id=1, source_target_pairs={{0,4},{4,0},{8,12},{12,8},{1,5},{5,1},{9,13},{13,9},{2,6},{6,2},{1... | collective-permute-start | bytes 49160 | tf_op jit(solution)/shard_map/ppermute | solution.py:66
  84.6 1.2 %collective-permute-start.30 = (f32[2,2048]{1,0:T(2,128)S(1)}, f32[2,2048]{1,0:T(2,128)S(1)}, u32[]{:S(2)}, u32[]{:S(2)}) collective-permute-start(f32[2,2048]{1,0:T(2,128)S(1)} %pad_maximum_fusion.24), channel_id=1, source_target_pairs={{0,1},{1,0},{2,3},{3,2},{4,5},{5,4},{6,7},{7,6},{8,9},{9,8},{10,11... | collective-permute-start | bytes 49160 | tf_op jit(solution)/shard_map/ppermute | solution.py:44
  85.9 5.6 %collective-permute-start.33 = (f32[2,2048]{1,0:T(2,128)S(1)}, f32[2,2048]{1,0:T(2,128)S(1)}, u32[]{:S(2)}, u32[]{:S(2)}) collective-permute-start(f32[2,2048]{1,0:T(2,128)S(1)} %get-tuple-element.108), channel_id=1, source_target_pairs={{0,12},{4,8},{8,4},{12,0},{1,13},{5,9},{9,5},{13,1},{2,14},{6,10},... | collective-permute-start | bytes 49160 | tf_op jit(solution)/shard_map/ppermute | solution.py:66
  87.9 4.8 %collective-permute-start.32 = (f32[2,2048]{1,0:T(2,128)S(1)}, f32[2,2048]{1,0:T(2,128)S(1)}, u32[]{:S(2)}, u32[]{:S(2)}) collective-permute-start(f32[2,2048]{1,0:T(2,128)S(1)} %get-tuple-element.108), channel_id=1, source_target_pairs={{0,8},{4,12},{8,0},{12,4},{1,9},{5,13},{9,1},{13,5},{2,10},{6,14},... | collective-permute-start | bytes 49160 | tf_op jit(solution)/shard_map/ppermute | solution.py:66
  88.8 3.9 %collective-permute-start.31 = (f32[2,2048]{1,0:T(2,128)S(1)}, f32[2,2048]{1,0:T(2,128)S(1)}, u32[]{:S(2)}, u32[]{:S(2)}) collective-permute-start(f32[2,2048]{1,0:T(2,128)S(1)} %get-tuple-element.108), channel_id=1, source_target_pairs={{0,4},{4,0},{8,12},{12,8},{1,5},{5,1},{9,13},{13,9},{2,6},{6,2},{1... | collective-permute-start | bytes 49160 | tf_op jit(solution)/shard_map/ppermute | solution.py:66
  96.0 1.4 %collective-permute-start.34 = (f32[4,128,66]{1,0,2:T(4,128)S(1)}, f32[4,128,66]{1,0,2:T(4,128)S(1)}, u32[]{:S(2)}, u32[]{:S(2)}) collective-permute-start(f32[4,128,66]{1,0,2:T(4,128)S(1)} %get-tuple-element.16), channel_id=1, source_target_pairs={{0,1},{1,0},{2,3},{3,2},{4,5},{5,4},{6,7},{7,6},{8,9},{9,8},{10,11... | collective-permute-start | bytes 405512 | tf_op jit(solution)/shard_map/ppermute | solution.py:189
  97.7 6.1 %collective-permute-start.37 = (f32[128,66]{0,1:T(8,128)S(1)}, f32[128,66]{0,1:T(8,128)S(1)}, u32[]{:S(2)}, u32[]{:S(2)}) collective-permute-start(f32[128,66]{0,1:T(8,128)S(1)} %bitcast.205), channel_id=1, source_target_pairs={{0,12},{4,8},{8,4},{12,0},{1,13},{5,9},{9,5},{13,1},{2,14},{6,10},... | collective-permute-start | bytes 101384 | tf_op jit(solution)/shard_map/ppermute | solution.py:152
  99.7 5.4 %collective-permute-start.36 = (f32[128,66]{0,1:T(8,128)S(1)}, f32[128,66]{0,1:T(8,128)S(1)}, u32[]{:S(2)}, u32[]{:S(2)}) collective-permute-start(f32[128,66]{0,1:T(8,128)S(1)} %bitcast.206), channel_id=1, source_target_pairs={{0,8},{4,12},{8,0},{12,4},{1,9},{5,13},{9,1},{13,5},{2,10},{6,14},... | collective-permute-start | bytes 101384 | tf_op jit(solution)/shard_map/ppermute | solution.py:152
  100.6 4.4 %collective-permute-start.35 = (f32[128,66]{0,1:T(8,128)S(1)}, f32[128,66]{0,1:T(8,128)S(1)}, u32[]{:S(2)}, u32[]{:S(2)}) collective-permute-start(f32[128,66]{0,1:T(8,128)S(1)} %bitcast.207), channel_id=1, source_target_pairs={{0,4},{4,0},{8,12},{12,8},{1,5},{5,1},{9,13},{13,9},{2,6},{6,2},{1... | collective-permute-start | bytes 101384 | tf_op jit(solution)/shard_map/ppermute | solution.py:152
  (4 other events, 6.8 us)

commit v12 on v11

--- a/solution.py
+++ b/solution.py
@@ -172,10 +172,12 @@
         scores = log_b[None, :] + (g_pot[None, :] - cost) / entropic
     maxima = jnp.max(scores, axis=1)
     weights = jnp.exp(scores - maxima[:, None])
-    totals = jnp.sum(weights, axis=1)
-    weighted = jnp.dot(
-        weights, fate_panel, precision=lax.Precision.HIGHEST, preferred_element_type=jnp.float32
-    )
+    panel = jnp.concatenate([fate_panel, jnp.ones((fate_panel.shape[0], 1), jnp.float32)], axis=1)
+    product = jnp.dot(
+        weights, panel, precision=lax.Precision.HIGHEST, preferred_element_type=jnp.float32
+    )
+    weighted = product[:, : fate_panel.shape[1]]
+    totals = product[:, fate_panel.shape[1]]
     col_size = lax.axis_size("cols")
     rep_size = lax.axis_size("rep")
     fates = fate_panel.shape[1]

time: 106 us -> 105 us (level)
  transfers between devices with their start and end apart: 38 -> 38, of which waited for: 27 -> 33; matrix products, arithmetic and copies ran while one was open for 2% -> 1% of each run, Pallas kernels for 0% -> 0%
where the time goes in v12:
time: 105 us
  starting transfers between devices  44.5 us (42%)
  waiting for transfers between devices  35 us (33%)
  other arithmetic  16.9 us (16%)
  matrix products  5.18 us (5%)
  local copies, waits for them, and re-layouts  1.82 us (2%)
  between operations  1.36 us (1%)
    ppermute x24, starting transfers between devices, lse_exchange(): received.append(lax.ppermute(payload, axes, perm))  35.6 us
    ppermute x24, waiting for transfers between devices, lse_exchange(): received.append(lax.ppermute(payload, axes, perm))  20.6 us
    ppermute x9, waiting for transfers between devices, lse_allreduce(): other = lax.ppermute(jnp.stack([maxima, totals]), name, perm)  11.1 us
    ppermute x3, starting transfers between devices, lse_scatter_exchange(): parts.append(lax.ppermute(send, name, perm))  4.45 us
    dot_general x2, matrix products, pair_cost(): lax.dot_general(lhs_rows, rhs_rows, (((1,), (1,)), ((), ())), precision=l...  4.17 us
    reduce_sum x8, other arithmetic, body(): totals = jnp.sum(jnp.exp(scores - maxima[None, :]), axis=0)  4 us
    reduce_sum x8, other arithmetic, body(): totals = jnp.sum(jnp.exp(scores - maxima[:, None]), axis=1)  3.27 us
    ppermute x1, starting transfers between devices, body(): theirs = lax.ppermute(mine, 'rows', [(0, 1), (1, 0)])  2.56 us
  transfers between devices with their start and end apart: 38, of which 33 were waited for; matrix products, arithmetic and copies ran while one was open for 1% of the time, Pallas kernels for 0%

profile of v12, /device:TPU:0, one launch (start us, length us, event | category | flops | bytes accessed | tf_op | source)
XLA Modules:
  0.0 104.7 jit_solution(170779284671342621)
XLA Ops:
  2.2 1.0 multiply_reduce_fusion.1
  3.2 2.1 %subtract_reduce_fusion.16 = (f32[1024]{0:T(1024)S(1)}, f32[1024,256]{0,1:T(8,128)S(1)}) fusion(f32[256]{0:T(256)S(1)} %multiply_log_fusion, f32[1024,64]{0,1:T(8,128)} %param.5, f32[256,64]{0,1:T(8,128)} %param.7, f32[256]{0:T(256)S(1)} %multiply_reduce_fusion.2, f32[1024]{0:T(1024)S(1)} %multiply_reduce_fusion.1), kind=kOutput, calls=%fused_computation.44 | convolution fusion | flops 202898432 | bytes 1386496 | tf_op jit(solution)/shard_map/dot_general | solution.py:15
  6.6 2.6 %collective-permute-start = (f32[520,128]{1,0:T(8,128)S(1)}, f32[520,128]{1,0:T(8,128)S(1)}, u32[]{:S(2)}, u32[]{:S(2)}) collective-permute-start(f32[520,128]{1,0:T(8,128)S(1)} %pad_maximum_fusion.2), channel_id=1, source_target_pairs={{0,2},{2,0},{1,3},{3,1},{4,6},{6,4},{5,7},{7,5},{8,10},{10,8},{9,1... | collective-permute-start | bytes 798728 | tf_op jit(solution)/shard_map/ppermute | solution.py:256
  9.2 3.7 %collective-permute-start.4 = (f32[2,1024]{1,0:T(2,128)S(1)}, f32[2,1024]{1,0:T(2,128)S(1)}, u32[]{:S(2)}, u32[]{:S(2)}) collective-permute-start(f32[2,1024]{1,0:T(2,128)S(1)} %get-tuple-element.124), channel_id=1, source_target_pairs={{0,12},{4,8},{8,4},{12,0},{1,13},{5,9},{9,5},{13,1},{2,14},{6,10},... | collective-permute-start | bytes 24584 | tf_op jit(solution)/shard_map/ppermute | solution.py:66
  13.7 1.1 %collective-permute-done.4 = f32[2,1024]{1,0:T(2,128)S(1)} collective-permute-done((f32[2,1024]{1,0:T(2,128)S(1)}, f32[2,1024]{1,0:T(2,128)S(1)}, u32[]{:S(2)}, u32[]{:S(2)}) %collective-permute-start.4) | collective-permute-done | bytes 8224 | tf_op jit(solution)/shard_map/ppermute | solution.py:66
  14.7 2.7 %collective-permute-done.3 = f32[2,1024]{1,0:T(2,128)S(1)} collective-permute-done((f32[2,1024]{1,0:T(2,128)S(1)}, f32[2,1024]{1,0:T(2,128)S(1)}, u32[]{:S(2)}, u32[]{:S(2)}) %collective-permute-start.3) | collective-permute-done | bytes 8224 | tf_op jit(solution)/shard_map/ppermute | solution.py:66
  18.4 2.0 %fusion.1 = f32[2048,256]{0,1:T(8,128)S(1)} fusion(f32[256,64]{0,1:T(8,128)S(1)} %copy-done.1, f32[256]{0:T(256)S(1)} %multiply_reduce_fusion.2, f32[2048]{0:T(1024)S(1)} %multiply_reduce_fusion, f32[1024,64]{1,0:T(8,128)S(1)} %get-tuple-element.14, f32[1024,64]{1,0:T(8,128)S(1)} %get-tuple-element.13), kind=kOutput, calls=%fused_computation.2 | convolution fusion | flops 404881408 | bytes 2696192 | tf_op jit(solution)/shard_map/dot_general | solution.py:15
  21.7 2.9 %collective-permute-done.5 = f32[2,256]{1,0:T(2,128)S(1)} collective-permute-done((f32[2,256]{1,0:T(2,128)S(1)}, f32[2,256]{1,0:T(2,128)S(1)}, u32[]{:S(2)}, u32[]{:S(2)}) %collective-permute-start.5) | collective-permute-done | bytes 2080 | tf_op jit(solution)/shard_map/ppermute | solution.py:44
  25.4 1.2 %collective-permute-done.6 = f32[2,2048]{1,0:T(2,128)S(1)} collective-permute-done((f32[2,2048]{1,0:T(2,128)S(1)}, f32[2,2048]{1,0:T(2,128)S(1)}, u32[]{:S(2)}, u32[]{:S(2)}) %collective-permute-start.6) | collective-permute-done | bytes 16416 | tf_op jit(solution)/shard_map/ppermute | solution.py:44
  26.7 2.6 %collective-permute-start.9 = (f32[2,2048]{1,0:T(2,128)S(1)}, f32[2,2048]{1,0:T(2,128)S(1)}, u32[]{:S(2)}, u32[]{:S(2)}) collective-permute-start(f32[2,2048]{1,0:T(2,128)S(1)} %get-tuple-element.120), channel_id=1, source_target_pairs={{0,12},{4,8},{8,4},{12,0},{1,13},{5,9},{9,5},{13,1},{2,14},{6,10},... | collective-permute-start | bytes 49160 | tf_op jit(solution)/shard_map/ppermute | solution.py:66
  29.3 1.9 %collective-permute-start.7 = (f32[2,2048]{1,0:T(2,128)S(1)}, f32[2,2048]{1,0:T(2,128)S(1)}, u32[]{:S(2)}, u32[]{:S(2)}) collective-permute-start(f32[2,2048]{1,0:T(2,128)S(1)} %get-tuple-element.120), channel_id=1, source_target_pairs={{0,4},{4,0},{8,12},{12,8},{1,5},{5,1},{9,13},{13,9},{2,6},{6,2},{1... | collective-permute-start | bytes 49160 | tf_op jit(solution)/shard_map/ppermute | solution.py:66
  31.1 1.3 %collective-permute-done.9 = f32[2,2048]{1,0:T(2,128)S(1)} collective-permute-done((f32[2,2048]{1,0:T(2,128)S(1)}, f32[2,2048]{1,0:T(2,128)S(1)}, u32[]{:S(2)}, u32[]{:S(2)}) %collective-permute-start.9) | collective-permute-done | bytes 16416 | tf_op jit(solution)/shard_map/ppermute | solution.py:66
  32.4 1.5 %collective-permute-done.8 = f32[2,2048]{1,0:T(2,128)S(1)} collective-permute-done((f32[2,2048]{1,0:T(2,128)S(1)}, f32[2,2048]{1,0:T(2,128)S(1)}, u32[]{:S(2)}, u32[]{:S(2)}) %collective-permute-start.8) | collective-permute-done | bytes 16416 | tf_op jit(solution)/shard_map/ppermute | solution.py:66
  35.6 1.2 %collective-permute-done.10 = f32[2,2048]{1,0:T(2,128)S(1)} collective-permute-done((f32[2,2048]{1,0:T(2,128)S(1)}, f32[2,2048]{1,0:T(2,128)S(1)}, u32[]{:S(2)}, u32[]{:S(2)}) %collective-permute-start.10) | collective-permute-done | bytes 16416 | tf_op jit(solution)/shard_map/ppermute | solution.py:44
  36.8 1.6 %collective-permute-start.13 = (f32[2,2048]{1,0:T(2,128)S(1)}, f32[2,2048]{1,0:T(2,128)S(1)}, u32[]{:S(2)}, u32[]{:S(2)}) collective-permute-start(f32[2,2048]{1,0:T(2,128)S(1)} %get-tuple-element.118), channel_id=1, source_target_pairs={{0,12},{4,8},{8,4},{12,0},{1,13},{5,9},{9,5},{13,1},{2,14},{6,10},... | collective-permute-start | bytes 49160 | tf_op jit(solution)/shard_map/ppermute | solution.py:66
  39.3 2.0 %collective-permute-start.11 = (f32[2,2048]{1,0:T(2,128)S(1)}, f32[2,2048]{1,0:T(2,128)S(1)}, u32[]{:S(2)}, u32[]{:S(2)}) collective-permute-start(f32[2,2048]{1,0:T(2,128)S(1)} %get-tuple-element.118), channel_id=1, source_target_pairs={{0,4},{4,0},{8,12},{12,8},{1,5},{5,1},{9,13},{13,9},{2,6},{6,2},{1... | collective-permute-start | bytes 49160 | tf_op jit(solution)/shard_map/ppermute | solution.py:66
  41.3 1.3 %collective-permute-done.13 = f32[2,2048]{1,0:T(2,128)S(1)} collective-permute-done((f32[2,2048]{1,0:T(2,128)S(1)}, f32[2,2048]{1,0:T(2,128)S(1)}, u32[]{:S(2)}, u32[]{:S(2)}) %collective-permute-start.13) | collective-permute-done | bytes 16416 | tf_op jit(solution)/shard_map/ppermute | solution.py:66
  44.9 1.2 %collective-permute-done.14 = f32[2,2048]{1,0:T(2,128)S(1)} collective-permute-done((f32[2,2048]{1,0:T(2,128)S(1)}, f32[2,2048]{1,0:T(2,128)S(1)}, u32[]{:S(2)}, u32[]{:S(2)}) %collective-permute-start.14) | collective-permute-done | bytes 16416 | tf_op jit(solution)/shard_map/ppermute | solution.py:44
  46.1 2.4 %collective-permute-start.17 = (f32[2,2048]{1,0:T(2,128)S(1)}, f32[2,2048]{1,0:T(2,128)S(1)}, u32[]{:S(2)}, u32[]{:S(2)}) collective-permute-start(f32[2,2048]{1,0:T(2,128)S(1)} %get-tuple-element.116), channel_id=1, source_target_pairs={{0,12},{4,8},{8,4},{12,0},{1,13},{5,9},{9,5},{13,1},{2,14},{6,10},... | collective-permute-start | bytes 49160 | tf_op jit(solution)/shard_map/ppermute | solution.py:66
  49.5 1.1 %collective-permute-start.15 = (f32[2,2048]{1,0:T(2,128)S(1)}, f32[2,2048]{1,0:T(2,128)S(1)}, u32[]{:S(2)}, u32[]{:S(2)}) collective-permute-start(f32[2,2048]{1,0:T(2,128)S(1)} %get-tuple-element.116), channel_id=1, source_target_pairs={{0,4},{4,0},{8,12},{12,8},{1,5},{5,1},{9,13},{13,9},{2,6},{6,2},{1... | collective-permute-start | bytes 49160 | tf_op jit(solution)/shard_map/ppermute | solution.py:66
  50.6 1.2 %collective-permute-done.17 = f32[2,2048]{1,0:T(2,128)S(1)} collective-permute-done((f32[2,2048]{1,0:T(2,128)S(1)}, f32[2,2048]{1,0:T(2,128)S(1)}, u32[]{:S(2)}, u32[]{:S(2)}) %collective-permute-start.17) | collective-permute-done | bytes 16416 | tf_op jit(solution)/shard_map/ppermute | solution.py:66
  51.8 1.4 %collective-permute-done.16 = f32[2,2048]{1,0:T(2,128)S(1)} collective-permute-done((f32[2,2048]{1,0:T(2,128)S(1)}, f32[2,2048]{1,0:T(2,128)S(1)}, u32[]{:S(2)}, u32[]{:S(2)}) %collective-permute-start.16) | collective-permute-done | bytes 16416 | tf_op jit(solution)/shard_map/ppermute | solution.py:66
  55.0 1.2 %collective-permute-done.18 = f32[2,2048]{1,0:T(2,128)S(1)} collective-permute-done((f32[2,2048]{1,0:T(2,128)S(1)}, f32[2,2048]{1,0:T(2,128)S(1)}, u32[]{:S(2)}, u32[]{:S(2)}) %collective-permute-start.18) | collective-permute-done | bytes 16416 | tf_op jit(solution)/shard_map/ppermute | solution.py:44
  56.3 1.5 %collective-permute-start.21 = (f32[2,2048]{1,0:T(2,128)S(1)}, f32[2,2048]{1,0:T(2,128)S(1)}, u32[]{:S(2)}, u32[]{:S(2)}) collective-permute-start(f32[2,2048]{1,0:T(2,128)S(1)} %get-tuple-element.114), channel_id=1, source_target_pairs={{0,12},{4,8},{8,4},{12,0},{1,13},{5,9},{9,5},{13,1},{2,14},{6,10},... | collective-permute-start | bytes 49160 | tf_op jit(solution)/shard_map/ppermute | solution.py:66
  57.8 1.0 collective-permute-start.20
  58.8 2.0 %collective-permute-start.19 = (f32[2,2048]{1,0:T(2,128)S(1)}, f32[2,2048]{1,0:T(2,128)S(1)}, u32[]{:S(2)}, u32[]{:S(2)}) collective-permute-start(f32[2,2048]{1,0:T(2,128)S(1)} %get-tuple-element.114), channel_id=1, source_target_pairs={{0,4},{4,0},{8,12},{12,8},{1,5},{5,1},{9,13},{13,9},{2,6},{6,2},{1... | collective-permute-start | bytes 49160 | tf_op jit(solution)/shard_map/ppermute | solution.py:66
  60.7 1.2 %collective-permute-done.21 = f32[2,2048]{1,0:T(2,128)S(1)} collective-permute-done((f32[2,2048]{1,0:T(2,128)S(1)}, f32[2,2048]{1,0:T(2,128)S(1)}, u32[]{:S(2)}, u32[]{:S(2)}) %collective-permute-start.21) | collective-permute-done | bytes 16416 | tf_op jit(solution)/shard_map/ppermute | solution.py:66
  64.5 1.2 %collective-permute-done.22 = f32[2,2048]{1,0:T(2,128)S(1)} collective-permute-done((f32[2,2048]{1,0:T(2,128)S(1)}, f32[2,2048]{1,0:T(2,128)S(1)}, u32[]{:S(2)}, u32[]{:S(2)}) %collective-permute-start.22) | collective-permute-done | bytes 16416 | tf_op jit(solution)/shard_map/ppermute | solution.py:44
  65.7 2.4 %collective-permute-start.25 = (f32[2,2048]{1,0:T(2,128)S(1)}, f32[2,2048]{1,0:T(2,128)S(1)}, u32[]{:S(2)}, u32[]{:S(2)}) collective-permute-start(f32[2,2048]{1,0:T(2,128)S(1)} %get-tuple-element.112), channel_id=1, source_target_pairs={{0,12},{4,8},{8,4},{12,0},{1,13},{5,9},{9,5},{13,1},{2,14},{6,10},... | collective-permute-start | bytes 49160 | tf_op jit(solution)/shard_map/ppermute | solution.py:66
  68.2 1.0 collective-permute-start.24
  69.1 1.1 %collective-permute-start.23 = (f32[2,2048]{1,0:T(2,128)S(1)}, f32[2,2048]{1,0:T(2,128)S(1)}, u32[]{:S(2)}, u32[]{:S(2)}) collective-permute-start(f32[2,2048]{1,0:T(2,128)S(1)} %get-tuple-element.112), channel_id=1, source_target_pairs={{0,4},{4,0},{8,12},{12,8},{1,5},{5,1},{9,13},{13,9},{2,6},{6,2},{1... | collective-permute-start | bytes 49160 | tf_op jit(solution)/shard_map/ppermute | solution.py:66
  70.2 1.2 %collective-permute-done.25 = f32[2,2048]{1,0:T(2,128)S(1)} collective-permute-done((f32[2,2048]{1,0:T(2,128)S(1)}, f32[2,2048]{1,0:T(2,128)S(1)}, u32[]{:S(2)}, u32[]{:S(2)}) %collective-permute-start.25) | collective-permute-done | bytes 16416 | tf_op jit(solution)/shard_map/ppermute | solution.py:66
  71.4 1.4 %collective-permute-done.24 = f32[2,2048]{1,0:T(2,128)S(1)} collective-permute-done((f32[2,2048]{1,0:T(2,128)S(1)}, f32[2,2048]{1,0:T(2,128)S(1)}, u32[]{:S(2)}, u32[]{:S(2)}) %collective-permute-start.24) | collective-permute-done | bytes 16416 | tf_op jit(solution)/shard_map/ppermute | solution.py:66
  74.6 1.2 %collective-permute-done.26 = f32[2,2048]{1,0:T(2,128)S(1)} collective-permute-done((f32[2,2048]{1,0:T(2,128)S(1)}, f32[2,2048]{1,0:T(2,128)S(1)}, u32[]{:S(2)}, u32[]{:S(2)}) %collective-permute-start.26) | collective-permute-done | bytes 16416 | tf_op jit(solution)/shard_map/ppermute | solution.py:44
  75.9 1.5 %collective-permute-start.29 = (f32[2,2048]{1,0:T(2,128)S(1)}, f32[2,2048]{1,0:T(2,128)S(1)}, u32[]{:S(2)}, u32[]{:S(2)}) collective-permute-start(f32[2,2048]{1,0:T(2,128)S(1)} %get-tuple-element.110), channel_id=1, source_target_pairs={{0,12},{4,8},{8,4},{12,0},{1,13},{5,9},{9,5},{13,1},{2,14},{6,10},... | collective-permute-start | bytes 49160 | tf_op jit(solution)/shard_map/ppermute | solution.py:66
  77.4 1.0 collective-permute-start.28
  78.4 2.0 %collective-permute-start.27 = (f32[2,2048]{1,0:T(2,128)S(1)}, f32[2,2048]{1,0:T(2,128)S(1)}, u32[]{:S(2)}, u32[]{:S(2)}) collective-permute-start(f32[2,2048]{1,0:T(2,128)S(1)} %get-tuple-element.110), channel_id=1, source_target_pairs={{0,4},{4,0},{8,12},{12,8},{1,5},{5,1},{9,13},{13,9},{2,6},{6,2},{1... | collective-permute-start | bytes 49160 | tf_op jit(solution)/shard_map/ppermute | solution.py:66
  80.3 1.2 %collective-permute-done.29 = f32[2,2048]{1,0:T(2,128)S(1)} collective-permute-done((f32[2,2048]{1,0:T(2,128)S(1)}, f32[2,2048]{1,0:T(2,128)S(1)}, u32[]{:S(2)}, u32[]{:S(2)}) %collective-permute-start.29) | collective-permute-done | bytes 16416 | tf_op jit(solution)/shard_map/ppermute | solution.py:66
  83.9 1.2 %collective-permute-done.30 = f32[2,2048]{1,0:T(2,128)S(1)} collective-permute-done((f32[2,2048]{1,0:T(2,128)S(1)}, f32[2,2048]{1,0:T(2,128)S(1)}, u32[]{:S(2)}, u32[]{:S(2)}) %collective-permute-start.30) | collective-permute-done | bytes 16416 | tf_op jit(solution)/shard_map/ppermute | solution.py:44
  85.1 2.4 %collective-permute-start.33 = (f32[2,2048]{1,0:T(2,128)S(1)}, f32[2,2048]{1,0:T(2,128)S(1)}, u32[]{:S(2)}, u32[]{:S(2)}) collective-permute-start(f32[2,2048]{1,0:T(2,128)S(1)} %get-tuple-element.108), channel_id=1, source_target_pairs={{0,12},{4,8},{8,4},{12,0},{1,13},{5,9},{9,5},{13,1},{2,14},{6,10},... | collective-permute-start | bytes 49160 | tf_op jit(solution)/shard_map/ppermute | solution.py:66
  88.5 1.1 %collective-permute-start.31 = (f32[2,2048]{1,0:T(2,128)S(1)}, f32[2,2048]{1,0:T(2,128)S(1)}, u32[]{:S(2)}, u32[]{:S(2)}) collective-permute-start(f32[2,2048]{1,0:T(2,128)S(1)} %get-tuple-element.108), channel_id=1, source_target_pairs={{0,4},{4,0},{8,12},{12,8},{1,5},{5,1},{9,13},{13,9},{2,6},{6,2},{1... | collective-permute-start | bytes 49160 | tf_op jit(solution)/shard_map/ppermute | solution.py:66
  89.6 1.2 %collective-permute-done.33 = f32[2,2048]{1,0:T(2,128)S(1)} collective-permute-done((f32[2,2048]{1,0:T(2,128)S(1)}, f32[2,2048]{1,0:T(2,128)S(1)}, u32[]{:S(2)}, u32[]{:S(2)}) %collective-permute-start.33) | collective-permute-done | bytes 16416 | tf_op jit(solution)/shard_map/ppermute | solution.py:66
  90.8 1.4 %collective-permute-done.32 = f32[2,2048]{1,0:T(2,128)S(1)} collective-permute-done((f32[2,2048]{1,0:T(2,128)S(1)}, f32[2,2048]{1,0:T(2,128)S(1)}, u32[]{:S(2)}, u32[]{:S(2)}) %collective-permute-start.32) | collective-permute-done | bytes 16416 | tf_op jit(solution)/shard_map/ppermute | solution.py:66
  94.0 1.0 fusion.4
  95.5 1.3 %collective-permute-done.34 = f32[4,128,66]{1,0,2:T(4,128)S(1)} collective-permute-done((f32[4,128,66]{1,0,2:T(4,128)S(1)}, f32[4,128,66]{1,0,2:T(4,128)S(1)}, u32[]{:S(2)}, u32[]{:S(2)}) %collective-permute-start.34) | collective-permute-done | bytes 135200 | tf_op jit(solution)/shard_map/ppermute | solution.py:191
  97.1 1.5 %collective-permute-start.37 = (f32[128,66]{0,1:T(8,128)S(1)}, f32[128,66]{0,1:T(8,128)S(1)}, u32[]{:S(2)}, u32[]{:S(2)}) collective-permute-start(f32[128,66]{0,1:T(8,128)S(1)} %bitcast.204), channel_id=1, source_target_pairs={{0,12},{4,8},{8,4},{12,0},{1,13},{5,9},{9,5},{13,1},{2,14},{6,10},... | collective-permute-start | bytes 101384 | tf_op jit(solution)/shard_map/ppermute | solution.py:152
  99.6 2.0 %collective-permute-start.35 = (f32[128,66]{0,1:T(8,128)S(1)}, f32[128,66]{0,1:T(8,128)S(1)}, u32[]{:S(2)}, u32[]{:S(2)}) collective-permute-start(f32[128,66]{0,1:T(8,128)S(1)} %bitcast.206), channel_id=1, source_target_pairs={{0,4},{4,0},{8,12},{12,8},{1,5},{5,1},{9,13},{13,9},{2,6},{6,2},{1... | collective-permute-start | bytes 101384 | tf_op jit(solution)/shard_map/ppermute | solution.py:152
  102.1 1.0 collective-permute-done.37
  (162 shorter events, 27.6 us)
Async XLA Ops:
  0.6 5.6 %copy-start = (f32[1024,64]{0,1:T(8,128)S(1)}, f32[1024,64]{0,1:T(8,128)}, u32[]{:S(2)}) copy-start(f32[1024,64]{0,1:T(8,128)} %param.5) | copy-start | bytes 786436
  3.2 3.4 %copy-start.4 = (f32[1024]{0:T(1024)S(1)}, f32[1024]{0:T(1024)}, u32[]{:S(2)}) copy-start(f32[1024]{0:T(1024)} %param.6) | copy-start | bytes 12292
  5.7 3.5 %collective-permute-start.1 = (f32[2,1024]{1,0:T(2,128)S(1)}, f32[2,1024]{1,0:T(2,128)S(1)}, u32[]{:S(2)}, u32[]{:S(2)}) collective-permute-start(f32[2,1024]{1,0:T(2,128)S(1)} %pad_maximum_fusion.26), channel_id=1, source_target_pairs={{0,1},{1,0},{2,3},{3,2},{4,5},{5,4},{6,7},{7,6},{8,9},{9,8},{10,11... | collective-permute-start | bytes 24584 | tf_op jit(solution)/shard_map/ppermute | solution.py:44
  6.6 10.9 %collective-permute-start = (f32[520,128]{1,0:T(8,128)S(1)}, f32[520,128]{1,0:T(8,128)S(1)}, u32[]{:S(2)}, u32[]{:S(2)}) collective-permute-start(f32[520,128]{1,0:T(8,128)S(1)} %pad_maximum_fusion.2), channel_id=1, source_target_pairs={{0,2},{2,0},{1,3},{3,1},{4,6},{6,4},{5,7},{7,5},{8,10},{10,8},{9,1... | collective-permute-start | bytes 798728 | tf_op jit(solution)/shard_map/ppermute | solution.py:256
  9.2 5.5 %collective-permute-start.4 = (f32[2,1024]{1,0:T(2,128)S(1)}, f32[2,1024]{1,0:T(2,128)S(1)}, u32[]{:S(2)}, u32[]{:S(2)}) collective-permute-start(f32[2,1024]{1,0:T(2,128)S(1)} %get-tuple-element.124), channel_id=1, source_target_pairs={{0,12},{4,8},{8,4},{12,0},{1,13},{5,9},{9,5},{13,1},{2,14},{6,10},... | collective-permute-start | bytes 24584 | tf_op jit(solution)/shard_map/ppermute | solution.py:66
  12.9 4.5 %collective-permute-start.3 = (f32[2,1024]{1,0:T(2,128)S(1)}, f32[2,1024]{1,0:T(2,128)S(1)}, u32[]{:S(2)}, u32[]{:S(2)}) collective-permute-start(f32[2,1024]{1,0:T(2,128)S(1)} %get-tuple-element.124), channel_id=1, source_target_pairs={{0,8},{4,12},{8,0},{12,4},{1,9},{5,13},{9,1},{13,5},{2,10},{6,14},... | collective-permute-start | bytes 24584 | tf_op jit(solution)/shard_map/ppermute | solution.py:66
  12.9 4.5 %collective-permute-start.2 = (f32[2,1024]{1,0:T(2,128)S(1)}, f32[2,1024]{1,0:T(2,128)S(1)}, u32[]{:S(2)}, u32[]{:S(2)}) collective-permute-start(f32[2,1024]{1,0:T(2,128)S(1)} %get-tuple-element.124), channel_id=1, source_target_pairs={{0,4},{4,0},{8,12},{12,8},{1,5},{5,1},{9,13},{13,9},{2,6},{6,2},{1... | collective-permute-start | bytes 24584 | tf_op jit(solution)/shard_map/ppermute | solution.py:66
  17.6 0.8 copy-start.1
  18.4 6.2 %copy-start.2 = (f32[256]{0:T(256)S(1)}, f32[256]{0:T(256)}, u32[]{:S(2)}) copy-start(f32[256]{0:T(256)} %param.8) | copy-start | bytes 3076
  21.0 3.7 %collective-permute-start.5 = (f32[2,256]{1,0:T(2,128)S(1)}, f32[2,256]{1,0:T(2,128)S(1)}, u32[]{:S(2)}, u32[]{:S(2)}) collective-permute-start(f32[2,256]{1,0:T(2,128)S(1)} %pad_maximum_fusion.28), channel_id=1, source_target_pairs={{0,2},{2,0},{1,3},{3,1},{4,6},{6,4},{5,7},{7,5},{8,10},{10,8},{9,1... | collective-permute-start | bytes 6152 | tf_op jit(solution)/shard_map/ppermute | solution.py:44
  25.4 1.2 %collective-permute-start.6 = (f32[2,2048]{1,0:T(2,128)S(1)}, f32[2,2048]{1,0:T(2,128)S(1)}, u32[]{:S(2)}, u32[]{:S(2)}) collective-permute-start(f32[2,2048]{1,0:T(2,128)S(1)} %pad_maximum_fusion.12), channel_id=1, source_target_pairs={{0,1},{1,0},{2,3},{3,2},{4,5},{5,4},{6,7},{7,6},{8,9},{9,8},{10,11... | collective-permute-start | bytes 49160 | tf_op jit(solution)/shard_map/ppermute | solution.py:44
  26.7 5.7 %collective-permute-start.9 = (f32[2,2048]{1,0:T(2,128)S(1)}, f32[2,2048]{1,0:T(2,128)S(1)}, u32[]{:S(2)}, u32[]{:S(2)}) collective-permute-start(f32[2,2048]{1,0:T(2,128)S(1)} %get-tuple-element.120), channel_id=1, source_target_pairs={{0,12},{4,8},{8,4},{12,0},{1,13},{5,9},{9,5},{13,1},{2,14},{6,10},... | collective-permute-start | bytes 49160 | tf_op jit(solution)/shard_map/ppermute | solution.py:66
  29.3 4.6 %collective-permute-start.8 = (f32[2,2048]{1,0:T(2,128)S(1)}, f32[2,2048]{1,0:T(2,128)S(1)}, u32[]{:S(2)}, u32[]{:S(2)}) collective-permute-start(f32[2,2048]{1,0:T(2,128)S(1)} %get-tuple-element.120), channel_id=1, source_target_pairs={{0,8},{4,12},{8,0},{12,4},{1,9},{5,13},{9,1},{13,5},{2,10},{6,14},... | collective-permute-start | bytes 49160 | tf_op jit(solution)/shard_map/ppermute | solution.py:66
  29.3 4.6 %collective-permute-start.7 = (f32[2,2048]{1,0:T(2,128)S(1)}, f32[2,2048]{1,0:T(2,128)S(1)}, u32[]{:S(2)}, u32[]{:S(2)}) collective-permute-start(f32[2,2048]{1,0:T(2,128)S(1)} %get-tuple-element.120), channel_id=1, source_target_pairs={{0,4},{4,0},{8,12},{12,8},{1,5},{5,1},{9,13},{13,9},{2,6},{6,2},{1... | collective-permute-start | bytes 49160 | tf_op jit(solution)/shard_map/ppermute | solution.py:66
  35.5 1.2 %collective-permute-start.10 = (f32[2,2048]{1,0:T(2,128)S(1)}, f32[2,2048]{1,0:T(2,128)S(1)}, u32[]{:S(2)}, u32[]{:S(2)}) collective-permute-start(f32[2,2048]{1,0:T(2,128)S(1)} %pad_maximum_fusion.14), channel_id=1, source_target_pairs={{0,1},{1,0},{2,3},{3,2},{4,5},{5,4},{6,7},{7,6},{8,9},{9,8},{10,11... | collective-permute-start | bytes 49160 | tf_op jit(solution)/shard_map/ppermute | solution.py:44
  36.8 5.7 %collective-permute-start.13 = (f32[2,2048]{1,0:T(2,128)S(1)}, f32[2,2048]{1,0:T(2,128)S(1)}, u32[]{:S(2)}, u32[]{:S(2)}) collective-permute-start(f32[2,2048]{1,0:T(2,128)S(1)} %get-tuple-element.118), channel_id=1, source_target_pairs={{0,12},{4,8},{8,4},{12,0},{1,13},{5,9},{9,5},{13,1},{2,14},{6,10},... | collective-permute-start | bytes 49160 | tf_op jit(solution)/shard_map/ppermute | solution.py:66
  38.4 4.6 %collective-permute-start.12 = (f32[2,2048]{1,0:T(2,128)S(1)}, f32[2,2048]{1,0:T(2,128)S(1)}, u32[]{:S(2)}, u32[]{:S(2)}) collective-permute-start(f32[2,2048]{1,0:T(2,128)S(1)} %get-tuple-element.118), channel_id=1, source_target_pairs={{0,8},{4,12},{8,0},{12,4},{1,9},{5,13},{9,1},{13,5},{2,10},{6,14},... | collective-permute-start | bytes 49160 | tf_op jit(solution)/shard_map/ppermute | solution.py:66
  39.3 3.9 %collective-permute-start.11 = (f32[2,2048]{1,0:T(2,128)S(1)}, f32[2,2048]{1,0:T(2,128)S(1)}, u32[]{:S(2)}, u32[]{:S(2)}) collective-permute-start(f32[2,2048]{1,0:T(2,128)S(1)} %get-tuple-element.118), channel_id=1, source_target_pairs={{0,4},{4,0},{8,12},{12,8},{1,5},{5,1},{9,13},{13,9},{2,6},{6,2},{1... | collective-permute-start | bytes 49160 | tf_op jit(solution)/shard_map/ppermute | solution.py:66
  44.8 1.2 %collective-permute-start.14 = (f32[2,2048]{1,0:T(2,128)S(1)}, f32[2,2048]{1,0:T(2,128)S(1)}, u32[]{:S(2)}, u32[]{:S(2)}) collective-permute-start(f32[2,2048]{1,0:T(2,128)S(1)} %pad_maximum_fusion.16), channel_id=1, source_target_pairs={{0,1},{1,0},{2,3},{3,2},{4,5},{5,4},{6,7},{7,6},{8,9},{9,8},{10,11... | collective-permute-start | bytes 49160 | tf_op jit(solution)/shard_map/ppermute | solution.py:44
  46.1 5.7 %collective-permute-start.17 = (f32[2,2048]{1,0:T(2,128)S(1)}, f32[2,2048]{1,0:T(2,128)S(1)}, u32[]{:S(2)}, u32[]{:S(2)}) collective-permute-start(f32[2,2048]{1,0:T(2,128)S(1)} %get-tuple-element.116), channel_id=1, source_target_pairs={{0,12},{4,8},{8,4},{12,0},{1,13},{5,9},{9,5},{13,1},{2,14},{6,10},... | collective-permute-start | bytes 49160 | tf_op jit(solution)/shard_map/ppermute | solution.py:66
  48.6 4.7 %collective-permute-start.16 = (f32[2,2048]{1,0:T(2,128)S(1)}, f32[2,2048]{1,0:T(2,128)S(1)}, u32[]{:S(2)}, u32[]{:S(2)}) collective-permute-start(f32[2,2048]{1,0:T(2,128)S(1)} %get-tuple-element.116), channel_id=1, source_target_pairs={{0,8},{4,12},{8,0},{12,4},{1,9},{5,13},{9,1},{13,5},{2,10},{6,14},... | collective-permute-start | bytes 49160 | tf_op jit(solution)/shard_map/ppermute | solution.py:66
  49.5 3.9 %collective-permute-start.15 = (f32[2,2048]{1,0:T(2,128)S(1)}, f32[2,2048]{1,0:T(2,128)S(1)}, u32[]{:S(2)}, u32[]{:S(2)}) collective-permute-start(f32[2,2048]{1,0:T(2,128)S(1)} %get-tuple-element.116), channel_id=1, source_target_pairs={{0,4},{4,0},{8,12},{12,8},{1,5},{5,1},{9,13},{13,9},{2,6},{6,2},{1... | collective-permute-start | bytes 49160 | tf_op jit(solution)/shard_map/ppermute | solution.py:66
  55.0 1.2 %collective-permute-start.18 = (f32[2,2048]{1,0:T(2,128)S(1)}, f32[2,2048]{1,0:T(2,128)S(1)}, u32[]{:S(2)}, u32[]{:S(2)}) collective-permute-start(f32[2,2048]{1,0:T(2,128)S(1)} %pad_maximum_fusion.18), channel_id=1, source_target_pairs={{0,1},{1,0},{2,3},{3,2},{4,5},{5,4},{6,7},{7,6},{8,9},{9,8},{10,11... | collective-permute-start | bytes 49160 | tf_op jit(solution)/shard_map/ppermute | solution.py:44
  56.3 5.6 %collective-permute-start.21 = (f32[2,2048]{1,0:T(2,128)S(1)}, f32[2,2048]{1,0:T(2,128)S(1)}, u32[]{:S(2)}, u32[]{:S(2)}) collective-permute-start(f32[2,2048]{1,0:T(2,128)S(1)} %get-tuple-element.114), channel_id=1, source_target_pairs={{0,12},{4,8},{8,4},{12,0},{1,13},{5,9},{9,5},{13,1},{2,14},{6,10},... | collective-permute-start | bytes 49160 | tf_op jit(solution)/shard_map/ppermute | solution.py:66
  57.8 4.6 %collective-permute-start.20 = (f32[2,2048]{1,0:T(2,128)S(1)}, f32[2,2048]{1,0:T(2,128)S(1)}, u32[]{:S(2)}, u32[]{:S(2)}) collective-permute-start(f32[2,2048]{1,0:T(2,128)S(1)} %get-tuple-element.114), channel_id=1, source_target_pairs={{0,8},{4,12},{8,0},{12,4},{1,9},{5,13},{9,1},{13,5},{2,10},{6,14},... | collective-permute-start | bytes 49160 | tf_op jit(solution)/shard_map/ppermute | solution.py:66
  58.8 3.9 %collective-permute-start.19 = (f32[2,2048]{1,0:T(2,128)S(1)}, f32[2,2048]{1,0:T(2,128)S(1)}, u32[]{:S(2)}, u32[]{:S(2)}) collective-permute-start(f32[2,2048]{1,0:T(2,128)S(1)} %get-tuple-element.114), channel_id=1, source_target_pairs={{0,4},{4,0},{8,12},{12,8},{1,5},{5,1},{9,13},{13,9},{2,6},{6,2},{1... | collective-permute-start | bytes 49160 | tf_op jit(solution)/shard_map/ppermute | solution.py:66
  64.4 1.2 %collective-permute-start.22 = (f32[2,2048]{1,0:T(2,128)S(1)}, f32[2,2048]{1,0:T(2,128)S(1)}, u32[]{:S(2)}, u32[]{:S(2)}) collective-permute-start(f32[2,2048]{1,0:T(2,128)S(1)} %pad_maximum_fusion.20), channel_id=1, source_target_pairs={{0,1},{1,0},{2,3},{3,2},{4,5},{5,4},{6,7},{7,6},{8,9},{9,8},{10,11... | collective-permute-start | bytes 49160 | tf_op jit(solution)/shard_map/ppermute | solution.py:44
  65.7 5.7 %collective-permute-start.25 = (f32[2,2048]{1,0:T(2,128)S(1)}, f32[2,2048]{1,0:T(2,128)S(1)}, u32[]{:S(2)}, u32[]{:S(2)}) collective-permute-start(f32[2,2048]{1,0:T(2,128)S(1)} %get-tuple-element.112), channel_id=1, source_target_pairs={{0,12},{4,8},{8,4},{12,0},{1,13},{5,9},{9,5},{13,1},{2,14},{6,10},... | collective-permute-start | bytes 49160 | tf_op jit(solution)/shard_map/ppermute | solution.py:66
  68.2 4.6 %collective-permute-start.24 = (f32[2,2048]{1,0:T(2,128)S(1)}, f32[2,2048]{1,0:T(2,128)S(1)}, u32[]{:S(2)}, u32[]{:S(2)}) collective-permute-start(f32[2,2048]{1,0:T(2,128)S(1)} %get-tuple-element.112), channel_id=1, source_target_pairs={{0,8},{4,12},{8,0},{12,4},{1,9},{5,13},{9,1},{13,5},{2,10},{6,14},... | collective-permute-start | bytes 49160 | tf_op jit(solution)/shard_map/ppermute | solution.py:66
  69.1 3.9 %collective-permute-start.23 = (f32[2,2048]{1,0:T(2,128)S(1)}, f32[2,2048]{1,0:T(2,128)S(1)}, u32[]{:S(2)}, u32[]{:S(2)}) collective-permute-start(f32[2,2048]{1,0:T(2,128)S(1)} %get-tuple-element.112), channel_id=1, source_target_pairs={{0,4},{4,0},{8,12},{12,8},{1,5},{5,1},{9,13},{13,9},{2,6},{6,2},{1... | collective-permute-start | bytes 49160 | tf_op jit(solution)/shard_map/ppermute | solution.py:66
  74.6 1.2 %collective-permute-start.26 = (f32[2,2048]{1,0:T(2,128)S(1)}, f32[2,2048]{1,0:T(2,128)S(1)}, u32[]{:S(2)}, u32[]{:S(2)}) collective-permute-start(f32[2,2048]{1,0:T(2,128)S(1)} %pad_maximum_fusion.22), channel_id=1, source_target_pairs={{0,1},{1,0},{2,3},{3,2},{4,5},{5,4},{6,7},{7,6},{8,9},{9,8},{10,11... | collective-permute-start | bytes 49160 | tf_op jit(solution)/shard_map/ppermute | solution.py:44
  75.9 5.6 %collective-permute-start.29 = (f32[2,2048]{1,0:T(2,128)S(1)}, f32[2,2048]{1,0:T(2,128)S(1)}, u32[]{:S(2)}, u32[]{:S(2)}) collective-permute-start(f32[2,2048]{1,0:T(2,128)S(1)} %get-tuple-element.110), channel_id=1, source_target_pairs={{0,12},{4,8},{8,4},{12,0},{1,13},{5,9},{9,5},{13,1},{2,14},{6,10},... | collective-permute-start | bytes 49160 | tf_op jit(solution)/shard_map/ppermute | solution.py:66
  77.4 4.6 %collective-permute-start.28 = (f32[2,2048]{1,0:T(2,128)S(1)}, f32[2,2048]{1,0:T(2,128)S(1)}, u32[]{:S(2)}, u32[]{:S(2)}) collective-permute-start(f32[2,2048]{1,0:T(2,128)S(1)} %get-tuple-element.110), channel_id=1, source_target_pairs={{0,8},{4,12},{8,0},{12,4},{1,9},{5,13},{9,1},{13,5},{2,10},{6,14},... | collective-permute-start | bytes 49160 | tf_op jit(solution)/shard_map/ppermute | solution.py:66
  78.4 3.9 %collective-permute-start.27 = (f32[2,2048]{1,0:T(2,128)S(1)}, f32[2,2048]{1,0:T(2,128)S(1)}, u32[]{:S(2)}, u32[]{:S(2)}) collective-permute-start(f32[2,2048]{1,0:T(2,128)S(1)} %get-tuple-element.110), channel_id=1, source_target_pairs={{0,4},{4,0},{8,12},{12,8},{1,5},{5,1},{9,13},{13,9},{2,6},{6,2},{1... | collective-permute-start | bytes 49160 | tf_op jit(solution)/shard_map/ppermute | solution.py:66
  83.8 1.2 %collective-permute-start.30 = (f32[2,2048]{1,0:T(2,128)S(1)}, f32[2,2048]{1,0:T(2,128)S(1)}, u32[]{:S(2)}, u32[]{:S(2)}) collective-permute-start(f32[2,2048]{1,0:T(2,128)S(1)} %pad_maximum_fusion.24), channel_id=1, source_target_pairs={{0,1},{1,0},{2,3},{3,2},{4,5},{5,4},{6,7},{7,6},{8,9},{9,8},{10,11... | collective-permute-start | bytes 49160 | tf_op jit(solution)/shard_map/ppermute | solution.py:44
  85.1 5.7 %collective-permute-start.33 = (f32[2,2048]{1,0:T(2,128)S(1)}, f32[2,2048]{1,0:T(2,128)S(1)}, u32[]{:S(2)}, u32[]{:S(2)}) collective-permute-start(f32[2,2048]{1,0:T(2,128)S(1)} %get-tuple-element.108), channel_id=1, source_target_pairs={{0,12},{4,8},{8,4},{12,0},{1,13},{5,9},{9,5},{13,1},{2,14},{6,10},... | collective-permute-start | bytes 49160 | tf_op jit(solution)/shard_map/ppermute | solution.py:66
  87.6 4.6 %collective-permute-start.32 = (f32[2,2048]{1,0:T(2,128)S(1)}, f32[2,2048]{1,0:T(2,128)S(1)}, u32[]{:S(2)}, u32[]{:S(2)}) collective-permute-start(f32[2,2048]{1,0:T(2,128)S(1)} %get-tuple-element.108), channel_id=1, source_target_pairs={{0,8},{4,12},{8,0},{12,4},{1,9},{5,13},{9,1},{13,5},{2,10},{6,14},... | collective-permute-start | bytes 49160 | tf_op jit(solution)/shard_map/ppermute | solution.py:66
  88.5 3.9 %collective-permute-start.31 = (f32[2,2048]{1,0:T(2,128)S(1)}, f32[2,2048]{1,0:T(2,128)S(1)}, u32[]{:S(2)}, u32[]{:S(2)}) collective-permute-start(f32[2,2048]{1,0:T(2,128)S(1)} %get-tuple-element.108), channel_id=1, source_target_pairs={{0,4},{4,0},{8,12},{12,8},{1,5},{5,1},{9,13},{13,9},{2,6},{6,2},{1... | collective-permute-start | bytes 49160 | tf_op jit(solution)/shard_map/ppermute | solution.py:66
  92.8 1.2 %copy-start.3 = (f32[256,64]{0,1:T(8,128)S(1)}, f32[256,64]{0,1:T(8,128)}, u32[]{:S(2)}) copy-start(f32[256,64]{0,1:T(8,128)} %param.9) | copy-start | bytes 196612
  95.4 1.4 %collective-permute-start.34 = (f32[4,128,66]{1,0,2:T(4,128)S(1)}, f32[4,128,66]{1,0,2:T(4,128)S(1)}, u32[]{:S(2)}, u32[]{:S(2)}) collective-permute-start(f32[4,128,66]{1,0,2:T(4,128)S(1)} %get-tuple-element.16), channel_id=1, source_target_pairs={{0,1},{1,0},{2,3},{3,2},{4,5},{5,4},{6,7},{7,6},{8,9},{9,8},{10,11... | collective-permute-start | bytes 405512 | tf_op jit(solution)/shard_map/ppermute | solution.py:191
  97.1 6.1 %collective-permute-start.37 = (f32[128,66]{0,1:T(8,128)S(1)}, f32[128,66]{0,1:T(8,128)S(1)}, u32[]{:S(2)}, u32[]{:S(2)}) collective-permute-start(f32[128,66]{0,1:T(8,128)S(1)} %bitcast.204), channel_id=1, source_target_pairs={{0,12},{4,8},{8,4},{12,0},{1,13},{5,9},{9,5},{13,1},{2,14},{6,10},... | collective-permute-start | bytes 101384 | tf_op jit(solution)/shard_map/ppermute | solution.py:152
  98.6 5.4 %collective-permute-start.36 = (f32[128,66]{0,1:T(8,128)S(1)}, f32[128,66]{0,1:T(8,128)S(1)}, u32[]{:S(2)}, u32[]{:S(2)}) collective-permute-start(f32[128,66]{0,1:T(8,128)S(1)} %bitcast.205), channel_id=1, source_target_pairs={{0,8},{4,12},{8,0},{12,4},{1,9},{5,13},{9,1},{13,5},{2,10},{6,14},... | collective-permute-start | bytes 101384 | tf_op jit(solution)/shard_map/ppermute | solution.py:152
  99.6 4.5 %collective-permute-start.35 = (f32[128,66]{0,1:T(8,128)S(1)}, f32[128,66]{0,1:T(8,128)S(1)}, u32[]{:S(2)}, u32[]{:S(2)}) collective-permute-start(f32[128,66]{0,1:T(8,128)S(1)} %bitcast.206), channel_id=1, source_target_pairs={{0,4},{4,0},{8,12},{12,8},{1,5},{5,1},{9,13},{13,9},{2,6},{6,2},{1... | collective-permute-start | bytes 101384 | tf_op jit(solution)/shard_map/ppermute | solution.py:152

commit v13 on v12

--- a/solution.py
+++ b/solution.py
@@ -184,15 +184,15 @@
     if rep_size == 2 and col_size <= 8:
         block = src_count // (col_size * rep_size)
         rep = lax.axis_index("rep")
-        packed = jnp.concatenate([weighted, maxima[:, None], totals[:, None]], axis=-1)
+        packed = jnp.concatenate([product, maxima[:, None]], axis=-1)
         packed = packed.reshape(col_size, rep_size, block, fates + 2)
         keep = lax.dynamic_index_in_dim(packed, rep, axis=1, keepdims=False)
         send = lax.dynamic_index_in_dim(packed, 1 - rep, axis=1, keepdims=False)
         recv = lax.ppermute(send, "rep", [(0, 1), (1, 0)])
-        maxima = jnp.maximum(keep[..., fates], recv[..., fates])
-        keep_f = jnp.exp(keep[..., fates] - maxima)
-        recv_f = jnp.exp(recv[..., fates] - maxima)
-        totals = keep[..., fates + 1] * keep_f + recv[..., fates + 1] * recv_f
+        maxima = jnp.maximum(keep[..., fates + 1], recv[..., fates + 1])
+        keep_f = jnp.exp(keep[..., fates + 1] - maxima)
+        recv_f = jnp.exp(recv[..., fates + 1] - maxima)
+        totals = keep[..., fates] * keep_f + recv[..., fates] * recv_f
         weighted = keep[..., :fates] * keep_f[..., None] + recv[..., :fates] * recv_f[..., None]
         maxima, totals, weighted = lse_scatter_exchange(maxima, totals, weighted, "cols")
         fate_rows = weighted / totals[:, None]

time: 105 us -> 105 us (level)
  no operation moved by 1% of the time
where the time goes in v13:
time: 105 us
  starting transfers between devices  44.5 us (42%)
  waiting for transfers between devices  35 us (33%)
  other arithmetic  16.9 us (16%)
  matrix products  5.18 us (5%)
  local copies, waits for them, and re-layouts  1.79 us (2%)
  between operations  1.35 us (1%)
    ppermute x24, starting transfers between devices, lse_exchange(): received.append(lax.ppermute(payload, axes, perm))  35.6 us
    ppermute x24, waiting for transfers between devices, lse_exchange(): received.append(lax.ppermute(payload, axes, perm))  20.6 us
    ppermute x9, waiting for transfers between devices, lse_allreduce(): other = lax.ppermute(jnp.stack([maxima, totals]), name, perm)  11.1 us
    ppermute x3, starting transfers between devices, lse_scatter_exchange(): parts.append(lax.ppermute(send, name, perm))  4.45 us
    dot_general x2, matrix products, pair_cost(): lax.dot_general(lhs_rows, rhs_rows, (((1,), (1,)), ((), ())), precision=l...  4.17 us
    reduce_sum x8, other arithmetic, body(): totals = jnp.sum(jnp.exp(scores - maxima[None, :]), axis=0)  4 us
    reduce_sum x8, other arithmetic, body(): totals = jnp.sum(jnp.exp(scores - maxima[:, None]), axis=1)  3.27 us
    ppermute x1, starting transfers between devices, body(): theirs = lax.ppermute(mine, 'rows', [(0, 1), (1, 0)])  2.56 us
  transfers between devices with their start and end apart: 38, of which 33 were waited for; matrix products, arithmetic and copies ran while one was open for 1% of the time, Pallas kernels for 0%

profile of v13, /device:TPU:0, one launch (start us, length us, event | category | flops | bytes accessed | tf_op | source)
XLA Modules:
  0.0 104.7 jit_solution(14041908157283269400)
XLA Ops:
  2.2 1.0 multiply_reduce_fusion.1
  3.2 2.1 %subtract_reduce_fusion.16 = (f32[1024]{0:T(1024)S(1)}, f32[1024,256]{0,1:T(8,128)S(1)}) fusion(f32[256]{0:T(256)S(1)} %multiply_log_fusion, f32[1024,64]{0,1:T(8,128)} %param.5, f32[256,64]{0,1:T(8,128)} %param.7, f32[256]{0:T(256)S(1)} %multiply_reduce_fusion.2, f32[1024]{0:T(1024)S(1)} %multiply_reduce_fusion.1), kind=kOutput, calls=%fused_computation.44 | convolution fusion | flops 202898432 | bytes 1386496 | tf_op jit(solution)/shard_map/dot_general | solution.py:15
  6.6 2.6 %collective-permute-start = (f32[520,128]{1,0:T(8,128)S(1)}, f32[520,128]{1,0:T(8,128)S(1)}, u32[]{:S(2)}, u32[]{:S(2)}) collective-permute-start(f32[520,128]{1,0:T(8,128)S(1)} %pad_maximum_fusion.2), channel_id=1, source_target_pairs={{0,2},{2,0},{1,3},{3,1},{4,6},{6,4},{5,7},{7,5},{8,10},{10,8},{9,1... | collective-permute-start | bytes 798728 | tf_op jit(solution)/shard_map/ppermute | solution.py:256
  9.2 3.7 %collective-permute-start.4 = (f32[2,1024]{1,0:T(2,128)S(1)}, f32[2,1024]{1,0:T(2,128)S(1)}, u32[]{:S(2)}, u32[]{:S(2)}) collective-permute-start(f32[2,1024]{1,0:T(2,128)S(1)} %get-tuple-element.124), channel_id=1, source_target_pairs={{0,12},{4,8},{8,4},{12,0},{1,13},{5,9},{9,5},{13,1},{2,14},{6,10},... | collective-permute-start | bytes 24584 | tf_op jit(solution)/shard_map/ppermute | solution.py:66
  13.7 1.1 %collective-permute-done.4 = f32[2,1024]{1,0:T(2,128)S(1)} collective-permute-done((f32[2,1024]{1,0:T(2,128)S(1)}, f32[2,1024]{1,0:T(2,128)S(1)}, u32[]{:S(2)}, u32[]{:S(2)}) %collective-permute-start.4) | collective-permute-done | bytes 8224 | tf_op jit(solution)/shard_map/ppermute | solution.py:66
  14.7 2.7 %collective-permute-done.3 = f32[2,1024]{1,0:T(2,128)S(1)} collective-permute-done((f32[2,1024]{1,0:T(2,128)S(1)}, f32[2,1024]{1,0:T(2,128)S(1)}, u32[]{:S(2)}, u32[]{:S(2)}) %collective-permute-start.3) | collective-permute-done | bytes 8224 | tf_op jit(solution)/shard_map/ppermute | solution.py:66
  18.4 2.0 %fusion.1 = f32[2048,256]{0,1:T(8,128)S(1)} fusion(f32[256,64]{0,1:T(8,128)S(1)} %copy-done.1, f32[256]{0:T(256)S(1)} %multiply_reduce_fusion.2, f32[2048]{0:T(1024)S(1)} %multiply_reduce_fusion, f32[1024,64]{1,0:T(8,128)S(1)} %get-tuple-element.14, f32[1024,64]{1,0:T(8,128)S(1)} %get-tuple-element.13), kind=kOutput, calls=%fused_computation.2 | convolution fusion | flops 404881408 | bytes 2696192 | tf_op jit(solution)/shard_map/dot_general | solution.py:15
  21.7 2.9 %collective-permute-done.5 = f32[2,256]{1,0:T(2,128)S(1)} collective-permute-done((f32[2,256]{1,0:T(2,128)S(1)}, f32[2,256]{1,0:T(2,128)S(1)}, u32[]{:S(2)}, u32[]{:S(2)}) %collective-permute-start.5) | collective-permute-done | bytes 2080 | tf_op jit(solution)/shard_map/ppermute | solution.py:44
  25.4 1.2 %collective-permute-done.6 = f32[2,2048]{1,0:T(2,128)S(1)} collective-permute-done((f32[2,2048]{1,0:T(2,128)S(1)}, f32[2,2048]{1,0:T(2,128)S(1)}, u32[]{:S(2)}, u32[]{:S(2)}) %collective-permute-start.6) | collective-permute-done | bytes 16416 | tf_op jit(solution)/shard_map/ppermute | solution.py:44
  26.7 2.6 %collective-permute-start.9 = (f32[2,2048]{1,0:T(2,128)S(1)}, f32[2,2048]{1,0:T(2,128)S(1)}, u32[]{:S(2)}, u32[]{:S(2)}) collective-permute-start(f32[2,2048]{1,0:T(2,128)S(1)} %get-tuple-element.120), channel_id=1, source_target_pairs={{0,12},{4,8},{8,4},{12,0},{1,13},{5,9},{9,5},{13,1},{2,14},{6,10},... | collective-permute-start | bytes 49160 | tf_op jit(solution)/shard_map/ppermute | solution.py:66
  29.3 1.9 %collective-permute-start.7 = (f32[2,2048]{1,0:T(2,128)S(1)}, f32[2,2048]{1,0:T(2,128)S(1)}, u32[]{:S(2)}, u32[]{:S(2)}) collective-permute-start(f32[2,2048]{1,0:T(2,128)S(1)} %get-tuple-element.120), channel_id=1, source_target_pairs={{0,4},{4,0},{8,12},{12,8},{1,5},{5,1},{9,13},{13,9},{2,6},{6,2},{1... | collective-permute-start | bytes 49160 | tf_op jit(solution)/shard_map/ppermute | solution.py:66
  31.1 1.3 %collective-permute-done.9 = f32[2,2048]{1,0:T(2,128)S(1)} collective-permute-done((f32[2,2048]{1,0:T(2,128)S(1)}, f32[2,2048]{1,0:T(2,128)S(1)}, u32[]{:S(2)}, u32[]{:S(2)}) %collective-permute-start.9) | collective-permute-done | bytes 16416 | tf_op jit(solution)/shard_map/ppermute | solution.py:66
  32.4 1.5 %collective-permute-done.8 = f32[2,2048]{1,0:T(2,128)S(1)} collective-permute-done((f32[2,2048]{1,0:T(2,128)S(1)}, f32[2,2048]{1,0:T(2,128)S(1)}, u32[]{:S(2)}, u32[]{:S(2)}) %collective-permute-start.8) | collective-permute-done | bytes 16416 | tf_op jit(solution)/shard_map/ppermute | solution.py:66
  35.6 1.2 %collective-permute-done.10 = f32[2,2048]{1,0:T(2,128)S(1)} collective-permute-done((f32[2,2048]{1,0:T(2,128)S(1)}, f32[2,2048]{1,0:T(2,128)S(1)}, u32[]{:S(2)}, u32[]{:S(2)}) %collective-permute-start.10) | collective-permute-done | bytes 16416 | tf_op jit(solution)/shard_map/ppermute | solution.py:44
  36.8 1.6 %collective-permute-start.13 = (f32[2,2048]{1,0:T(2,128)S(1)}, f32[2,2048]{1,0:T(2,128)S(1)}, u32[]{:S(2)}, u32[]{:S(2)}) collective-permute-start(f32[2,2048]{1,0:T(2,128)S(1)} %get-tuple-element.118), channel_id=1, source_target_pairs={{0,12},{4,8},{8,4},{12,0},{1,13},{5,9},{9,5},{13,1},{2,14},{6,10},... | collective-permute-start | bytes 49160 | tf_op jit(solution)/shard_map/ppermute | solution.py:66
  39.3 2.0 %collective-permute-start.11 = (f32[2,2048]{1,0:T(2,128)S(1)}, f32[2,2048]{1,0:T(2,128)S(1)}, u32[]{:S(2)}, u32[]{:S(2)}) collective-permute-start(f32[2,2048]{1,0:T(2,128)S(1)} %get-tuple-element.118), channel_id=1, source_target_pairs={{0,4},{4,0},{8,12},{12,8},{1,5},{5,1},{9,13},{13,9},{2,6},{6,2},{1... | collective-permute-start | bytes 49160 | tf_op jit(solution)/shard_map/ppermute | solution.py:66
  41.3 1.3 %collective-permute-done.13 = f32[2,2048]{1,0:T(2,128)S(1)} collective-permute-done((f32[2,2048]{1,0:T(2,128)S(1)}, f32[2,2048]{1,0:T(2,128)S(1)}, u32[]{:S(2)}, u32[]{:S(2)}) %collective-permute-start.13) | collective-permute-done | bytes 16416 | tf_op jit(solution)/shard_map/ppermute | solution.py:66
  44.9 1.2 %collective-permute-done.14 = f32[2,2048]{1,0:T(2,128)S(1)} collective-permute-done((f32[2,2048]{1,0:T(2,128)S(1)}, f32[2,2048]{1,0:T(2,128)S(1)}, u32[]{:S(2)}, u32[]{:S(2)}) %collective-permute-start.14) | collective-permute-done | bytes 16416 | tf_op jit(solution)/shard_map/ppermute | solution.py:44
  46.1 2.4 %collective-permute-start.17 = (f32[2,2048]{1,0:T(2,128)S(1)}, f32[2,2048]{1,0:T(2,128)S(1)}, u32[]{:S(2)}, u32[]{:S(2)}) collective-permute-start(f32[2,2048]{1,0:T(2,128)S(1)} %get-tuple-element.116), channel_id=1, source_target_pairs={{0,12},{4,8},{8,4},{12,0},{1,13},{5,9},{9,5},{13,1},{2,14},{6,10},... | collective-permute-start | bytes 49160 | tf_op jit(solution)/shard_map/ppermute | solution.py:66
  49.5 1.1 %collective-permute-start.15 = (f32[2,2048]{1,0:T(2,128)S(1)}, f32[2,2048]{1,0:T(2,128)S(1)}, u32[]{:S(2)}, u32[]{:S(2)}) collective-permute-start(f32[2,2048]{1,0:T(2,128)S(1)} %get-tuple-element.116), channel_id=1, source_target_pairs={{0,4},{4,0},{8,12},{12,8},{1,5},{5,1},{9,13},{13,9},{2,6},{6,2},{1... | collective-permute-start | bytes 49160 | tf_op jit(solution)/shard_map/ppermute | solution.py:66
  50.6 1.2 %collective-permute-done.17 = f32[2,2048]{1,0:T(2,128)S(1)} collective-permute-done((f32[2,2048]{1,0:T(2,128)S(1)}, f32[2,2048]{1,0:T(2,128)S(1)}, u32[]{:S(2)}, u32[]{:S(2)}) %collective-permute-start.17) | collective-permute-done | bytes 16416 | tf_op jit(solution)/shard_map/ppermute | solution.py:66
  51.8 1.4 %collective-permute-done.16 = f32[2,2048]{1,0:T(2,128)S(1)} collective-permute-done((f32[2,2048]{1,0:T(2,128)S(1)}, f32[2,2048]{1,0:T(2,128)S(1)}, u32[]{:S(2)}, u32[]{:S(2)}) %collective-permute-start.16) | collective-permute-done | bytes 16416 | tf_op jit(solution)/shard_map/ppermute | solution.py:66
  55.0 1.2 %collective-permute-done.18 = f32[2,2048]{1,0:T(2,128)S(1)} collective-permute-done((f32[2,2048]{1,0:T(2,128)S(1)}, f32[2,2048]{1,0:T(2,128)S(1)}, u32[]{:S(2)}, u32[]{:S(2)}) %collective-permute-start.18) | collective-permute-done | bytes 16416 | tf_op jit(solution)/shard_map/ppermute | solution.py:44
  56.3 1.5 %collective-permute-start.21 = (f32[2,2048]{1,0:T(2,128)S(1)}, f32[2,2048]{1,0:T(2,128)S(1)}, u32[]{:S(2)}, u32[]{:S(2)}) collective-permute-start(f32[2,2048]{1,0:T(2,128)S(1)} %get-tuple-element.114), channel_id=1, source_target_pairs={{0,12},{4,8},{8,4},{12,0},{1,13},{5,9},{9,5},{13,1},{2,14},{6,10},... | collective-permute-start | bytes 49160 | tf_op jit(solution)/shard_map/ppermute | solution.py:66
  57.8 1.0 collective-permute-start.20
  58.8 2.0 %collective-permute-start.19 = (f32[2,2048]{1,0:T(2,128)S(1)}, f32[2,2048]{1,0:T(2,128)S(1)}, u32[]{:S(2)}, u32[]{:S(2)}) collective-permute-start(f32[2,2048]{1,0:T(2,128)S(1)} %get-tuple-element.114), channel_id=1, source_target_pairs={{0,4},{4,0},{8,12},{12,8},{1,5},{5,1},{9,13},{13,9},{2,6},{6,2},{1... | collective-permute-start | bytes 49160 | tf_op jit(solution)/shard_map/ppermute | solution.py:66
  60.7 1.2 %collective-permute-done.21 = f32[2,2048]{1,0:T(2,128)S(1)} collective-permute-done((f32[2,2048]{1,0:T(2,128)S(1)}, f32[2,2048]{1,0:T(2,128)S(1)}, u32[]{:S(2)}, u32[]{:S(2)}) %collective-permute-start.21) | collective-permute-done | bytes 16416 | tf_op jit(solution)/shard_map/ppermute | solution.py:66
  64.5 1.2 %collective-permute-done.22 = f32[2,2048]{1,0:T(2,128)S(1)} collective-permute-done((f32[2,2048]{1,0:T(2,128)S(1)}, f32[2,2048]{1,0:T(2,128)S(1)}, u32[]{:S(2)}, u32[]{:S(2)}) %collective-permute-start.22) | collective-permute-done | bytes 16416 | tf_op jit(solution)/shard_map/ppermute | solution.py:44
  65.7 2.4 %collective-permute-start.25 = (f32[2,2048]{1,0:T(2,128)S(1)}, f32[2,2048]{1,0:T(2,128)S(1)}, u32[]{:S(2)}, u32[]{:S(2)}) collective-permute-start(f32[2,2048]{1,0:T(2,128)S(1)} %get-tuple-element.112), channel_id=1, source_target_pairs={{0,12},{4,8},{8,4},{12,0},{1,13},{5,9},{9,5},{13,1},{2,14},{6,10},... | collective-permute-start | bytes 49160 | tf_op jit(solution)/shard_map/ppermute | solution.py:66
  68.2 1.0 collective-permute-start.24
  69.1 1.1 %collective-permute-start.23 = (f32[2,2048]{1,0:T(2,128)S(1)}, f32[2,2048]{1,0:T(2,128)S(1)}, u32[]{:S(2)}, u32[]{:S(2)}) collective-permute-start(f32[2,2048]{1,0:T(2,128)S(1)} %get-tuple-element.112), channel_id=1, source_target_pairs={{0,4},{4,0},{8,12},{12,8},{1,5},{5,1},{9,13},{13,9},{2,6},{6,2},{1... | collective-permute-start | bytes 49160 | tf_op jit(solution)/shard_map/ppermute | solution.py:66
  70.2 1.2 %collective-permute-done.25 = f32[2,2048]{1,0:T(2,128)S(1)} collective-permute-done((f32[2,2048]{1,0:T(2,128)S(1)}, f32[2,2048]{1,0:T(2,128)S(1)}, u32[]{:S(2)}, u32[]{:S(2)}) %collective-permute-start.25) | collective-permute-done | bytes 16416 | tf_op jit(solution)/shard_map/ppermute | solution.py:66
  71.4 1.4 %collective-permute-done.24 = f32[2,2048]{1,0:T(2,128)S(1)} collective-permute-done((f32[2,2048]{1,0:T(2,128)S(1)}, f32[2,2048]{1,0:T(2,128)S(1)}, u32[]{:S(2)}, u32[]{:S(2)}) %collective-permute-start.24) | collective-permute-done | bytes 16416 | tf_op jit(solution)/shard_map/ppermute | solution.py:66
  74.6 1.2 %collective-permute-done.26 = f32[2,2048]{1,0:T(2,128)S(1)} collective-permute-done((f32[2,2048]{1,0:T(2,128)S(1)}, f32[2,2048]{1,0:T(2,128)S(1)}, u32[]{:S(2)}, u32[]{:S(2)}) %collective-permute-start.26) | collective-permute-done | bytes 16416 | tf_op jit(solution)/shard_map/ppermute | solution.py:44
  75.9 1.5 %collective-permute-start.29 = (f32[2,2048]{1,0:T(2,128)S(1)}, f32[2,2048]{1,0:T(2,128)S(1)}, u32[]{:S(2)}, u32[]{:S(2)}) collective-permute-start(f32[2,2048]{1,0:T(2,128)S(1)} %get-tuple-element.110), channel_id=1, source_target_pairs={{0,12},{4,8},{8,4},{12,0},{1,13},{5,9},{9,5},{13,1},{2,14},{6,10},... | collective-permute-start | bytes 49160 | tf_op jit(solution)/shard_map/ppermute | solution.py:66
  77.4 1.0 collective-permute-start.28
  78.4 2.0 %collective-permute-start.27 = (f32[2,2048]{1,0:T(2,128)S(1)}, f32[2,2048]{1,0:T(2,128)S(1)}, u32[]{:S(2)}, u32[]{:S(2)}) collective-permute-start(f32[2,2048]{1,0:T(2,128)S(1)} %get-tuple-element.110), channel_id=1, source_target_pairs={{0,4},{4,0},{8,12},{12,8},{1,5},{5,1},{9,13},{13,9},{2,6},{6,2},{1... | collective-permute-start | bytes 49160 | tf_op jit(solution)/shard_map/ppermute | solution.py:66
  80.3 1.2 %collective-permute-done.29 = f32[2,2048]{1,0:T(2,128)S(1)} collective-permute-done((f32[2,2048]{1,0:T(2,128)S(1)}, f32[2,2048]{1,0:T(2,128)S(1)}, u32[]{:S(2)}, u32[]{:S(2)}) %collective-permute-start.29) | collective-permute-done | bytes 16416 | tf_op jit(solution)/shard_map/ppermute | solution.py:66
  83.9 1.2 %collective-permute-done.30 = f32[2,2048]{1,0:T(2,128)S(1)} collective-permute-done((f32[2,2048]{1,0:T(2,128)S(1)}, f32[2,2048]{1,0:T(2,128)S(1)}, u32[]{:S(2)}, u32[]{:S(2)}) %collective-permute-start.30) | collective-permute-done | bytes 16416 | tf_op jit(solution)/shard_map/ppermute | solution.py:44
  85.1 2.4 %collective-permute-start.33 = (f32[2,2048]{1,0:T(2,128)S(1)}, f32[2,2048]{1,0:T(2,128)S(1)}, u32[]{:S(2)}, u32[]{:S(2)}) collective-permute-start(f32[2,2048]{1,0:T(2,128)S(1)} %get-tuple-element.108), channel_id=1, source_target_pairs={{0,12},{4,8},{8,4},{12,0},{1,13},{5,9},{9,5},{13,1},{2,14},{6,10},... | collective-permute-start | bytes 49160 | tf_op jit(solution)/shard_map/ppermute | solution.py:66
  88.5 1.1 %collective-permute-start.31 = (f32[2,2048]{1,0:T(2,128)S(1)}, f32[2,2048]{1,0:T(2,128)S(1)}, u32[]{:S(2)}, u32[]{:S(2)}) collective-permute-start(f32[2,2048]{1,0:T(2,128)S(1)} %get-tuple-element.108), channel_id=1, source_target_pairs={{0,4},{4,0},{8,12},{12,8},{1,5},{5,1},{9,13},{13,9},{2,6},{6,2},{1... | collective-permute-start | bytes 49160 | tf_op jit(solution)/shard_map/ppermute | solution.py:66
  89.6 1.2 %collective-permute-done.33 = f32[2,2048]{1,0:T(2,128)S(1)} collective-permute-done((f32[2,2048]{1,0:T(2,128)S(1)}, f32[2,2048]{1,0:T(2,128)S(1)}, u32[]{:S(2)}, u32[]{:S(2)}) %collective-permute-start.33) | collective-permute-done | bytes 16416 | tf_op jit(solution)/shard_map/ppermute | solution.py:66
  90.8 1.4 %collective-permute-done.32 = f32[2,2048]{1,0:T(2,128)S(1)} collective-permute-done((f32[2,2048]{1,0:T(2,128)S(1)}, f32[2,2048]{1,0:T(2,128)S(1)}, u32[]{:S(2)}, u32[]{:S(2)}) %collective-permute-start.32) | collective-permute-done | bytes 16416 | tf_op jit(solution)/shard_map/ppermute | solution.py:66
  94.0 1.0 fusion.4
  95.4 1.3 %collective-permute-done.34 = f32[4,128,66]{1,0,2:T(4,128)S(1)} collective-permute-done((f32[4,128,66]{1,0,2:T(4,128)S(1)}, f32[4,128,66]{1,0,2:T(4,128)S(1)}, u32[]{:S(2)}, u32[]{:S(2)}) %collective-permute-start.34) | collective-permute-done | bytes 135200 | tf_op jit(solution)/shard_map/ppermute | solution.py:191
  97.0 1.5 %collective-permute-start.37 = (f32[128,66]{0,1:T(8,128)S(1)}, f32[128,66]{0,1:T(8,128)S(1)}, u32[]{:S(2)}, u32[]{:S(2)}) collective-permute-start(f32[128,66]{0,1:T(8,128)S(1)} %bitcast.203), channel_id=1, source_target_pairs={{0,12},{4,8},{8,4},{12,0},{1,13},{5,9},{9,5},{13,1},{2,14},{6,10},... | collective-permute-start | bytes 101384 | tf_op jit(solution)/shard_map/ppermute | solution.py:152
  99.5 2.0 %collective-permute-start.35 = (f32[128,66]{0,1:T(8,128)S(1)}, f32[128,66]{0,1:T(8,128)S(1)}, u32[]{:S(2)}, u32[]{:S(2)}) collective-permute-start(f32[128,66]{0,1:T(8,128)S(1)} %bitcast.205), channel_id=1, source_target_pairs={{0,4},{4,0},{8,12},{12,8},{1,5},{5,1},{9,13},{13,9},{2,6},{6,2},{1... | collective-permute-start | bytes 101384 | tf_op jit(solution)/shard_map/ppermute | solution.py:152
  102.1 1.0 collective-permute-done.37
  (159 shorter events, 27.5 us)
Async XLA Ops:
  0.6 5.6 %copy-start = (f32[1024,64]{0,1:T(8,128)S(1)}, f32[1024,64]{0,1:T(8,128)}, u32[]{:S(2)}) copy-start(f32[1024,64]{0,1:T(8,128)} %param.5) | copy-start | bytes 786436
  3.2 3.4 %copy-start.4 = (f32[1024]{0:T(1024)S(1)}, f32[1024]{0:T(1024)}, u32[]{:S(2)}) copy-start(f32[1024]{0:T(1024)} %param.6) | copy-start | bytes 12292
  5.7 3.5 %collective-permute-start.1 = (f32[2,1024]{1,0:T(2,128)S(1)}, f32[2,1024]{1,0:T(2,128)S(1)}, u32[]{:S(2)}, u32[]{:S(2)}) collective-permute-start(f32[2,1024]{1,0:T(2,128)S(1)} %pad_maximum_fusion.26), channel_id=1, source_target_pairs={{0,1},{1,0},{2,3},{3,2},{4,5},{5,4},{6,7},{7,6},{8,9},{9,8},{10,11... | collective-permute-start | bytes 24584 | tf_op jit(solution)/shard_map/ppermute | solution.py:44
  6.6 10.9 %collective-permute-start = (f32[520,128]{1,0:T(8,128)S(1)}, f32[520,128]{1,0:T(8,128)S(1)}, u32[]{:S(2)}, u32[]{:S(2)}) collective-permute-start(f32[520,128]{1,0:T(8,128)S(1)} %pad_maximum_fusion.2), channel_id=1, source_target_pairs={{0,2},{2,0},{1,3},{3,1},{4,6},{6,4},{5,7},{7,5},{8,10},{10,8},{9,1... | collective-permute-start | bytes 798728 | tf_op jit(solution)/shard_map/ppermute | solution.py:256
  9.2 5.5 %collective-permute-start.4 = (f32[2,1024]{1,0:T(2,128)S(1)}, f32[2,1024]{1,0:T(2,128)S(1)}, u32[]{:S(2)}, u32[]{:S(2)}) collective-permute-start(f32[2,1024]{1,0:T(2,128)S(1)} %get-tuple-element.124), channel_id=1, source_target_pairs={{0,12},{4,8},{8,4},{12,0},{1,13},{5,9},{9,5},{13,1},{2,14},{6,10},... | collective-permute-start | bytes 24584 | tf_op jit(solution)/shard_map/ppermute | solution.py:66
  12.9 4.5 %collective-permute-start.3 = (f32[2,1024]{1,0:T(2,128)S(1)}, f32[2,1024]{1,0:T(2,128)S(1)}, u32[]{:S(2)}, u32[]{:S(2)}) collective-permute-start(f32[2,1024]{1,0:T(2,128)S(1)} %get-tuple-element.124), channel_id=1, source_target_pairs={{0,8},{4,12},{8,0},{12,4},{1,9},{5,13},{9,1},{13,5},{2,10},{6,14},... | collective-permute-start | bytes 24584 | tf_op jit(solution)/shard_map/ppermute | solution.py:66
  12.9 4.5 %collective-permute-start.2 = (f32[2,1024]{1,0:T(2,128)S(1)}, f32[2,1024]{1,0:T(2,128)S(1)}, u32[]{:S(2)}, u32[]{:S(2)}) collective-permute-start(f32[2,1024]{1,0:T(2,128)S(1)} %get-tuple-element.124), channel_id=1, source_target_pairs={{0,4},{4,0},{8,12},{12,8},{1,5},{5,1},{9,13},{13,9},{2,6},{6,2},{1... | collective-permute-start | bytes 24584 | tf_op jit(solution)/shard_map/ppermute | solution.py:66
  17.6 0.8 copy-start.1
  18.4 6.2 %copy-start.2 = (f32[256]{0:T(256)S(1)}, f32[256]{0:T(256)}, u32[]{:S(2)}) copy-start(f32[256]{0:T(256)} %param.8) | copy-start | bytes 3076
  21.0 3.7 %collective-permute-start.5 = (f32[2,256]{1,0:T(2,128)S(1)}, f32[2,256]{1,0:T(2,128)S(1)}, u32[]{:S(2)}, u32[]{:S(2)}) collective-permute-start(f32[2,256]{1,0:T(2,128)S(1)} %pad_maximum_fusion.28), channel_id=1, source_target_pairs={{0,2},{2,0},{1,3},{3,1},{4,6},{6,4},{5,7},{7,5},{8,10},{10,8},{9,1... | collective-permute-start | bytes 6152 | tf_op jit(solution)/shard_map/ppermute | solution.py:44
  25.4 1.2 %collective-permute-start.6 = (f32[2,2048]{1,0:T(2,128)S(1)}, f32[2,2048]{1,0:T(2,128)S(1)}, u32[]{:S(2)}, u32[]{:S(2)}) collective-permute-start(f32[2,2048]{1,0:T(2,128)S(1)} %pad_maximum_fusion.12), channel_id=1, source_target_pairs={{0,1},{1,0},{2,3},{3,2},{4,5},{5,4},{6,7},{7,6},{8,9},{9,8},{10,11... | collective-permute-start | bytes 49160 | tf_op jit(solution)/shard_map/ppermute | solution.py:44
  26.7 5.7 %collective-permute-start.9 = (f32[2,2048]{1,0:T(2,128)S(1)}, f32[2,2048]{1,0:T(2,128)S(1)}, u32[]{:S(2)}, u32[]{:S(2)}) collective-permute-start(f32[2,2048]{1,0:T(2,128)S(1)} %get-tuple-element.120), channel_id=1, source_target_pairs={{0,12},{4,8},{8,4},{12,0},{1,13},{5,9},{9,5},{13,1},{2,14},{6,10},... | collective-permute-start | bytes 49160 | tf_op jit(solution)/shard_map/ppermute | solution.py:66
  29.3 4.6 %collective-permute-start.8 = (f32[2,2048]{1,0:T(2,128)S(1)}, f32[2,2048]{1,0:T(2,128)S(1)}, u32[]{:S(2)}, u32[]{:S(2)}) collective-permute-start(f32[2,2048]{1,0:T(2,128)S(1)} %get-tuple-element.120), channel_id=1, source_target_pairs={{0,8},{4,12},{8,0},{12,4},{1,9},{5,13},{9,1},{13,5},{2,10},{6,14},... | collective-permute-start | bytes 49160 | tf_op jit(solution)/shard_map/ppermute | solution.py:66
  29.3 4.6 %collective-permute-start.7 = (f32[2,2048]{1,0:T(2,128)S(1)}, f32[2,2048]{1,0:T(2,128)S(1)}, u32[]{:S(2)}, u32[]{:S(2)}) collective-permute-start(f32[2,2048]{1,0:T(2,128)S(1)} %get-tuple-element.120), channel_id=1, source_target_pairs={{0,4},{4,0},{8,12},{12,8},{1,5},{5,1},{9,13},{13,9},{2,6},{6,2},{1... | collective-permute-start | bytes 49160 | tf_op jit(solution)/shard_map/ppermute | solution.py:66
  35.5 1.2 %collective-permute-start.10 = (f32[2,2048]{1,0:T(2,128)S(1)}, f32[2,2048]{1,0:T(2,128)S(1)}, u32[]{:S(2)}, u32[]{:S(2)}) collective-permute-start(f32[2,2048]{1,0:T(2,128)S(1)} %pad_maximum_fusion.14), channel_id=1, source_target_pairs={{0,1},{1,0},{2,3},{3,2},{4,5},{5,4},{6,7},{7,6},{8,9},{9,8},{10,11... | collective-permute-start | bytes 49160 | tf_op jit(solution)/shard_map/ppermute | solution.py:44
  36.8 5.7 %collective-permute-start.13 = (f32[2,2048]{1,0:T(2,128)S(1)}, f32[2,2048]{1,0:T(2,128)S(1)}, u32[]{:S(2)}, u32[]{:S(2)}) collective-permute-start(f32[2,2048]{1,0:T(2,128)S(1)} %get-tuple-element.118), channel_id=1, source_target_pairs={{0,12},{4,8},{8,4},{12,0},{1,13},{5,9},{9,5},{13,1},{2,14},{6,10},... | collective-permute-start | bytes 49160 | tf_op jit(solution)/shard_map/ppermute | solution.py:66
  38.4 4.6 %collective-permute-start.12 = (f32[2,2048]{1,0:T(2,128)S(1)}, f32[2,2048]{1,0:T(2,128)S(1)}, u32[]{:S(2)}, u32[]{:S(2)}) collective-permute-start(f32[2,2048]{1,0:T(2,128)S(1)} %get-tuple-element.118), channel_id=1, source_target_pairs={{0,8},{4,12},{8,0},{12,4},{1,9},{5,13},{9,1},{13,5},{2,10},{6,14},... | collective-permute-start | bytes 49160 | tf_op jit(solution)/shard_map/ppermute | solution.py:66
  39.3 3.9 %collective-permute-start.11 = (f32[2,2048]{1,0:T(2,128)S(1)}, f32[2,2048]{1,0:T(2,128)S(1)}, u32[]{:S(2)}, u32[]{:S(2)}) collective-permute-start(f32[2,2048]{1,0:T(2,128)S(1)} %get-tuple-element.118), channel_id=1, source_target_pairs={{0,4},{4,0},{8,12},{12,8},{1,5},{5,1},{9,13},{13,9},{2,6},{6,2},{1... | collective-permute-start | bytes 49160 | tf_op jit(solution)/shard_map/ppermute | solution.py:66
  44.8 1.2 %collective-permute-start.14 = (f32[2,2048]{1,0:T(2,128)S(1)}, f32[2,2048]{1,0:T(2,128)S(1)}, u32[]{:S(2)}, u32[]{:S(2)}) collective-permute-start(f32[2,2048]{1,0:T(2,128)S(1)} %pad_maximum_fusion.16), channel_id=1, source_target_pairs={{0,1},{1,0},{2,3},{3,2},{4,5},{5,4},{6,7},{7,6},{8,9},{9,8},{10,11... | collective-permute-start | bytes 49160 | tf_op jit(solution)/shard_map/ppermute | solution.py:44
  46.1 5.7 %collective-permute-start.17 = (f32[2,2048]{1,0:T(2,128)S(1)}, f32[2,2048]{1,0:T(2,128)S(1)}, u32[]{:S(2)}, u32[]{:S(2)}) collective-permute-start(f32[2,2048]{1,0:T(2,128)S(1)} %get-tuple-element.116), channel_id=1, source_target_pairs={{0,12},{4,8},{8,4},{12,0},{1,13},{5,9},{9,5},{13,1},{2,14},{6,10},... | collective-permute-start | bytes 49160 | tf_op jit(solution)/shard_map/ppermute | solution.py:66
  48.6 4.7 %collective-permute-start.16 = (f32[2,2048]{1,0:T(2,128)S(1)}, f32[2,2048]{1,0:T(2,128)S(1)}, u32[]{:S(2)}, u32[]{:S(2)}) collective-permute-start(f32[2,2048]{1,0:T(2,128)S(1)} %get-tuple-element.116), channel_id=1, source_target_pairs={{0,8},{4,12},{8,0},{12,4},{1,9},{5,13},{9,1},{13,5},{2,10},{6,14},... | collective-permute-start | bytes 49160 | tf_op jit(solution)/shard_map/ppermute | solution.py:66
  49.5 3.9 %collective-permute-start.15 = (f32[2,2048]{1,0:T(2,128)S(1)}, f32[2,2048]{1,0:T(2,128)S(1)}, u32[]{:S(2)}, u32[]{:S(2)}) collective-permute-start(f32[2,2048]{1,0:T(2,128)S(1)} %get-tuple-element.116), channel_id=1, source_target_pairs={{0,4},{4,0},{8,12},{12,8},{1,5},{5,1},{9,13},{13,9},{2,6},{6,2},{1... | collective-permute-start | bytes 49160 | tf_op jit(solution)/shard_map/ppermute | solution.py:66
  55.0 1.2 %collective-permute-start.18 = (f32[2,2048]{1,0:T(2,128)S(1)}, f32[2,2048]{1,0:T(2,128)S(1)}, u32[]{:S(2)}, u32[]{:S(2)}) collective-permute-start(f32[2,2048]{1,0:T(2,128)S(1)} %pad_maximum_fusion.18), channel_id=1, source_target_pairs={{0,1},{1,0},{2,3},{3,2},{4,5},{5,4},{6,7},{7,6},{8,9},{9,8},{10,11... | collective-permute-start | bytes 49160 | tf_op jit(solution)/shard_map/ppermute | solution.py:44
  56.3 5.6 %collective-permute-start.21 = (f32[2,2048]{1,0:T(2,128)S(1)}, f32[2,2048]{1,0:T(2,128)S(1)}, u32[]{:S(2)}, u32[]{:S(2)}) collective-permute-start(f32[2,2048]{1,0:T(2,128)S(1)} %get-tuple-element.114), channel_id=1, source_target_pairs={{0,12},{4,8},{8,4},{12,0},{1,13},{5,9},{9,5},{13,1},{2,14},{6,10},... | collective-permute-start | bytes 49160 | tf_op jit(solution)/shard_map/ppermute | solution.py:66
  57.8 4.6 %collective-permute-start.20 = (f32[2,2048]{1,0:T(2,128)S(1)}, f32[2,2048]{1,0:T(2,128)S(1)}, u32[]{:S(2)}, u32[]{:S(2)}) collective-permute-start(f32[2,2048]{1,0:T(2,128)S(1)} %get-tuple-element.114), channel_id=1, source_target_pairs={{0,8},{4,12},{8,0},{12,4},{1,9},{5,13},{9,1},{13,5},{2,10},{6,14},... | collective-permute-start | bytes 49160 | tf_op jit(solution)/shard_map/ppermute | solution.py:66
  58.8 3.9 %collective-permute-start.19 = (f32[2,2048]{1,0:T(2,128)S(1)}, f32[2,2048]{1,0:T(2,128)S(1)}, u32[]{:S(2)}, u32[]{:S(2)}) collective-permute-start(f32[2,2048]{1,0:T(2,128)S(1)} %get-tuple-element.114), channel_id=1, source_target_pairs={{0,4},{4,0},{8,12},{12,8},{1,5},{5,1},{9,13},{13,9},{2,6},{6,2},{1... | collective-permute-start | bytes 49160 | tf_op jit(solution)/shard_map/ppermute | solution.py:66
  64.4 1.2 %collective-permute-start.22 = (f32[2,2048]{1,0:T(2,128)S(1)}, f32[2,2048]{1,0:T(2,128)S(1)}, u32[]{:S(2)}, u32[]{:S(2)}) collective-permute-start(f32[2,2048]{1,0:T(2,128)S(1)} %pad_maximum_fusion.20), channel_id=1, source_target_pairs={{0,1},{1,0},{2,3},{3,2},{4,5},{5,4},{6,7},{7,6},{8,9},{9,8},{10,11... | collective-permute-start | bytes 49160 | tf_op jit(solution)/shard_map/ppermute | solution.py:44
  65.7 5.7 %collective-permute-start.25 = (f32[2,2048]{1,0:T(2,128)S(1)}, f32[2,2048]{1,0:T(2,128)S(1)}, u32[]{:S(2)}, u32[]{:S(2)}) collective-permute-start(f32[2,2048]{1,0:T(2,128)S(1)} %get-tuple-element.112), channel_id=1, source_target_pairs={{0,12},{4,8},{8,4},{12,0},{1,13},{5,9},{9,5},{13,1},{2,14},{6,10},... | collective-permute-start | bytes 49160 | tf_op jit(solution)/shard_map/ppermute | solution.py:66
  68.2 4.6 %collective-permute-start.24 = (f32[2,2048]{1,0:T(2,128)S(1)}, f32[2,2048]{1,0:T(2,128)S(1)}, u32[]{:S(2)}, u32[]{:S(2)}) collective-permute-start(f32[2,2048]{1,0:T(2,128)S(1)} %get-tuple-element.112), channel_id=1, source_target_pairs={{0,8},{4,12},{8,0},{12,4},{1,9},{5,13},{9,1},{13,5},{2,10},{6,14},... | collective-permute-start | bytes 49160 | tf_op jit(solution)/shard_map/ppermute | solution.py:66
  69.1 3.9 %collective-permute-start.23 = (f32[2,2048]{1,0:T(2,128)S(1)}, f32[2,2048]{1,0:T(2,128)S(1)}, u32[]{:S(2)}, u32[]{:S(2)}) collective-permute-start(f32[2,2048]{1,0:T(2,128)S(1)} %get-tuple-element.112), channel_id=1, source_target_pairs={{0,4},{4,0},{8,12},{12,8},{1,5},{5,1},{9,13},{13,9},{2,6},{6,2},{1... | collective-permute-start | bytes 49160 | tf_op jit(solution)/shard_map/ppermute | solution.py:66
  74.6 1.2 %collective-permute-start.26 = (f32[2,2048]{1,0:T(2,128)S(1)}, f32[2,2048]{1,0:T(2,128)S(1)}, u32[]{:S(2)}, u32[]{:S(2)}) collective-permute-start(f32[2,2048]{1,0:T(2,128)S(1)} %pad_maximum_fusion.22), channel_id=1, source_target_pairs={{0,1},{1,0},{2,3},{3,2},{4,5},{5,4},{6,7},{7,6},{8,9},{9,8},{10,11... | collective-permute-start | bytes 49160 | tf_op jit(solution)/shard_map/ppermute | solution.py:44
  75.9 5.6 %collective-permute-start.29 = (f32[2,2048]{1,0:T(2,128)S(1)}, f32[2,2048]{1,0:T(2,128)S(1)}, u32[]{:S(2)}, u32[]{:S(2)}) collective-permute-start(f32[2,2048]{1,0:T(2,128)S(1)} %get-tuple-element.110), channel_id=1, source_target_pairs={{0,12},{4,8},{8,4},{12,0},{1,13},{5,9},{9,5},{13,1},{2,14},{6,10},... | collective-permute-start | bytes 49160 | tf_op jit(solution)/shard_map/ppermute | solution.py:66
  77.4 4.6 %collective-permute-start.28 = (f32[2,2048]{1,0:T(2,128)S(1)}, f32[2,2048]{1,0:T(2,128)S(1)}, u32[]{:S(2)}, u32[]{:S(2)}) collective-permute-start(f32[2,2048]{1,0:T(2,128)S(1)} %get-tuple-element.110), channel_id=1, source_target_pairs={{0,8},{4,12},{8,0},{12,4},{1,9},{5,13},{9,1},{13,5},{2,10},{6,14},... | collective-permute-start | bytes 49160 | tf_op jit(solution)/shard_map/ppermute | solution.py:66
  78.4 3.9 %collective-permute-start.27 = (f32[2,2048]{1,0:T(2,128)S(1)}, f32[2,2048]{1,0:T(2,128)S(1)}, u32[]{:S(2)}, u32[]{:S(2)}) collective-permute-start(f32[2,2048]{1,0:T(2,128)S(1)} %get-tuple-element.110), channel_id=1, source_target_pairs={{0,4},{4,0},{8,12},{12,8},{1,5},{5,1},{9,13},{13,9},{2,6},{6,2},{1... | collective-permute-start | bytes 49160 | tf_op jit(solution)/shard_map/ppermute | solution.py:66
  83.8 1.2 %collective-permute-start.30 = (f32[2,2048]{1,0:T(2,128)S(1)}, f32[2,2048]{1,0:T(2,128)S(1)}, u32[]{:S(2)}, u32[]{:S(2)}) collective-permute-start(f32[2,2048]{1,0:T(2,128)S(1)} %pad_maximum_fusion.24), channel_id=1, source_target_pairs={{0,1},{1,0},{2,3},{3,2},{4,5},{5,4},{6,7},{7,6},{8,9},{9,8},{10,11... | collective-permute-start | bytes 49160 | tf_op jit(solution)/shard_map/ppermute | solution.py:44
  85.1 5.7 %collective-permute-start.33 = (f32[2,2048]{1,0:T(2,128)S(1)}, f32[2,2048]{1,0:T(2,128)S(1)}, u32[]{:S(2)}, u32[]{:S(2)}) collective-permute-start(f32[2,2048]{1,0:T(2,128)S(1)} %get-tuple-element.108), channel_id=1, source_target_pairs={{0,12},{4,8},{8,4},{12,0},{1,13},{5,9},{9,5},{13,1},{2,14},{6,10},... | collective-permute-start | bytes 49160 | tf_op jit(solution)/shard_map/ppermute | solution.py:66
  87.6 4.6 %collective-permute-start.32 = (f32[2,2048]{1,0:T(2,128)S(1)}, f32[2,2048]{1,0:T(2,128)S(1)}, u32[]{:S(2)}, u32[]{:S(2)}) collective-permute-start(f32[2,2048]{1,0:T(2,128)S(1)} %get-tuple-element.108), channel_id=1, source_target_pairs={{0,8},{4,12},{8,0},{12,4},{1,9},{5,13},{9,1},{13,5},{2,10},{6,14},... | collective-permute-start | bytes 49160 | tf_op jit(solution)/shard_map/ppermute | solution.py:66
  88.5 3.9 %collective-permute-start.31 = (f32[2,2048]{1,0:T(2,128)S(1)}, f32[2,2048]{1,0:T(2,128)S(1)}, u32[]{:S(2)}, u32[]{:S(2)}) collective-permute-start(f32[2,2048]{1,0:T(2,128)S(1)} %get-tuple-element.108), channel_id=1, source_target_pairs={{0,4},{4,0},{8,12},{12,8},{1,5},{5,1},{9,13},{13,9},{2,6},{6,2},{1... | collective-permute-start | bytes 49160 | tf_op jit(solution)/shard_map/ppermute | solution.py:66
  92.8 1.2 %copy-start.3 = (f32[256,64]{0,1:T(8,128)S(1)}, f32[256,64]{0,1:T(8,128)}, u32[]{:S(2)}) copy-start(f32[256,64]{0,1:T(8,128)} %param.9) | copy-start | bytes 196612
  95.4 1.4 %collective-permute-start.34 = (f32[4,128,66]{1,0,2:T(4,128)S(1)}, f32[4,128,66]{1,0,2:T(4,128)S(1)}, u32[]{:S(2)}, u32[]{:S(2)}) collective-permute-start(f32[4,128,66]{1,0,2:T(4,128)S(1)} %get-tuple-element.16), channel_id=1, source_target_pairs={{0,1},{1,0},{2,3},{3,2},{4,5},{5,4},{6,7},{7,6},{8,9},{9,8},{10,11... | collective-permute-start | bytes 405512 | tf_op jit(solution)/shard_map/ppermute | solution.py:191
  97.0 6.1 %collective-permute-start.37 = (f32[128,66]{0,1:T(8,128)S(1)}, f32[128,66]{0,1:T(8,128)S(1)}, u32[]{:S(2)}, u32[]{:S(2)}) collective-permute-start(f32[128,66]{0,1:T(8,128)S(1)} %bitcast.203), channel_id=1, source_target_pairs={{0,12},{4,8},{8,4},{12,0},{1,13},{5,9},{9,5},{13,1},{2,14},{6,10},... | collective-permute-start | bytes 101384 | tf_op jit(solution)/shard_map/ppermute | solution.py:152
  98.6 5.4 %collective-permute-start.36 = (f32[128,66]{0,1:T(8,128)S(1)}, f32[128,66]{0,1:T(8,128)S(1)}, u32[]{:S(2)}, u32[]{:S(2)}) collective-permute-start(f32[128,66]{0,1:T(8,128)S(1)} %bitcast.204), channel_id=1, source_target_pairs={{0,8},{4,12},{8,0},{12,4},{1,9},{5,13},{9,1},{13,5},{2,10},{6,14},... | collective-permute-start | bytes 101384 | tf_op jit(solution)/shard_map/ppermute | solution.py:152
  99.5 4.5 %collective-permute-start.35 = (f32[128,66]{0,1:T(8,128)S(1)}, f32[128,66]{0,1:T(8,128)S(1)}, u32[]{:S(2)}, u32[]{:S(2)}) collective-permute-start(f32[128,66]{0,1:T(8,128)S(1)} %bitcast.205), channel_id=1, source_target_pairs={{0,4},{4,0},{8,12},{12,8},{1,5},{5,1},{9,13},{13,9},{2,6},{6,2},{1... | collective-permute-start | bytes 101384 | tf_op jit(solution)/shard_map/ppermute | solution.py:152
